TPU v7x, 256 devices: a whole 4x4x8 slice. The times are simulated.
256 devices in a mesh: row: 8 (over y, core), col: 32 (over x, z).
Axes of the slice: x: 4, y: 4, z: 8, core: 2. Of those that a mesh axis runs over, the one named last changes fastest.
Arguments:
- trailing_adjoint: float32 [12288, 12288], P('row', 'col'), may hold values from -3 to 3, as said below
- panel: float32 [12288, 256], P(('row', 'col')), may hold values from -0.0546875 to 0.0546875
- panel_adjoint: float32 [12288, 256], P(('row', 'col')), may hold values from -6 to 6
- diag_factor: float32 [256, 256], replicated, may hold values from -1 to 2, as said below
- diag_adjoint: float32 [256, 256], P('row', 'col'), may hold values from -6 to 6
Outputs:
- off_adjoint: float32 [12288, 256], P(('row', 'col'))
- block_adjoint: float32 [256, 256], replicated
Inputs may be any that keep to these rules, and one draw needn't show every extreme that they name: `trailing_adjoint`: symmetric. `diag_factor`: lower triangular with diagonal entries from 1 to 2.
All inputs are finite; a program needn't handle non-finite values.
Results may differ from a plain program's by a relative error of at most 0.000071.
Values sent between devices are 32-bit elements; how exact they have to be, the bound alone decides.
No kernel may reach another device: no remote copies, remote signals or barrier semaphores. Data moves between devices by JAX's collectives and lax.ppermute only.
A program may use at most 64 MiB of HBM per device.

v0:
```python
import jax
import jax.numpy as jnp
from jax import lax
from jax.sharding import PartitionSpec as P


def right_solve(factor, rows):
    return jax.scipy.linalg.solve_triangular(factor, rows.T, lower=True, trans=1).T


def left_solve(factor, matrix):
    return jax.scipy.linalg.solve_triangular(factor, matrix, lower=True, trans=1)


def diagonal_adjoint(factor, adjoint):
    product = jnp.dot(
        factor.T, adjoint, precision=lax.Precision.HIGHEST, preferred_element_type=jnp.float32
    )
    lower = jnp.tril(product) - 0.5 * jnp.diag(jnp.diag(product))
    symmetric = lower + lower.T
    half = left_solve(factor, symmetric)
    return 0.5 * left_solve(factor, half.T).T


def body(trailing_adjoint, panel, panel_adjoint, diag_factor, diag_adjoint):
    nrows = lax.axis_size("row")
    stretch = panel.shape[0]
    span = stretch * nrows
    col_index = lax.axis_index("col")
    gathered = lax.all_gather(panel, ("row", "col"), axis=0, tiled=True)
    column_rows = lax.dynamic_slice_in_dim(gathered, col_index * span, span, 0)
    product = lax.psum_scatter(
        jnp.dot(
            trailing_adjoint,
            column_rows,
            precision=lax.Precision.HIGHEST,
            preferred_element_type=jnp.float32,
        ),
        "col",
        scatter_dimension=0,
        tiled=True,
    )
    updated = panel_adjoint - 2.0 * product
    off_adjoint = right_solve(diag_factor, updated)
    local_term = jnp.dot(
        off_adjoint.T, panel, precision=lax.Precision.HIGHEST, preferred_element_type=jnp.float32
    )
    row_piece = lax.all_gather(diag_adjoint, "col", axis=1, tiled=True)
    full_adjoint = lax.all_gather(row_piece, "row", axis=0, tiled=True)
    total = lax.psum(local_term, ("row", "col"))
    accumulated = full_adjoint - total
    return (off_adjoint, diagonal_adjoint(diag_factor, accumulated))


def solution(mesh):
    return jax.shard_map(
        body,
        mesh=mesh,
        in_specs=(
            P("row", "col"),
            P(("row", "col"), None),
            P(("row", "col"), None),
            P(),
            P("row", "col"),
        ),
        out_specs=(P(("row", "col"), None), P()),
        check_vma=False,
    )
```

profile of v0, /device:TPU:1, one launch (start us, length us, event | category | flops | bytes accessed | tf_op | source)
XLA Modules:
  0.0 632.0 jit_solution(16761037603501634626)
XLA Ops:
  7.2 0.7 all-gather.2.cloned.1.call-update
  8.0 128.7 %all-gather.2.cloned.1.call-done = f32[12288,256]{1,0:T(8,128)} async-done(((f32[48,256]{1,0:T(8,128)}), f32[12288,256]{1,0:T(8,128)}) %all-gather.2.cloned.1.call-update) | async-done | bytes 12582928 | tf_op jit(solution)/shard_map/all_gather | solution.py:30
  136.7 6.2 convolution_bitcast_fusion
  142.8 3.1 copy.24
  146.0 34.7 %all_gather.10 = f32[32,256]{0,1:T(8,128)S(1)} all-gather(f32[32,8]{0,1:T(8,128)S(1)} %copy-done.4), channel_id=1, replica_groups=mesh['row'=8,'col'=32] {'col'}, dimensions={1}, use_global_device_ids=true | all-gather | bytes 33792 | tf_op jit(solution)/shard_map/all_gather | solution.py:48
  180.9 4.1 while.5
  180.9 0.6 fusion.32
  181.5 1.4 bitcast_dynamic-update-slice_fusion.2
  182.9 0.6 fusion.32
  183.5 1.4 bitcast_dynamic-update-slice_fusion.2
  185.0 19.7 %custom-call.7 = f32[2,128,128]{1,2,0:T(8,128)S(1)} custom-call(f32[2,128,128]{2,1,0:T(8,128)S(1)} %get-tuple-element.18), custom_call_target="InvertDiagBlocksLowerTriangular" | custom-call | tf_op jit(solution)/shard_map/jit(_solve_triangular)/triangular_solve | solution.py:8
  204.7 21.0 %all_gather.11 = f32[256,256]{1,0:T(8,128)S(1)} all-gather(f32[32,256]{1,0:T(8,128)S(1)} %copy.19), channel_id=1, replica_groups=mesh['row'=8,'col'=32] {'row'}, dimensions={0}, use_global_device_ids=true | all-gather | bytes 294912 | tf_op jit(solution)/shard_map/all_gather | solution.py:49
  225.7 130.4 %reduce-scatter.4.cloned.1.call-done = f32[48,256]{1,0:T(8,128)} async-done(((f32[1536,256]{1,0:T(8,128)}), f32[48,256]{1,0:T(8,128)}) %reduce-scatter.4.cloned.1.call-update) | async-done | bytes 49168 | tf_op jit(solution)/shard_map/reduce_scatter | solution.py:32
  356.1 0.8 subtract_bitcast_fusion
  357.6 1.1 fusion.16
  358.7 0.6 fusion.17
  359.3 259.2 %all-reduce.2.cloned.1.call-done = f32[256,256]{1,0:T(8,128)} async-done(((f32[256,256]{1,0:T(8,128)}), f32[256,256]{1,0:T(8,128)}) %all-reduce.2.cloned.1.call-update) | async-done | bytes 262160 | tf_op jit(solution)/shard_map/psum | solution.py:50
  618.6 1.6 fusion.2
  620.3 2.3 gather_fusion
  623.0 0.3 convolution_subtract_fusion.1
  623.6 0.3 fusion.5
  623.9 0.4 convolution_subtract_fusion
  624.3 0.3 fusion.10
  624.6 0.8 copy.22
  (32 shorter events, 1.8 us)
Async XLA Ops:
  7.2 129.5 %copy-start = (f32[1536,384]{1,0:T(8,128)S(1)}, f32[1536,384]{1,0:T(8,128)}, u32[]{:S(2)}) copy-start(f32[1536,384]{1,0:T(8,128)} %param.7) | copy-start | bytes 7077892
  7.2 129.5 %all-gather.2.cloned.1.call-start = ((), (), s32[]{:S(2)}) async-start(), calls=%async_computation.1 | async-start | bytes 12632064 | tf_op jit(solution)/shard_map/all_gather | solution.py:30
  7.9 348.2 %reduce-scatter.4.cloned.1.call-start = ((), (), s32[]{:S(2)}) async-start(), calls=%async_computation.3 | async-start | bytes 1622016 | tf_op jit(solution)/shard_map/reduce_scatter | solution.py:32
  142.8 3.2 copy-start.4
  142.8 37.9 %copy-start.1 = (f32[256,256]{1,0:T(8,128)S(1)}, f32[256,256]{1,0:T(8,128)}, u32[]{:S(2)}) copy-start(f32[256,256]{1,0:T(8,128)} %param.10) | copy-start | bytes 786436
  145.9 210.2 %copy-start.3 = (f32[48,256]{1,0:T(8,128)S(1)}, f32[48,256]{1,0:T(8,128)}, u32[]{:S(2)}) copy-start(f32[48,256]{1,0:T(8,128)} %param.9) | copy-start | bytes 147460
  145.9 211.6 %copy-start.2 = (f32[48,256]{1,0:T(8,128)S(1)}, f32[48,256]{1,0:T(8,128)}, u32[]{:S(2)}) copy-start(f32[48,256]{1,0:T(8,128)} %param.8) | copy-start | bytes 147460
  146.0 472.6 %all-reduce.2.cloned.1.call-start = ((), (), s32[]{:S(2)}) async-start(), calls=%async_computation.2 | async-start | bytes 524288 | tf_op jit(solution)/shard_map/psum | solution.py:50
Sparse Core Ops, SparseCore 0:
  11.8 124.8 all-gather.1
  146.1 209.9 reduce-scatter.3
  362.1 256.4 all-reduce.1
where the time goes:
time: 633 us; the launch traced here: 632 us
  waiting for transfers between devices  519 us (82%)
  blocking collectives  55.7 us (9%)
  other arithmetic  21.3 us (3%)
  between operations  13.9 us (2%)
  matrix products  11.2 us (2%)
  local copies, waits for them, and re-layouts  10.6 us (2%)
    psum x1, waiting for transfers between devices, body(): total = lax.psum(local_term, ('row', 'col'))  259 us
    reduce_scatter x1, waiting for transfers between devices, body(): lax.psum_scatter(jnp.dot(trailing_adjoint, column_rows, precision=lax.Pre...  130 us
    all_gather x1, waiting for transfers between devices, body(): gathered = lax.all_gather(panel, ('row', 'col'), axis=0, tiled=True)  129 us
    all_gather x1, blocking collectives, body(): row_piece = lax.all_gather(diag_adjoint, 'col', axis=1, tiled=True)  34.7 us
    all_gather x1, blocking collectives, body(): full_adjoint = lax.all_gather(row_piece, 'row', axis=0, tiled=True)  21 us
    another operation x3, other arithmetic, right_solve(): jax.scipy.linalg.solve_triangular(factor, rows.T, lower=True, trans=1)  19.7 us
  transfers between devices with their start and end apart: 3, of which 3 were waited for; matrix products, arithmetic and copies ran while one was open for 4% of the time, Pallas kernels for 0%

commit v1 on v0

v1 whole, which is shorter than its diff:
```python
import jax
import jax.numpy as jnp
from jax import lax
from jax.sharding import PartitionSpec as P

ALL = ("row", "col")


def right_solve(factor, rows):
    return jax.scipy.linalg.solve_triangular(factor, rows.T, lower=True, trans=1).T


def left_solve(factor, matrix):
    return jax.scipy.linalg.solve_triangular(factor, matrix, lower=True, trans=1)


def diagonal_adjoint(factor, adjoint):
    product = jnp.dot(
        factor.T, adjoint, precision=lax.Precision.HIGHEST, preferred_element_type=jnp.float32
    )
    lower = jnp.tril(product) - 0.5 * jnp.diag(jnp.diag(product))
    symmetric = lower + lower.T
    half = left_solve(factor, symmetric)
    return 0.5 * left_solve(factor, half.T).T


def bit_reverse(value, bits):
    out = 0
    for k in range(bits):
        out |= ((value >> k) & 1) << (bits - 1 - k)
    return out


def xor_perm(size, mask):
    return [(i, i ^ mask) for i in range(size)]


def make_body(nrow, ncol):
    assert nrow & (nrow - 1) == 0 and ncol & (ncol - 1) == 0
    row_bits = nrow.bit_length() - 1
    ndev = nrow * ncol
    owner_perm = [
        (r * ncol + c, c * nrow + bit_reverse(r, row_bits)) for r in range(nrow) for c in range(ncol)
    ]

    def body(trailing_adjoint, panel, panel_adjoint, diag_factor, diag_adjoint):
        r = lax.axis_index("row")
        c = lax.axis_index("col")

        gathered = panel
        m = 1
        while m < ncol:
            got = lax.ppermute(gathered, "col", xor_perm(ncol, m))
            upper = (c & m) != 0
            gathered = jnp.where(
                upper,
                jnp.concatenate([got, gathered], axis=0),
                jnp.concatenate([gathered, got], axis=0),
            )
            m *= 2

        share = lax.dot_general(
            trailing_adjoint,
            gathered,
            (((0,), (0,)), ((), ())),
            precision=lax.Precision.HIGHEST,
            preferred_element_type=jnp.float32,
        )

        m = 1
        while m < nrow:
            half = share.shape[0] // 2
            low, high = share[:half], share[half:]
            upper = (r & m) != 0
            keep = jnp.where(upper, high, low)
            send = jnp.where(upper, low, high)
            share = keep + lax.ppermute(send, "row", xor_perm(nrow, m))
            m *= 2
        product = lax.ppermute(share, ALL, owner_perm)

        updated = panel_adjoint - 2.0 * product
        off_adjoint = right_solve(diag_factor, updated)
        local_term = jnp.dot(
            off_adjoint.T, panel, precision=lax.Precision.HIGHEST, preferred_element_type=jnp.float32
        )
        rows, cols = diag_adjoint.shape
        placed = lax.dynamic_update_slice(
            jnp.zeros((rows * nrow, cols * ncol), jnp.float32), diag_adjoint, (r * rows, c * cols)
        )
        accumulated = placed - local_term
        m = 1
        while m < ndev:
            accumulated = accumulated + lax.ppermute(accumulated, ALL, xor_perm(ndev, m))
            m *= 2
        return (off_adjoint, diagonal_adjoint(diag_factor, accumulated))

    return body


def solution(mesh):
    return jax.shard_map(
        make_body(mesh.shape["row"], mesh.shape["col"]),
        mesh=mesh,
        in_specs=(
            P("row", "col"),
            P(ALL, None),
            P(ALL, None),
            P(),
            P("row", "col"),
        ),
        out_specs=(P(ALL, None), P()),
        check_vma=False,
    )
```

time: 633 us -> 193 us (0.30)
  waiting for transfers between devices: 519 us -> 90.5 us
  starting transfers between devices: 0.12 us -> 55.9 us
  blocking collectives: 55.7 us -> 0 us
  between operations: 13.9 us -> 0.98 us
    psum x1 -> x0, waiting for transfers between devices: 259 us -> none  [body(): total = lax.psum(local_term, ('row', 'col'))]
    reduce_scatter x1 -> x0, waiting for transfers between devices: 130 us -> none  [body(): lax.psum_scatter(jnp.dot(trailing_adjoint, column_rows, precision=lax.Pre...]
    all_gather x1 -> x0, waiting for transfers between devices: 129 us -> none  [body(): gathered = lax.all_gather(panel, ('row', 'col'), axis=0, tiled=True)]
    ppermute x0 -> x17, waiting for transfers between devices: none -> 90.5 us  [the longest x8 57.1 us: body(): lax.ppermute(accumulated, ALL, xor_perm(ndev, m))]
    ppermute x0 -> x17, starting transfers between devices: none -> 55.9 us  [the longest x5 17 us: body(): got = lax.ppermute(gathered, 'col', xor_perm(ncol, m))]
    all_gather x2 -> x0, blocking collectives: 55.7 us -> none  [the longest x1 34.7 us: body(): row_piece = lax.all_gather(diag_adjoint, 'col', axis=1, tiled=True)]
  transfers between devices with their start and end apart: 3 -> 17, of which waited for: 3 -> 16; matrix products, arithmetic and copies ran while one was open for 4% -> 14% of each run, Pallas kernels for 0% -> 0%
where the time goes in v1:
time: 193 us; the launch traced here: 192 us
  waiting for transfers between devices  90.5 us (47%)
  starting transfers between devices  55.9 us (29%)
  other arithmetic  26.8 us (14%)
  local copies, waits for them, and re-layouts  9.58 us (5%)
  matrix products  7.72 us (4%)
    ppermute x8, waiting for transfers between devices, body(): lax.ppermute(accumulated, ALL, xor_perm(ndev, m))  57.1 us
    ppermute x5, waiting for transfers between devices, body(): got = lax.ppermute(gathered, 'col', xor_perm(ncol, m))  26.4 us
    another operation x3, other arithmetic, right_solve(): jax.scipy.linalg.solve_triangular(factor, rows.T, lower=True, trans=1)  20.5 us
    ppermute x5, starting transfers between devices, body(): got = lax.ppermute(gathered, 'col', xor_perm(ncol, m))  17 us
    ppermute x8, starting transfers between devices, body(): lax.ppermute(accumulated, ALL, xor_perm(ndev, m))  15 us
    ppermute x3, starting transfers between devices, body(): share = keep + lax.ppermute(send, 'row', xor_perm(nrow, m))  14.1 us
    ppermute x1, starting transfers between devices, body(): product = lax.ppermute(share, ALL, owner_perm)  9.79 us
    ppermute x3, waiting for transfers between devices, body(): share = keep + lax.ppermute(send, 'row', xor_perm(nrow, m))  7.05 us
  transfers between devices with their start and end apart: 17, of which 16 were waited for; matrix products, arithmetic and copies ran while one was open for 14% of the time, Pallas kernels for 0%

profile of v1, /device:TPU:1, one launch (start us, length us, event | category | flops | bytes accessed | tf_op | source)
XLA Modules:
  0.0 191.6 jit_solution(12047251599729139648)
XLA Ops:
  0.6 2.5 %collective-permute-start = (f32[48,256]{1,0:T(8,128)}, f32[48,256]{1,0:T(8,128)S(1)}, u32[]{:S(2)}, u32[]{:S(2)}) collective-permute-start(f32[48,256]{1,0:T(8,128)} %param.8), channel_id=1, source_target_pairs={{0,1},{1,0},{2,3},{3,2},{4,5},{5,4},{6,7},{7,6},{8,9},{9,8},{10,11... | collective-permute-start | bytes 147464 | tf_op jit(solution)/shard_map/ppermute | solution.py:53
  5.8 3.1 %collective-permute-start.1 = (f32[96,256]{1,0:T(8,128)S(1)}, f32[96,256]{1,0:T(8,128)S(1)}, u32[]{:S(2)}, u32[]{:S(2)}) collective-permute-start(f32[96,256]{1,0:T(8,128)S(1)} %maximum_select_fusion.7), channel_id=1, source_target_pairs={{0,2},{1,3},{2,0},{3,1},{4,6},{5,7},{6,4},{7,5},{8,10},{9,11},{10,... | collective-permute-start | bytes 294920 | tf_op jit(solution)/shard_map/ppermute | solution.py:53
  10.9 7.2 %collective-permute-start.2 = (f32[192,256]{1,0:T(8,128)S(1)}, f32[192,256]{1,0:T(8,128)S(1)}, u32[]{:S(2)}, u32[]{:S(2)}) collective-permute-start(f32[192,256]{1,0:T(8,128)S(1)} %maximum_select_fusion.6), channel_id=1, source_target_pairs={{0,4},{1,5},{2,6},{3,7},{4,0},{5,1},{6,2},{7,3},{8,12},{9,13},{10,... | collective-permute-start | bytes 589832 | tf_op jit(solution)/shard_map/ppermute | solution.py:53
  18.1 3.1 %collective-permute-done.2 = f32[192,256]{1,0:T(8,128)S(1)} collective-permute-done((f32[192,256]{1,0:T(8,128)S(1)}, f32[192,256]{1,0:T(8,128)S(1)}, u32[]{:S(2)}, u32[]{:S(2)}) %collective-permute-start.2) | collective-permute-done | bytes 196640 | tf_op jit(solution)/shard_map/ppermute | solution.py:53
  22.5 5.7 %collective-permute-done.3 = f32[384,256]{1,0:T(8,128)} collective-permute-done((f32[384,256]{1,0:T(8,128)S(1)}, f32[384,256]{1,0:T(8,128)}, u32[]{:S(2)}, u32[]{:S(2)}) %collective-permute-start.3) | collective-permute-done | bytes 393248 | tf_op jit(solution)/shard_map/ppermute | solution.py:53
  29.4 2.8 %collective-permute-start.4 = (f32[768,256]{1,0:T(8,128)S(1)}, f32[768,256]{1,0:T(8,128)}, u32[]{:S(2)}, u32[]{:S(2)}) collective-permute-start(f32[768,256]{1,0:T(8,128)S(1)} %maximum_select_fusion.4), channel_id=1, source_target_pairs={{0,16},{1,17},{2,18},{3,19},{4,20},{5,21},{6,22},{7,23},{8,24},{9,... | collective-permute-start | bytes 2359304 | tf_op jit(solution)/shard_map/ppermute | solution.py:53
  32.2 13.9 %collective-permute-done.4 = f32[768,256]{1,0:T(8,128)} collective-permute-done((f32[768,256]{1,0:T(8,128)S(1)}, f32[768,256]{1,0:T(8,128)}, u32[]{:S(2)}, u32[]{:S(2)}) %collective-permute-start.4) | collective-permute-done | bytes 786464 | tf_op jit(solution)/shard_map/ppermute | solution.py:53
  46.2 4.1 %fusion.6 = f32[384,256]{0,1:T(8,128)S(1)} fusion(f32[1536,384]{1,0:T(8,128)S(1)} %copy-done, f32[768,256]{1,0:T(8,128)S(1)} %maximum_select_fusion.4, f32[768,256]{1,0:T(8,128)} %collective-permute-done.4, pred[]{:T(512)S(6)} %ne.27), kind=kOutput, calls=%fused_computation.10 | convolution fusion | flops 1813118976 | bytes 4325377 | tf_op jit(solution)/shard_map/dot_general | solution.py:62
  50.4 9.8 %collective-permute-start.5 = (f32[192,256]{0,1:T(8,128)S(1)}, f32[192,256]{0,1:T(8,128)}, u32[]{:S(2)}, u32[]{:S(2)}) collective-permute-start(f32[192,256]{0,1:T(8,128)S(1)} %slice_select_fusion), channel_id=1, source_target_pairs={{0,32},{32,0},{64,96},{96,64},{128,160},{160,128},{192,224},{224,1... | collective-permute-start | bytes 589832 | tf_op jit(solution)/shard_map/ppermute | solution.py:77
  64.1 3.4 %collective-permute-done.6 = f32[96,256]{0,1:T(8,128)S(1)} collective-permute-done((f32[96,256]{0,1:T(8,128)S(1)}, f32[96,256]{0,1:T(8,128)S(1)}, u32[]{:S(2)}, u32[]{:S(2)}) %collective-permute-start.6) | collective-permute-done | bytes 98336 | tf_op jit(solution)/shard_map/ppermute | solution.py:77
  67.7 3.0 %collective-permute-start.7 = (f32[48,256]{0,1:T(8,128)S(1)}, f32[48,256]{0,1:T(8,128)S(1)}, u32[]{:S(2)}, u32[]{:S(2)}) collective-permute-start(f32[48,256]{0,1:T(8,128)S(1)} %slice_select_fusion.1), channel_id=1, source_target_pairs={{0,128},{32,160},{64,192},{96,224},{128,0},{160,32},{192,64},{224,... | collective-permute-start | bytes 147464 | tf_op jit(solution)/shard_map/ppermute | solution.py:77
  70.7 2.4 %collective-permute-done.7 = f32[48,256]{0,1:T(8,128)S(1)} collective-permute-done((f32[48,256]{0,1:T(8,128)S(1)}, f32[48,256]{0,1:T(8,128)S(1)}, u32[]{:S(2)}, u32[]{:S(2)}) %collective-permute-start.7) | collective-permute-done | bytes 49184 | tf_op jit(solution)/shard_map/ppermute | solution.py:77
  73.9 9.8 %collective-permute-start.8 = (f32[48,256]{0,1:T(8,128)}, f32[48,256]{0,1:T(8,128)}, u32[]{:S(2)}, u32[]{:S(2)}) collective-permute-start(f32[48,256]{0,1:T(8,128)} %select_add_fusion.1), channel_id=1, source_target_pairs={{0,0},{1,8},{2,16},{3,24},{4,32},{5,40},{6,48},{7,56},{8,64},{9,72... | collective-permute-start | bytes 147464 | tf_op jit(solution)/shard_map/ppermute | solution.py:79
  83.7 5.1 %while.5 = (s32[]{:T(128)}, f32[256,256]{1,0:T(8,128)S(1)}, s32[2,2]{1,0:T(2,128)S(1)}, f32[2,128,128]{2,1,0:T(8,128)}, s32[]{:T(128)}) while((s32[]{:T(128)}, f32[256,256]{1,0:T(8,128)S(1)}, s32[2,2]{1,0:T(2,128)S(1)}, f32[2,128,128]{2,1,0:T(8,128)}, s32[]{:T(128)}) %tuple.33), condition=%wide.while_cond.1, body=%wide.while_body.1.sunk | while | flops 2 | bytes 132705 | solution.py:10
  89.0 20.5 %custom-call.7 = f32[2,128,128]{1,2,0:T(8,128)S(1)} custom-call(f32[2,128,128]{2,1,0:T(8,128)} %get-tuple-element.18), custom_call_target="InvertDiagBlocksLowerTriangular" | custom-call | tf_op jit(solution)/shard_map/jit(_solve_triangular)/triangular_solve | solution.py:10
  114.4 3.8 %collective-permute-done.9 = f32[256,256]{1,0:T(8,128)S(1)} collective-permute-done((f32[256,256]{1,0:T(8,128)S(1)}, f32[256,256]{1,0:T(8,128)S(1)}, u32[]{:S(2)}, u32[]{:S(2)}) %collective-permute-start.9) | collective-permute-done | bytes 262176 | tf_op jit(solution)/shard_map/ppermute | solution.py:93
  118.2 3.7 %collective-permute-start.10 = (f32[256,256]{1,0:T(8,128)S(1)}, f32[256,256]{1,0:T(8,128)S(1)}, u32[]{:S(2)}, u32[]{:S(2)}) collective-permute-start(f32[256,256]{1,0:T(8,128)S(1)} %add.58), channel_id=1, source_target_pairs={{0,2},{1,3},{2,0},{3,1},{4,6},{5,7},{6,4},{7,5},{8,10},{9,11},{10,... | collective-permute-start | bytes 786440 | tf_op jit(solution)/shard_map/ppermute | solution.py:93
  121.9 10.9 %collective-permute-done.10 = f32[256,256]{1,0:T(8,128)S(1)} collective-permute-done((f32[256,256]{1,0:T(8,128)S(1)}, f32[256,256]{1,0:T(8,128)S(1)}, u32[]{:S(2)}, u32[]{:S(2)}) %collective-permute-start.10) | collective-permute-done | bytes 262176 | tf_op jit(solution)/shard_map/ppermute | solution.py:93
  134.9 14.7 %collective-permute-done.11 = f32[256,256]{1,0:T(8,128)S(1)} collective-permute-done((f32[256,256]{1,0:T(8,128)S(1)}, f32[256,256]{1,0:T(8,128)S(1)}, u32[]{:S(2)}, u32[]{:S(2)}) %collective-permute-start.11) | collective-permute-done | bytes 262176 | tf_op jit(solution)/shard_map/ppermute | solution.py:93
  151.2 6.0 %collective-permute-done.12 = f32[256,256]{1,0:T(8,128)S(1)} collective-permute-done((f32[256,256]{1,0:T(8,128)S(1)}, f32[256,256]{1,0:T(8,128)S(1)}, u32[]{:S(2)}, u32[]{:S(2)}) %collective-permute-start.12) | collective-permute-done | bytes 262176 | tf_op jit(solution)/shard_map/ppermute | solution.py:93
  157.3 3.9 %collective-permute-start.13 = (f32[256,256]{1,0:T(8,128)S(1)}, f32[256,256]{1,0:T(8,128)S(1)}, u32[]{:S(2)}, u32[]{:S(2)}) collective-permute-start(f32[256,256]{1,0:T(8,128)S(1)} %add.61), channel_id=1, source_target_pairs={{0,16},{1,17},{2,18},{3,19},{4,20},{5,21},{6,22},{7,23},{8,24},{9,... | collective-permute-start | bytes 786440 | tf_op jit(solution)/shard_map/ppermute | solution.py:93
  161.2 5.5 %collective-permute-done.13 = f32[256,256]{1,0:T(8,128)S(1)} collective-permute-done((f32[256,256]{1,0:T(8,128)S(1)}, f32[256,256]{1,0:T(8,128)S(1)}, u32[]{:S(2)}, u32[]{:S(2)}) %collective-permute-start.13) | collective-permute-done | bytes 262176 | tf_op jit(solution)/shard_map/ppermute | solution.py:93
  169.9 7.5 %collective-permute-done.15 = f32[256,256]{1,0:T(8,128)S(1)} collective-permute-done((f32[256,256]{1,0:T(8,128)S(1)}, f32[256,256]{1,0:T(8,128)S(1)}, u32[]{:S(2)}, u32[]{:S(2)}) %collective-permute-start.15) | collective-permute-done | bytes 262176 | tf_op jit(solution)/shard_map/ppermute | solution.py:93
  178.2 7.5 %collective-permute-done.16 = f32[256,256]{1,0:T(8,128)S(1)} collective-permute-done((f32[256,256]{1,0:T(8,128)S(1)}, f32[256,256]{1,0:T(8,128)S(1)}, u32[]{:S(2)}, u32[]{:S(2)}) %collective-permute-start.16) | collective-permute-done | bytes 262176 | tf_op jit(solution)/shard_map/ppermute | solution.py:93
  (74 shorter events, 35.8 us)
Async XLA Ops:
  0.6 45.5 %copy-start = (f32[1536,384]{1,0:T(8,128)S(1)}, f32[1536,384]{1,0:T(8,128)}, u32[]{:S(2)}) copy-start(f32[1536,384]{1,0:T(8,128)} %param.7) | copy-start | bytes 7077892
  0.6 4.2 %collective-permute-start = (f32[48,256]{1,0:T(8,128)}, f32[48,256]{1,0:T(8,128)S(1)}, u32[]{:S(2)}, u32[]{:S(2)}) collective-permute-start(f32[48,256]{1,0:T(8,128)} %param.8), channel_id=1, source_target_pairs={{0,1},{1,0},{2,3},{3,2},{4,5},{5,4},{6,7},{7,6},{8,9},{9,8},{10,11... | collective-permute-start | bytes 147464 | tf_op jit(solution)/shard_map/ppermute | solution.py:53
  5.8 5.1 %collective-permute-start.1 = (f32[96,256]{1,0:T(8,128)S(1)}, f32[96,256]{1,0:T(8,128)S(1)}, u32[]{:S(2)}, u32[]{:S(2)}) collective-permute-start(f32[96,256]{1,0:T(8,128)S(1)} %maximum_select_fusion.7), channel_id=1, source_target_pairs={{0,2},{1,3},{2,0},{3,1},{4,6},{5,7},{6,4},{7,5},{8,10},{9,11},{10,... | collective-permute-start | bytes 294920 | tf_op jit(solution)/shard_map/ppermute | solution.py:53
  10.9 10.3 %collective-permute-start.2 = (f32[192,256]{1,0:T(8,128)S(1)}, f32[192,256]{1,0:T(8,128)S(1)}, u32[]{:S(2)}, u32[]{:S(2)}) collective-permute-start(f32[192,256]{1,0:T(8,128)S(1)} %maximum_select_fusion.6), channel_id=1, source_target_pairs={{0,4},{1,5},{2,6},{3,7},{4,0},{5,1},{6,2},{7,3},{8,12},{9,13},{10,... | collective-permute-start | bytes 589832 | tf_op jit(solution)/shard_map/ppermute | solution.py:53
  21.2 7.0 %collective-permute-start.3 = (f32[384,256]{1,0:T(8,128)S(1)}, f32[384,256]{1,0:T(8,128)}, u32[]{:S(2)}, u32[]{:S(2)}) collective-permute-start(f32[384,256]{1,0:T(8,128)S(1)} %maximum_select_fusion.5), channel_id=1, source_target_pairs={{0,8},{1,9},{2,10},{3,11},{4,12},{5,13},{6,14},{7,15},{8,0},{9,1},... | collective-permute-start | bytes 1179656 | tf_op jit(solution)/shard_map/ppermute | solution.py:53
  29.4 16.8 %collective-permute-start.4 = (f32[768,256]{1,0:T(8,128)S(1)}, f32[768,256]{1,0:T(8,128)}, u32[]{:S(2)}, u32[]{:S(2)}) collective-permute-start(f32[768,256]{1,0:T(8,128)S(1)} %maximum_select_fusion.4), channel_id=1, source_target_pairs={{0,16},{1,17},{2,18},{3,19},{4,20},{5,21},{6,22},{7,23},{8,24},{9,... | collective-permute-start | bytes 2359304 | tf_op jit(solution)/shard_map/ppermute | solution.py:53
  50.3 13.8 %copy-start.1 = (f32[256,256]{1,0:T(8,128)S(1)}, f32[256,256]{1,0:T(8,128)}, u32[]{:S(2)}) copy-start(f32[256,256]{1,0:T(8,128)} %param.10) | copy-start | bytes 786436
  50.4 11.1 %collective-permute-start.5 = (f32[192,256]{0,1:T(8,128)S(1)}, f32[192,256]{0,1:T(8,128)}, u32[]{:S(2)}, u32[]{:S(2)}) collective-permute-start(f32[192,256]{0,1:T(8,128)S(1)} %slice_select_fusion), channel_id=1, source_target_pairs={{0,32},{32,0},{64,96},{96,64},{128,160},{160,128},{192,224},{224,1... | collective-permute-start | bytes 589832 | tf_op jit(solution)/shard_map/ppermute | solution.py:77
  62.6 26.3 %copy-start.3 = (f32[48,256]{1,0:T(8,128)S(1)}, f32[48,256]{1,0:T(8,128)}, u32[]{:S(2)}) copy-start(f32[48,256]{1,0:T(8,128)} %param.9) | copy-start | bytes 147460
  62.7 46.8 %copy-start.4 = (f32[32,8]{0,1:T(8,128)S(1)}, f32[32,8]{0,1:T(8,128)}, u32[]{:S(2)}) copy-start(f32[32,8]{0,1:T(8,128)} %param.11) | copy-start | bytes 3076
  62.7 4.8 %collective-permute-start.6 = (f32[96,256]{0,1:T(8,128)S(1)}, f32[96,256]{0,1:T(8,128)S(1)}, u32[]{:S(2)}, u32[]{:S(2)}) collective-permute-start(f32[96,256]{0,1:T(8,128)S(1)} %slice_select_fusion.2), channel_id=1, source_target_pairs={{0,64},{32,96},{64,0},{96,32},{128,192},{160,224},{192,128},{224,1... | collective-permute-start | bytes 294920 | tf_op jit(solution)/shard_map/ppermute | solution.py:77
  67.6 44.6 %copy-start.2 = (f32[48,256]{1,0:T(8,128)S(1)}, f32[48,256]{1,0:T(8,128)}, u32[]{:S(2)}) copy-start(f32[48,256]{1,0:T(8,128)} %param.8) | copy-start | bytes 147460
  67.7 5.4 %collective-permute-start.7 = (f32[48,256]{0,1:T(8,128)S(1)}, f32[48,256]{0,1:T(8,128)S(1)}, u32[]{:S(2)}, u32[]{:S(2)}) collective-permute-start(f32[48,256]{0,1:T(8,128)S(1)} %slice_select_fusion.1), channel_id=1, source_target_pairs={{0,128},{32,160},{64,192},{96,224},{128,0},{160,32},{192,64},{224,... | collective-permute-start | bytes 147464 | tf_op jit(solution)/shard_map/ppermute | solution.py:77
  73.9 36.6 %collective-permute-start.8 = (f32[48,256]{0,1:T(8,128)}, f32[48,256]{0,1:T(8,128)}, u32[]{:S(2)}, u32[]{:S(2)}) collective-permute-start(f32[48,256]{0,1:T(8,128)} %select_add_fusion.1), channel_id=1, source_target_pairs={{0,0},{1,8},{2,16},{3,24},{4,32},{5,40},{6,48},{7,56},{8,64},{9,72... | collective-permute-start | bytes 147464 | tf_op jit(solution)/shard_map/ppermute | solution.py:79
  112.6 5.5 %collective-permute-start.9 = (f32[256,256]{1,0:T(8,128)S(1)}, f32[256,256]{1,0:T(8,128)S(1)}, u32[]{:S(2)}, u32[]{:S(2)}) collective-permute-start(f32[256,256]{1,0:T(8,128)S(1)} %convolution_subtract_fusion), channel_id=1, source_target_pairs={{0,1},{1,0},{2,3},{3,2},{4,5},{5,4},{6,7},{7,6},{8,9},{9,8},{10,11... | collective-permute-start | bytes 786440 | tf_op jit(solution)/shard_map/ppermute | solution.py:93
  118.2 14.6 %collective-permute-start.10 = (f32[256,256]{1,0:T(8,128)S(1)}, f32[256,256]{1,0:T(8,128)S(1)}, u32[]{:S(2)}, u32[]{:S(2)}) collective-permute-start(f32[256,256]{1,0:T(8,128)S(1)} %add.58), channel_id=1, source_target_pairs={{0,2},{1,3},{2,0},{3,1},{4,6},{5,7},{6,4},{7,5},{8,10},{9,11},{10,... | collective-permute-start | bytes 786440 | tf_op jit(solution)/shard_map/ppermute | solution.py:93
  132.8 16.9 %collective-permute-start.11 = (f32[256,256]{1,0:T(8,128)S(1)}, f32[256,256]{1,0:T(8,128)S(1)}, u32[]{:S(2)}, u32[]{:S(2)}) collective-permute-start(f32[256,256]{1,0:T(8,128)S(1)} %add.59), channel_id=1, source_target_pairs={{0,4},{1,5},{2,6},{3,7},{4,0},{5,1},{6,2},{7,3},{8,12},{9,13},{10,... | collective-permute-start | bytes 786440 | tf_op jit(solution)/shard_map/ppermute | solution.py:93
  149.7 7.6 %collective-permute-start.12 = (f32[256,256]{1,0:T(8,128)S(1)}, f32[256,256]{1,0:T(8,128)S(1)}, u32[]{:S(2)}, u32[]{:S(2)}) collective-permute-start(f32[256,256]{1,0:T(8,128)S(1)} %add.60), channel_id=1, source_target_pairs={{0,8},{1,9},{2,10},{3,11},{4,12},{5,13},{6,14},{7,15},{8,0},{9,1},... | collective-permute-start | bytes 786440 | tf_op jit(solution)/shard_map/ppermute | solution.py:93
  157.3 9.5 %collective-permute-start.13 = (f32[256,256]{1,0:T(8,128)S(1)}, f32[256,256]{1,0:T(8,128)S(1)}, u32[]{:S(2)}, u32[]{:S(2)}) collective-permute-start(f32[256,256]{1,0:T(8,128)S(1)} %add.61), channel_id=1, source_target_pairs={{0,16},{1,17},{2,18},{3,19},{4,20},{5,21},{6,22},{7,23},{8,24},{9,... | collective-permute-start | bytes 786440 | tf_op jit(solution)/shard_map/ppermute | solution.py:93
  166.8 3.0 %collective-permute-start.14 = (f32[256,256]{1,0:T(8,128)S(1)}, f32[256,256]{1,0:T(8,128)S(1)}, u32[]{:S(2)}, u32[]{:S(2)}) collective-permute-start(f32[256,256]{1,0:T(8,128)S(1)} %add.62), channel_id=1, source_target_pairs={{0,32},{1,33},{2,34},{3,35},{4,36},{5,37},{6,38},{7,39},{8,40},{9,... | collective-permute-start | bytes 786440 | tf_op jit(solution)/shard_map/ppermute | solution.py:93
  169.8 7.6 %collective-permute-start.15 = (f32[256,256]{1,0:T(8,128)S(1)}, f32[256,256]{1,0:T(8,128)S(1)}, u32[]{:S(2)}, u32[]{:S(2)}) collective-permute-start(f32[256,256]{1,0:T(8,128)S(1)} %add.63), channel_id=1, source_target_pairs={{0,64},{1,65},{2,66},{3,67},{4,68},{5,69},{6,70},{7,71},{8,72},{9,... | collective-permute-start | bytes 786440 | tf_op jit(solution)/shard_map/ppermute | solution.py:93
  177.4 8.2 %collective-permute-start.16 = (f32[256,256]{1,0:T(8,128)S(1)}, f32[256,256]{1,0:T(8,128)S(1)}, u32[]{:S(2)}, u32[]{:S(2)}) collective-permute-start(f32[256,256]{1,0:T(8,128)S(1)} %add.64), channel_id=1, source_target_pairs={{0,128},{1,129},{2,130},{3,131},{4,132},{5,133},{6,134},{7,135},{8... | collective-permute-start | bytes 786440 | tf_op jit(solution)/shard_map/ppermute | solution.py:93

commit v2 on v1

--- a/solution.py
+++ b/solution.py
@@ -35,21 +35,49 @@
     return [(i, i ^ mask) for i in range(size)]
 
 
+def gather_order(ncol):
+    bits = [1 << k for k in range(ncol.bit_length() - 1)]
+    low = [m for m in bits if m < 8][::-1]
+    high = [m for m in bits if m >= 8][::-1]
+    return low + high
+
+
+def all_reduce(value, nrow, ncol):
+    ndev = nrow * ncol
+    outer = [ncol * m for m in (1, 2) if m < nrow]
+    inner = [m for m in (1 << k for k in range(ndev.bit_length() - 1)) if m not in outer]
+    for m in outer:
+        half = value.shape[0] // 2
+        low, high = value[:half], value[half:]
+        upper = (lax.axis_index(ALL) & m) != 0
+        keep = jnp.where(upper, high, low)
+        send = jnp.where(upper, low, high)
+        value = keep + lax.ppermute(send, ALL, xor_perm(ndev, m))
+    for m in inner:
+        value = value + lax.ppermute(value, ALL, xor_perm(ndev, m))
+    for m in outer[::-1]:
+        got = lax.ppermute(value, ALL, xor_perm(ndev, m))
+        upper = (lax.axis_index(ALL) & m) != 0
+        value = jnp.where(
+            upper, jnp.concatenate([got, value], axis=0), jnp.concatenate([value, got], axis=0)
+        )
+    return value
+
+
 def make_body(nrow, ncol):
     assert nrow & (nrow - 1) == 0 and ncol & (ncol - 1) == 0
     row_bits = nrow.bit_length() - 1
-    ndev = nrow * ncol
     owner_perm = [
         (r * ncol + c, c * nrow + bit_reverse(r, row_bits)) for r in range(nrow) for c in range(ncol)
     ]
 
-    def body(trailing_adjoint, panel, panel_adjoint, diag_factor, diag_adjoint):
+    def inner(trailing_adjoint, panel, panel_adjoint, diag_factor, diag_adjoint):
         r = lax.axis_index("row")
         c = lax.axis_index("col")
 
         gathered = panel
-        m = 1
-        while m < ncol:
+        order = gather_order(ncol)
+        for m in order:
             got = lax.ppermute(gathered, "col", xor_perm(ncol, m))
             upper = (c & m) != 0
             gathered = jnp.where(
@@ -57,7 +85,11 @@
                 jnp.concatenate([got, gathered], axis=0),
                 jnp.concatenate([gathered, got], axis=0),
             )
-            m *= 2
+        blocks = gathered.reshape((2,) * len(order) + panel.shape)
+        nbits = len(order)
+        axis_of_bit = {m.bit_length() - 1: nbits - 1 - t for t, m in enumerate(order)}
+        perm = [axis_of_bit[nbits - 1 - a] for a in range(nbits)] + [nbits, nbits + 1]
+        gathered = blocks.transpose(perm).reshape((ncol * panel.shape[0], panel.shape[1]))
 
         share = lax.dot_general(
             trailing_adjoint,
@@ -87,14 +119,10 @@
         placed = lax.dynamic_update_slice(
             jnp.zeros((rows * nrow, cols * ncol), jnp.float32), diag_adjoint, (r * rows, c * cols)
         )
-        accumulated = placed - local_term
-        m = 1
-        while m < ndev:
-            accumulated = accumulated + lax.ppermute(accumulated, ALL, xor_perm(ndev, m))
-            m *= 2
+        accumulated = all_reduce(placed - local_term, nrow, ncol)
         return (off_adjoint, diagonal_adjoint(diag_factor, accumulated))
 
-    return body
+    return inner
 
 
 def solution(mesh):

time: 193 us -> 166 us (0.86)
  waiting for transfers between devices: 90.5 us -> 66.8 us
  starting transfers between devices: 55.9 us -> 52.6 us
    ppermute x17 -> x19, waiting for transfers between devices: 90.5 us -> 66.8 us  [the longest x5 28.9 us: inner(): got = lax.ppermute(gathered, 'col', xor_perm(ncol, m))]
    ppermute x17 -> x19, starting transfers between devices: 55.9 us -> 52.6 us  [the longest x5 14.7 us: inner(): got = lax.ppermute(gathered, 'col', xor_perm(ncol, m))]
    select_n x7 -> x11, other arithmetic: 2.45 us -> 4.04 us  [the longest x5 3.67 us: inner(): jnp.where(upper, jnp.concatenate([got, gathered], axis=0), jnp.concatenat...]
  transfers between devices with their start and end apart: 17 -> 19, of which waited for: 16 -> 18; matrix products, arithmetic and copies ran while one was open for 14% -> 16% of each run, Pallas kernels for 0% -> 0%
where the time goes in v2:
time: 166 us; the launch traced here: 165 us
  waiting for transfers between devices  66.8 us (40%)
  starting transfers between devices  52.6 us (32%)
  other arithmetic  28.4 us (17%)
  local copies, waits for them, and re-layouts  9.19 us (6%)
  matrix products  7.24 us (4%)
    ppermute x5, waiting for transfers between devices, inner(): got = lax.ppermute(gathered, 'col', xor_perm(ncol, m))  28.9 us
    ppermute x6, waiting for transfers between devices, all_reduce(): value = value + lax.ppermute(value, ALL, xor_perm(ndev, m))  22.7 us
    another operation x3, other arithmetic, right_solve(): jax.scipy.linalg.solve_triangular(factor, rows.T, lower=True, trans=1)  19.7 us
    ppermute x5, starting transfers between devices, inner(): got = lax.ppermute(gathered, 'col', xor_perm(ncol, m))  14.7 us
    ppermute x1, starting transfers between devices, inner(): product = lax.ppermute(share, ALL, owner_perm)  12.4 us
    ppermute x2, starting transfers between devices, all_reduce(): got = lax.ppermute(value, ALL, xor_perm(ndev, m))  9.92 us
    ppermute x3, starting transfers between devices, inner(): share = keep + lax.ppermute(send, 'row', xor_perm(nrow, m))  9.87 us
    ppermute x3, waiting for transfers between devices, inner(): share = keep + lax.ppermute(send, 'row', xor_perm(nrow, m))  7.05 us
  transfers between devices with their start and end apart: 19, of which 18 were waited for; matrix products, arithmetic and copies ran while one was open for 16% of the time, Pallas kernels for 0%

profile of v2, /device:TPU:1, one launch (start us, length us, event | category | flops | bytes accessed | tf_op | source)
XLA Modules:
  0.0 165.3 jit_solution(1974773644773091041)
XLA Ops:
  0.6 7.8 %collective-permute-start = (f32[48,256]{1,0:T(8,128)}, f32[48,256]{1,0:T(8,128)S(1)}, u32[]{:S(2)}, u32[]{:S(2)}) collective-permute-start(f32[48,256]{1,0:T(8,128)} %param.8), channel_id=1, source_target_pairs={{0,4},{1,5},{2,6},{3,7},{4,0},{5,1},{6,2},{7,3},{8,12},{9,13},{10,... | collective-permute-start | bytes 147464 | tf_op jit(solution)/shard_map/ppermute | solution.py:81
  12.6 4.0 %collective-permute-done.1 = f32[96,256]{1,0:T(8,128)S(1)} collective-permute-done((f32[96,256]{1,0:T(8,128)S(1)}, f32[96,256]{1,0:T(8,128)S(1)}, u32[]{:S(2)}, u32[]{:S(2)}) %collective-permute-start.1) | collective-permute-done | bytes 98336 | tf_op jit(solution)/shard_map/ppermute | solution.py:81
  16.7 4.5 %collective-permute-done.2 = f32[192,256]{1,0:T(8,128)S(1)} collective-permute-done((f32[192,256]{1,0:T(8,128)S(1)}, f32[192,256]{1,0:T(8,128)S(1)}, u32[]{:S(2)}, u32[]{:S(2)}) %collective-permute-start.2) | collective-permute-done | bytes 196640 | tf_op jit(solution)/shard_map/ppermute | solution.py:81
  21.2 3.2 %collective-permute-start.3 = (f32[384,256]{1,0:T(8,128)S(1)}, f32[384,256]{1,0:T(8,128)}, u32[]{:S(2)}, u32[]{:S(2)}) collective-permute-start(f32[384,256]{1,0:T(8,128)S(1)} %maximum_select_fusion.2), channel_id=1, source_target_pairs={{0,16},{1,17},{2,18},{3,19},{4,20},{5,21},{6,22},{7,23},{8,24},{9,... | collective-permute-start | bytes 1179656 | tf_op jit(solution)/shard_map/ppermute | solution.py:81
  24.4 5.3 %collective-permute-done.3 = f32[384,256]{1,0:T(8,128)} collective-permute-done((f32[384,256]{1,0:T(8,128)S(1)}, f32[384,256]{1,0:T(8,128)}, u32[]{:S(2)}, u32[]{:S(2)}) %collective-permute-start.3) | collective-permute-done | bytes 393248 | tf_op jit(solution)/shard_map/ppermute | solution.py:81
  32.9 13.5 %collective-permute-done.4 = f32[768,256]{1,0:T(8,128)} collective-permute-done((f32[768,256]{1,0:T(8,128)S(1)}, f32[768,256]{1,0:T(8,128)}, u32[]{:S(2)}, u32[]{:S(2)}) %collective-permute-start.4) | collective-permute-done | bytes 786464 | tf_op jit(solution)/shard_map/ppermute | solution.py:81
  48.0 2.8 %convolution_bitcast_fusion = f32[384,256]{0,1:T(8,128)S(1)} fusion(f32[1536,256]{1,0:T(8,128)S(1)} %bitcast.58, f32[1536,384]{1,0:T(8,128)S(1)} %copy-done), kind=kOutput, calls=%fused_computation.4 | convolution fusion | flops 1811939328 | bytes 4325376 | tf_op jit(solution)/shard_map/dot_general | solution.py:94
  51.0 5.5 %collective-permute-start.5 = (f32[192,256]{0,1:T(8,128)S(1)}, f32[192,256]{0,1:T(8,128)}, u32[]{:S(2)}, u32[]{:S(2)}) collective-permute-start(f32[192,256]{0,1:T(8,128)S(1)} %slice_select_fusion), channel_id=1, source_target_pairs={{0,32},{32,0},{64,96},{96,64},{128,160},{160,128},{192,224},{224,1... | collective-permute-start | bytes 589832 | tf_op jit(solution)/shard_map/ppermute | solution.py:109
  60.4 3.4 %collective-permute-done.6 = f32[96,256]{0,1:T(8,128)S(1)} collective-permute-done((f32[96,256]{0,1:T(8,128)S(1)}, f32[96,256]{0,1:T(8,128)S(1)}, u32[]{:S(2)}, u32[]{:S(2)}) %collective-permute-start.6) | collective-permute-done | bytes 98336 | tf_op jit(solution)/shard_map/ppermute | solution.py:109
  64.0 3.0 %collective-permute-start.7 = (f32[48,256]{0,1:T(8,128)S(1)}, f32[48,256]{0,1:T(8,128)S(1)}, u32[]{:S(2)}, u32[]{:S(2)}) collective-permute-start(f32[48,256]{0,1:T(8,128)S(1)} %slice_select_fusion.2), channel_id=1, source_target_pairs={{0,128},{32,160},{64,192},{96,224},{128,0},{160,32},{192,64},{224,... | collective-permute-start | bytes 147464 | tf_op jit(solution)/shard_map/ppermute | solution.py:109
  67.0 2.4 %collective-permute-done.7 = f32[48,256]{0,1:T(8,128)S(1)} collective-permute-done((f32[48,256]{0,1:T(8,128)S(1)}, f32[48,256]{0,1:T(8,128)S(1)}, u32[]{:S(2)}, u32[]{:S(2)}) %collective-permute-start.7) | collective-permute-done | bytes 49184 | tf_op jit(solution)/shard_map/ppermute | solution.py:109
  70.2 12.4 %collective-permute-start.8 = (f32[48,256]{0,1:T(8,128)}, f32[48,256]{0,1:T(8,128)}, u32[]{:S(2)}, u32[]{:S(2)}) collective-permute-start(f32[48,256]{0,1:T(8,128)} %select_add_fusion.2), channel_id=1, source_target_pairs={{0,0},{1,8},{2,16},{3,24},{4,32},{5,40},{6,48},{7,56},{8,64},{9,72... | collective-permute-start | bytes 147464 | tf_op jit(solution)/shard_map/ppermute | solution.py:111
  82.7 3.8 %while.5 = (s32[]{:T(128)}, f32[256,256]{1,0:T(8,128)S(1)}, s32[2,2]{1,0:T(2,128)S(1)}, f32[2,128,128]{2,1,0:T(8,128)S(1)}, s32[]{:T(128)}) while((s32[]{:T(128)}, f32[256,256]{1,0:T(8,128)S(1)}, s32[2,2]{1,0:T(2,128)S(1)}, f32[2,128,128]{2,1,0:T(8,128)S(1)}, s32[]{:T(128)}) %tuple.34), condition=%wide.while_cond.1, body=%wide.while_body.1.sunk | while | flops 2 | bytes 131181 | solution.py:10
  87.5 19.7 %custom-call.7 = f32[2,128,128]{1,2,0:T(8,128)S(1)} custom-call(f32[2,128,128]{2,1,0:T(8,128)S(1)} %get-tuple-element.18), custom_call_target="InvertDiagBlocksLowerTriangular" | custom-call | tf_op jit(solution)/shard_map/jit(_solve_triangular)/triangular_solve | solution.py:10
  114.0 3.5 %collective-permute-done.10 = f32[64,256]{1,0:T(8,128)S(1)} collective-permute-done((f32[64,256]{1,0:T(8,128)S(1)}, f32[64,256]{1,0:T(8,128)S(1)}, u32[]{:S(2)}, u32[]{:S(2)}) %collective-permute-start.10) | collective-permute-done | bytes 65568 | tf_op jit(solution)/shard_map/ppermute | solution.py:55
  117.9 2.8 %collective-permute-done.11 = f32[64,256]{1,0:T(8,128)S(1)} collective-permute-done((f32[64,256]{1,0:T(8,128)S(1)}, f32[64,256]{1,0:T(8,128)S(1)}, u32[]{:S(2)}, u32[]{:S(2)}) %collective-permute-start.11) | collective-permute-done | bytes 65568 | tf_op jit(solution)/shard_map/ppermute | solution.py:57
  121.5 4.0 %collective-permute-done.12 = f32[64,256]{1,0:T(8,128)S(1)} collective-permute-done((f32[64,256]{1,0:T(8,128)S(1)}, f32[64,256]{1,0:T(8,128)S(1)}, u32[]{:S(2)}, u32[]{:S(2)}) %collective-permute-start.12) | collective-permute-done | bytes 65568 | tf_op jit(solution)/shard_map/ppermute | solution.py:57
  125.6 7.0 %collective-permute-done.13 = f32[64,256]{1,0:T(8,128)S(1)} collective-permute-done((f32[64,256]{1,0:T(8,128)S(1)}, f32[64,256]{1,0:T(8,128)S(1)}, u32[]{:S(2)}, u32[]{:S(2)}) %collective-permute-start.13) | collective-permute-done | bytes 65568 | tf_op jit(solution)/shard_map/ppermute | solution.py:57
  133.7 2.5 %collective-permute-done.14 = f32[64,256]{1,0:T(8,128)S(1)} collective-permute-done((f32[64,256]{1,0:T(8,128)S(1)}, f32[64,256]{1,0:T(8,128)S(1)}, u32[]{:S(2)}, u32[]{:S(2)}) %collective-permute-start.14) | collective-permute-done | bytes 65568 | tf_op jit(solution)/shard_map/ppermute | solution.py:57
  136.2 2.9 %collective-permute-start.15 = (f32[64,256]{1,0:T(8,128)S(1)}, f32[64,256]{1,0:T(8,128)S(1)}, u32[]{:S(2)}, u32[]{:S(2)}) collective-permute-start(f32[64,256]{1,0:T(8,128)S(1)} %add.70), channel_id=1, source_target_pairs={{0,16},{1,17},{2,18},{3,19},{4,20},{5,21},{6,22},{7,23},{8,24},{9,... | collective-permute-start | bytes 196616 | tf_op jit(solution)/shard_map/ppermute | solution.py:57
  141.1 4.5 %collective-permute-done.16 = f32[64,256]{1,0:T(8,128)S(1)} collective-permute-done((f32[64,256]{1,0:T(8,128)S(1)}, f32[64,256]{1,0:T(8,128)S(1)}, u32[]{:S(2)}, u32[]{:S(2)}) %collective-permute-start.16) | collective-permute-done | bytes 65568 | tf_op jit(solution)/shard_map/ppermute | solution.py:57
  146.0 2.8 %collective-permute-done.17 = f32[64,256]{1,0:T(8,128)S(1)} collective-permute-done((f32[64,256]{1,0:T(8,128)S(1)}, f32[64,256]{1,0:T(8,128)S(1)}, u32[]{:S(2)}, u32[]{:S(2)}) %collective-permute-start.17) | collective-permute-done | bytes 65568 | tf_op jit(solution)/shard_map/ppermute | solution.py:59
  148.8 9.5 %collective-permute-start.18 = (f32[128,256]{1,0:T(8,128)S(1)}, f32[128,256]{1,0:T(8,128)S(1)}, u32[]{:S(2)}, u32[]{:S(2)}) collective-permute-start(f32[128,256]{1,0:T(8,128)S(1)} %maximum_select_fusion.6), channel_id=1, source_target_pairs={{0,32},{1,33},{2,34},{3,35},{4,36},{5,37},{6,38},{7,39},{8,40},{9,... | collective-permute-start | bytes 393224 | tf_op jit(solution)/shard_map/ppermute | solution.py:59
  160.1 2.3 %gather_fusion = f32[256]{0:T(256)S(1)} fusion(f32[256,256]{1,0:T(8,128)S(1)} %bitcast.57, s32[256]{0:T(256)S(1)} %bitcast.56), kind=kCustom, calls=%fused_computation | custom fusion | bytes 4096 | tf_op jit(solution)/shard_map/jit(_diag)/jit(diagonal)/cond/branch_0_fun/gather | solution.py:21
  (88 shorter events, 34.8 us)
Async XLA Ops:
  0.6 47.4 %copy-start = (f32[1536,384]{1,0:T(8,128)S(1)}, f32[1536,384]{1,0:T(8,128)}, u32[]{:S(2)}) copy-start(f32[1536,384]{1,0:T(8,128)} %param.7) | copy-start | bytes 7077892
  0.6 9.5 %collective-permute-start = (f32[48,256]{1,0:T(8,128)}, f32[48,256]{1,0:T(8,128)S(1)}, u32[]{:S(2)}, u32[]{:S(2)}) collective-permute-start(f32[48,256]{1,0:T(8,128)} %param.8), channel_id=1, source_target_pairs={{0,4},{1,5},{2,6},{3,7},{4,0},{5,1},{6,2},{7,3},{8,12},{9,13},{10,... | collective-permute-start | bytes 147464 | tf_op jit(solution)/shard_map/ppermute | solution.py:81
  11.0 5.5 %collective-permute-start.1 = (f32[96,256]{1,0:T(8,128)S(1)}, f32[96,256]{1,0:T(8,128)S(1)}, u32[]{:S(2)}, u32[]{:S(2)}) collective-permute-start(f32[96,256]{1,0:T(8,128)S(1)} %maximum_select_fusion.7), channel_id=1, source_target_pairs={{0,2},{1,3},{2,0},{3,1},{4,6},{5,7},{6,4},{7,5},{8,10},{9,11},{10,... | collective-permute-start | bytes 294920 | tf_op jit(solution)/shard_map/ppermute | solution.py:81
  16.6 4.6 %collective-permute-start.2 = (f32[192,256]{1,0:T(8,128)S(1)}, f32[192,256]{1,0:T(8,128)S(1)}, u32[]{:S(2)}, u32[]{:S(2)}) collective-permute-start(f32[192,256]{1,0:T(8,128)S(1)} %maximum_select_fusion.5), channel_id=1, source_target_pairs={{0,1},{1,0},{2,3},{3,2},{4,5},{5,4},{6,7},{7,6},{8,9},{9,8},{10,11... | collective-permute-start | bytes 589832 | tf_op jit(solution)/shard_map/ppermute | solution.py:81
  21.2 8.5 %collective-permute-start.3 = (f32[384,256]{1,0:T(8,128)S(1)}, f32[384,256]{1,0:T(8,128)}, u32[]{:S(2)}, u32[]{:S(2)}) collective-permute-start(f32[384,256]{1,0:T(8,128)S(1)} %maximum_select_fusion.2), channel_id=1, source_target_pairs={{0,16},{1,17},{2,18},{3,19},{4,20},{5,21},{6,22},{7,23},{8,24},{9,... | collective-permute-start | bytes 1179656 | tf_op jit(solution)/shard_map/ppermute | solution.py:81
  30.9 15.5 %collective-permute-start.4 = (f32[768,256]{1,0:T(8,128)S(1)}, f32[768,256]{1,0:T(8,128)}, u32[]{:S(2)}, u32[]{:S(2)}) collective-permute-start(f32[768,256]{1,0:T(8,128)S(1)} %maximum_select_fusion.1), channel_id=1, source_target_pairs={{0,8},{1,9},{2,10},{3,11},{4,12},{5,13},{6,14},{7,15},{8,0},{9,1},... | collective-permute-start | bytes 2359304 | tf_op jit(solution)/shard_map/ppermute | solution.py:81
  50.9 9.5 %copy-start.1 = (f32[256,256]{1,0:T(8,128)S(1)}, f32[256,256]{1,0:T(8,128)}, u32[]{:S(2)}) copy-start(f32[256,256]{1,0:T(8,128)} %param.10) | copy-start | bytes 786436
  51.0 6.8 %collective-permute-start.5 = (f32[192,256]{0,1:T(8,128)S(1)}, f32[192,256]{0,1:T(8,128)}, u32[]{:S(2)}, u32[]{:S(2)}) collective-permute-start(f32[192,256]{0,1:T(8,128)S(1)} %slice_select_fusion), channel_id=1, source_target_pairs={{0,32},{32,0},{64,96},{96,64},{128,160},{160,128},{192,224},{224,1... | collective-permute-start | bytes 589832 | tf_op jit(solution)/shard_map/ppermute | solution.py:109
  59.0 48.1 %copy-start.6 = (f32[32,8]{0,1:T(8,128)S(1)}, f32[32,8]{0,1:T(8,128)}, u32[]{:S(2)}) copy-start(f32[32,8]{0,1:T(8,128)} %param.11) | copy-start | bytes 3076
  59.0 4.8 %collective-permute-start.6 = (f32[96,256]{0,1:T(8,128)S(1)}, f32[96,256]{0,1:T(8,128)S(1)}, u32[]{:S(2)}, u32[]{:S(2)}) collective-permute-start(f32[96,256]{0,1:T(8,128)S(1)} %slice_select_fusion.3), channel_id=1, source_target_pairs={{0,64},{32,96},{64,0},{96,32},{128,192},{160,224},{192,128},{224,1... | collective-permute-start | bytes 294920 | tf_op jit(solution)/shard_map/ppermute | solution.py:109
  64.0 5.4 %collective-permute-start.7 = (f32[48,256]{0,1:T(8,128)S(1)}, f32[48,256]{0,1:T(8,128)S(1)}, u32[]{:S(2)}, u32[]{:S(2)}) collective-permute-start(f32[48,256]{0,1:T(8,128)S(1)} %slice_select_fusion.2), channel_id=1, source_target_pairs={{0,128},{32,160},{64,192},{96,224},{128,0},{160,32},{192,64},{224,... | collective-permute-start | bytes 147464 | tf_op jit(solution)/shard_map/ppermute | solution.py:109
  70.2 37.9 %collective-permute-start.8 = (f32[48,256]{0,1:T(8,128)}, f32[48,256]{0,1:T(8,128)}, u32[]{:S(2)}, u32[]{:S(2)}) collective-permute-start(f32[48,256]{0,1:T(8,128)} %select_add_fusion.2), channel_id=1, source_target_pairs={{0,0},{1,8},{2,16},{3,24},{4,32},{5,40},{6,48},{7,56},{8,64},{9,72... | collective-permute-start | bytes 147464 | tf_op jit(solution)/shard_map/ppermute | solution.py:111
  111.2 47.2 %copy-start.3 = (f32[128,48]{0,1:T(8,128)S(1)}, f32[128,48]{0,1:T(8,128)}, u32[]{:S(2)}) copy-start(f32[128,48]{0,1:T(8,128)} %copy-done.2) | copy-start | bytes 73732
  111.2 1.7 %collective-permute-start.9 = (f32[128,256]{1,0:T(8,128)S(1)}, f32[128,256]{1,0:T(8,128)}, u32[]{:S(2)}, u32[]{:S(2)}) collective-permute-start(f32[128,256]{1,0:T(8,128)S(1)} %slice_select_fusion.1), channel_id=1, source_target_pairs={{0,32},{1,33},{2,34},{3,35},{4,36},{5,37},{6,38},{7,39},{8,40},{9,... | collective-permute-start | bytes 393224 | tf_op jit(solution)/shard_map/ppermute | solution.py:55
  111.5 46.9 %copy-start.5 = (f32[128,48]{0,1:T(8,128)S(1)}, f32[128,48]{0,1:T(8,128)}, u32[]{:S(2)}) copy-start(f32[128,48]{0,1:T(8,128)} %copy-done.4) | copy-start | bytes 73732
  113.9 3.6 %collective-permute-start.10 = (f32[64,256]{1,0:T(8,128)S(1)}, f32[64,256]{1,0:T(8,128)S(1)}, u32[]{:S(2)}, u32[]{:S(2)}) collective-permute-start(f32[64,256]{1,0:T(8,128)S(1)} %slice_select_fusion.4), channel_id=1, source_target_pairs={{0,64},{1,65},{2,66},{3,67},{4,68},{5,69},{6,70},{7,71},{8,72},{9,... | collective-permute-start | bytes 196616 | tf_op jit(solution)/shard_map/ppermute | solution.py:55
  117.5 3.2 %collective-permute-start.11 = (f32[64,256]{1,0:T(8,128)S(1)}, f32[64,256]{1,0:T(8,128)S(1)}, u32[]{:S(2)}, u32[]{:S(2)}) collective-permute-start(f32[64,256]{1,0:T(8,128)S(1)} %select_add_fusion.4), channel_id=1, source_target_pairs={{0,1},{1,0},{2,3},{3,2},{4,5},{5,4},{6,7},{7,6},{8,9},{9,8},{10,11... | collective-permute-start | bytes 196616 | tf_op jit(solution)/shard_map/ppermute | solution.py:57
  120.7 4.8 %collective-permute-start.12 = (f32[64,256]{1,0:T(8,128)S(1)}, f32[64,256]{1,0:T(8,128)S(1)}, u32[]{:S(2)}, u32[]{:S(2)}) collective-permute-start(f32[64,256]{1,0:T(8,128)S(1)} %add.67), channel_id=1, source_target_pairs={{0,2},{1,3},{2,0},{3,1},{4,6},{5,7},{6,4},{7,5},{8,10},{9,11},{10,... | collective-permute-start | bytes 196616 | tf_op jit(solution)/shard_map/ppermute | solution.py:57
  125.5 7.1 %collective-permute-start.13 = (f32[64,256]{1,0:T(8,128)S(1)}, f32[64,256]{1,0:T(8,128)S(1)}, u32[]{:S(2)}, u32[]{:S(2)}) collective-permute-start(f32[64,256]{1,0:T(8,128)S(1)} %add.68), channel_id=1, source_target_pairs={{0,4},{1,5},{2,6},{3,7},{4,0},{5,1},{6,2},{7,3},{8,12},{9,13},{10,... | collective-permute-start | bytes 196616 | tf_op jit(solution)/shard_map/ppermute | solution.py:57
  132.7 3.5 %collective-permute-start.14 = (f32[64,256]{1,0:T(8,128)S(1)}, f32[64,256]{1,0:T(8,128)S(1)}, u32[]{:S(2)}, u32[]{:S(2)}) collective-permute-start(f32[64,256]{1,0:T(8,128)S(1)} %add.69), channel_id=1, source_target_pairs={{0,8},{1,9},{2,10},{3,11},{4,12},{5,13},{6,14},{7,15},{8,0},{9,1},... | collective-permute-start | bytes 196616 | tf_op jit(solution)/shard_map/ppermute | solution.py:57
  136.2 4.7 %collective-permute-start.15 = (f32[64,256]{1,0:T(8,128)S(1)}, f32[64,256]{1,0:T(8,128)S(1)}, u32[]{:S(2)}, u32[]{:S(2)}) collective-permute-start(f32[64,256]{1,0:T(8,128)S(1)} %add.70), channel_id=1, source_target_pairs={{0,16},{1,17},{2,18},{3,19},{4,20},{5,21},{6,22},{7,23},{8,24},{9,... | collective-permute-start | bytes 196616 | tf_op jit(solution)/shard_map/ppermute | solution.py:57
  140.9 4.7 %collective-permute-start.16 = (f32[64,256]{1,0:T(8,128)S(1)}, f32[64,256]{1,0:T(8,128)S(1)}, u32[]{:S(2)}, u32[]{:S(2)}) collective-permute-start(f32[64,256]{1,0:T(8,128)S(1)} %add.71), channel_id=1, source_target_pairs={{0,128},{1,129},{2,130},{3,131},{4,132},{5,133},{6,134},{7,135},{8... | collective-permute-start | bytes 196616 | tf_op jit(solution)/shard_map/ppermute | solution.py:57
  145.6 3.2 %collective-permute-start.17 = (f32[64,256]{1,0:T(8,128)S(1)}, f32[64,256]{1,0:T(8,128)S(1)}, u32[]{:S(2)}, u32[]{:S(2)}) collective-permute-start(f32[64,256]{1,0:T(8,128)S(1)} %add.72), channel_id=1, source_target_pairs={{0,64},{1,65},{2,66},{3,67},{4,68},{5,69},{6,70},{7,71},{8,72},{9,... | collective-permute-start | bytes 196616 | tf_op jit(solution)/shard_map/ppermute | solution.py:59
  148.8 10.5 %collective-permute-start.18 = (f32[128,256]{1,0:T(8,128)S(1)}, f32[128,256]{1,0:T(8,128)S(1)}, u32[]{:S(2)}, u32[]{:S(2)}) collective-permute-start(f32[128,256]{1,0:T(8,128)S(1)} %maximum_select_fusion.6), channel_id=1, source_target_pairs={{0,32},{1,33},{2,34},{3,35},{4,36},{5,37},{6,38},{7,39},{8,40},{9,... | collective-permute-start | bytes 393224 | tf_op jit(solution)/shard_map/ppermute | solution.py:59
  (2 other events, 3.1 us)

commit v3 on v1

v3 whole, which is shorter than its diff:
```python
import jax
import jax.numpy as jnp
from jax import lax
from jax.sharding import PartitionSpec as P

ALL = ("row", "col")


def right_solve(factor, rows):
    return jax.scipy.linalg.solve_triangular(factor, rows.T, lower=True, trans=1).T


def left_solve(factor, matrix):
    return jax.scipy.linalg.solve_triangular(factor, matrix, lower=True, trans=1)


def diagonal_adjoint(factor, adjoint):
    product = jnp.dot(
        factor.T, adjoint, precision=lax.Precision.HIGHEST, preferred_element_type=jnp.float32
    )
    lower = jnp.tril(product) - 0.5 * jnp.diag(jnp.diag(product))
    symmetric = lower + lower.T
    half = left_solve(factor, symmetric)
    return 0.5 * left_solve(factor, half.T).T


def xor_perm(size, mask):
    return [(i, i ^ mask) for i in range(size)]


def offset(k, masks):
    return sum(m for b, m in enumerate(masks) if (k >> b) & 1)


def position(idx, masks):
    return sum(((idx & m) != 0).astype(jnp.int32) << b for b, m in enumerate(masks))


def exchange(value, axis, size, masks):
    got = [value]
    for k in range(1, 1 << len(masks)):
        got.append(lax.ppermute(value, axis, xor_perm(size, offset(k, masks))))
    return jnp.stack(got)


def gather_step(value, axis, size, masks):
    p = position(lax.axis_index(axis), masks)
    got = exchange(value, axis, size, masks)
    return jnp.concatenate(
        [lax.dynamic_index_in_dim(got, k ^ p, keepdims=False) for k in range(1 << len(masks))], axis=0
    )


def sum_step(value, axis, size, masks):
    p = position(lax.axis_index(axis), masks)
    got = exchange(value, axis, size, masks)
    terms = [lax.dynamic_index_in_dim(got, k ^ p, keepdims=False) for k in range(1 << len(masks))]
    while len(terms) > 1:
        terms = [terms[i] + terms[i + 1] for i in range(0, len(terms), 2)]
    return terms[0]


def scatter_step(value, axis, size, masks):
    n = 1 << len(masks)
    p = position(lax.axis_index(axis), masks)
    chunks = value.reshape((n, value.shape[0] // n) + value.shape[1:])
    total = lax.dynamic_index_in_dim(chunks, p, keepdims=False)
    for k in range(1, n):
        send = lax.dynamic_index_in_dim(chunks, p ^ k, keepdims=False)
        total = total + lax.ppermute(send, axis, xor_perm(size, offset(k, masks)))
    return total


def gather_groups(ncol):
    bits = [1 << k for k in range(ncol.bit_length() - 1)]
    order = [m for m in bits if m < 8][::-1] + [m for m in bits if m >= 8][::-1]
    return [tuple(order[i : i + 2]) for i in range(0, len(order), 2)]


def kept_chunk(idx, groups, nblocks):
    lo, span = 0, nblocks
    for masks in groups:
        n = 1 << len(masks)
        span //= n
        lo += span * sum(((idx & m) != 0) << b for b, m in enumerate(masks))
    return lo


def all_reduce(value, nrow, ncol):
    ndev = nrow * ncol
    bits = [1 << k for k in range(ndev.bit_length() - 1)]
    outer = tuple(ncol * m for m in (1, 2) if m < nrow)
    rest = [m for m in bits if m not in outer]
    inner = [tuple(rest[i : i + 2]) for i in range(0, len(rest), 2)]
    value = scatter_step(value, ALL, ndev, outer)
    for masks in inner:
        value = sum_step(value, ALL, ndev, masks)
    return gather_step(value, ALL, ndev, outer)


def make_body(nrow, ncol):
    assert nrow & (nrow - 1) == 0 and ncol & (ncol - 1) == 0
    row_bits = [1 << k for k in range(nrow.bit_length() - 1)]
    row_groups = [tuple(row_bits[i : i + 2]) for i in range(0, len(row_bits), 2)]
    owner_perm = [
        (r * ncol + c, c * nrow + kept_chunk(r, row_groups, nrow)) for r in range(nrow) for c in range(ncol)
    ]

    def inner(trailing_adjoint, panel, panel_adjoint, diag_factor, diag_adjoint):
        r = lax.axis_index("row")
        c = lax.axis_index("col")

        groups = gather_groups(ncol)
        gathered = panel
        for masks in groups:
            gathered = gather_step(gathered, "col", ncol, masks)
        order = [m for masks in groups for m in masks]
        blocks = gathered.reshape((2,) * len(order) + panel.shape)
        nbits = len(order)
        axis_of_bit = {m.bit_length() - 1: nbits - 1 - t for t, m in enumerate(order)}
        perm = [axis_of_bit[nbits - 1 - a] for a in range(nbits)] + [nbits, nbits + 1]
        gathered = blocks.transpose(perm).reshape((ncol * panel.shape[0], panel.shape[1]))

        share = lax.dot_general(
            trailing_adjoint,
            gathered,
            (((0,), (0,)), ((), ())),
            precision=lax.Precision.HIGHEST,
            preferred_element_type=jnp.float32,
        )

        for masks in row_groups:
            share = scatter_step(share, "row", nrow, masks)
        product = lax.ppermute(share, ALL, owner_perm)

        updated = panel_adjoint - 2.0 * product
        off_adjoint = right_solve(diag_factor, updated)
        local_term = jnp.dot(
            off_adjoint.T, panel, precision=lax.Precision.HIGHEST, preferred_element_type=jnp.float32
        )
        rows, cols = diag_adjoint.shape
        placed = lax.dynamic_update_slice(
            jnp.zeros((rows * nrow, cols * ncol), jnp.float32), diag_adjoint, (r * rows, c * cols)
        )
        accumulated = all_reduce(placed - local_term, nrow, ncol)
        return (off_adjoint, diagonal_adjoint(diag_factor, accumulated))

    return inner


def solution(mesh):
    return jax.shard_map(
        make_body(mesh.shape["row"], mesh.shape["col"]),
        mesh=mesh,
        in_specs=(
            P("row", "col"),
            P(ALL, None),
            P(ALL, None),
            P(),
            P("row", "col"),
        ),
        out_specs=(P(ALL, None), P()),
        check_vma=False,
    )
```

time: 193 us -> 155 us (0.80)
  waiting for transfers between devices: 90.5 us -> 59.2 us
  starting transfers between devices: 55.9 us -> 52 us
    ppermute x17 -> x27, waiting for transfers between devices: 90.5 us -> 59.2 us  [the longest x19 48.4 us: exchange(): got.append(lax.ppermute(value, axis, xor_perm(size, offset(k, masks))))]
    ppermute x17 -> x27, starting transfers between devices: 55.9 us -> 52 us  [the longest x19 36.2 us: exchange(): got.append(lax.ppermute(value, axis, xor_perm(size, offset(k, masks))))]
    select_n x7 -> x0, other arithmetic: 2.45 us -> none  [the longest x4 2.12 us: body(): jnp.where(upper, jnp.concatenate([got, gathered], axis=0), jnp.concatenat...]
  transfers between devices with their start and end apart: 17 -> 27, of which waited for: 16 -> 20; matrix products, arithmetic and copies ran while one was open for 14% -> 17% of each run, Pallas kernels for 0% -> 0%
where the time goes in v3:
time: 155 us
  waiting for transfers between devices  59.2 us (38%)
  starting transfers between devices  52 us (34%)
  other arithmetic  25 us (16%)
  local copies, waits for them, and re-layouts  10.4 us (7%)
  matrix products  7.18 us (5%)
    ppermute x19, waiting for transfers between devices, exchange(): got.append(lax.ppermute(value, axis, xor_perm(size, offset(k, masks))))  48.4 us
    ppermute x19, starting transfers between devices, exchange(): got.append(lax.ppermute(value, axis, xor_perm(size, offset(k, masks))))  36.2 us
    another operation x3, other arithmetic, right_solve(): jax.scipy.linalg.solve_triangular(factor, rows.T, lower=True, trans=1)  19.7 us
    ppermute x7, starting transfers between devices, scatter_step(): total = total + lax.ppermute(send, axis, xor_perm(size, offset(k, masks)))  11.5 us
    ppermute x7, waiting for transfers between devices, scatter_step(): total = total + lax.ppermute(send, axis, xor_perm(size, offset(k, masks)))  10.8 us
    ppermute x1, starting transfers between devices, inner(): product = lax.ppermute(share, ALL, owner_perm)  4.31 us
    another operation x6, local copies, waits for them, and re-layouts  3.93 us
  transfers between devices with their start and end apart: 27, of which 20 were waited for; matrix products, arithmetic and copies ran while one was open for 17% of the time, Pallas kernels for 0%

profile of v3, /device:TPU:1, one launch (start us, length us, event | category | flops | bytes accessed | tf_op | source)
XLA Modules:
  0.0 155.0 jit_solution(7430829259057765659)
XLA Ops:
  0.6 7.8 %collective-permute-start = (f32[48,256]{1,0:T(8,128)}, f32[48,256]{1,0:T(8,128)S(1)}, u32[]{:S(2)}, u32[]{:S(2)}) collective-permute-start(f32[48,256]{1,0:T(8,128)} %param.8), channel_id=1, source_target_pairs={{0,4},{1,5},{2,6},{3,7},{4,0},{5,1},{6,2},{7,3},{8,12},{9,13},{10,... | collective-permute-start | bytes 147464 | tf_op jit(solution)/shard_map/ppermute | solution.py:42
  10.2 3.7 %collective-permute-done.1 = f32[48,256]{1,0:T(8,128)S(1)} collective-permute-done((f32[48,256]{1,0:T(8,128)}, f32[48,256]{1,0:T(8,128)S(1)}, u32[]{:S(2)}, u32[]{:S(2)}) %collective-permute-start.1) | collective-permute-done | bytes 49184 | tf_op jit(solution)/shard_map/ppermute | solution.py:42
  16.6 2.7 %collective-permute-start.4 = (f32[192,256]{1,0:T(8,128)S(1)}, f32[192,256]{1,0:T(8,128)S(1)}, u32[]{:S(2)}, u32[]{:S(2)}) collective-permute-start(f32[192,256]{1,0:T(8,128)S(1)} %get-tuple-element.62), channel_id=1, source_target_pairs={{0,16},{1,17},{2,18},{3,19},{4,20},{5,21},{6,22},{7,23},{8,24},{9,... | collective-permute-start | bytes 589832 | tf_op jit(solution)/shard_map/ppermute | solution.py:42
  20.5 2.3 %collective-permute-done.4 = f32[192,256]{1,0:T(8,128)S(1)} collective-permute-done((f32[192,256]{1,0:T(8,128)S(1)}, f32[192,256]{1,0:T(8,128)S(1)}, u32[]{:S(2)}, u32[]{:S(2)}) %collective-permute-start.4) | collective-permute-done | bytes 196640 | tf_op jit(solution)/shard_map/ppermute | solution.py:42
  22.8 5.7 %collective-permute-done.5 = f32[192,256]{1,0:T(8,128)S(1)} collective-permute-done((f32[192,256]{1,0:T(8,128)S(1)}, f32[192,256]{1,0:T(8,128)S(1)}, u32[]{:S(2)}, u32[]{:S(2)}) %collective-permute-start.5) | collective-permute-done | bytes 196640 | tf_op jit(solution)/shard_map/ppermute | solution.py:42
  29.9 16.9 %collective-permute-done.6 = f32[768,256]{1,0:T(8,128)} collective-permute-done((f32[768,256]{1,0:T(8,128)}, f32[768,256]{1,0:T(8,128)}, u32[]{:S(2)}, u32[]{:S(2)}) %collective-permute-start.6) | collective-permute-done | bytes 786464 | tf_op jit(solution)/shard_map/ppermute | solution.py:42
  48.4 2.8 %convolution_bitcast_fusion = f32[384,256]{0,1:T(8,128)S(1)} fusion(f32[1536,256]{1,0:T(8,128)S(1)} %bitcast.149, f32[1536,384]{1,0:T(8,128)S(1)} %copy-done), kind=kOutput, calls=%fused_computation.8 | convolution fusion | flops 1811939328 | bytes 4325376 | tf_op jit(solution)/shard_map/dot_general | solution.py:124
  52.1 3.1 %collective-permute-start.7 = (f32[96,256]{1,0:T(8,128)}, f32[96,256]{1,0:T(8,128)S(1)}, u32[]{:S(2)}, u32[]{:S(2)}) collective-permute-start(f32[96,256]{1,0:T(8,128)} %get-tuple-element.51), channel_id=1, source_target_pairs={{0,32},{32,0},{64,96},{96,64},{128,160},{160,128},{192,224},{224,1... | collective-permute-start | bytes 294920 | tf_op jit(solution)/shard_map/ppermute | solution.py:70
  56.9 3.0 %collective-permute-done.8 = f32[96,256]{1,0:T(8,128)} collective-permute-done((f32[96,256]{1,0:T(8,128)}, f32[96,256]{1,0:T(8,128)}, u32[]{:S(2)}, u32[]{:S(2)}) %collective-permute-start.8) | collective-permute-done | bytes 98336 | tf_op jit(solution)/shard_map/ppermute | solution.py:70
  59.9 2.3 %collective-permute-done.9 = f32[96,256]{1,0:T(8,128)} collective-permute-done((f32[96,256]{1,0:T(8,128)S(1)}, f32[96,256]{1,0:T(8,128)}, u32[]{:S(2)}, u32[]{:S(2)}) %collective-permute-start.9) | collective-permute-done | bytes 98336 | tf_op jit(solution)/shard_map/ppermute | solution.py:70
  63.2 3.0 %collective-permute-start.10 = (f32[48,256]{1,0:T(8,128)S(1)}, f32[48,256]{1,0:T(8,128)S(1)}, u32[]{:S(2)}, u32[]{:S(2)}) collective-permute-start(f32[48,256]{1,0:T(8,128)S(1)} %dynamic-slice_bitcast_fusion.14), channel_id=1, source_target_pairs={{0,128},{32,160},{64,192},{96,224},{128,0},{160,32},{192,64},{224,... | collective-permute-start | bytes 147464 | tf_op jit(solution)/shard_map/ppermute | solution.py:70
  67.7 4.3 %collective-permute-start.11 = (f32[48,256]{1,0:T(8,128)S(1)}, f32[48,256]{1,0:T(8,128)S(1)}, u32[]{:S(2)}, u32[]{:S(2)}) collective-permute-start(f32[48,256]{1,0:T(8,128)S(1)} %bitcast_add_fusion.2), channel_id=1, source_target_pairs={{0,0},{1,8},{2,16},{3,24},{4,32},{5,40},{6,48},{7,56},{8,64},{9,72... | collective-permute-start | bytes 147464 | tf_op jit(solution)/shard_map/ppermute | solution.py:134
  72.1 4.0 %while.5 = (s32[]{:T(128)}, f32[256,256]{1,0:T(8,128)S(1)}, s32[2,2]{1,0:T(2,128)S(1)}, f32[2,128,128]{2,1,0:T(8,128)S(1)}, s32[]{:T(128)}) while((s32[]{:T(128)}, f32[256,256]{1,0:T(8,128)S(1)}, s32[2,2]{1,0:T(2,128)S(1)}, f32[2,128,128]{2,1,0:T(8,128)S(1)}, s32[]{:T(128)}) %tuple.50), condition=%wide.while_cond.1, body=%wide.while_body.1.sunk | while | flops 2 | bytes 131181 | solution.py:10
  76.1 19.7 %custom-call.7 = f32[2,128,128]{1,2,0:T(8,128)S(1)} custom-call(f32[2,128,128]{2,1,0:T(8,128)S(1)} %get-tuple-element.18), custom_call_target="InvertDiagBlocksLowerTriangular" | custom-call | tf_op jit(solution)/shard_map/jit(_solve_triangular)/triangular_solve | solution.py:10
  99.9 3.6 %collective-permute-start.13 = (f32[64,256]{1,0:T(8,128)S(1)}, f32[64,256]{1,0:T(8,128)S(1)}, u32[]{:S(2)}, u32[]{:S(2)}) collective-permute-start(f32[64,256]{1,0:T(8,128)S(1)} %get-tuple-element.60), channel_id=1, source_target_pairs={{0,64},{1,65},{2,66},{3,67},{4,68},{5,69},{6,70},{7,71},{8,72},{9,... | collective-permute-start | bytes 196616 | tf_op jit(solution)/shard_map/ppermute | solution.py:70
  103.6 2.3 %collective-permute-done.13 = f32[64,256]{1,0:T(8,128)S(1)} collective-permute-done((f32[64,256]{1,0:T(8,128)S(1)}, f32[64,256]{1,0:T(8,128)S(1)}, u32[]{:S(2)}, u32[]{:S(2)}) %collective-permute-start.13) | collective-permute-done | bytes 65568 | tf_op jit(solution)/shard_map/ppermute | solution.py:70
  108.3 3.2 %collective-permute-start.16 = (f32[64,256]{1,0:T(8,128)S(1)}, f32[64,256]{1,0:T(8,128)S(1)}, u32[]{:S(2)}, u32[]{:S(2)}) collective-permute-start(f32[64,256]{1,0:T(8,128)S(1)} %fusion.21), channel_id=1, source_target_pairs={{0,2},{1,3},{2,0},{3,1},{4,6},{5,7},{6,4},{7,5},{8,10},{9,11},{10,... | collective-permute-start | bytes 196616 | tf_op jit(solution)/shard_map/ppermute | solution.py:42
  113.5 4.0 %collective-permute-done.17 = f32[64,256]{1,0:T(8,128)S(1)} collective-permute-done((f32[64,256]{1,0:T(8,128)S(1)}, f32[64,256]{1,0:T(8,128)S(1)}, u32[]{:S(2)}, u32[]{:S(2)}) %collective-permute-start.17) | collective-permute-done | bytes 65568 | tf_op jit(solution)/shard_map/ppermute | solution.py:42
  119.0 5.2 %collective-permute-start.20 = (f32[64,256]{1,0:T(8,128)S(1)}, f32[64,256]{1,0:T(8,128)S(1)}, u32[]{:S(2)}, u32[]{:S(2)}) collective-permute-start(f32[64,256]{1,0:T(8,128)S(1)} %fusion.48), channel_id=1, source_target_pairs={{0,12},{1,13},{2,14},{3,15},{4,8},{5,9},{6,10},{7,11},{8,4},{9,5},... | collective-permute-start | bytes 196616 | tf_op jit(solution)/shard_map/ppermute | solution.py:42
  124.7 3.6 %collective-permute-done.20 = f32[64,256]{1,0:T(8,128)S(1)} collective-permute-done((f32[64,256]{1,0:T(8,128)S(1)}, f32[64,256]{1,0:T(8,128)S(1)}, u32[]{:S(2)}, u32[]{:S(2)}) %collective-permute-start.20) | collective-permute-done | bytes 65568 | tf_op jit(solution)/shard_map/ppermute | solution.py:42
  128.3 2.8 %collective-permute-start.21 = (f32[64,256]{1,0:T(8,128)S(1)}, f32[64,256]{1,0:T(8,128)S(1)}, u32[]{:S(2)}, u32[]{:S(2)}) collective-permute-start(f32[64,256]{1,0:T(8,128)S(1)} %fusion.47), channel_id=1, source_target_pairs={{0,16},{1,17},{2,18},{3,19},{4,20},{5,21},{6,22},{7,23},{8,24},{9,... | collective-permute-start | bytes 196616 | tf_op jit(solution)/shard_map/ppermute | solution.py:42
  136.0 4.1 %collective-permute-done.23 = f32[64,256]{1,0:T(8,128)S(1)} collective-permute-done((f32[64,256]{1,0:T(8,128)S(1)}, f32[64,256]{1,0:T(8,128)S(1)}, u32[]{:S(2)}, u32[]{:S(2)}) %collective-permute-start.23) | collective-permute-done | bytes 65568 | tf_op jit(solution)/shard_map/ppermute | solution.py:42
  140.2 3.6 %collective-permute-start.24 = (f32[64,256]{1,0:T(8,128)S(1)}, f32[64,256]{1,0:T(8,128)S(1)}, u32[]{:S(2)}, u32[]{:S(2)}) collective-permute-start(f32[64,256]{1,0:T(8,128)S(1)} %fusion.46), channel_id=1, source_target_pairs={{0,32},{1,33},{2,34},{3,35},{4,36},{5,37},{6,38},{7,39},{8,40},{9,... | collective-permute-start | bytes 196616 | tf_op jit(solution)/shard_map/ppermute | solution.py:42
  149.8 2.3 %gather_fusion = f32[256]{0:T(256)S(1)} fusion(f32[256,256]{1,0:T(8,128)S(1)} %bitcast.147, s32[256]{0:T(256)S(1)} %bitcast.146), kind=kCustom, calls=%fused_computation | custom fusion | bytes 4096 | tf_op jit(solution)/shard_map/jit(_diag)/jit(diagonal)/cond/branch_0_fun/gather | solution.py:21
  (103 shorter events, 41.7 us)
Async XLA Ops:
  0.6 9.5 %collective-permute-start = (f32[48,256]{1,0:T(8,128)}, f32[48,256]{1,0:T(8,128)S(1)}, u32[]{:S(2)}, u32[]{:S(2)}) collective-permute-start(f32[48,256]{1,0:T(8,128)} %param.8), channel_id=1, source_target_pairs={{0,4},{1,5},{2,6},{3,7},{4,0},{5,1},{6,2},{7,3},{8,12},{9,13},{10,... | collective-permute-start | bytes 147464 | tf_op jit(solution)/shard_map/ppermute | solution.py:42
  8.5 5.4 %collective-permute-start.1 = (f32[48,256]{1,0:T(8,128)}, f32[48,256]{1,0:T(8,128)S(1)}, u32[]{:S(2)}, u32[]{:S(2)}) collective-permute-start(f32[48,256]{1,0:T(8,128)} %param.8), channel_id=1, source_target_pairs={{0,2},{1,3},{2,0},{3,1},{4,6},{5,7},{6,4},{7,5},{8,10},{9,11},{10,... | collective-permute-start | bytes 147464 | tf_op jit(solution)/shard_map/ppermute | solution.py:42
  9.7 5.3 %collective-permute-start.2 = (f32[48,256]{1,0:T(8,128)}, f32[48,256]{1,0:T(8,128)S(1)}, u32[]{:S(2)}, u32[]{:S(2)}) collective-permute-start(f32[48,256]{1,0:T(8,128)} %param.8), channel_id=1, source_target_pairs={{0,6},{1,7},{2,4},{3,5},{4,2},{5,3},{6,0},{7,1},{8,14},{9,15},{10,... | collective-permute-start | bytes 147464 | tf_op jit(solution)/shard_map/ppermute | solution.py:42
  15.9 4.6 %collective-permute-start.3 = (f32[192,256]{1,0:T(8,128)S(1)}, f32[192,256]{1,0:T(8,128)S(1)}, u32[]{:S(2)}, u32[]{:S(2)}) collective-permute-start(f32[192,256]{1,0:T(8,128)S(1)} %get-tuple-element.62), channel_id=1, source_target_pairs={{0,1},{1,0},{2,3},{3,2},{4,5},{5,4},{6,7},{7,6},{8,9},{9,8},{10,11... | collective-permute-start | bytes 589832 | tf_op jit(solution)/shard_map/ppermute | solution.py:42
  16.6 6.2 %collective-permute-start.4 = (f32[192,256]{1,0:T(8,128)S(1)}, f32[192,256]{1,0:T(8,128)S(1)}, u32[]{:S(2)}, u32[]{:S(2)}) collective-permute-start(f32[192,256]{1,0:T(8,128)S(1)} %get-tuple-element.62), channel_id=1, source_target_pairs={{0,16},{1,17},{2,18},{3,19},{4,20},{5,21},{6,22},{7,23},{8,24},{9,... | collective-permute-start | bytes 589832 | tf_op jit(solution)/shard_map/ppermute | solution.py:42
  19.4 9.1 %collective-permute-start.5 = (f32[192,256]{1,0:T(8,128)S(1)}, f32[192,256]{1,0:T(8,128)S(1)}, u32[]{:S(2)}, u32[]{:S(2)}) collective-permute-start(f32[192,256]{1,0:T(8,128)S(1)} %get-tuple-element.62), channel_id=1, source_target_pairs={{0,17},{1,16},{2,19},{3,18},{4,21},{5,20},{6,23},{7,22},{8,25},{9,... | collective-permute-start | bytes 589832 | tf_op jit(solution)/shard_map/ppermute | solution.py:42
  29.6 17.2 %collective-permute-start.6 = (f32[768,256]{1,0:T(8,128)}, f32[768,256]{1,0:T(8,128)}, u32[]{:S(2)}, u32[]{:S(2)}) collective-permute-start(f32[768,256]{1,0:T(8,128)} %get-tuple-element.45), channel_id=1, source_target_pairs={{0,8},{1,9},{2,10},{3,11},{4,12},{5,13},{6,14},{7,15},{8,0},{9,1},... | collective-permute-start | bytes 2359304 | tf_op jit(solution)/shard_map/ppermute | solution.py:42
  52.1 4.7 %collective-permute-start.7 = (f32[96,256]{1,0:T(8,128)}, f32[96,256]{1,0:T(8,128)S(1)}, u32[]{:S(2)}, u32[]{:S(2)}) collective-permute-start(f32[96,256]{1,0:T(8,128)} %get-tuple-element.51), channel_id=1, source_target_pairs={{0,32},{32,0},{64,96},{96,64},{128,160},{160,128},{192,224},{224,1... | collective-permute-start | bytes 294920 | tf_op jit(solution)/shard_map/ppermute | solution.py:70
  55.2 4.7 %collective-permute-start.8 = (f32[96,256]{1,0:T(8,128)}, f32[96,256]{1,0:T(8,128)}, u32[]{:S(2)}, u32[]{:S(2)}) collective-permute-start(f32[96,256]{1,0:T(8,128)} %get-tuple-element.53), channel_id=1, source_target_pairs={{0,64},{32,96},{64,0},{96,32},{128,192},{160,224},{192,128},{224,1... | collective-permute-start | bytes 294920 | tf_op jit(solution)/shard_map/ppermute | solution.py:70
  56.5 5.6 %collective-permute-start.9 = (f32[96,256]{1,0:T(8,128)S(1)}, f32[96,256]{1,0:T(8,128)}, u32[]{:S(2)}, u32[]{:S(2)}) collective-permute-start(f32[96,256]{1,0:T(8,128)S(1)} %get-tuple-element.52), channel_id=1, source_target_pairs={{0,96},{32,64},{64,32},{96,0},{128,224},{160,192},{192,160},{224,1... | collective-permute-start | bytes 294920 | tf_op jit(solution)/shard_map/ppermute | solution.py:70
  63.2 4.5 %collective-permute-start.10 = (f32[48,256]{1,0:T(8,128)S(1)}, f32[48,256]{1,0:T(8,128)S(1)}, u32[]{:S(2)}, u32[]{:S(2)}) collective-permute-start(f32[48,256]{1,0:T(8,128)S(1)} %dynamic-slice_bitcast_fusion.14), channel_id=1, source_target_pairs={{0,128},{32,160},{64,192},{96,224},{128,0},{160,32},{192,64},{224,... | collective-permute-start | bytes 147464 | tf_op jit(solution)/shard_map/ppermute | solution.py:70
  67.7 29.8 %collective-permute-start.11 = (f32[48,256]{1,0:T(8,128)S(1)}, f32[48,256]{1,0:T(8,128)S(1)}, u32[]{:S(2)}, u32[]{:S(2)}) collective-permute-start(f32[48,256]{1,0:T(8,128)S(1)} %bitcast_add_fusion.2), channel_id=1, source_target_pairs={{0,0},{1,8},{2,16},{3,24},{4,32},{5,40},{6,48},{7,56},{8,64},{9,72... | collective-permute-start | bytes 147464 | tf_op jit(solution)/shard_map/ppermute | solution.py:134
  99.9 6.0 %collective-permute-start.13 = (f32[64,256]{1,0:T(8,128)S(1)}, f32[64,256]{1,0:T(8,128)S(1)}, u32[]{:S(2)}, u32[]{:S(2)}) collective-permute-start(f32[64,256]{1,0:T(8,128)S(1)} %get-tuple-element.60), channel_id=1, source_target_pairs={{0,64},{1,65},{2,66},{3,67},{4,68},{5,69},{6,70},{7,71},{8,72},{9,... | collective-permute-start | bytes 196616 | tf_op jit(solution)/shard_map/ppermute | solution.py:70
  107.6 5.6 %collective-permute-start.15 = (f32[64,256]{1,0:T(8,128)S(1)}, f32[64,256]{1,0:T(8,128)S(1)}, u32[]{:S(2)}, u32[]{:S(2)}) collective-permute-start(f32[64,256]{1,0:T(8,128)S(1)} %fusion.21), channel_id=1, source_target_pairs={{0,1},{1,0},{2,3},{3,2},{4,5},{5,4},{6,7},{7,6},{8,9},{9,8},{10,11... | collective-permute-start | bytes 196616 | tf_op jit(solution)/shard_map/ppermute | solution.py:42
  108.3 5.2 %collective-permute-start.16 = (f32[64,256]{1,0:T(8,128)S(1)}, f32[64,256]{1,0:T(8,128)S(1)}, u32[]{:S(2)}, u32[]{:S(2)}) collective-permute-start(f32[64,256]{1,0:T(8,128)S(1)} %fusion.21), channel_id=1, source_target_pairs={{0,2},{1,3},{2,0},{3,1},{4,6},{5,7},{6,4},{7,5},{8,10},{9,11},{10,... | collective-permute-start | bytes 196616 | tf_op jit(solution)/shard_map/ppermute | solution.py:42
  111.5 6.0 %collective-permute-start.17 = (f32[64,256]{1,0:T(8,128)S(1)}, f32[64,256]{1,0:T(8,128)S(1)}, u32[]{:S(2)}, u32[]{:S(2)}) collective-permute-start(f32[64,256]{1,0:T(8,128)S(1)} %fusion.21), channel_id=1, source_target_pairs={{0,3},{1,2},{2,1},{3,0},{4,7},{5,6},{6,5},{7,4},{8,11},{9,10},{10,... | collective-permute-start | bytes 196616 | tf_op jit(solution)/shard_map/ppermute | solution.py:42
  117.6 7.1 %collective-permute-start.18 = (f32[64,256]{1,0:T(8,128)S(1)}, f32[64,256]{1,0:T(8,128)S(1)}, u32[]{:S(2)}, u32[]{:S(2)}) collective-permute-start(f32[64,256]{1,0:T(8,128)S(1)} %fusion.48), channel_id=1, source_target_pairs={{0,4},{1,5},{2,6},{3,7},{4,0},{5,1},{6,2},{7,3},{8,12},{9,13},{10,... | collective-permute-start | bytes 196616 | tf_op jit(solution)/shard_map/ppermute | solution.py:42
  118.2 6.5 %collective-permute-start.19 = (f32[64,256]{1,0:T(8,128)S(1)}, f32[64,256]{1,0:T(8,128)S(1)}, u32[]{:S(2)}, u32[]{:S(2)}) collective-permute-start(f32[64,256]{1,0:T(8,128)S(1)} %fusion.48), channel_id=1, source_target_pairs={{0,8},{1,9},{2,10},{3,11},{4,12},{5,13},{6,14},{7,15},{8,0},{9,1},... | collective-permute-start | bytes 196616 | tf_op jit(solution)/shard_map/ppermute | solution.py:42
  119.0 9.3 %collective-permute-start.20 = (f32[64,256]{1,0:T(8,128)S(1)}, f32[64,256]{1,0:T(8,128)S(1)}, u32[]{:S(2)}, u32[]{:S(2)}) collective-permute-start(f32[64,256]{1,0:T(8,128)S(1)} %fusion.48), channel_id=1, source_target_pairs={{0,12},{1,13},{2,14},{3,15},{4,8},{5,9},{6,10},{7,11},{8,4},{9,5},... | collective-permute-start | bytes 196616 | tf_op jit(solution)/shard_map/ppermute | solution.py:42
  128.3 5.8 %collective-permute-start.21 = (f32[64,256]{1,0:T(8,128)S(1)}, f32[64,256]{1,0:T(8,128)S(1)}, u32[]{:S(2)}, u32[]{:S(2)}) collective-permute-start(f32[64,256]{1,0:T(8,128)S(1)} %fusion.47), channel_id=1, source_target_pairs={{0,16},{1,17},{2,18},{3,19},{4,20},{5,21},{6,22},{7,23},{8,24},{9,... | collective-permute-start | bytes 196616 | tf_op jit(solution)/shard_map/ppermute | solution.py:42
  131.1 4.9 %collective-permute-start.22 = (f32[64,256]{1,0:T(8,128)S(1)}, f32[64,256]{1,0:T(8,128)S(1)}, u32[]{:S(2)}, u32[]{:S(2)}) collective-permute-start(f32[64,256]{1,0:T(8,128)S(1)} %fusion.47), channel_id=1, source_target_pairs={{0,128},{1,129},{2,130},{3,131},{4,132},{5,133},{6,134},{7,135},{8... | collective-permute-start | bytes 196616 | tf_op jit(solution)/shard_map/ppermute | solution.py:42
  133.1 7.0 %collective-permute-start.23 = (f32[64,256]{1,0:T(8,128)S(1)}, f32[64,256]{1,0:T(8,128)S(1)}, u32[]{:S(2)}, u32[]{:S(2)}) collective-permute-start(f32[64,256]{1,0:T(8,128)S(1)} %fusion.47), channel_id=1, source_target_pairs={{0,144},{1,145},{2,146},{3,147},{4,148},{5,149},{6,150},{7,151},{8... | collective-permute-start | bytes 196616 | tf_op jit(solution)/shard_map/ppermute | solution.py:42
  140.2 5.3 %collective-permute-start.24 = (f32[64,256]{1,0:T(8,128)S(1)}, f32[64,256]{1,0:T(8,128)S(1)}, u32[]{:S(2)}, u32[]{:S(2)}) collective-permute-start(f32[64,256]{1,0:T(8,128)S(1)} %fusion.46), channel_id=1, source_target_pairs={{0,32},{1,33},{2,34},{3,35},{4,36},{5,37},{6,38},{7,39},{8,40},{9,... | collective-permute-start | bytes 196616 | tf_op jit(solution)/shard_map/ppermute | solution.py:42
  143.8 5.2 %collective-permute-start.26 = (f32[64,256]{1,0:T(8,128)S(1)}, f32[64,256]{1,0:T(8,128)S(1)}, u32[]{:S(2)}, u32[]{:S(2)}) collective-permute-start(f32[64,256]{1,0:T(8,128)S(1)} %fusion.46), channel_id=1, source_target_pairs={{0,96},{1,97},{2,98},{3,99},{4,100},{5,101},{6,102},{7,103},{8,104... | collective-permute-start | bytes 196616 | tf_op jit(solution)/shard_map/ppermute | solution.py:42
  (8 other events, 144.7 us)

commit v4 on v3

--- a/solution.py
+++ b/solution.py
@@ -100,16 +100,17 @@
 
 def make_body(nrow, ncol):
     assert nrow & (nrow - 1) == 0 and ncol & (ncol - 1) == 0
+    ndev = nrow * ncol
     row_bits = [1 << k for k in range(nrow.bit_length() - 1)]
     row_groups = [tuple(row_bits[i : i + 2]) for i in range(0, len(row_bits), 2)]
+    row_groups_natural = row_groups
+    col_bits = [1 << k for k in range(ncol.bit_length() - 1)]
+    col_groups_natural = [tuple(col_bits[i : i + 2]) for i in range(0, len(col_bits), 2)]
     owner_perm = [
         (r * ncol + c, c * nrow + kept_chunk(r, row_groups, nrow)) for r in range(nrow) for c in range(ncol)
     ]
 
     def inner(trailing_adjoint, panel, panel_adjoint, diag_factor, diag_adjoint):
-        r = lax.axis_index("row")
-        c = lax.axis_index("col")
-
         groups = gather_groups(ncol)
         gathered = panel
         for masks in groups:
@@ -129,20 +130,32 @@
             preferred_element_type=jnp.float32,
         )
 
+        blocks_perm = [(b, (b % nrow) * ncol + b // nrow) for b in range(ndev)]
+        col_panel = lax.ppermute(panel, ALL, blocks_perm)
+        for masks in row_groups_natural:
+            col_panel = gather_step(col_panel, "row", nrow, masks)
+
+        local_term = jnp.dot(
+            panel_adjoint.T, panel, precision=lax.Precision.HIGHEST, preferred_element_type=jnp.float32
+        ) - 2.0 * jnp.dot(
+            share.T, col_panel, precision=lax.Precision.HIGHEST, preferred_element_type=jnp.float32
+        )
+        total = all_reduce(local_term, nrow, ncol)
+
+        piece = diag_adjoint.T
+        for masks in col_groups_natural:
+            piece = gather_step(piece, "col", ncol, masks)
+        whole = piece.T
+        for masks in row_groups_natural:
+            whole = gather_step(whole, "row", nrow, masks)
+
         for masks in row_groups:
             share = scatter_step(share, "row", nrow, masks)
         product = lax.ppermute(share, ALL, owner_perm)
-
         updated = panel_adjoint - 2.0 * product
         off_adjoint = right_solve(diag_factor, updated)
-        local_term = jnp.dot(
-            off_adjoint.T, panel, precision=lax.Precision.HIGHEST, preferred_element_type=jnp.float32
-        )
-        rows, cols = diag_adjoint.shape
-        placed = lax.dynamic_update_slice(
-            jnp.zeros((rows * nrow, cols * ncol), jnp.float32), diag_adjoint, (r * rows, c * cols)
-        )
-        accumulated = all_reduce(placed - local_term, nrow, ncol)
+
+        accumulated = whole - left_solve(diag_factor, total)
         return (off_adjoint, diagonal_adjoint(diag_factor, accumulated))
 
     return inner

time: 155 us -> 156 us (level)
  starting transfers between devices: 52 us -> 82.1 us
  waiting for transfers between devices: 59.2 us -> 30.1 us
    ppermute x19 -> x34, starting transfers between devices: 36.2 us -> 58.5 us  [exchange(): got.append(lax.ppermute(value, axis, xor_perm(size, offset(k, masks))))]
    ppermute x19 -> x34, waiting for transfers between devices: 48.4 us -> 28.2 us  [exchange(): got.append(lax.ppermute(value, axis, xor_perm(size, offset(k, masks))))]
    ppermute x7, waiting for transfers between devices: 10.8 us -> 1.91 us  [scatter_step(): total = total + lax.ppermute(send, axis, xor_perm(size, offset(k, masks)))]
    ppermute x0 -> x1, starting transfers between devices: none -> 8.51 us  [inner(): col_panel = lax.ppermute(panel, ALL, blocks_perm)]
    ppermute x7, starting transfers between devices: 11.5 us -> 8.52 us  [scatter_step(): total = total + lax.ppermute(send, axis, xor_perm(size, offset(k, masks)))]
    ppermute x1, starting transfers between devices: 4.31 us -> 6.54 us  [inner(): product = lax.ppermute(share, ALL, owner_perm)]
  transfers between devices with their start and end apart: 27 -> 43, of which waited for: 20 -> 13; matrix products, arithmetic and copies ran while one was open for 17% -> 20% of each run, Pallas kernels for 0% -> 0%
where the time goes in v4:
time: 156 us
  starting transfers between devices  82.1 us (53%)
  waiting for transfers between devices  30.1 us (19%)
  other arithmetic  25 us (16%)
  local copies, waits for them, and re-layouts  8.91 us (6%)
  matrix products  8.37 us (5%)
    ppermute x34, starting transfers between devices, exchange(): got.append(lax.ppermute(value, axis, xor_perm(size, offset(k, masks))))  58.5 us
    ppermute x34, waiting for transfers between devices, exchange(): got.append(lax.ppermute(value, axis, xor_perm(size, offset(k, masks))))  28.2 us
    another operation x3, other arithmetic, right_solve(): jax.scipy.linalg.solve_triangular(factor, rows.T, lower=True, trans=1)  20.6 us
    ppermute x7, starting transfers between devices, scatter_step(): total = total + lax.ppermute(send, axis, xor_perm(size, offset(k, masks)))  8.52 us
    ppermute x1, starting transfers between devices, inner(): col_panel = lax.ppermute(panel, ALL, blocks_perm)  8.51 us
    ppermute x1, starting transfers between devices, inner(): product = lax.ppermute(share, ALL, owner_perm)  6.54 us
    another operation x6, local copies, waits for them, and re-layouts  3.9 us
  transfers between devices with their start and end apart: 43, of which 13 were waited for; matrix products, arithmetic and copies ran while one was open for 20% of the time, Pallas kernels for 0%

profile of v4, /device:TPU:1, one launch (start us, length us, event | category | flops | bytes accessed | tf_op | source)
XLA Modules:
  0.0 156.0 jit_solution(897160058978603965)
XLA Ops:
  0.7 7.8 %collective-permute-start = (f32[48,256]{1,0:T(8,128)}, f32[48,256]{1,0:T(8,128)S(1)}, u32[]{:S(2)}, u32[]{:S(2)}) collective-permute-start(f32[48,256]{1,0:T(8,128)} %param.8), channel_id=1, source_target_pairs={{0,4},{1,5},{2,6},{3,7},{4,0},{5,1},{6,2},{7,3},{8,12},{9,13},{10,... | collective-permute-start | bytes 147464 | tf_op jit(solution)/shard_map/ppermute | solution.py:42
  18.5 5.0 %collective-permute-start.17 = (f32[32,32]{1,0:T(8,128)S(1)}, f32[32,32]{1,0:T(8,128)S(1)}, u32[]{:S(2)}, u32[]{:S(2)}) collective-permute-start(f32[32,32]{1,0:T(8,128)S(1)} %get-tuple-element.103), channel_id=1, source_target_pairs={{0,12},{1,13},{2,14},{3,15},{4,8},{5,9},{6,10},{7,11},{8,4},{9,5},... | collective-permute-start | bytes 12296 | tf_op jit(solution)/shard_map/ppermute | solution.py:42
  23.5 3.9 %while.7 = (s32[]{:T(128)}, f32[256,256]{1,0:T(8,128)S(1)}, s32[2,2]{1,0:T(2,128)S(1)}, f32[2,128,128]{2,1,0:T(8,128)S(1)}, s32[]{:T(128)}) while((s32[]{:T(128)}, f32[256,256]{1,0:T(8,128)S(1)}, s32[2,2]{1,0:T(2,128)S(1)}, f32[2,128,128]{2,1,0:T(8,128)S(1)}, s32[]{:T(128)}) %tuple.74), condition=%wide.while_cond.1, body=%wide.while_body.1.sunk | while | flops 2 | bytes 131181 | solution.py:10
  27.6 8.5 %collective-permute-start.23 = (f32[48,256]{1,0:T(8,128)S(1)}, f32[48,256]{1,0:T(8,128)S(1)}, u32[]{:S(2)}, u32[]{:S(2)}) collective-permute-start(f32[48,256]{1,0:T(8,128)S(1)} %copy-done.6), channel_id=1, source_target_pairs={{0,0},{1,32},{2,64},{3,96},{4,128},{5,160},{6,192},{7,224},{8,1},{... | collective-permute-start | bytes 147464 | tf_op jit(solution)/shard_map/ppermute | solution.py:134
  36.5 3.6 %collective-permute-start.18 = (f32[128,32]{0,1:T(8,128)S(1)}, f32[128,32]{0,1:T(8,128)S(1)}, u32[]{:S(2)}, u32[]{:S(2)}) collective-permute-start(f32[128,32]{0,1:T(8,128)S(1)} %pad_maximum_fusion.17), channel_id=1, source_target_pairs={{0,16},{1,17},{2,18},{3,19},{4,20},{5,21},{6,22},{7,23},{8,24},{9,... | collective-permute-start | bytes 49160 | tf_op jit(solution)/shard_map/ppermute | solution.py:42
  41.3 19.7 %custom-call.7 = f32[2,128,128]{1,2,0:T(8,128)S(1)} custom-call(f32[2,128,128]{2,1,0:T(8,128)S(1)} %get-tuple-element.18), custom_call_target="InvertDiagBlocksLowerTriangular" | custom-call | tf_op jit(solution)/shard_map/jit(_solve_triangular)/triangular_solve | solution.py:10
  63.7 4.0 %collective-permute-start.5 = (f32[192,256]{1,0:T(8,128)S(1)}, f32[192,256]{1,0:T(8,128)S(1)}, u32[]{:S(2)}, u32[]{:S(2)}) collective-permute-start(f32[192,256]{1,0:T(8,128)S(1)} %get-tuple-element.83), channel_id=1, source_target_pairs={{0,17},{1,16},{2,19},{3,18},{4,21},{5,20},{6,23},{7,22},{8,25},{9,... | collective-permute-start | bytes 589832 | tf_op jit(solution)/shard_map/ppermute | solution.py:42
  70.1 2.1 %collective-permute-start.26 = (f32[48,256]{1,0:T(8,128)S(1)}, f32[48,256]{1,0:T(8,128)S(1)}, u32[]{:S(2)}, u32[]{:S(2)}) collective-permute-start(f32[48,256]{1,0:T(8,128)S(1)} %collective-permute-done.23), channel_id=1, source_target_pairs={{0,96},{32,64},{64,32},{96,0},{128,224},{160,192},{192,160},{224,1... | collective-permute-start | bytes 147464 | tf_op jit(solution)/shard_map/ppermute | solution.py:42
  72.2 3.7 %collective-permute-done.4 = f32[192,256]{1,0:T(8,128)S(1)} collective-permute-done((f32[192,256]{1,0:T(8,128)S(1)}, f32[192,256]{1,0:T(8,128)S(1)}, u32[]{:S(2)}, u32[]{:S(2)}) %collective-permute-start.4) | collective-permute-done | bytes 196640 | tf_op jit(solution)/shard_map/ppermute | solution.py:42
  76.3 3.4 %collective-permute-start.22 = (f32[128,256]{1,0:T(8,128)S(1)}, f32[128,256]{1,0:T(8,128)S(1)}, u32[]{:S(2)}, u32[]{:S(2)}) collective-permute-start(f32[128,256]{1,0:T(8,128)S(1)} %get-tuple-element.88), channel_id=1, source_target_pairs={{0,128},{32,160},{64,192},{96,224},{128,0},{160,32},{192,64},{224,... | collective-permute-start | bytes 393224 | tf_op jit(solution)/shard_map/ppermute | solution.py:42
  80.0 2.1 %collective-permute-done.22 = f32[128,256]{1,0:T(8,128)S(1)} collective-permute-done((f32[128,256]{1,0:T(8,128)S(1)}, f32[128,256]{1,0:T(8,128)S(1)}, u32[]{:S(2)}, u32[]{:S(2)}) %collective-permute-start.22) | collective-permute-done | bytes 131104 | tf_op jit(solution)/shard_map/ppermute | solution.py:42
  82.9 3.4 %collective-permute-done.27 = f32[192,256]{1,0:T(8,128)S(1)} collective-permute-done((f32[192,256]{1,0:T(8,128)S(1)}, f32[192,256]{1,0:T(8,128)S(1)}, u32[]{:S(2)}, u32[]{:S(2)}) %collective-permute-start.27) | collective-permute-done | bytes 196640 | tf_op jit(solution)/shard_map/ppermute | solution.py:42
  86.4 8.3 %collective-permute-done.6 = f32[768,256]{1,0:T(8,128)S(1)} collective-permute-done((f32[768,256]{1,0:T(8,128)S(1)}, f32[768,256]{1,0:T(8,128)S(1)}, u32[]{:S(2)}, u32[]{:S(2)}) %collective-permute-start.6) | collective-permute-done | bytes 786464 | tf_op jit(solution)/shard_map/ppermute | solution.py:42
  95.2 2.8 %fusion.70 = f32[256,384]{1,0:T(8,128)S(1)} fusion(f32[1536,256]{1,0:T(8,128)S(1)} %bitcast.234, f32[1536,384]{1,0:T(8,128)S(1)} %copy-done), kind=kOutput, calls=%fused_computation.167 | convolution fusion | flops 1811939328 | bytes 4325376 | tf_op jit(solution)/shard_map/dot_general | solution.py:125
  109.2 3.2 %collective-permute-start.32 = (f32[64,256]{1,0:T(8,128)S(1)}, f32[64,256]{1,0:T(8,128)S(1)}, u32[]{:S(2)}, u32[]{:S(2)}) collective-permute-start(f32[64,256]{1,0:T(8,128)S(1)} %fusion.35), channel_id=1, source_target_pairs={{0,2},{1,3},{2,0},{3,1},{4,6},{5,7},{6,4},{7,5},{8,10},{9,11},{10,... | collective-permute-start | bytes 196616 | tf_op jit(solution)/shard_map/ppermute | solution.py:42
  112.6 3.1 %collective-permute-start.10 = (f32[48,256]{1,0:T(8,128)S(1)}, f32[48,256]{1,0:T(8,128)S(1)}, u32[]{:S(2)}, u32[]{:S(2)}) collective-permute-start(f32[48,256]{1,0:T(8,128)S(1)} %dynamic-slice_bitcast_fusion.18), channel_id=1, source_target_pairs={{0,128},{32,160},{64,192},{96,224},{128,0},{160,32},{192,64},{224,... | collective-permute-start | bytes 147464 | tf_op jit(solution)/shard_map/ppermute | solution.py:70
  117.3 4.4 %collective-permute-start.34 = (f32[64,256]{1,0:T(8,128)S(1)}, f32[64,256]{1,0:T(8,128)S(1)}, u32[]{:S(2)}, u32[]{:S(2)}) collective-permute-start(f32[64,256]{1,0:T(8,128)S(1)} %fusion.87), channel_id=1, source_target_pairs={{0,4},{1,5},{2,6},{3,7},{4,0},{5,1},{6,2},{7,3},{8,12},{9,13},{10,... | collective-permute-start | bytes 196616 | tf_op jit(solution)/shard_map/ppermute | solution.py:42
  121.8 2.2 %collective-permute-start.36 = (f32[64,256]{1,0:T(8,128)S(1)}, f32[64,256]{1,0:T(8,128)S(1)}, u32[]{:S(2)}, u32[]{:S(2)}) collective-permute-start(f32[64,256]{1,0:T(8,128)S(1)} %fusion.87), channel_id=1, source_target_pairs={{0,12},{1,13},{2,14},{3,15},{4,8},{5,9},{6,10},{7,11},{8,4},{9,5},... | collective-permute-start | bytes 196616 | tf_op jit(solution)/shard_map/ppermute | solution.py:42
  124.0 6.5 %collective-permute-start.11 = (f32[48,256]{1,0:T(8,128)S(1)}, f32[48,256]{1,0:T(8,128)S(1)}, u32[]{:S(2)}, u32[]{:S(2)}) collective-permute-start(f32[48,256]{1,0:T(8,128)S(1)} %bitcast_add_fusion.2), channel_id=1, source_target_pairs={{0,0},{1,8},{2,16},{3,24},{4,32},{5,40},{6,48},{7,56},{8,64},{9,72... | collective-permute-start | bytes 147464 | tf_op jit(solution)/shard_map/ppermute | solution.py:154
  130.7 2.8 %collective-permute-start.38 = (f32[64,256]{1,0:T(8,128)S(1)}, f32[64,256]{1,0:T(8,128)S(1)}, u32[]{:S(2)}, u32[]{:S(2)}) collective-permute-start(f32[64,256]{1,0:T(8,128)S(1)} %fusion.86), channel_id=1, source_target_pairs={{0,128},{1,129},{2,130},{3,131},{4,132},{5,133},{6,134},{7,135},{8... | collective-permute-start | bytes 196616 | tf_op jit(solution)/shard_map/ppermute | solution.py:42
  133.5 5.4 %collective-permute-start.39 = (f32[64,256]{1,0:T(8,128)S(1)}, f32[64,256]{1,0:T(8,128)S(1)}, u32[]{:S(2)}, u32[]{:S(2)}) collective-permute-start(f32[64,256]{1,0:T(8,128)S(1)} %fusion.86), channel_id=1, source_target_pairs={{0,144},{1,145},{2,146},{3,147},{4,148},{5,149},{6,150},{7,151},{8... | collective-permute-start | bytes 196616 | tf_op jit(solution)/shard_map/ppermute | solution.py:42
  140.5 3.1 %collective-permute-done.37 = f32[64,256]{1,0:T(8,128)S(1)} collective-permute-done((f32[64,256]{1,0:T(8,128)S(1)}, f32[64,256]{1,0:T(8,128)S(1)}, u32[]{:S(2)}, u32[]{:S(2)}) %collective-permute-start.37) | collective-permute-done | bytes 65568 | tf_op jit(solution)/shard_map/ppermute | solution.py:42
  147.0 2.1 %collective-permute-done.42 = f32[64,256]{1,0:T(8,128)S(1)} collective-permute-done((f32[64,256]{1,0:T(8,128)S(1)}, f32[64,256]{1,0:T(8,128)S(1)}, u32[]{:S(2)}, u32[]{:S(2)}) %collective-permute-start.42) | collective-permute-done | bytes 65568 | tf_op jit(solution)/shard_map/ppermute | solution.py:42
  150.8 2.3 %gather_fusion = f32[256]{0:T(256)S(1)} fusion(f32[256,256]{1,0:T(8,128)S(1)} %bitcast.232, s32[256]{0:T(256)S(1)} %bitcast.231), kind=kCustom, calls=%fused_computation | custom fusion | bytes 4096 | tf_op jit(solution)/shard_map/jit(_diag)/jit(diagonal)/cond/branch_0_fun/gather | solution.py:21
  (164 shorter events, 44.8 us)
Async XLA Ops:
  0.7 60.6 %collective-permute-start = (f32[48,256]{1,0:T(8,128)}, f32[48,256]{1,0:T(8,128)S(1)}, u32[]{:S(2)}, u32[]{:S(2)}) collective-permute-start(f32[48,256]{1,0:T(8,128)} %param.8), channel_id=1, source_target_pairs={{0,4},{1,5},{2,6},{3,7},{4,0},{5,1},{6,2},{7,3},{8,12},{9,13},{10,... | collective-permute-start | bytes 147464 | tf_op jit(solution)/shard_map/ppermute | solution.py:42
  8.5 54.1 %collective-permute-start.1 = (f32[48,256]{1,0:T(8,128)}, f32[48,256]{1,0:T(8,128)S(1)}, u32[]{:S(2)}, u32[]{:S(2)}) collective-permute-start(f32[48,256]{1,0:T(8,128)} %param.8), channel_id=1, source_target_pairs={{0,2},{1,3},{2,0},{3,1},{4,6},{5,7},{6,4},{7,5},{8,10},{9,11},{10,... | collective-permute-start | bytes 147464 | tf_op jit(solution)/shard_map/ppermute | solution.py:42
  16.8 10.7 %collective-permute-start.15 = (f32[32,32]{1,0:T(8,128)S(1)}, f32[32,32]{1,0:T(8,128)S(1)}, u32[]{:S(2)}, u32[]{:S(2)}) collective-permute-start(f32[32,32]{1,0:T(8,128)S(1)} %get-tuple-element.103), channel_id=1, source_target_pairs={{0,4},{1,5},{2,6},{3,7},{4,0},{5,1},{6,2},{7,3},{8,12},{9,13},{10,... | collective-permute-start | bytes 12296 | tf_op jit(solution)/shard_map/ppermute | solution.py:42
  17.2 10.3 %collective-permute-start.16 = (f32[32,32]{1,0:T(8,128)S(1)}, f32[32,32]{1,0:T(8,128)S(1)}, u32[]{:S(2)}, u32[]{:S(2)}) collective-permute-start(f32[32,32]{1,0:T(8,128)S(1)} %get-tuple-element.103), channel_id=1, source_target_pairs={{0,8},{1,9},{2,10},{3,11},{4,12},{5,13},{6,14},{7,15},{8,0},{9,1},... | collective-permute-start | bytes 12296 | tf_op jit(solution)/shard_map/ppermute | solution.py:42
  18.5 17.6 %collective-permute-start.17 = (f32[32,32]{1,0:T(8,128)S(1)}, f32[32,32]{1,0:T(8,128)S(1)}, u32[]{:S(2)}, u32[]{:S(2)}) collective-permute-start(f32[32,32]{1,0:T(8,128)S(1)} %get-tuple-element.103), channel_id=1, source_target_pairs={{0,12},{1,13},{2,14},{3,15},{4,8},{5,9},{6,10},{7,11},{8,4},{9,5},... | collective-permute-start | bytes 12296 | tf_op jit(solution)/shard_map/ppermute | solution.py:42
  27.5 35.9 %collective-permute-start.2 = (f32[48,256]{1,0:T(8,128)S(1)}, f32[48,256]{1,0:T(8,128)S(1)}, u32[]{:S(2)}, u32[]{:S(2)}) collective-permute-start(f32[48,256]{1,0:T(8,128)S(1)} %copy-done.6), channel_id=1, source_target_pairs={{0,6},{1,7},{2,4},{3,5},{4,2},{5,3},{6,0},{7,1},{8,14},{9,15},{10,... | collective-permute-start | bytes 147464 | tf_op jit(solution)/shard_map/ppermute | solution.py:42
  27.6 36.0 %collective-permute-start.23 = (f32[48,256]{1,0:T(8,128)S(1)}, f32[48,256]{1,0:T(8,128)S(1)}, u32[]{:S(2)}, u32[]{:S(2)}) collective-permute-start(f32[48,256]{1,0:T(8,128)S(1)} %copy-done.6), channel_id=1, source_target_pairs={{0,0},{1,32},{2,64},{3,96},{4,128},{5,160},{6,192},{7,224},{8,1},{... | collective-permute-start | bytes 147464 | tf_op jit(solution)/shard_map/ppermute | solution.py:134
  36.5 24.5 %collective-permute-start.18 = (f32[128,32]{0,1:T(8,128)S(1)}, f32[128,32]{0,1:T(8,128)S(1)}, u32[]{:S(2)}, u32[]{:S(2)}) collective-permute-start(f32[128,32]{0,1:T(8,128)S(1)} %pad_maximum_fusion.17), channel_id=1, source_target_pairs={{0,16},{1,17},{2,18},{3,19},{4,20},{5,21},{6,22},{7,23},{8,24},{9,... | collective-permute-start | bytes 49160 | tf_op jit(solution)/shard_map/ppermute | solution.py:42
  63.6 12.4 %collective-permute-start.4 = (f32[192,256]{1,0:T(8,128)S(1)}, f32[192,256]{1,0:T(8,128)S(1)}, u32[]{:S(2)}, u32[]{:S(2)}) collective-permute-start(f32[192,256]{1,0:T(8,128)S(1)} %get-tuple-element.83), channel_id=1, source_target_pairs={{0,16},{1,17},{2,18},{3,19},{4,20},{5,21},{6,22},{7,23},{8,24},{9,... | collective-permute-start | bytes 589832 | tf_op jit(solution)/shard_map/ppermute | solution.py:42
  63.7 12.3 %collective-permute-start.5 = (f32[192,256]{1,0:T(8,128)S(1)}, f32[192,256]{1,0:T(8,128)S(1)}, u32[]{:S(2)}, u32[]{:S(2)}) collective-permute-start(f32[192,256]{1,0:T(8,128)S(1)} %get-tuple-element.83), channel_id=1, source_target_pairs={{0,17},{1,16},{2,19},{3,18},{4,21},{5,20},{6,23},{7,22},{8,25},{9,... | collective-permute-start | bytes 589832 | tf_op jit(solution)/shard_map/ppermute | solution.py:42
  67.7 12.0 %collective-permute-start.24 = (f32[48,256]{1,0:T(8,128)S(1)}, f32[48,256]{1,0:T(8,128)S(1)}, u32[]{:S(2)}, u32[]{:S(2)}) collective-permute-start(f32[48,256]{1,0:T(8,128)S(1)} %collective-permute-done.23), channel_id=1, source_target_pairs={{0,32},{32,0},{64,96},{96,64},{128,160},{160,128},{192,224},{224,1... | collective-permute-start | bytes 147464 | tf_op jit(solution)/shard_map/ppermute | solution.py:42
  68.4 11.3 %collective-permute-start.25 = (f32[48,256]{1,0:T(8,128)S(1)}, f32[48,256]{1,0:T(8,128)S(1)}, u32[]{:S(2)}, u32[]{:S(2)}) collective-permute-start(f32[48,256]{1,0:T(8,128)S(1)} %collective-permute-done.23), channel_id=1, source_target_pairs={{0,64},{32,96},{64,0},{96,32},{128,192},{160,224},{192,128},{224,1... | collective-permute-start | bytes 147464 | tf_op jit(solution)/shard_map/ppermute | solution.py:42
  70.1 9.6 %collective-permute-start.26 = (f32[48,256]{1,0:T(8,128)S(1)}, f32[48,256]{1,0:T(8,128)S(1)}, u32[]{:S(2)}, u32[]{:S(2)}) collective-permute-start(f32[48,256]{1,0:T(8,128)S(1)} %collective-permute-done.23), channel_id=1, source_target_pairs={{0,96},{32,64},{64,32},{96,0},{128,224},{160,192},{192,160},{224,1... | collective-permute-start | bytes 147464 | tf_op jit(solution)/shard_map/ppermute | solution.py:42
  76.2 18.5 %collective-permute-start.6 = (f32[768,256]{1,0:T(8,128)S(1)}, f32[768,256]{1,0:T(8,128)S(1)}, u32[]{:S(2)}, u32[]{:S(2)}) collective-permute-start(f32[768,256]{1,0:T(8,128)S(1)} %get-tuple-element.56), channel_id=1, source_target_pairs={{0,8},{1,9},{2,10},{3,11},{4,12},{5,13},{6,14},{7,15},{8,0},{9,1},... | collective-permute-start | bytes 2359304 | tf_op jit(solution)/shard_map/ppermute | solution.py:42
  102.9 9.4 %collective-permute-start.7 = (f32[96,256]{1,0:T(8,128)S(1)}, f32[96,256]{1,0:T(8,128)S(1)}, u32[]{:S(2)}, u32[]{:S(2)}) collective-permute-start(f32[96,256]{1,0:T(8,128)S(1)} %get-tuple-element.64), channel_id=1, source_target_pairs={{0,32},{32,0},{64,96},{96,64},{128,160},{160,128},{192,224},{224,1... | collective-permute-start | bytes 294920 | tf_op jit(solution)/shard_map/ppermute | solution.py:70
  103.2 9.3 %collective-permute-start.8 = (f32[96,256]{1,0:T(8,128)S(1)}, f32[96,256]{1,0:T(8,128)S(1)}, u32[]{:S(2)}, u32[]{:S(2)}) collective-permute-start(f32[96,256]{1,0:T(8,128)S(1)} %get-tuple-element.66), channel_id=1, source_target_pairs={{0,64},{32,96},{64,0},{96,32},{128,192},{160,224},{192,128},{224,1... | collective-permute-start | bytes 294920 | tf_op jit(solution)/shard_map/ppermute | solution.py:70
  104.5 8.1 %collective-permute-start.9 = (f32[96,256]{1,0:T(8,128)S(1)}, f32[96,256]{1,0:T(8,128)S(1)}, u32[]{:S(2)}, u32[]{:S(2)}) collective-permute-start(f32[96,256]{1,0:T(8,128)S(1)} %get-tuple-element.65), channel_id=1, source_target_pairs={{0,96},{32,64},{64,32},{96,0},{128,224},{160,192},{192,160},{224,1... | collective-permute-start | bytes 294920 | tf_op jit(solution)/shard_map/ppermute | solution.py:70
  108.0 7.7 %collective-permute-start.31 = (f32[64,256]{1,0:T(8,128)S(1)}, f32[64,256]{1,0:T(8,128)S(1)}, u32[]{:S(2)}, u32[]{:S(2)}) collective-permute-start(f32[64,256]{1,0:T(8,128)S(1)} %fusion.35), channel_id=1, source_target_pairs={{0,1},{1,0},{2,3},{3,2},{4,5},{5,4},{6,7},{7,6},{8,9},{9,8},{10,11... | collective-permute-start | bytes 196616 | tf_op jit(solution)/shard_map/ppermute | solution.py:42
  112.6 11.4 %collective-permute-start.10 = (f32[48,256]{1,0:T(8,128)S(1)}, f32[48,256]{1,0:T(8,128)S(1)}, u32[]{:S(2)}, u32[]{:S(2)}) collective-permute-start(f32[48,256]{1,0:T(8,128)S(1)} %dynamic-slice_bitcast_fusion.18), channel_id=1, source_target_pairs={{0,128},{32,160},{64,192},{96,224},{128,0},{160,32},{192,64},{224,... | collective-permute-start | bytes 147464 | tf_op jit(solution)/shard_map/ppermute | solution.py:70
  117.3 13.2 %collective-permute-start.34 = (f32[64,256]{1,0:T(8,128)S(1)}, f32[64,256]{1,0:T(8,128)S(1)}, u32[]{:S(2)}, u32[]{:S(2)}) collective-permute-start(f32[64,256]{1,0:T(8,128)S(1)} %fusion.87), channel_id=1, source_target_pairs={{0,4},{1,5},{2,6},{3,7},{4,0},{5,1},{6,2},{7,3},{8,12},{9,13},{10,... | collective-permute-start | bytes 196616 | tf_op jit(solution)/shard_map/ppermute | solution.py:42
  121.8 8.8 %collective-permute-start.35 = (f32[64,256]{1,0:T(8,128)S(1)}, f32[64,256]{1,0:T(8,128)S(1)}, u32[]{:S(2)}, u32[]{:S(2)}) collective-permute-start(f32[64,256]{1,0:T(8,128)S(1)} %fusion.87), channel_id=1, source_target_pairs={{0,8},{1,9},{2,10},{3,11},{4,12},{5,13},{6,14},{7,15},{8,0},{9,1},... | collective-permute-start | bytes 196616 | tf_op jit(solution)/shard_map/ppermute | solution.py:42
  121.8 8.8 %collective-permute-start.36 = (f32[64,256]{1,0:T(8,128)S(1)}, f32[64,256]{1,0:T(8,128)S(1)}, u32[]{:S(2)}, u32[]{:S(2)}) collective-permute-start(f32[64,256]{1,0:T(8,128)S(1)} %fusion.87), channel_id=1, source_target_pairs={{0,12},{1,13},{2,14},{3,15},{4,8},{5,9},{6,10},{7,11},{8,4},{9,5},... | collective-permute-start | bytes 196616 | tf_op jit(solution)/shard_map/ppermute | solution.py:42
  124.0 14.8 %collective-permute-start.11 = (f32[48,256]{1,0:T(8,128)S(1)}, f32[48,256]{1,0:T(8,128)S(1)}, u32[]{:S(2)}, u32[]{:S(2)}) collective-permute-start(f32[48,256]{1,0:T(8,128)S(1)} %bitcast_add_fusion.2), channel_id=1, source_target_pairs={{0,0},{1,8},{2,16},{3,24},{4,32},{5,40},{6,48},{7,56},{8,64},{9,72... | collective-permute-start | bytes 147464 | tf_op jit(solution)/shard_map/ppermute | solution.py:154
  130.7 9.5 %collective-permute-start.38 = (f32[64,256]{1,0:T(8,128)S(1)}, f32[64,256]{1,0:T(8,128)S(1)}, u32[]{:S(2)}, u32[]{:S(2)}) collective-permute-start(f32[64,256]{1,0:T(8,128)S(1)} %fusion.86), channel_id=1, source_target_pairs={{0,128},{1,129},{2,130},{3,131},{4,132},{5,133},{6,134},{7,135},{8... | collective-permute-start | bytes 196616 | tf_op jit(solution)/shard_map/ppermute | solution.py:42
  (28 other events, 312.4 us)

commit v5 on v4

--- a/solution.py
+++ b/solution.py
@@ -6,22 +6,40 @@
 ALL = ("row", "col")
 
 
-def right_solve(factor, rows):
-    return jax.scipy.linalg.solve_triangular(factor, rows.T, lower=True, trans=1).T
+def mm(a, b):
+    return jnp.dot(a, b, precision=lax.Precision.HIGHEST, preferred_element_type=jnp.float32)
 
 
-def left_solve(factor, matrix):
-    return jax.scipy.linalg.solve_triangular(factor, matrix, lower=True, trans=1)
+def lower_inverse(factor, base=32):
+    n = factor.shape[0]
+    base = min(base, n)
+    blocks = jnp.stack([factor[i : i + base, i : i + base] for i in range(0, n, base)])
+    eye = jnp.broadcast_to(jnp.eye(base, dtype=factor.dtype), blocks.shape)
+    inv = jax.scipy.linalg.solve_triangular(blocks, eye, lower=True)
+    s = base
+    while s < n:
+        first, second = inv[0::2], inv[1::2]
+        below = jnp.stack(
+            [factor[i + s : i + 2 * s, i : i + s] for i in range(0, n, 2 * s)]
+        )
+        corner = -jnp.matmul(
+            jnp.matmul(second, below, precision=lax.Precision.HIGHEST),
+            first,
+            precision=lax.Precision.HIGHEST,
+        )
+        top = jnp.concatenate([first, jnp.zeros_like(first)], axis=2)
+        bottom = jnp.concatenate([corner, second], axis=2)
+        inv = jnp.concatenate([top, bottom], axis=1)
+        s *= 2
+    return inv[0]
 
 
-def diagonal_adjoint(factor, adjoint):
-    product = jnp.dot(
-        factor.T, adjoint, precision=lax.Precision.HIGHEST, preferred_element_type=jnp.float32
-    )
+def diagonal_adjoint(factor, inverse, adjoint):
+    product = mm(factor.T, adjoint)
     lower = jnp.tril(product) - 0.5 * jnp.diag(jnp.diag(product))
     symmetric = lower + lower.T
-    half = left_solve(factor, symmetric)
-    return 0.5 * left_solve(factor, half.T).T
+    half = mm(inverse.T, symmetric)
+    return 0.5 * mm(half, inverse)
 
 
 def xor_perm(size, mask):
@@ -111,6 +129,8 @@
     ]
 
     def inner(trailing_adjoint, panel, panel_adjoint, diag_factor, diag_adjoint):
+        inverse = lower_inverse(diag_factor)
+
         groups = gather_groups(ncol)
         gathered = panel
         for masks in groups:
@@ -153,10 +173,10 @@
             share = scatter_step(share, "row", nrow, masks)
         product = lax.ppermute(share, ALL, owner_perm)
         updated = panel_adjoint - 2.0 * product
-        off_adjoint = right_solve(diag_factor, updated)
+        off_adjoint = mm(updated, inverse)
 
-        accumulated = whole - left_solve(diag_factor, total)
-        return (off_adjoint, diagonal_adjoint(diag_factor, accumulated))
+        accumulated = whole - mm(inverse.T, total)
+        return (off_adjoint, diagonal_adjoint(diag_factor, inverse, accumulated))
 
     return inner
 

time: 156 us -> 163 us (1.045)
  starting transfers between devices: 82.1 us -> 87.9 us
  waiting for transfers between devices: 30.1 us -> 26.4 us
  local copies, waits for them, and re-layouts: 8.91 us -> 12.6 us
  matrix products: 8.37 us -> 10.6 us
  other arithmetic: 25 us -> 22.8 us
    ppermute x34, starting transfers between devices: 58.5 us -> 64.7 us  [exchange(): got.append(lax.ppermute(value, axis, xor_perm(size, offset(k, masks))))]
    unnamed x19 -> x27, local copies, waits for them, and re-layouts: 0.89 us -> 5.45 us
    dot_general x1 -> x11, matrix products: 0.6 us -> 4.81 us  [the longest x5 3.64 us: mm(): jnp.dot(a, b, precision=lax.Precision.HIGHEST, preferred_element_type=jnp...]
    ppermute x34, waiting for transfers between devices: 28.2 us -> 24.5 us  [exchange(): got.append(lax.ppermute(value, axis, xor_perm(size, offset(k, masks))))]
    another operation x12 -> x1, matrix products: 3.22 us -> 0.41 us  [lower_inverse(): inv = jax.scipy.linalg.solve_triangular(blocks, eye, lower=True)]
    another operation x7 -> x3, local copies, waits for them, and re-layouts: 3.97 us -> 2.42 us  [the longest x2 1.63 us: lower_inverse(): jnp.stack([factor[i + s:i + 2 * s, i:i + s] for i in range(0, n, 2 * s)])]
  transfers between devices with their start and end apart: 43 -> 43, of which waited for: 13 -> 11; matrix products, arithmetic and copies ran while one was open for 20% -> 22% of each run, Pallas kernels for 0% -> 0%
where the time goes in v5:
time: 163 us; the launch traced here: 162 us
  starting transfers between devices  87.9 us (54%)
  waiting for transfers between devices  26.4 us (16%)
  other arithmetic  22.8 us (14%)
  local copies, waits for them, and re-layouts  12.6 us (8%)
  matrix products  10.6 us (7%)
    ppermute x34, starting transfers between devices, exchange(): got.append(lax.ppermute(value, axis, xor_perm(size, offset(k, masks))))  64.7 us
    ppermute x34, waiting for transfers between devices, exchange(): got.append(lax.ppermute(value, axis, xor_perm(size, offset(k, masks))))  24.5 us
    another operation x3, other arithmetic, lower_inverse(): inv = jax.scipy.linalg.solve_triangular(blocks, eye, lower=True)  19.7 us
    ppermute x1, starting transfers between devices, inner(): col_panel = lax.ppermute(panel, ALL, blocks_perm)  8.54 us
    ppermute x7, starting transfers between devices, scatter_step(): total = total + lax.ppermute(send, axis, xor_perm(size, offset(k, masks)))  8.43 us
    ppermute x1, starting transfers between devices, inner(): product = lax.ppermute(share, ALL, owner_perm)  6.22 us
    unnamed x27, local copies, waits for them, and re-layouts  5.45 us
    dot_general x5, matrix products, mm(): jnp.dot(a, b, precision=lax.Precision.HIGHEST, preferred_element_type=jnp...  3.64 us
  transfers between devices with their start and end apart: 43, of which 11 were waited for; matrix products, arithmetic and copies ran while one was open for 22% of the time, Pallas kernels for 0%

profile of v5, /device:TPU:1, one launch (start us, length us, event | category | flops | bytes accessed | tf_op | source)
XLA Modules:
  0.0 161.9 jit_solution(15648644117151407825)
XLA Ops:
  0.6 7.8 %collective-permute-start = (f32[48,256]{1,0:T(8,128)}, f32[48,256]{1,0:T(8,128)S(1)}, u32[]{:S(2)}, u32[]{:S(2)}) collective-permute-start(f32[48,256]{1,0:T(8,128)} %param.6), channel_id=1, source_target_pairs={{0,4},{1,5},{2,6},{3,7},{4,0},{5,1},{6,2},{7,3},{8,12},{9,13},{10,... | collective-permute-start | bytes 147464 | tf_op jit(solution)/shard_map/ppermute | solution.py:60
  15.6 2.0 %fusion.118 = f32[256,256]{1,0:T(8,128)} fusion(f32[48,256]{1,0:T(8,128)} %param.7, f32[48,256]{1,0:T(8,128)} %param.6), kind=kOutput, calls=%fused_computation.224 | convolution fusion | flops 37748736 | bytes 360448 | tf_op jit(solution)/shard_map/dot_general | solution.py:158
  23.0 19.7 %custom-call.4 = f32[8,1,32,32]{2,3,1,0:T(8,128)S(1)} custom-call(f32[8,1,32,32]{3,2,1,0:T(8,128)S(1)} %broadcast_select_fusion), custom_call_target="InvertDiagBlocksLowerTriangular" | custom-call | tf_op jit(solution)/shard_map/jit(_solve_triangular)/vmap()/triangular_solve | solution.py:18
  46.3 4.9 %collective-permute-start.17 = (f32[32,32]{1,0:T(8,128)S(1)}, f32[32,32]{1,0:T(8,128)S(1)}, u32[]{:S(2)}, u32[]{:S(2)}) collective-permute-start(f32[32,32]{1,0:T(8,128)S(1)} %get-tuple-element.63), channel_id=1, source_target_pairs={{0,12},{1,13},{2,14},{3,15},{4,8},{5,9},{6,10},{7,11},{8,4},{9,5},... | collective-permute-start | bytes 12296 | tf_op jit(solution)/shard_map/ppermute | solution.py:60
  51.8 8.5 %collective-permute-start.23 = (f32[48,256]{1,0:T(8,128)S(1)}, f32[48,256]{1,0:T(8,128)S(1)}, u32[]{:S(2)}, u32[]{:S(2)}) collective-permute-start(f32[48,256]{1,0:T(8,128)S(1)} %copy-done.5), channel_id=1, source_target_pairs={{0,0},{1,32},{2,64},{3,96},{4,128},{5,160},{6,192},{7,224},{8,1},{... | collective-permute-start | bytes 147464 | tf_op jit(solution)/shard_map/ppermute | solution.py:154
  60.8 2.7 %collective-permute-start.18 = (f32[128,32]{0,1:T(8,128)S(1)}, f32[128,32]{0,1:T(8,128)S(1)}, u32[]{:S(2)}, u32[]{:S(2)}) collective-permute-start(f32[128,32]{0,1:T(8,128)S(1)} %pad_maximum_fusion.17), channel_id=1, source_target_pairs={{0,16},{1,17},{2,18},{3,19},{4,20},{5,21},{6,22},{7,23},{8,24},{9,... | collective-permute-start | bytes 49160 | tf_op jit(solution)/shard_map/ppermute | solution.py:60
  65.1 2.2 %collective-permute-start.20 = (f32[32,256]{1,0:T(8,128)S(1)}, f32[32,256]{1,0:T(8,128)S(1)}, u32[]{:S(2)}, u32[]{:S(2)}) collective-permute-start(f32[32,256]{1,0:T(8,128)S(1)} %get-tuple-element.59), channel_id=1, source_target_pairs={{0,64},{32,96},{64,0},{96,32},{128,192},{160,224},{192,128},{224,1... | collective-permute-start | bytes 98312 | tf_op jit(solution)/shard_map/ppermute | solution.py:60
  67.7 2.6 %collective-permute-start.4 = (f32[192,256]{1,0:T(8,128)S(1)}, f32[192,256]{1,0:T(8,128)S(1)}, u32[]{:S(2)}, u32[]{:S(2)}) collective-permute-start(f32[192,256]{1,0:T(8,128)S(1)} %get-tuple-element.37), channel_id=1, source_target_pairs={{0,16},{1,17},{2,18},{3,19},{4,20},{5,21},{6,22},{7,23},{8,24},{9,... | collective-permute-start | bytes 589832 | tf_op jit(solution)/shard_map/ppermute | solution.py:60
  74.4 4.6 %collective-permute-done.4 = f32[192,256]{1,0:T(8,128)S(1)} collective-permute-done((f32[192,256]{1,0:T(8,128)S(1)}, f32[192,256]{1,0:T(8,128)S(1)}, u32[]{:S(2)}, u32[]{:S(2)}) %collective-permute-start.4) | collective-permute-done | bytes 196640 | tf_op jit(solution)/shard_map/ppermute | solution.py:60
  79.0 3.4 %collective-permute-start.26 = (f32[48,256]{1,0:T(8,128)S(1)}, f32[48,256]{1,0:T(8,128)S(1)}, u32[]{:S(2)}, u32[]{:S(2)}) collective-permute-start(f32[48,256]{1,0:T(8,128)S(1)} %collective-permute-done.23), channel_id=1, source_target_pairs={{0,96},{32,64},{64,32},{96,0},{128,224},{160,192},{192,160},{224,1... | collective-permute-start | bytes 147464 | tf_op jit(solution)/shard_map/ppermute | solution.py:60
  83.5 4.0 %collective-permute-start.22 = (f32[128,256]{1,0:T(8,128)S(1)}, f32[128,256]{1,0:T(8,128)S(1)}, u32[]{:S(2)}, u32[]{:S(2)}) collective-permute-start(f32[128,256]{1,0:T(8,128)S(1)} %get-tuple-element.42), channel_id=1, source_target_pairs={{0,128},{32,160},{64,192},{96,224},{128,0},{160,32},{192,64},{224,... | collective-permute-start | bytes 393224 | tf_op jit(solution)/shard_map/ppermute | solution.py:60
  89.4 1.9 %collective-permute-done.22 = f32[128,256]{1,0:T(8,128)S(1)} collective-permute-done((f32[128,256]{1,0:T(8,128)S(1)}, f32[128,256]{1,0:T(8,128)S(1)}, u32[]{:S(2)}, u32[]{:S(2)}) %collective-permute-start.22) | collective-permute-done | bytes 131104 | tf_op jit(solution)/shard_map/ppermute | solution.py:60
  92.1 3.2 %collective-permute-done.27 = f32[192,256]{1,0:T(8,128)S(1)} collective-permute-done((f32[192,256]{1,0:T(8,128)S(1)}, f32[192,256]{1,0:T(8,128)S(1)}, u32[]{:S(2)}, u32[]{:S(2)}) %collective-permute-start.27) | collective-permute-done | bytes 196640 | tf_op jit(solution)/shard_map/ppermute | solution.py:60
  95.4 6.6 %collective-permute-done.6 = f32[768,256]{1,0:T(8,128)S(1)} collective-permute-done((f32[768,256]{1,0:T(8,128)S(1)}, f32[768,256]{1,0:T(8,128)S(1)}, u32[]{:S(2)}, u32[]{:S(2)}) %collective-permute-start.6) | collective-permute-done | bytes 786464 | tf_op jit(solution)/shard_map/ppermute | solution.py:60
  102.6 2.8 %fusion.117 = f32[256,384]{1,0:T(8,128)S(1)} fusion(f32[1536,256]{1,0:T(8,128)S(1)} %bitcast.235, f32[1536,384]{1,0:T(8,128)S(1)} %copy-done), kind=kOutput, calls=%fused_computation.223 | convolution fusion | flops 1811939328 | bytes 4325376 | tf_op jit(solution)/shard_map/dot_general | solution.py:145
  116.2 1.9 %collective-permute-start.33 = (f32[64,256]{1,0:T(8,128)S(1)}, f32[64,256]{1,0:T(8,128)S(1)}, u32[]{:S(2)}, u32[]{:S(2)}) collective-permute-start(f32[64,256]{1,0:T(8,128)S(1)} %fusion.56), channel_id=1, source_target_pairs={{0,3},{1,2},{2,1},{3,0},{4,7},{5,6},{6,5},{7,4},{8,11},{9,10},{10,... | collective-permute-start | bytes 196616 | tf_op jit(solution)/shard_map/ppermute | solution.py:60
  118.2 3.9 %collective-permute-start.10 = (f32[48,256]{1,0:T(8,128)S(1)}, f32[48,256]{1,0:T(8,128)S(1)}, u32[]{:S(2)}, u32[]{:S(2)}) collective-permute-start(f32[48,256]{1,0:T(8,128)S(1)} %dynamic-slice_bitcast_fusion.18), channel_id=1, source_target_pairs={{0,128},{32,160},{64,192},{96,224},{128,0},{160,32},{192,64},{224,... | collective-permute-start | bytes 147464 | tf_op jit(solution)/shard_map/ppermute | solution.py:88
  122.2 3.4 %collective-permute-start.34 = (f32[64,256]{1,0:T(8,128)S(1)}, f32[64,256]{1,0:T(8,128)S(1)}, u32[]{:S(2)}, u32[]{:S(2)}) collective-permute-start(f32[64,256]{1,0:T(8,128)S(1)} %fusion.133), channel_id=1, source_target_pairs={{0,4},{1,5},{2,6},{3,7},{4,0},{5,1},{6,2},{7,3},{8,12},{9,13},{10,... | collective-permute-start | bytes 196616 | tf_op jit(solution)/shard_map/ppermute | solution.py:60
  125.7 3.2 %collective-permute-start.36 = (f32[64,256]{1,0:T(8,128)S(1)}, f32[64,256]{1,0:T(8,128)S(1)}, u32[]{:S(2)}, u32[]{:S(2)}) collective-permute-start(f32[64,256]{1,0:T(8,128)S(1)} %fusion.133), channel_id=1, source_target_pairs={{0,12},{1,13},{2,14},{3,15},{4,8},{5,9},{6,10},{7,11},{8,4},{9,5},... | collective-permute-start | bytes 196616 | tf_op jit(solution)/shard_map/ppermute | solution.py:60
  128.9 6.2 %collective-permute-start.11 = (f32[48,256]{1,0:T(8,128)S(1)}, f32[48,256]{1,0:T(8,128)S(1)}, u32[]{:S(2)}, u32[]{:S(2)}) collective-permute-start(f32[48,256]{1,0:T(8,128)S(1)} %bitcast_add_fusion.2), channel_id=1, source_target_pairs={{0,0},{1,8},{2,16},{3,24},{4,32},{5,40},{6,48},{7,56},{8,64},{9,72... | collective-permute-start | bytes 147464 | tf_op jit(solution)/shard_map/ppermute | solution.py:174
  135.2 6.5 %collective-permute-start.37 = (f32[64,256]{1,0:T(8,128)S(1)}, f32[64,256]{1,0:T(8,128)S(1)}, u32[]{:S(2)}, u32[]{:S(2)}) collective-permute-start(f32[64,256]{1,0:T(8,128)S(1)} %fusion.132), channel_id=1, source_target_pairs={{0,16},{1,17},{2,18},{3,19},{4,20},{5,21},{6,22},{7,23},{8,24},{9,... | collective-permute-start | bytes 196616 | tf_op jit(solution)/shard_map/ppermute | solution.py:60
  141.7 2.8 %collective-permute-start.39 = (f32[64,256]{1,0:T(8,128)S(1)}, f32[64,256]{1,0:T(8,128)S(1)}, u32[]{:S(2)}, u32[]{:S(2)}) collective-permute-start(f32[64,256]{1,0:T(8,128)S(1)} %fusion.132), channel_id=1, source_target_pairs={{0,144},{1,145},{2,146},{3,147},{4,148},{5,149},{6,150},{7,151},{8... | collective-permute-start | bytes 196616 | tf_op jit(solution)/shard_map/ppermute | solution.py:60
  148.8 2.3 %collective-permute-start.40 = (f32[64,256]{1,0:T(8,128)S(1)}, f32[64,256]{1,0:T(8,128)S(1)}, u32[]{:S(2)}, u32[]{:S(2)}) collective-permute-start(f32[64,256]{1,0:T(8,128)S(1)} %fusion.131), channel_id=1, source_target_pairs={{0,32},{1,33},{2,34},{3,35},{4,36},{5,37},{6,38},{7,39},{8,40},{9,... | collective-permute-start | bytes 196616 | tf_op jit(solution)/shard_map/ppermute | solution.py:60
  157.8 2.3 %gather_fusion = f32[256]{0:T(256)S(1)} fusion(f32[256,256]{1,0:T(8,128)S(1)} %bitcast.233, s32[256]{0:T(256)S(1)} %bitcast.232), kind=kCustom, calls=%fused_computation | custom fusion | bytes 4096 | tf_op jit(solution)/shard_map/jit(_diag)/jit(diagonal)/cond/branch_0_fun/gather | solution.py:39
  (166 shorter events, 50.6 us)
Async XLA Ops:
  0.6 64.4 %collective-permute-start = (f32[48,256]{1,0:T(8,128)}, f32[48,256]{1,0:T(8,128)S(1)}, u32[]{:S(2)}, u32[]{:S(2)}) collective-permute-start(f32[48,256]{1,0:T(8,128)} %param.6), channel_id=1, source_target_pairs={{0,4},{1,5},{2,6},{3,7},{4,0},{5,1},{6,2},{7,3},{8,12},{9,13},{10,... | collective-permute-start | bytes 147464 | tf_op jit(solution)/shard_map/ppermute | solution.py:60
  8.5 58.8 %collective-permute-start.1 = (f32[48,256]{1,0:T(8,128)}, f32[48,256]{1,0:T(8,128)S(1)}, u32[]{:S(2)}, u32[]{:S(2)}) collective-permute-start(f32[48,256]{1,0:T(8,128)} %param.6), channel_id=1, source_target_pairs={{0,2},{1,3},{2,0},{3,1},{4,6},{5,7},{6,4},{7,5},{8,10},{9,11},{10,... | collective-permute-start | bytes 147464 | tf_op jit(solution)/shard_map/ppermute | solution.py:60
  9.7 34.8 %collective-permute-start.12 = (f32[8,32]{1,0:T(8,128)}, f32[8,32]{1,0:T(8,128)S(1)}, u32[]{:S(2)}, u32[]{:S(2)}) collective-permute-start(f32[8,32]{1,0:T(8,128)} %bitcast.278), channel_id=1, source_target_pairs={{0,1},{1,0},{2,3},{3,2},{4,5},{5,4},{6,7},{7,6},{8,9},{9,8},{10,11... | collective-permute-start | bytes 3080 | tf_op jit(solution)/shard_map/ppermute | solution.py:60
  10.4 34.0 %collective-permute-start.13 = (f32[8,32]{1,0:T(8,128)}, f32[8,32]{1,0:T(8,128)S(1)}, u32[]{:S(2)}, u32[]{:S(2)}) collective-permute-start(f32[8,32]{1,0:T(8,128)} %bitcast.279), channel_id=1, source_target_pairs={{0,2},{1,3},{2,0},{3,1},{4,6},{5,7},{6,4},{7,5},{8,10},{9,11},{10,... | collective-permute-start | bytes 3080 | tf_op jit(solution)/shard_map/ppermute | solution.py:60
  11.6 32.9 %collective-permute-start.14 = (f32[8,32]{1,0:T(8,128)}, f32[8,32]{1,0:T(8,128)S(1)}, u32[]{:S(2)}, u32[]{:S(2)}) collective-permute-start(f32[8,32]{1,0:T(8,128)} %bitcast.280), channel_id=1, source_target_pairs={{0,3},{1,2},{2,1},{3,0},{4,7},{5,6},{6,5},{7,4},{8,11},{9,10},{10,... | collective-permute-start | bytes 3080 | tf_op jit(solution)/shard_map/ppermute | solution.py:60
  46.3 14.1 %collective-permute-start.17 = (f32[32,32]{1,0:T(8,128)S(1)}, f32[32,32]{1,0:T(8,128)S(1)}, u32[]{:S(2)}, u32[]{:S(2)}) collective-permute-start(f32[32,32]{1,0:T(8,128)S(1)} %get-tuple-element.63), channel_id=1, source_target_pairs={{0,12},{1,13},{2,14},{3,15},{4,8},{5,9},{6,10},{7,11},{8,4},{9,5},... | collective-permute-start | bytes 12296 | tf_op jit(solution)/shard_map/ppermute | solution.py:60
  51.8 15.8 %collective-permute-start.2 = (f32[48,256]{1,0:T(8,128)S(1)}, f32[48,256]{1,0:T(8,128)S(1)}, u32[]{:S(2)}, u32[]{:S(2)}) collective-permute-start(f32[48,256]{1,0:T(8,128)S(1)} %copy-done.5), channel_id=1, source_target_pairs={{0,6},{1,7},{2,4},{3,5},{4,2},{5,3},{6,0},{7,1},{8,14},{9,15},{10,... | collective-permute-start | bytes 147464 | tf_op jit(solution)/shard_map/ppermute | solution.py:60
  51.8 18.5 %collective-permute-start.23 = (f32[48,256]{1,0:T(8,128)S(1)}, f32[48,256]{1,0:T(8,128)S(1)}, u32[]{:S(2)}, u32[]{:S(2)}) collective-permute-start(f32[48,256]{1,0:T(8,128)S(1)} %copy-done.5), channel_id=1, source_target_pairs={{0,0},{1,32},{2,64},{3,96},{4,128},{5,160},{6,192},{7,224},{8,1},{... | collective-permute-start | bytes 147464 | tf_op jit(solution)/shard_map/ppermute | solution.py:154
  67.7 11.3 %collective-permute-start.4 = (f32[192,256]{1,0:T(8,128)S(1)}, f32[192,256]{1,0:T(8,128)S(1)}, u32[]{:S(2)}, u32[]{:S(2)}) collective-permute-start(f32[192,256]{1,0:T(8,128)S(1)} %get-tuple-element.37), channel_id=1, source_target_pairs={{0,16},{1,17},{2,18},{3,19},{4,20},{5,21},{6,22},{7,23},{8,24},{9,... | collective-permute-start | bytes 589832 | tf_op jit(solution)/shard_map/ppermute | solution.py:60
  70.4 12.0 %collective-permute-start.5 = (f32[192,256]{1,0:T(8,128)S(1)}, f32[192,256]{1,0:T(8,128)S(1)}, u32[]{:S(2)}, u32[]{:S(2)}) collective-permute-start(f32[192,256]{1,0:T(8,128)S(1)} %get-tuple-element.37), channel_id=1, source_target_pairs={{0,17},{1,16},{2,19},{3,18},{4,21},{5,20},{6,23},{7,22},{8,25},{9,... | collective-permute-start | bytes 589832 | tf_op jit(solution)/shard_map/ppermute | solution.py:60
  70.4 12.0 %collective-permute-start.3 = (f32[192,256]{1,0:T(8,128)S(1)}, f32[192,256]{1,0:T(8,128)S(1)}, u32[]{:S(2)}, u32[]{:S(2)}) collective-permute-start(f32[192,256]{1,0:T(8,128)S(1)} %get-tuple-element.37), channel_id=1, source_target_pairs={{0,1},{1,0},{2,3},{3,2},{4,5},{5,4},{6,7},{7,6},{8,9},{9,8},{10,11... | collective-permute-start | bytes 589832 | tf_op jit(solution)/shard_map/ppermute | solution.py:60
  72.0 15.6 %collective-permute-start.24 = (f32[48,256]{1,0:T(8,128)S(1)}, f32[48,256]{1,0:T(8,128)S(1)}, u32[]{:S(2)}, u32[]{:S(2)}) collective-permute-start(f32[48,256]{1,0:T(8,128)S(1)} %collective-permute-done.23), channel_id=1, source_target_pairs={{0,32},{32,0},{64,96},{96,64},{128,160},{160,128},{192,224},{224,1... | collective-permute-start | bytes 147464 | tf_op jit(solution)/shard_map/ppermute | solution.py:60
  73.1 14.4 %collective-permute-start.25 = (f32[48,256]{1,0:T(8,128)S(1)}, f32[48,256]{1,0:T(8,128)S(1)}, u32[]{:S(2)}, u32[]{:S(2)}) collective-permute-start(f32[48,256]{1,0:T(8,128)S(1)} %collective-permute-done.23), channel_id=1, source_target_pairs={{0,64},{32,96},{64,0},{96,32},{128,192},{160,224},{192,128},{224,1... | collective-permute-start | bytes 147464 | tf_op jit(solution)/shard_map/ppermute | solution.py:60
  79.0 8.5 %collective-permute-start.26 = (f32[48,256]{1,0:T(8,128)S(1)}, f32[48,256]{1,0:T(8,128)S(1)}, u32[]{:S(2)}, u32[]{:S(2)}) collective-permute-start(f32[48,256]{1,0:T(8,128)S(1)} %collective-permute-done.23), channel_id=1, source_target_pairs={{0,96},{32,64},{64,32},{96,0},{128,224},{160,192},{192,160},{224,1... | collective-permute-start | bytes 147464 | tf_op jit(solution)/shard_map/ppermute | solution.py:60
  82.7 19.4 %collective-permute-start.6 = (f32[768,256]{1,0:T(8,128)S(1)}, f32[768,256]{1,0:T(8,128)S(1)}, u32[]{:S(2)}, u32[]{:S(2)}) collective-permute-start(f32[768,256]{1,0:T(8,128)S(1)} %get-tuple-element.4), channel_id=1, source_target_pairs={{0,8},{1,9},{2,10},{3,11},{4,12},{5,13},{6,14},{7,15},{8,0},{9,1},... | collective-permute-start | bytes 2359304 | tf_op jit(solution)/shard_map/ppermute | solution.py:60
  83.5 7.8 %collective-permute-start.22 = (f32[128,256]{1,0:T(8,128)S(1)}, f32[128,256]{1,0:T(8,128)S(1)}, u32[]{:S(2)}, u32[]{:S(2)}) collective-permute-start(f32[128,256]{1,0:T(8,128)S(1)} %get-tuple-element.42), channel_id=1, source_target_pairs={{0,128},{32,160},{64,192},{96,224},{128,0},{160,32},{192,64},{224,... | collective-permute-start | bytes 393224 | tf_op jit(solution)/shard_map/ppermute | solution.py:60
  109.7 8.4 %collective-permute-start.8 = (f32[96,256]{1,0:T(8,128)S(1)}, f32[96,256]{1,0:T(8,128)S(1)}, u32[]{:S(2)}, u32[]{:S(2)}) collective-permute-start(f32[96,256]{1,0:T(8,128)S(1)} %get-tuple-element.14), channel_id=1, source_target_pairs={{0,64},{32,96},{64,0},{96,32},{128,192},{160,224},{192,128},{224,1... | collective-permute-start | bytes 294920 | tf_op jit(solution)/shard_map/ppermute | solution.py:88
  110.1 8.0 %collective-permute-start.9 = (f32[96,256]{1,0:T(8,128)S(1)}, f32[96,256]{1,0:T(8,128)S(1)}, u32[]{:S(2)}, u32[]{:S(2)}) collective-permute-start(f32[96,256]{1,0:T(8,128)S(1)} %get-tuple-element.13), channel_id=1, source_target_pairs={{0,96},{32,64},{64,32},{96,0},{128,224},{160,192},{192,160},{224,1... | collective-permute-start | bytes 294920 | tf_op jit(solution)/shard_map/ppermute | solution.py:88
  118.2 10.7 %collective-permute-start.10 = (f32[48,256]{1,0:T(8,128)S(1)}, f32[48,256]{1,0:T(8,128)S(1)}, u32[]{:S(2)}, u32[]{:S(2)}) collective-permute-start(f32[48,256]{1,0:T(8,128)S(1)} %dynamic-slice_bitcast_fusion.18), channel_id=1, source_target_pairs={{0,128},{32,160},{64,192},{96,224},{128,0},{160,32},{192,64},{224,... | collective-permute-start | bytes 147464 | tf_op jit(solution)/shard_map/ppermute | solution.py:88
  122.2 12.9 %collective-permute-start.34 = (f32[64,256]{1,0:T(8,128)S(1)}, f32[64,256]{1,0:T(8,128)S(1)}, u32[]{:S(2)}, u32[]{:S(2)}) collective-permute-start(f32[64,256]{1,0:T(8,128)S(1)} %fusion.133), channel_id=1, source_target_pairs={{0,4},{1,5},{2,6},{3,7},{4,0},{5,1},{6,2},{7,3},{8,12},{9,13},{10,... | collective-permute-start | bytes 196616 | tf_op jit(solution)/shard_map/ppermute | solution.py:60
  125.7 9.5 %collective-permute-start.35 = (f32[64,256]{1,0:T(8,128)S(1)}, f32[64,256]{1,0:T(8,128)S(1)}, u32[]{:S(2)}, u32[]{:S(2)}) collective-permute-start(f32[64,256]{1,0:T(8,128)S(1)} %fusion.133), channel_id=1, source_target_pairs={{0,8},{1,9},{2,10},{3,11},{4,12},{5,13},{6,14},{7,15},{8,0},{9,1},... | collective-permute-start | bytes 196616 | tf_op jit(solution)/shard_map/ppermute | solution.py:60
  125.7 9.5 %collective-permute-start.36 = (f32[64,256]{1,0:T(8,128)S(1)}, f32[64,256]{1,0:T(8,128)S(1)}, u32[]{:S(2)}, u32[]{:S(2)}) collective-permute-start(f32[64,256]{1,0:T(8,128)S(1)} %fusion.133), channel_id=1, source_target_pairs={{0,12},{1,13},{2,14},{3,15},{4,8},{5,9},{6,10},{7,11},{8,4},{9,5},... | collective-permute-start | bytes 196616 | tf_op jit(solution)/shard_map/ppermute | solution.py:60
  128.9 15.6 %collective-permute-start.11 = (f32[48,256]{1,0:T(8,128)S(1)}, f32[48,256]{1,0:T(8,128)S(1)}, u32[]{:S(2)}, u32[]{:S(2)}) collective-permute-start(f32[48,256]{1,0:T(8,128)S(1)} %bitcast_add_fusion.2), channel_id=1, source_target_pairs={{0,0},{1,8},{2,16},{3,24},{4,32},{5,40},{6,48},{7,56},{8,64},{9,72... | collective-permute-start | bytes 147464 | tf_op jit(solution)/shard_map/ppermute | solution.py:174
  135.2 10.1 %collective-permute-start.37 = (f32[64,256]{1,0:T(8,128)S(1)}, f32[64,256]{1,0:T(8,128)S(1)}, u32[]{:S(2)}, u32[]{:S(2)}) collective-permute-start(f32[64,256]{1,0:T(8,128)S(1)} %fusion.132), channel_id=1, source_target_pairs={{0,16},{1,17},{2,18},{3,19},{4,20},{5,21},{6,22},{7,23},{8,24},{9,... | collective-permute-start | bytes 196616 | tf_op jit(solution)/shard_map/ppermute | solution.py:60
  (29 other events, 414.1 us)

commit v6 on v3

--- a/solution.py
+++ b/solution.py
@@ -6,22 +6,30 @@
 ALL = ("row", "col")
 
 
-def right_solve(factor, rows):
-    return jax.scipy.linalg.solve_triangular(factor, rows.T, lower=True, trans=1).T
+def mm(a, b):
+    return jnp.dot(a, b, precision=lax.Precision.HIGHEST, preferred_element_type=jnp.float32)
 
 
-def left_solve(factor, matrix):
-    return jax.scipy.linalg.solve_triangular(factor, matrix, lower=True, trans=1)
+def lower_inverse(factor):
+    n = factor.shape[0]
+    index = jnp.arange(n)
+    inverse = jnp.diag(1.0 / jnp.diagonal(factor))
+    s = 1
+    while s < n:
+        inside = (index[:, None] // (2 * s)) == (index[None, :] // (2 * s))
+        outside = (index[:, None] // s) != (index[None, :] // s)
+        between = jnp.where(inside & outside, factor, 0.0)
+        inverse = inverse - mm(mm(inverse, between), inverse)
+        s *= 2
+    return inverse
 
 
-def diagonal_adjoint(factor, adjoint):
-    product = jnp.dot(
-        factor.T, adjoint, precision=lax.Precision.HIGHEST, preferred_element_type=jnp.float32
-    )
+def diagonal_adjoint(factor, inverse, adjoint):
+    product = mm(factor.T, adjoint)
     lower = jnp.tril(product) - 0.5 * jnp.diag(jnp.diag(product))
     symmetric = lower + lower.T
-    half = left_solve(factor, symmetric)
-    return 0.5 * left_solve(factor, half.T).T
+    half = mm(inverse.T, symmetric)
+    return 0.5 * mm(half, inverse)
 
 
 def xor_perm(size, mask):
@@ -109,6 +117,7 @@
     def inner(trailing_adjoint, panel, panel_adjoint, diag_factor, diag_adjoint):
         r = lax.axis_index("row")
         c = lax.axis_index("col")
+        inverse = lower_inverse(diag_factor)
 
         groups = gather_groups(ncol)
         gathered = panel
@@ -134,7 +143,7 @@
         product = lax.ppermute(share, ALL, owner_perm)
 
         updated = panel_adjoint - 2.0 * product
-        off_adjoint = right_solve(diag_factor, updated)
+        off_adjoint = mm(updated, inverse)
         local_term = jnp.dot(
             off_adjoint.T, panel, precision=lax.Precision.HIGHEST, preferred_element_type=jnp.float32
         )
@@ -143,7 +152,7 @@
             jnp.zeros((rows * nrow, cols * ncol), jnp.float32), diag_adjoint, (r * rows, c * cols)
         )
         accumulated = all_reduce(placed - local_term, nrow, ncol)
-        return (off_adjoint, diagonal_adjoint(diag_factor, accumulated))
+        return (off_adjoint, diagonal_adjoint(diag_factor, inverse, accumulated))
 
     return inner
 

time: 155 us -> 141 us (0.910)
  other arithmetic: 25 us -> 3.87 us
  matrix products: 7.18 us -> 17.9 us
  waiting for transfers between devices: 59.2 us -> 54.3 us
  starting transfers between devices: 52 us -> 54.1 us
    another operation x3 -> x0, other arithmetic: 19.7 us -> none  [right_solve(): jax.scipy.linalg.solve_triangular(factor, rows.T, lower=True, trans=1)]
    dot_general x1 -> x20, matrix products: 0.6 us -> 14.8 us  [mm(): jnp.dot(a, b, precision=lax.Precision.HIGHEST, preferred_element_type=jnp...]
    ppermute x19, waiting for transfers between devices: 48.4 us -> 40.3 us  [exchange(): got.append(lax.ppermute(value, axis, xor_perm(size, offset(k, masks))))]
    another operation x8 -> x0, local copies, waits for them, and re-layouts: 4.02 us -> none
    ppermute x1, waiting for transfers between devices: 0.01 us -> 3.89 us  [inner(): product = lax.ppermute(share, ALL, owner_perm)]
    gather x0 -> x1, local copies, waits for them, and re-layouts: none -> 2.57 us  [lower_inverse(): inverse = jnp.diag(1.0 / jnp.diagonal(factor))]
    another operation x9 -> x0, matrix products: 2.38 us -> none  [the longest x6 1.76 us: left_solve(): jax.scipy.linalg.solve_triangular(factor, matrix, lower=True, trans=1)]
    ppermute x19, starting transfers between devices: 36.2 us -> 38.3 us  [exchange(): got.append(lax.ppermute(value, axis, xor_perm(size, offset(k, masks))))]
  transfers between devices with their start and end apart: 27 -> 27, of which waited for: 20 -> 18; matrix products, arithmetic and copies ran while one was open for 17% -> 11% of each run, Pallas kernels for 0% -> 0%
where the time goes in v6:
time: 141 us
  waiting for transfers between devices  54.3 us (39%)
  starting transfers between devices  54.1 us (38%)
  matrix products  17.9 us (13%)
  local copies, waits for them, and re-layouts  9.62 us (7%)
  other arithmetic  3.87 us (3%)
    ppermute x19, waiting for transfers between devices, exchange(): got.append(lax.ppermute(value, axis, xor_perm(size, offset(k, masks))))  40.3 us
    ppermute x19, starting transfers between devices, exchange(): got.append(lax.ppermute(value, axis, xor_perm(size, offset(k, masks))))  38.3 us
    dot_general x20, matrix products, mm(): jnp.dot(a, b, precision=lax.Precision.HIGHEST, preferred_element_type=jnp...  14.8 us
    ppermute x7, starting transfers between devices, scatter_step(): total = total + lax.ppermute(send, axis, xor_perm(size, offset(k, masks)))  11.4 us
    ppermute x7, waiting for transfers between devices, scatter_step(): total = total + lax.ppermute(send, axis, xor_perm(size, offset(k, masks)))  10.1 us
    ppermute x1, starting transfers between devices, inner(): product = lax.ppermute(share, ALL, owner_perm)  4.34 us
    ppermute x1, waiting for transfers between devices, inner(): product = lax.ppermute(share, ALL, owner_perm)  3.89 us
  transfers between devices with their start and end apart: 27, of which 18 were waited for; matrix products, arithmetic and copies ran while one was open for 11% of the time, Pallas kernels for 0%

profile of v6, /device:TPU:1, one launch (start us, length us, event | category | flops | bytes accessed | tf_op | source)
XLA Modules:
  0.0 141.0 jit_solution(17562059076217205875)
XLA Ops:
  0.7 7.8 %collective-permute-start = (f32[48,256]{1,0:T(8,128)}, f32[48,256]{1,0:T(8,128)S(1)}, u32[]{:S(2)}, u32[]{:S(2)}) collective-permute-start(f32[48,256]{1,0:T(8,128)} %param.6), channel_id=1, source_target_pairs={{0,4},{1,5},{2,6},{3,7},{4,0},{5,1},{6,2},{7,3},{8,12},{9,13},{10,... | collective-permute-start | bytes 147464 | tf_op jit(solution)/shard_map/ppermute | solution.py:50
  9.7 2.6 %gather_fusion = f32[256]{0:T(256)S(1)} fusion(f32[256,256]{1,0:T(8,128)} %param.8, s32[256]{0:T(256)S(1)} %bitcast.133), kind=kCustom, calls=%fused_computation | custom fusion | bytes 4096 | tf_op jit(solution)/shard_map/jit(diagonal)/cond/branch_0_fun/gather | solution.py:16
  17.5 2.8 %collective-permute-start.4 = (f32[192,256]{1,0:T(8,128)S(1)}, f32[192,256]{1,0:T(8,128)S(1)}, u32[]{:S(2)}, u32[]{:S(2)}) collective-permute-start(f32[192,256]{1,0:T(8,128)S(1)} %get-tuple-element.21), channel_id=1, source_target_pairs={{0,16},{1,17},{2,18},{3,19},{4,20},{5,21},{6,22},{7,23},{8,24},{9,... | collective-permute-start | bytes 589832 | tf_op jit(solution)/shard_map/ppermute | solution.py:50
  22.9 4.6 %collective-permute-done.4 = f32[192,256]{1,0:T(8,128)S(1)} collective-permute-done((f32[192,256]{1,0:T(8,128)S(1)}, f32[192,256]{1,0:T(8,128)S(1)}, u32[]{:S(2)}, u32[]{:S(2)}) %collective-permute-start.4) | collective-permute-done | bytes 196640 | tf_op jit(solution)/shard_map/ppermute | solution.py:50
  36.0 11.6 %collective-permute-done.6 = f32[768,256]{1,0:T(8,128)} collective-permute-done((f32[768,256]{1,0:T(8,128)}, f32[768,256]{1,0:T(8,128)}, u32[]{:S(2)}, u32[]{:S(2)}) %collective-permute-start.6) | collective-permute-done | bytes 786464 | tf_op jit(solution)/shard_map/ppermute | solution.py:50
  49.3 2.7 %convolution_bitcast_fusion = f32[384,256]{0,1:T(8,128)S(1)} fusion(f32[1536,256]{1,0:T(8,128)S(1)} %bitcast.137, f32[1536,384]{1,0:T(8,128)S(1)} %copy-done), kind=kOutput, calls=%fused_computation.7 | convolution fusion | flops 1811939328 | bytes 4325376 | tf_op jit(solution)/shard_map/dot_general | solution.py:133
  54.6 3.4 %collective-permute-start.7 = (f32[96,256]{1,0:T(8,128)}, f32[96,256]{1,0:T(8,128)S(1)}, u32[]{:S(2)}, u32[]{:S(2)}) collective-permute-start(f32[96,256]{1,0:T(8,128)} %get-tuple-element.10), channel_id=1, source_target_pairs={{0,32},{32,0},{64,96},{96,64},{128,160},{160,128},{192,224},{224,1... | collective-permute-start | bytes 294920 | tf_op jit(solution)/shard_map/ppermute | solution.py:78
  60.0 2.6 %collective-permute-done.8 = f32[96,256]{1,0:T(8,128)} collective-permute-done((f32[96,256]{1,0:T(8,128)}, f32[96,256]{1,0:T(8,128)}, u32[]{:S(2)}, u32[]{:S(2)}) %collective-permute-start.8) | collective-permute-done | bytes 98336 | tf_op jit(solution)/shard_map/ppermute | solution.py:78
  62.7 2.3 %collective-permute-done.9 = f32[96,256]{1,0:T(8,128)} collective-permute-done((f32[96,256]{1,0:T(8,128)}, f32[96,256]{1,0:T(8,128)}, u32[]{:S(2)}, u32[]{:S(2)}) %collective-permute-start.9) | collective-permute-done | bytes 98336 | tf_op jit(solution)/shard_map/ppermute | solution.py:78
  66.0 3.0 %collective-permute-start.10 = (f32[48,256]{1,0:T(8,128)S(1)}, f32[48,256]{1,0:T(8,128)S(1)}, u32[]{:S(2)}, u32[]{:S(2)}) collective-permute-start(f32[48,256]{1,0:T(8,128)S(1)} %dynamic-slice_bitcast_fusion.14), channel_id=1, source_target_pairs={{0,128},{32,160},{64,192},{96,224},{128,0},{160,32},{192,64},{224,... | collective-permute-start | bytes 147464 | tf_op jit(solution)/shard_map/ppermute | solution.py:78
  70.5 4.3 %collective-permute-start.11 = (f32[48,256]{1,0:T(8,128)S(1)}, f32[48,256]{1,0:T(8,128)}, u32[]{:S(2)}, u32[]{:S(2)}) collective-permute-start(f32[48,256]{1,0:T(8,128)S(1)} %bitcast_add_fusion.2), channel_id=1, source_target_pairs={{0,0},{1,8},{2,16},{3,24},{4,32},{5,40},{6,48},{7,56},{8,64},{9,72... | collective-permute-start | bytes 147464 | tf_op jit(solution)/shard_map/ppermute | solution.py:143
  76.2 3.9 %collective-permute-done.11 = f32[48,256]{1,0:T(8,128)} collective-permute-done((f32[48,256]{1,0:T(8,128)S(1)}, f32[48,256]{1,0:T(8,128)}, u32[]{:S(2)}, u32[]{:S(2)}) %collective-permute-start.11) | collective-permute-done | bytes 49184 | tf_op jit(solution)/shard_map/ppermute | solution.py:143
  82.3 3.0 %collective-permute-start.13 = (f32[64,256]{1,0:T(8,128)}, f32[64,256]{1,0:T(8,128)S(1)}, u32[]{:S(2)}, u32[]{:S(2)}) collective-permute-start(f32[64,256]{1,0:T(8,128)} %get-tuple-element.19), channel_id=1, source_target_pairs={{0,64},{1,65},{2,66},{3,67},{4,68},{5,69},{6,70},{7,71},{8,72},{9,... | collective-permute-start | bytes 196616 | tf_op jit(solution)/shard_map/ppermute | solution.py:78
  87.5 2.4 %collective-permute-done.14 = f32[64,256]{1,0:T(8,128)S(1)} collective-permute-done((f32[64,256]{1,0:T(8,128)S(1)}, f32[64,256]{1,0:T(8,128)S(1)}, u32[]{:S(2)}, u32[]{:S(2)}) %collective-permute-start.14) | collective-permute-done | bytes 65568 | tf_op jit(solution)/shard_map/ppermute | solution.py:78
  91.0 1.9 %collective-permute-start.16 = (f32[64,256]{1,0:T(8,128)S(1)}, f32[64,256]{1,0:T(8,128)S(1)}, u32[]{:S(2)}, u32[]{:S(2)}) collective-permute-start(f32[64,256]{1,0:T(8,128)S(1)} %fusion.112), channel_id=1, source_target_pairs={{0,2},{1,3},{2,0},{3,1},{4,6},{5,7},{6,4},{7,5},{8,10},{9,11},{10,... | collective-permute-start | bytes 196616 | tf_op jit(solution)/shard_map/ppermute | solution.py:50
  93.6 3.3 %collective-permute-done.16 = f32[64,256]{1,0:T(8,128)S(1)} collective-permute-done((f32[64,256]{1,0:T(8,128)S(1)}, f32[64,256]{1,0:T(8,128)S(1)}, u32[]{:S(2)}, u32[]{:S(2)}) %collective-permute-start.16) | collective-permute-done | bytes 65568 | tf_op jit(solution)/shard_map/ppermute | solution.py:50
  98.0 6.5 %collective-permute-start.18 = (f32[64,256]{1,0:T(8,128)S(1)}, f32[64,256]{1,0:T(8,128)S(1)}, u32[]{:S(2)}, u32[]{:S(2)}) collective-permute-start(f32[64,256]{1,0:T(8,128)S(1)} %fusion.167), channel_id=1, source_target_pairs={{0,4},{1,5},{2,6},{3,7},{4,0},{5,1},{6,2},{7,3},{8,12},{9,13},{10,... | collective-permute-start | bytes 196616 | tf_op jit(solution)/shard_map/ppermute | solution.py:50
  104.5 2.0 %collective-permute-start.19 = (f32[64,256]{1,0:T(8,128)S(1)}, f32[64,256]{1,0:T(8,128)S(1)}, u32[]{:S(2)}, u32[]{:S(2)}) collective-permute-start(f32[64,256]{1,0:T(8,128)S(1)} %fusion.167), channel_id=1, source_target_pairs={{0,8},{1,9},{2,10},{3,11},{4,12},{5,13},{6,14},{7,15},{8,0},{9,1},... | collective-permute-start | bytes 196616 | tf_op jit(solution)/shard_map/ppermute | solution.py:50
  108.1 6.8 %collective-permute-done.20 = f32[64,256]{1,0:T(8,128)S(1)} collective-permute-done((f32[64,256]{1,0:T(8,128)S(1)}, f32[64,256]{1,0:T(8,128)S(1)}, u32[]{:S(2)}, u32[]{:S(2)}) %collective-permute-start.20) | collective-permute-done | bytes 65568 | tf_op jit(solution)/shard_map/ppermute | solution.py:50
  115.0 1.8 %collective-permute-start.21 = (f32[64,256]{1,0:T(8,128)S(1)}, f32[64,256]{1,0:T(8,128)S(1)}, u32[]{:S(2)}, u32[]{:S(2)}) collective-permute-start(f32[64,256]{1,0:T(8,128)S(1)} %fusion.166), channel_id=1, source_target_pairs={{0,16},{1,17},{2,18},{3,19},{4,20},{5,21},{6,22},{7,23},{8,24},{9,... | collective-permute-start | bytes 196616 | tf_op jit(solution)/shard_map/ppermute | solution.py:50
  116.8 2.2 %collective-permute-start.22 = (f32[64,256]{1,0:T(8,128)S(1)}, f32[64,256]{1,0:T(8,128)S(1)}, u32[]{:S(2)}, u32[]{:S(2)}) collective-permute-start(f32[64,256]{1,0:T(8,128)S(1)} %fusion.166), channel_id=1, source_target_pairs={{0,128},{1,129},{2,130},{3,131},{4,132},{5,133},{6,134},{7,135},{8... | collective-permute-start | bytes 196616 | tf_op jit(solution)/shard_map/ppermute | solution.py:50
  121.4 5.0 %collective-permute-done.23 = f32[64,256]{1,0:T(8,128)S(1)} collective-permute-done((f32[64,256]{1,0:T(8,128)S(1)}, f32[64,256]{1,0:T(8,128)S(1)}, u32[]{:S(2)}, u32[]{:S(2)}) %collective-permute-start.23) | collective-permute-done | bytes 65568 | tf_op jit(solution)/shard_map/ppermute | solution.py:50
  126.4 4.3 %collective-permute-start.24 = (f32[64,256]{1,0:T(8,128)S(1)}, f32[64,256]{1,0:T(8,128)S(1)}, u32[]{:S(2)}, u32[]{:S(2)}) collective-permute-start(f32[64,256]{1,0:T(8,128)S(1)} %fusion.165), channel_id=1, source_target_pairs={{0,32},{1,33},{2,34},{3,35},{4,36},{5,37},{6,38},{7,39},{8,40},{9,... | collective-permute-start | bytes 196616 | tf_op jit(solution)/shard_map/ppermute | solution.py:50
  136.9 2.3 %gather_fusion.1 = f32[256]{0:T(256)S(1)} fusion(f32[256,256]{1,0:T(8,128)S(1)} %bitcast.135, s32[256]{0:T(256)S(1)} %bitcast.134), kind=kCustom, calls=%fused_computation.1 | custom fusion | bytes 4096 | tf_op jit(solution)/shard_map/jit(_diag)/jit(diagonal)/cond/branch_0_fun/gather | solution.py:29
  (109 shorter events, 46.6 us)
Async XLA Ops:
  0.7 16.8 %collective-permute-start = (f32[48,256]{1,0:T(8,128)}, f32[48,256]{1,0:T(8,128)S(1)}, u32[]{:S(2)}, u32[]{:S(2)}) collective-permute-start(f32[48,256]{1,0:T(8,128)} %param.6), channel_id=1, source_target_pairs={{0,4},{1,5},{2,6},{3,7},{4,0},{5,1},{6,2},{7,3},{8,12},{9,13},{10,... | collective-permute-start | bytes 147464 | tf_op jit(solution)/shard_map/ppermute | solution.py:50
  8.5 8.9 %collective-permute-start.1 = (f32[48,256]{1,0:T(8,128)}, f32[48,256]{1,0:T(8,128)S(1)}, u32[]{:S(2)}, u32[]{:S(2)}) collective-permute-start(f32[48,256]{1,0:T(8,128)} %param.6), channel_id=1, source_target_pairs={{0,2},{1,3},{2,0},{3,1},{4,6},{5,7},{6,4},{7,5},{8,10},{9,11},{10,... | collective-permute-start | bytes 147464 | tf_op jit(solution)/shard_map/ppermute | solution.py:50
  9.7 7.8 %collective-permute-start.2 = (f32[48,256]{1,0:T(8,128)}, f32[48,256]{1,0:T(8,128)S(1)}, u32[]{:S(2)}, u32[]{:S(2)}) collective-permute-start(f32[48,256]{1,0:T(8,128)} %param.6), channel_id=1, source_target_pairs={{0,6},{1,7},{2,4},{3,5},{4,2},{5,3},{6,0},{7,1},{8,14},{9,15},{10,... | collective-permute-start | bytes 147464 | tf_op jit(solution)/shard_map/ppermute | solution.py:50
  17.5 9.9 %collective-permute-start.4 = (f32[192,256]{1,0:T(8,128)S(1)}, f32[192,256]{1,0:T(8,128)S(1)}, u32[]{:S(2)}, u32[]{:S(2)}) collective-permute-start(f32[192,256]{1,0:T(8,128)S(1)} %get-tuple-element.21), channel_id=1, source_target_pairs={{0,16},{1,17},{2,18},{3,19},{4,20},{5,21},{6,22},{7,23},{8,24},{9,... | collective-permute-start | bytes 589832 | tf_op jit(solution)/shard_map/ppermute | solution.py:50
  20.4 7.4 %collective-permute-start.5 = (f32[192,256]{1,0:T(8,128)S(1)}, f32[192,256]{1,0:T(8,128)S(1)}, u32[]{:S(2)}, u32[]{:S(2)}) collective-permute-start(f32[192,256]{1,0:T(8,128)S(1)} %get-tuple-element.21), channel_id=1, source_target_pairs={{0,17},{1,16},{2,19},{3,18},{4,21},{5,20},{6,23},{7,22},{8,25},{9,... | collective-permute-start | bytes 589832 | tf_op jit(solution)/shard_map/ppermute | solution.py:50
  21.1 8.5 %collective-permute-start.3 = (f32[192,256]{1,0:T(8,128)S(1)}, f32[192,256]{1,0:T(8,128)S(1)}, u32[]{:S(2)}, u32[]{:S(2)}) collective-permute-start(f32[192,256]{1,0:T(8,128)S(1)} %get-tuple-element.21), channel_id=1, source_target_pairs={{0,1},{1,0},{2,3},{3,2},{4,5},{5,4},{6,7},{7,6},{8,9},{9,8},{10,11... | collective-permute-start | bytes 589832 | tf_op jit(solution)/shard_map/ppermute | solution.py:50
  30.7 16.9 %collective-permute-start.6 = (f32[768,256]{1,0:T(8,128)}, f32[768,256]{1,0:T(8,128)}, u32[]{:S(2)}, u32[]{:S(2)}) collective-permute-start(f32[768,256]{1,0:T(8,128)} %get-tuple-element.4), channel_id=1, source_target_pairs={{0,8},{1,9},{2,10},{3,11},{4,12},{5,13},{6,14},{7,15},{8,0},{9,1},... | collective-permute-start | bytes 2359304 | tf_op jit(solution)/shard_map/ppermute | solution.py:50
  54.6 5.4 %collective-permute-start.7 = (f32[96,256]{1,0:T(8,128)}, f32[96,256]{1,0:T(8,128)S(1)}, u32[]{:S(2)}, u32[]{:S(2)}) collective-permute-start(f32[96,256]{1,0:T(8,128)} %get-tuple-element.10), channel_id=1, source_target_pairs={{0,32},{32,0},{64,96},{96,64},{128,160},{160,128},{192,224},{224,1... | collective-permute-start | bytes 294920 | tf_op jit(solution)/shard_map/ppermute | solution.py:78
  58.0 4.7 %collective-permute-start.8 = (f32[96,256]{1,0:T(8,128)}, f32[96,256]{1,0:T(8,128)}, u32[]{:S(2)}, u32[]{:S(2)}) collective-permute-start(f32[96,256]{1,0:T(8,128)} %get-tuple-element.12), channel_id=1, source_target_pairs={{0,64},{32,96},{64,0},{96,32},{128,192},{160,224},{192,128},{224,1... | collective-permute-start | bytes 294920 | tf_op jit(solution)/shard_map/ppermute | solution.py:78
  59.3 5.7 %collective-permute-start.9 = (f32[96,256]{1,0:T(8,128)}, f32[96,256]{1,0:T(8,128)}, u32[]{:S(2)}, u32[]{:S(2)}) collective-permute-start(f32[96,256]{1,0:T(8,128)} %get-tuple-element.11), channel_id=1, source_target_pairs={{0,96},{32,64},{64,32},{96,0},{128,224},{160,192},{192,160},{224,1... | collective-permute-start | bytes 294920 | tf_op jit(solution)/shard_map/ppermute | solution.py:78
  66.0 4.5 %collective-permute-start.10 = (f32[48,256]{1,0:T(8,128)S(1)}, f32[48,256]{1,0:T(8,128)S(1)}, u32[]{:S(2)}, u32[]{:S(2)}) collective-permute-start(f32[48,256]{1,0:T(8,128)S(1)} %dynamic-slice_bitcast_fusion.14), channel_id=1, source_target_pairs={{0,128},{32,160},{64,192},{96,224},{128,0},{160,32},{192,64},{224,... | collective-permute-start | bytes 147464 | tf_op jit(solution)/shard_map/ppermute | solution.py:78
  70.5 9.6 %collective-permute-start.11 = (f32[48,256]{1,0:T(8,128)S(1)}, f32[48,256]{1,0:T(8,128)}, u32[]{:S(2)}, u32[]{:S(2)}) collective-permute-start(f32[48,256]{1,0:T(8,128)S(1)} %bitcast_add_fusion.2), channel_id=1, source_target_pairs={{0,0},{1,8},{2,16},{3,24},{4,32},{5,40},{6,48},{7,56},{8,64},{9,72... | collective-permute-start | bytes 147464 | tf_op jit(solution)/shard_map/ppermute | solution.py:143
  82.3 5.2 %collective-permute-start.13 = (f32[64,256]{1,0:T(8,128)}, f32[64,256]{1,0:T(8,128)S(1)}, u32[]{:S(2)}, u32[]{:S(2)}) collective-permute-start(f32[64,256]{1,0:T(8,128)} %get-tuple-element.19), channel_id=1, source_target_pairs={{0,64},{1,65},{2,66},{3,67},{4,68},{5,69},{6,70},{7,71},{8,72},{9,... | collective-permute-start | bytes 196616 | tf_op jit(solution)/shard_map/ppermute | solution.py:78
  85.4 4.6 %collective-permute-start.14 = (f32[64,256]{1,0:T(8,128)S(1)}, f32[64,256]{1,0:T(8,128)S(1)}, u32[]{:S(2)}, u32[]{:S(2)}) collective-permute-start(f32[64,256]{1,0:T(8,128)S(1)} %get-tuple-element.18), channel_id=1, source_target_pairs={{0,96},{1,97},{2,98},{3,99},{4,100},{5,101},{6,102},{7,103},{8,104... | collective-permute-start | bytes 196616 | tf_op jit(solution)/shard_map/ppermute | solution.py:78
  90.0 3.6 %collective-permute-start.15 = (f32[64,256]{1,0:T(8,128)S(1)}, f32[64,256]{1,0:T(8,128)S(1)}, u32[]{:S(2)}, u32[]{:S(2)}) collective-permute-start(f32[64,256]{1,0:T(8,128)S(1)} %fusion.112), channel_id=1, source_target_pairs={{0,1},{1,0},{2,3},{3,2},{4,5},{5,4},{6,7},{7,6},{8,9},{9,8},{10,11... | collective-permute-start | bytes 196616 | tf_op jit(solution)/shard_map/ppermute | solution.py:50
  91.0 5.9 %collective-permute-start.16 = (f32[64,256]{1,0:T(8,128)S(1)}, f32[64,256]{1,0:T(8,128)S(1)}, u32[]{:S(2)}, u32[]{:S(2)}) collective-permute-start(f32[64,256]{1,0:T(8,128)S(1)} %fusion.112), channel_id=1, source_target_pairs={{0,2},{1,3},{2,0},{3,1},{4,6},{5,7},{6,4},{7,5},{8,10},{9,11},{10,... | collective-permute-start | bytes 196616 | tf_op jit(solution)/shard_map/ppermute | solution.py:50
  92.9 5.0 %collective-permute-start.17 = (f32[64,256]{1,0:T(8,128)S(1)}, f32[64,256]{1,0:T(8,128)S(1)}, u32[]{:S(2)}, u32[]{:S(2)}) collective-permute-start(f32[64,256]{1,0:T(8,128)S(1)} %fusion.112), channel_id=1, source_target_pairs={{0,3},{1,2},{2,1},{3,0},{4,7},{5,6},{6,5},{7,4},{8,11},{9,10},{10,... | collective-permute-start | bytes 196616 | tf_op jit(solution)/shard_map/ppermute | solution.py:50
  98.0 8.5 %collective-permute-start.18 = (f32[64,256]{1,0:T(8,128)S(1)}, f32[64,256]{1,0:T(8,128)S(1)}, u32[]{:S(2)}, u32[]{:S(2)}) collective-permute-start(f32[64,256]{1,0:T(8,128)S(1)} %fusion.167), channel_id=1, source_target_pairs={{0,4},{1,5},{2,6},{3,7},{4,0},{5,1},{6,2},{7,3},{8,12},{9,13},{10,... | collective-permute-start | bytes 196616 | tf_op jit(solution)/shard_map/ppermute | solution.py:50
  106.4 8.5 %collective-permute-start.20 = (f32[64,256]{1,0:T(8,128)S(1)}, f32[64,256]{1,0:T(8,128)S(1)}, u32[]{:S(2)}, u32[]{:S(2)}) collective-permute-start(f32[64,256]{1,0:T(8,128)S(1)} %fusion.167), channel_id=1, source_target_pairs={{0,12},{1,13},{2,14},{3,15},{4,8},{5,9},{6,10},{7,11},{8,4},{9,5},... | collective-permute-start | bytes 196616 | tf_op jit(solution)/shard_map/ppermute | solution.py:50
  115.0 5.8 %collective-permute-start.21 = (f32[64,256]{1,0:T(8,128)S(1)}, f32[64,256]{1,0:T(8,128)S(1)}, u32[]{:S(2)}, u32[]{:S(2)}) collective-permute-start(f32[64,256]{1,0:T(8,128)S(1)} %fusion.166), channel_id=1, source_target_pairs={{0,16},{1,17},{2,18},{3,19},{4,20},{5,21},{6,22},{7,23},{8,24},{9,... | collective-permute-start | bytes 196616 | tf_op jit(solution)/shard_map/ppermute | solution.py:50
  116.8 4.6 %collective-permute-start.22 = (f32[64,256]{1,0:T(8,128)S(1)}, f32[64,256]{1,0:T(8,128)S(1)}, u32[]{:S(2)}, u32[]{:S(2)}) collective-permute-start(f32[64,256]{1,0:T(8,128)S(1)} %fusion.166), channel_id=1, source_target_pairs={{0,128},{1,129},{2,130},{3,131},{4,132},{5,133},{6,134},{7,135},{8... | collective-permute-start | bytes 196616 | tf_op jit(solution)/shard_map/ppermute | solution.py:50
  119.0 7.3 %collective-permute-start.23 = (f32[64,256]{1,0:T(8,128)S(1)}, f32[64,256]{1,0:T(8,128)S(1)}, u32[]{:S(2)}, u32[]{:S(2)}) collective-permute-start(f32[64,256]{1,0:T(8,128)S(1)} %fusion.166), channel_id=1, source_target_pairs={{0,144},{1,145},{2,146},{3,147},{4,148},{5,149},{6,150},{7,151},{8... | collective-permute-start | bytes 196616 | tf_op jit(solution)/shard_map/ppermute | solution.py:50
  126.4 6.1 %collective-permute-start.24 = (f32[64,256]{1,0:T(8,128)S(1)}, f32[64,256]{1,0:T(8,128)S(1)}, u32[]{:S(2)}, u32[]{:S(2)}) collective-permute-start(f32[64,256]{1,0:T(8,128)S(1)} %fusion.165), channel_id=1, source_target_pairs={{0,32},{1,33},{2,34},{3,35},{4,36},{5,37},{6,38},{7,39},{8,40},{9,... | collective-permute-start | bytes 196616 | tf_op jit(solution)/shard_map/ppermute | solution.py:50
  131.7 4.4 %collective-permute-start.26 = (f32[64,256]{1,0:T(8,128)S(1)}, f32[64,256]{1,0:T(8,128)S(1)}, u32[]{:S(2)}, u32[]{:S(2)}) collective-permute-start(f32[64,256]{1,0:T(8,128)S(1)} %fusion.165), channel_id=1, source_target_pairs={{0,96},{1,97},{2,98},{3,99},{4,100},{5,101},{6,102},{7,103},{8,104... | collective-permute-start | bytes 196616 | tf_op jit(solution)/shard_map/ppermute | solution.py:50
  (12 other events, 179.1 us)

commit v7 on v6

--- a/solution.py
+++ b/solution.py
@@ -81,8 +81,10 @@
 
 def gather_groups(ncol):
     bits = [1 << k for k in range(ncol.bit_length() - 1)]
-    order = [m for m in bits if m < 8][::-1] + [m for m in bits if m >= 8][::-1]
-    return [tuple(order[i : i + 2]) for i in range(0, len(order), 2)]
+    low = [m for m in bits if m < 8][::-1]
+    high = [m for m in bits if m >= 8]
+    groups = [tuple(low[i : i + 2]) for i in range(0, len(low), 2)]
+    return groups + [tuple(high[i : i + 2]) for i in range(0, len(high), 2)]
 
 
 def kept_chunk(idx, groups, nblocks):
@@ -108,8 +110,10 @@
 
 def make_body(nrow, ncol):
     assert nrow & (nrow - 1) == 0 and ncol & (ncol - 1) == 0
+    ndev = nrow * ncol
     row_bits = [1 << k for k in range(nrow.bit_length() - 1)]
     row_groups = [tuple(row_bits[i : i + 2]) for i in range(0, len(row_bits), 2)]
+    blocks_perm = [(b, (b % nrow) * ncol + b // nrow) for b in range(ndev)]
     owner_perm = [
         (r * ncol + c, c * nrow + kept_chunk(r, row_groups, nrow)) for r in range(nrow) for c in range(ncol)
     ]
@@ -138,20 +142,25 @@
             preferred_element_type=jnp.float32,
         )
 
+        col_panel = lax.ppermute(panel, ALL, blocks_perm)
         for masks in row_groups:
-            share = scatter_step(share, "row", nrow, masks)
-        product = lax.ppermute(share, ALL, owner_perm)
+            col_panel = gather_step(col_panel, "row", nrow, masks)
 
-        updated = panel_adjoint - 2.0 * product
-        off_adjoint = mm(updated, inverse)
-        local_term = jnp.dot(
-            off_adjoint.T, panel, precision=lax.Precision.HIGHEST, preferred_element_type=jnp.float32
-        )
+        local_term = mm(panel_adjoint.T, panel) - 2.0 * mm(share.T, col_panel)
         rows, cols = diag_adjoint.shape
         placed = lax.dynamic_update_slice(
             jnp.zeros((rows * nrow, cols * ncol), jnp.float32), diag_adjoint, (r * rows, c * cols)
         )
-        accumulated = all_reduce(placed - local_term, nrow, ncol)
+        summed = all_reduce(jnp.concatenate([local_term, placed], axis=0), nrow, ncol)
+        total, whole = summed[: local_term.shape[0]], summed[local_term.shape[0] :]
+
+        for masks in row_groups:
+            share = scatter_step(share, "row", nrow, masks)
+        product = lax.ppermute(share, ALL, owner_perm)
+        updated = panel_adjoint - 2.0 * product
+        off_adjoint = mm(updated, inverse)
+
+        accumulated = whole - mm(inverse.T, total)
         return (off_adjoint, diagonal_adjoint(diag_factor, inverse, accumulated))
 
     return inner

time: 141 us -> 139 us (0.986); the launches traced: 141 us -> 136 us
  waiting for transfers between devices: 54.3 us -> 42.6 us
  starting transfers between devices: 54.1 us -> 63.9 us
  matrix products: 17.9 us -> 16.2 us
    ppermute x0 -> x1, starting transfers between devices: none -> 7.76 us  [inner(): col_panel = lax.ppermute(panel, ALL, blocks_perm)]
    ppermute x7, waiting for transfers between devices: 10.1 us -> 2.43 us  [scatter_step(): total = total + lax.ppermute(send, axis, xor_perm(size, offset(k, masks)))]
    ppermute x1, waiting for transfers between devices: 3.89 us -> 0.01 us  [inner(): product = lax.ppermute(share, ALL, owner_perm)]
    ppermute x19 -> x23, starting transfers between devices: 38.3 us -> 41.6 us  [exchange(): got.append(lax.ppermute(value, axis, xor_perm(size, offset(k, masks))))]
    ppermute x7, starting transfers between devices: 11.4 us -> 8.79 us  [scatter_step(): total = total + lax.ppermute(send, axis, xor_perm(size, offset(k, masks)))]
    dot_general x20 -> x23, matrix products: 14.8 us -> 13.5 us  [mm(): jnp.dot(a, b, precision=lax.Precision.HIGHEST, preferred_element_type=jnp...]
    ppermute x19 -> x23, waiting for transfers between devices: 40.3 us -> 40.2 us  [exchange(): got.append(lax.ppermute(value, axis, xor_perm(size, offset(k, masks))))]
  transfers between devices with their start and end apart: 27 -> 32, of which waited for: 18 -> 13; matrix products, arithmetic and copies ran while one was open for 11% -> 13% of each run, Pallas kernels for 0% -> 0%
where the time goes in v7:
time: 139 us; the launch traced here: 136 us
  starting transfers between devices  63.9 us (46%)
  waiting for transfers between devices  42.6 us (31%)
  matrix products  16.2 us (12%)
  local copies, waits for them, and re-layouts  9.17 us (7%)
  other arithmetic  3.01 us (2%)
    ppermute x23, starting transfers between devices, exchange(): got.append(lax.ppermute(value, axis, xor_perm(size, offset(k, masks))))  41.6 us
    ppermute x23, waiting for transfers between devices, exchange(): got.append(lax.ppermute(value, axis, xor_perm(size, offset(k, masks))))  40.2 us
    dot_general x23, matrix products, mm(): jnp.dot(a, b, precision=lax.Precision.HIGHEST, preferred_element_type=jnp...  13.5 us
    ppermute x7, starting transfers between devices, scatter_step(): total = total + lax.ppermute(send, axis, xor_perm(size, offset(k, masks)))  8.79 us
    ppermute x1, starting transfers between devices, inner(): col_panel = lax.ppermute(panel, ALL, blocks_perm)  7.76 us
    ppermute x1, starting transfers between devices, inner(): product = lax.ppermute(share, ALL, owner_perm)  5.72 us
  transfers between devices with their start and end apart: 32, of which 13 were waited for; matrix products, arithmetic and copies ran while one was open for 13% of the time, Pallas kernels for 0%

profile of v7, /device:TPU:1, one launch (start us, length us, event | category | flops | bytes accessed | tf_op | source)
XLA Modules:
  0.0 136.2 jit_solution(6059116911655664511)
XLA Ops:
  0.7 7.8 %collective-permute-start = (f32[48,256]{1,0:T(8,128)}, f32[48,256]{1,0:T(8,128)S(1)}, u32[]{:S(2)}, u32[]{:S(2)}) collective-permute-start(f32[48,256]{1,0:T(8,128)} %param.6), channel_id=1, source_target_pairs={{0,4},{1,5},{2,6},{3,7},{4,0},{5,1},{6,2},{7,3},{8,12},{9,13},{10,... | collective-permute-start | bytes 147464 | tf_op jit(solution)/shard_map/ppermute | solution.py:50
  9.7 7.8 %collective-permute-start.12 = (f32[48,256]{1,0:T(8,128)}, f32[48,256]{1,0:T(8,128)S(1)}, u32[]{:S(2)}, u32[]{:S(2)}) collective-permute-start(f32[48,256]{1,0:T(8,128)} %param.6), channel_id=1, source_target_pairs={{0,0},{1,32},{2,64},{3,96},{4,128},{5,160},{6,192},{7,224},{8,1},{... | collective-permute-start | bytes 147464 | tf_op jit(solution)/shard_map/ppermute | solution.py:145
  17.5 2.6 %gather_fusion = f32[256]{0:T(256)S(1)} fusion(f32[256,256]{1,0:T(8,128)} %param.8, s32[256]{0:T(256)S(1)} %bitcast.154), kind=kCustom, calls=%fused_computation | custom fusion | bytes 4096 | tf_op jit(solution)/shard_map/jit(diagonal)/cond/branch_0_fun/gather | solution.py:16
  29.7 2.2 %collective-permute-start.14 = (f32[48,256]{1,0:T(8,128)S(1)}, f32[48,256]{1,0:T(8,128)S(1)}, u32[]{:S(2)}, u32[]{:S(2)}) collective-permute-start(f32[48,256]{1,0:T(8,128)S(1)} %collective-permute-done.12), channel_id=1, source_target_pairs={{0,64},{32,96},{64,0},{96,32},{128,192},{160,224},{192,128},{224,1... | collective-permute-start | bytes 147464 | tf_op jit(solution)/shard_map/ppermute | solution.py:50
  33.4 2.9 %collective-permute-done.15 = f32[48,256]{1,0:T(8,128)S(1)} collective-permute-done((f32[48,256]{1,0:T(8,128)S(1)}, f32[48,256]{1,0:T(8,128)S(1)}, u32[]{:S(2)}, u32[]{:S(2)}) %collective-permute-start.15) | collective-permute-done | bytes 49184 | tf_op jit(solution)/shard_map/ppermute | solution.py:50
  36.3 2.1 %collective-permute-done.3 = f32[192,256]{1,0:T(8,128)S(1)} collective-permute-done((f32[192,256]{1,0:T(8,128)S(1)}, f32[192,256]{1,0:T(8,128)S(1)}, u32[]{:S(2)}, u32[]{:S(2)}) %collective-permute-start.3) | collective-permute-done | bytes 196640 | tf_op jit(solution)/shard_map/ppermute | solution.py:50
  42.7 5.4 %collective-permute-start.16 = (f32[192,256]{1,0:T(8,128)S(1)}, f32[192,256]{1,0:T(8,128)S(1)}, u32[]{:S(2)}, u32[]{:S(2)}) collective-permute-start(f32[192,256]{1,0:T(8,128)S(1)} %get-tuple-element.22), channel_id=1, source_target_pairs={{0,128},{32,160},{64,192},{96,224},{128,0},{160,32},{192,64},{224,... | collective-permute-start | bytes 589832 | tf_op jit(solution)/shard_map/ppermute | solution.py:50
  48.5 3.3 %collective-permute-done.16 = f32[192,256]{1,0:T(8,128)S(1)} collective-permute-done((f32[192,256]{1,0:T(8,128)S(1)}, f32[192,256]{1,0:T(8,128)S(1)}, u32[]{:S(2)}, u32[]{:S(2)}) %collective-permute-start.16) | collective-permute-done | bytes 196640 | tf_op jit(solution)/shard_map/ppermute | solution.py:50
  52.0 5.5 %collective-permute-done.5 = f32[384,256]{1,0:T(8,128)S(1)} collective-permute-done((f32[384,256]{1,0:T(8,128)S(1)}, f32[384,256]{1,0:T(8,128)S(1)}, u32[]{:S(2)}, u32[]{:S(2)}) %collective-permute-start.5) | collective-permute-done | bytes 393248 | tf_op jit(solution)/shard_map/ppermute | solution.py:50
  60.1 2.7 %fusion.139 = f32[256,384]{1,0:T(8,128)S(1)} fusion(f32[1536,256]{1,0:T(8,128)S(1)} %bitcast.158, f32[1536,384]{1,0:T(8,128)S(1)} %copy-done), kind=kOutput, calls=%fused_computation.232 | convolution fusion | flops 1811939328 | bytes 4325376 | tf_op jit(solution)/shard_map/dot_general | solution.py:137
  64.3 2.7 %collective-permute-start.17 = (f32[128,256]{1,0:T(8,128)}, f32[128,256]{1,0:T(8,128)}, u32[]{:S(2)}, u32[]{:S(2)}) collective-permute-start(f32[128,256]{1,0:T(8,128)} %get-tuple-element.10), channel_id=1, source_target_pairs={{0,32},{1,33},{2,34},{3,35},{4,36},{5,37},{6,38},{7,39},{8,40},{9,... | collective-permute-start | bytes 393224 | tf_op jit(solution)/shard_map/ppermute | solution.py:78
  66.9 2.3 %collective-permute-start.18 = (f32[128,256]{1,0:T(8,128)}, f32[128,256]{1,0:T(8,128)}, u32[]{:S(2)}, u32[]{:S(2)}) collective-permute-start(f32[128,256]{1,0:T(8,128)} %get-tuple-element.12), channel_id=1, source_target_pairs={{0,64},{1,65},{2,66},{3,67},{4,68},{5,69},{6,70},{7,71},{8,72},{9,... | collective-permute-start | bytes 393224 | tf_op jit(solution)/shard_map/ppermute | solution.py:78
  73.9 2.4 %collective-permute-done.19 = f32[128,256]{1,0:T(8,128)} collective-permute-done((f32[128,256]{1,0:T(8,128)}, f32[128,256]{1,0:T(8,128)}, u32[]{:S(2)}, u32[]{:S(2)}) %collective-permute-start.19) | collective-permute-done | bytes 131104 | tf_op jit(solution)/shard_map/ppermute | solution.py:78
  77.8 2.7 %collective-permute-start.21 = (f32[128,256]{1,0:T(8,128)S(1)}, f32[128,256]{1,0:T(8,128)S(1)}, u32[]{:S(2)}, u32[]{:S(2)}) collective-permute-start(f32[128,256]{1,0:T(8,128)S(1)} %fusion.68), channel_id=1, source_target_pairs={{0,2},{1,3},{2,0},{3,1},{4,6},{5,7},{6,4},{7,5},{8,10},{9,11},{10,... | collective-permute-start | bytes 393224 | tf_op jit(solution)/shard_map/ppermute | solution.py:50
  82.3 2.7 %collective-permute-done.20 = f32[128,256]{1,0:T(8,128)S(1)} collective-permute-done((f32[128,256]{1,0:T(8,128)S(1)}, f32[128,256]{1,0:T(8,128)S(1)}, u32[]{:S(2)}, u32[]{:S(2)}) %collective-permute-start.20) | collective-permute-done | bytes 131104 | tf_op jit(solution)/shard_map/ppermute | solution.py:50
  85.1 5.8 %collective-permute-done.22 = f32[128,256]{1,0:T(8,128)S(1)} collective-permute-done((f32[128,256]{1,0:T(8,128)S(1)}, f32[128,256]{1,0:T(8,128)S(1)}, u32[]{:S(2)}, u32[]{:S(2)}) %collective-permute-start.22) | collective-permute-done | bytes 131104 | tf_op jit(solution)/shard_map/ppermute | solution.py:50
  91.0 4.0 %collective-permute-start.23 = (f32[128,256]{1,0:T(8,128)S(1)}, f32[128,256]{1,0:T(8,128)S(1)}, u32[]{:S(2)}, u32[]{:S(2)}) collective-permute-start(f32[128,256]{1,0:T(8,128)S(1)} %fusion.178), channel_id=1, source_target_pairs={{0,4},{1,5},{2,6},{3,7},{4,0},{5,1},{6,2},{7,3},{8,12},{9,13},{10,... | collective-permute-start | bytes 393224 | tf_op jit(solution)/shard_map/ppermute | solution.py:50
  95.0 2.8 %collective-permute-start.25 = (f32[128,256]{1,0:T(8,128)S(1)}, f32[128,256]{1,0:T(8,128)S(1)}, u32[]{:S(2)}, u32[]{:S(2)}) collective-permute-start(f32[128,256]{1,0:T(8,128)S(1)} %fusion.178), channel_id=1, source_target_pairs={{0,12},{1,13},{2,14},{3,15},{4,8},{5,9},{6,10},{7,11},{8,4},{9,5},... | collective-permute-start | bytes 393224 | tf_op jit(solution)/shard_map/ppermute | solution.py:50
  99.6 8.7 %collective-permute-done.25 = f32[128,256]{1,0:T(8,128)S(1)} collective-permute-done((f32[128,256]{1,0:T(8,128)S(1)}, f32[128,256]{1,0:T(8,128)S(1)}, u32[]{:S(2)}, u32[]{:S(2)}) %collective-permute-start.25) | collective-permute-done | bytes 131104 | tf_op jit(solution)/shard_map/ppermute | solution.py:50
  109.1 5.1 %collective-permute-start.28 = (f32[128,256]{1,0:T(8,128)S(1)}, f32[128,256]{1,0:T(8,128)S(1)}, u32[]{:S(2)}, u32[]{:S(2)}) collective-permute-start(f32[128,256]{1,0:T(8,128)S(1)} %fusion.177), channel_id=1, source_target_pairs={{0,144},{1,145},{2,146},{3,147},{4,148},{5,149},{6,150},{7,151},{8... | collective-permute-start | bytes 393224 | tf_op jit(solution)/shard_map/ppermute | solution.py:50
  114.2 5.7 %collective-permute-start.11 = (f32[48,256]{1,0:T(8,128)S(1)}, f32[48,256]{1,0:T(8,128)S(1)}, u32[]{:S(2)}, u32[]{:S(2)}) collective-permute-start(f32[48,256]{1,0:T(8,128)S(1)} %bitcast_add_fusion.2), channel_id=1, source_target_pairs={{0,0},{1,8},{2,16},{3,24},{4,32},{5,40},{6,48},{7,56},{8,64},{9,72... | collective-permute-start | bytes 147464 | tf_op jit(solution)/shard_map/ppermute | solution.py:159
  124.8 3.0 %collective-permute-done.30 = f32[128,256]{1,0:T(8,128)S(1)} collective-permute-done((f32[128,256]{1,0:T(8,128)S(1)}, f32[128,256]{1,0:T(8,128)S(1)}, u32[]{:S(2)}, u32[]{:S(2)}) %collective-permute-start.30) | collective-permute-done | bytes 131104 | tf_op jit(solution)/shard_map/ppermute | solution.py:50
  127.8 2.8 %collective-permute-done.31 = f32[128,256]{1,0:T(8,128)S(1)} collective-permute-done((f32[128,256]{1,0:T(8,128)S(1)}, f32[128,256]{1,0:T(8,128)S(1)}, u32[]{:S(2)}, u32[]{:S(2)}) %collective-permute-start.31) | collective-permute-done | bytes 131104 | tf_op jit(solution)/shard_map/ppermute | solution.py:50
  132.0 2.3 %gather_fusion.1 = f32[256]{0:T(256)S(1)} fusion(f32[256,256]{1,0:T(8,128)S(1)} %bitcast.156, s32[256]{0:T(256)S(1)} %bitcast.155), kind=kCustom, calls=%fused_computation.1 | custom fusion | bytes 4096 | tf_op jit(solution)/shard_map/jit(_diag)/jit(diagonal)/cond/branch_0_fun/gather | solution.py:29
  (124 shorter events, 39.4 us)
Async XLA Ops:
  0.7 28.8 %collective-permute-start = (f32[48,256]{1,0:T(8,128)}, f32[48,256]{1,0:T(8,128)S(1)}, u32[]{:S(2)}, u32[]{:S(2)}) collective-permute-start(f32[48,256]{1,0:T(8,128)} %param.6), channel_id=1, source_target_pairs={{0,4},{1,5},{2,6},{3,7},{4,0},{5,1},{6,2},{7,3},{8,12},{9,13},{10,... | collective-permute-start | bytes 147464 | tf_op jit(solution)/shard_map/ppermute | solution.py:50
  8.5 21.0 %collective-permute-start.1 = (f32[48,256]{1,0:T(8,128)}, f32[48,256]{1,0:T(8,128)S(1)}, u32[]{:S(2)}, u32[]{:S(2)}) collective-permute-start(f32[48,256]{1,0:T(8,128)} %param.6), channel_id=1, source_target_pairs={{0,2},{1,3},{2,0},{3,1},{4,6},{5,7},{6,4},{7,5},{8,10},{9,11},{10,... | collective-permute-start | bytes 147464 | tf_op jit(solution)/shard_map/ppermute | solution.py:50
  9.7 19.8 %collective-permute-start.2 = (f32[48,256]{1,0:T(8,128)}, f32[48,256]{1,0:T(8,128)S(1)}, u32[]{:S(2)}, u32[]{:S(2)}) collective-permute-start(f32[48,256]{1,0:T(8,128)} %param.6), channel_id=1, source_target_pairs={{0,6},{1,7},{2,4},{3,5},{4,2},{5,3},{6,0},{7,1},{8,14},{9,15},{10,... | collective-permute-start | bytes 147464 | tf_op jit(solution)/shard_map/ppermute | solution.py:50
  9.7 19.9 %collective-permute-start.12 = (f32[48,256]{1,0:T(8,128)}, f32[48,256]{1,0:T(8,128)S(1)}, u32[]{:S(2)}, u32[]{:S(2)}) collective-permute-start(f32[48,256]{1,0:T(8,128)} %param.6), channel_id=1, source_target_pairs={{0,0},{1,32},{2,64},{3,96},{4,128},{5,160},{6,192},{7,224},{8,1},{... | collective-permute-start | bytes 147464 | tf_op jit(solution)/shard_map/ppermute | solution.py:145
  38.5 13.5 %collective-permute-start.4 = (f32[384,256]{1,0:T(8,128)S(1)}, f32[384,256]{1,0:T(8,128)S(1)}, u32[]{:S(2)}, u32[]{:S(2)}) collective-permute-start(f32[384,256]{1,0:T(8,128)S(1)} %get-tuple-element.19), channel_id=1, source_target_pairs={{0,8},{1,9},{2,10},{3,11},{4,12},{5,13},{6,14},{7,15},{8,0},{9,1},... | collective-permute-start | bytes 1179656 | tf_op jit(solution)/shard_map/ppermute | solution.py:50
  39.9 17.6 %collective-permute-start.5 = (f32[384,256]{1,0:T(8,128)S(1)}, f32[384,256]{1,0:T(8,128)S(1)}, u32[]{:S(2)}, u32[]{:S(2)}) collective-permute-start(f32[384,256]{1,0:T(8,128)S(1)} %get-tuple-element.19), channel_id=1, source_target_pairs={{0,16},{1,17},{2,18},{3,19},{4,20},{5,21},{6,22},{7,23},{8,24},{9,... | collective-permute-start | bytes 1179656 | tf_op jit(solution)/shard_map/ppermute | solution.py:50
  41.1 18.5 %collective-permute-start.6 = (f32[384,256]{1,0:T(8,128)S(1)}, f32[384,256]{1,0:T(8,128)S(1)}, u32[]{:S(2)}, u32[]{:S(2)}) collective-permute-start(f32[384,256]{1,0:T(8,128)S(1)} %get-tuple-element.19), channel_id=1, source_target_pairs={{0,24},{1,25},{2,26},{3,27},{4,28},{5,29},{6,30},{7,31},{8,16},{9,... | collective-permute-start | bytes 1179656 | tf_op jit(solution)/shard_map/ppermute | solution.py:50
  42.7 9.2 %collective-permute-start.16 = (f32[192,256]{1,0:T(8,128)S(1)}, f32[192,256]{1,0:T(8,128)S(1)}, u32[]{:S(2)}, u32[]{:S(2)}) collective-permute-start(f32[192,256]{1,0:T(8,128)S(1)} %get-tuple-element.22), channel_id=1, source_target_pairs={{0,128},{32,160},{64,192},{96,224},{128,0},{160,32},{192,64},{224,... | collective-permute-start | bytes 589832 | tf_op jit(solution)/shard_map/ppermute | solution.py:50
  64.3 9.3 %collective-permute-start.17 = (f32[128,256]{1,0:T(8,128)}, f32[128,256]{1,0:T(8,128)}, u32[]{:S(2)}, u32[]{:S(2)}) collective-permute-start(f32[128,256]{1,0:T(8,128)} %get-tuple-element.10), channel_id=1, source_target_pairs={{0,32},{1,33},{2,34},{3,35},{4,36},{5,37},{6,38},{7,39},{8,40},{9,... | collective-permute-start | bytes 393224 | tf_op jit(solution)/shard_map/ppermute | solution.py:78
  69.3 7.1 %collective-permute-start.19 = (f32[128,256]{1,0:T(8,128)}, f32[128,256]{1,0:T(8,128)}, u32[]{:S(2)}, u32[]{:S(2)}) collective-permute-start(f32[128,256]{1,0:T(8,128)} %get-tuple-element.11), channel_id=1, source_target_pairs={{0,96},{1,97},{2,98},{3,99},{4,100},{5,101},{6,102},{7,103},{8,104... | collective-permute-start | bytes 393224 | tf_op jit(solution)/shard_map/ppermute | solution.py:78
  71.7 8.8 %collective-permute-start.7 = (f32[96,256]{1,0:T(8,128)S(1)}, f32[96,256]{1,0:T(8,128)S(1)}, u32[]{:S(2)}, u32[]{:S(2)}) collective-permute-start(f32[96,256]{1,0:T(8,128)S(1)} %get-tuple-element.15), channel_id=1, source_target_pairs={{0,32},{32,0},{64,96},{96,64},{128,160},{160,128},{192,224},{224,1... | collective-permute-start | bytes 294920 | tf_op jit(solution)/shard_map/ppermute | solution.py:78
  72.2 9.3 %collective-permute-start.8 = (f32[96,256]{1,0:T(8,128)S(1)}, f32[96,256]{1,0:T(8,128)S(1)}, u32[]{:S(2)}, u32[]{:S(2)}) collective-permute-start(f32[96,256]{1,0:T(8,128)S(1)} %get-tuple-element.17), channel_id=1, source_target_pairs={{0,64},{32,96},{64,0},{96,32},{128,192},{160,224},{192,128},{224,1... | collective-permute-start | bytes 294920 | tf_op jit(solution)/shard_map/ppermute | solution.py:78
  73.6 7.8 %collective-permute-start.9 = (f32[96,256]{1,0:T(8,128)S(1)}, f32[96,256]{1,0:T(8,128)S(1)}, u32[]{:S(2)}, u32[]{:S(2)}) collective-permute-start(f32[96,256]{1,0:T(8,128)S(1)} %get-tuple-element.16), channel_id=1, source_target_pairs={{0,96},{32,64},{64,32},{96,0},{128,224},{160,192},{192,160},{224,1... | collective-permute-start | bytes 294920 | tf_op jit(solution)/shard_map/ppermute | solution.py:78
  77.5 7.6 %collective-permute-start.20 = (f32[128,256]{1,0:T(8,128)S(1)}, f32[128,256]{1,0:T(8,128)S(1)}, u32[]{:S(2)}, u32[]{:S(2)}) collective-permute-start(f32[128,256]{1,0:T(8,128)S(1)} %fusion.68), channel_id=1, source_target_pairs={{0,1},{1,0},{2,3},{3,2},{4,5},{5,4},{6,7},{7,6},{8,9},{9,8},{10,11... | collective-permute-start | bytes 393224 | tf_op jit(solution)/shard_map/ppermute | solution.py:50
  77.8 7.3 %collective-permute-start.21 = (f32[128,256]{1,0:T(8,128)S(1)}, f32[128,256]{1,0:T(8,128)S(1)}, u32[]{:S(2)}, u32[]{:S(2)}) collective-permute-start(f32[128,256]{1,0:T(8,128)S(1)} %fusion.68), channel_id=1, source_target_pairs={{0,2},{1,3},{2,0},{3,1},{4,6},{5,7},{6,4},{7,5},{8,10},{9,11},{10,... | collective-permute-start | bytes 393224 | tf_op jit(solution)/shard_map/ppermute | solution.py:50
  80.5 10.4 %collective-permute-start.22 = (f32[128,256]{1,0:T(8,128)S(1)}, f32[128,256]{1,0:T(8,128)S(1)}, u32[]{:S(2)}, u32[]{:S(2)}) collective-permute-start(f32[128,256]{1,0:T(8,128)S(1)} %fusion.68), channel_id=1, source_target_pairs={{0,3},{1,2},{2,1},{3,0},{4,7},{5,6},{6,5},{7,4},{8,11},{9,10},{10,... | collective-permute-start | bytes 393224 | tf_op jit(solution)/shard_map/ppermute | solution.py:50
  91.0 8.6 %collective-permute-start.23 = (f32[128,256]{1,0:T(8,128)S(1)}, f32[128,256]{1,0:T(8,128)S(1)}, u32[]{:S(2)}, u32[]{:S(2)}) collective-permute-start(f32[128,256]{1,0:T(8,128)S(1)} %fusion.178), channel_id=1, source_target_pairs={{0,4},{1,5},{2,6},{3,7},{4,0},{5,1},{6,2},{7,3},{8,12},{9,13},{10,... | collective-permute-start | bytes 393224 | tf_op jit(solution)/shard_map/ppermute | solution.py:50
  95.0 13.3 %collective-permute-start.25 = (f32[128,256]{1,0:T(8,128)S(1)}, f32[128,256]{1,0:T(8,128)S(1)}, u32[]{:S(2)}, u32[]{:S(2)}) collective-permute-start(f32[128,256]{1,0:T(8,128)S(1)} %fusion.178), channel_id=1, source_target_pairs={{0,12},{1,13},{2,14},{3,15},{4,8},{5,9},{6,10},{7,11},{8,4},{9,5},... | collective-permute-start | bytes 393224 | tf_op jit(solution)/shard_map/ppermute | solution.py:50
  97.9 16.3 %collective-permute-start.10 = (f32[48,256]{1,0:T(8,128)S(1)}, f32[48,256]{1,0:T(8,128)S(1)}, u32[]{:S(2)}, u32[]{:S(2)}) collective-permute-start(f32[48,256]{1,0:T(8,128)S(1)} %dynamic-slice_bitcast_fusion.18), channel_id=1, source_target_pairs={{0,128},{32,160},{64,192},{96,224},{128,0},{160,32},{192,64},{224,... | collective-permute-start | bytes 147464 | tf_op jit(solution)/shard_map/ppermute | solution.py:78
  108.4 11.5 %collective-permute-start.26 = (f32[128,256]{1,0:T(8,128)S(1)}, f32[128,256]{1,0:T(8,128)S(1)}, u32[]{:S(2)}, u32[]{:S(2)}) collective-permute-start(f32[128,256]{1,0:T(8,128)S(1)} %fusion.177), channel_id=1, source_target_pairs={{0,16},{1,17},{2,18},{3,19},{4,20},{5,21},{6,22},{7,23},{8,24},{9,... | collective-permute-start | bytes 393224 | tf_op jit(solution)/shard_map/ppermute | solution.py:50
  108.5 11.5 %collective-permute-start.27 = (f32[128,256]{1,0:T(8,128)S(1)}, f32[128,256]{1,0:T(8,128)S(1)}, u32[]{:S(2)}, u32[]{:S(2)}) collective-permute-start(f32[128,256]{1,0:T(8,128)S(1)} %fusion.177), channel_id=1, source_target_pairs={{0,128},{1,129},{2,130},{3,131},{4,132},{5,133},{6,134},{7,135},{8... | collective-permute-start | bytes 393224 | tf_op jit(solution)/shard_map/ppermute | solution.py:50
  109.1 10.9 %collective-permute-start.28 = (f32[128,256]{1,0:T(8,128)S(1)}, f32[128,256]{1,0:T(8,128)S(1)}, u32[]{:S(2)}, u32[]{:S(2)}) collective-permute-start(f32[128,256]{1,0:T(8,128)S(1)} %fusion.177), channel_id=1, source_target_pairs={{0,144},{1,145},{2,146},{3,147},{4,148},{5,149},{6,150},{7,151},{8... | collective-permute-start | bytes 393224 | tf_op jit(solution)/shard_map/ppermute | solution.py:50
  114.2 9.7 %collective-permute-start.11 = (f32[48,256]{1,0:T(8,128)S(1)}, f32[48,256]{1,0:T(8,128)S(1)}, u32[]{:S(2)}, u32[]{:S(2)}) collective-permute-start(f32[48,256]{1,0:T(8,128)S(1)} %bitcast_add_fusion.2), channel_id=1, source_target_pairs={{0,0},{1,8},{2,16},{3,24},{4,32},{5,40},{6,48},{7,56},{8,64},{9,72... | collective-permute-start | bytes 147464 | tf_op jit(solution)/shard_map/ppermute | solution.py:159
  123.5 7.1 %collective-permute-start.31 = (f32[128,256]{1,0:T(8,128)S(1)}, f32[128,256]{1,0:T(8,128)S(1)}, u32[]{:S(2)}, u32[]{:S(2)}) collective-permute-start(f32[128,256]{1,0:T(8,128)S(1)} %fusion.176), channel_id=1, source_target_pairs={{0,96},{1,97},{2,98},{3,99},{4,100},{5,101},{6,102},{7,103},{8,104... | collective-permute-start | bytes 393224 | tf_op jit(solution)/shard_map/ppermute | solution.py:50
  (16 other events, 164.9 us)

commit v8 on v6

--- a/solution.py
+++ b/solution.py
@@ -81,8 +81,10 @@
 
 def gather_groups(ncol):
     bits = [1 << k for k in range(ncol.bit_length() - 1)]
-    order = [m for m in bits if m < 8][::-1] + [m for m in bits if m >= 8][::-1]
-    return [tuple(order[i : i + 2]) for i in range(0, len(order), 2)]
+    low = [m for m in bits if m < 8][::-1]
+    high = [m for m in bits if m >= 8]
+    groups = [tuple(high[i : i + 2]) for i in range(0, len(high), 2)]
+    return groups + [tuple(low[i : i + 2]) for i in range(0, len(low), 2)]
 
 
 def kept_chunk(idx, groups, nblocks):

time: 141 us -> 150 us (1.064)
  starting transfers between devices: 54.1 us -> 61.4 us
    ppermute x19, starting transfers between devices: 38.3 us -> 46.4 us  [exchange(): got.append(lax.ppermute(value, axis, xor_perm(size, offset(k, masks))))]
    ppermute x19, waiting for transfers between devices: 40.3 us -> 42.3 us  [exchange(): got.append(lax.ppermute(value, axis, xor_perm(size, offset(k, masks))))]
  transfers between devices with their start and end apart: 27 -> 27, of which waited for: 18 -> 18; matrix products, arithmetic and copies ran while one was open for 11% -> 10% of each run, Pallas kernels for 0% -> 0%
where the time goes in v8:
time: 150 us
  starting transfers between devices  61.4 us (41%)
  waiting for transfers between devices  55.5 us (37%)
  matrix products  17.9 us (12%)
  local copies, waits for them, and re-layouts  9.62 us (6%)
  other arithmetic  3.87 us (3%)
    ppermute x19, starting transfers between devices, exchange(): got.append(lax.ppermute(value, axis, xor_perm(size, offset(k, masks))))  46.4 us
    ppermute x19, waiting for transfers between devices, exchange(): got.append(lax.ppermute(value, axis, xor_perm(size, offset(k, masks))))  42.3 us
    dot_general x20, matrix products, mm(): jnp.dot(a, b, precision=lax.Precision.HIGHEST, preferred_element_type=jnp...  14.8 us
    ppermute x7, waiting for transfers between devices, scatter_step(): total = total + lax.ppermute(send, axis, xor_perm(size, offset(k, masks)))  10.1 us
    ppermute x7, starting transfers between devices, scatter_step(): total = total + lax.ppermute(send, axis, xor_perm(size, offset(k, masks)))  9.93 us
    ppermute x1, starting transfers between devices, inner(): product = lax.ppermute(share, ALL, owner_perm)  5.13 us
    ppermute x1, waiting for transfers between devices, inner(): product = lax.ppermute(share, ALL, owner_perm)  3.09 us
  transfers between devices with their start and end apart: 27, of which 18 were waited for; matrix products, arithmetic and copies ran while one was open for 10% of the time, Pallas kernels for 0%

profile of v8, /device:TPU:1, one launch (start us, length us, event | category | flops | bytes accessed | tf_op | source)
XLA Modules:
  0.0 149.6 jit_solution(17752491309946694420)
XLA Ops:
  0.7 2.1 %collective-permute-start = (f32[48,256]{1,0:T(8,128)}, f32[48,256]{1,0:T(8,128)S(1)}, u32[]{:S(2)}, u32[]{:S(2)}) collective-permute-start(f32[48,256]{1,0:T(8,128)} %param.6), channel_id=1, source_target_pairs={{0,8},{1,9},{2,10},{3,11},{4,12},{5,13},{6,14},{7,15},{8,0},{9,1},... | collective-permute-start | bytes 147464 | tf_op jit(solution)/shard_map/ppermute | solution.py:50
  2.8 2.5 %collective-permute-start.1 = (f32[48,256]{1,0:T(8,128)}, f32[48,256]{1,0:T(8,128)S(1)}, u32[]{:S(2)}, u32[]{:S(2)}) collective-permute-start(f32[48,256]{1,0:T(8,128)} %param.6), channel_id=1, source_target_pairs={{0,16},{1,17},{2,18},{3,19},{4,20},{5,21},{6,22},{7,23},{8,24},{9,... | collective-permute-start | bytes 147464 | tf_op jit(solution)/shard_map/ppermute | solution.py:50
  5.3 2.6 %gather_fusion = f32[256]{0:T(256)S(1)} fusion(f32[256,256]{1,0:T(8,128)} %param.8, s32[256]{0:T(256)S(1)} %bitcast.133), kind=kCustom, calls=%fused_computation | custom fusion | bytes 4096 | tf_op jit(solution)/shard_map/jit(diagonal)/cond/branch_0_fun/gather | solution.py:16
  13.1 3.2 %collective-permute-start.4 = (f32[192,256]{1,0:T(8,128)S(1)}, f32[192,256]{1,0:T(8,128)S(1)}, u32[]{:S(2)}, u32[]{:S(2)}) collective-permute-start(f32[192,256]{1,0:T(8,128)S(1)} %get-tuple-element.21), channel_id=1, source_target_pairs={{0,2},{1,3},{2,0},{3,1},{4,6},{5,7},{6,4},{7,5},{8,10},{9,11},{10,... | collective-permute-start | bytes 589832 | tf_op jit(solution)/shard_map/ppermute | solution.py:50
  16.4 4.2 %collective-permute-start.5 = (f32[192,256]{1,0:T(8,128)S(1)}, f32[192,256]{1,0:T(8,128)S(1)}, u32[]{:S(2)}, u32[]{:S(2)}) collective-permute-start(f32[192,256]{1,0:T(8,128)S(1)} %get-tuple-element.21), channel_id=1, source_target_pairs={{0,6},{1,7},{2,4},{3,5},{4,2},{5,3},{6,0},{7,1},{8,14},{9,15},{10,... | collective-permute-start | bytes 589832 | tf_op jit(solution)/shard_map/ppermute | solution.py:50
  26.6 5.3 %collective-permute-done.3 = f32[192,256]{1,0:T(8,128)S(1)} collective-permute-done((f32[192,256]{1,0:T(8,128)S(1)}, f32[192,256]{1,0:T(8,128)S(1)}, u32[]{:S(2)}, u32[]{:S(2)}) %collective-permute-start.3) | collective-permute-done | bytes 196640 | tf_op jit(solution)/shard_map/ppermute | solution.py:50
  33.0 7.6 %collective-permute-start.6 = (f32[768,256]{1,0:T(8,128)}, f32[768,256]{1,0:T(8,128)}, u32[]{:S(2)}, u32[]{:S(2)}) collective-permute-start(f32[768,256]{1,0:T(8,128)} %get-tuple-element.4), channel_id=1, source_target_pairs={{0,1},{1,0},{2,3},{3,2},{4,5},{5,4},{6,7},{7,6},{8,9},{9,8},{10,11... | collective-permute-start | bytes 2359304 | tf_op jit(solution)/shard_map/ppermute | solution.py:50
  44.7 12.9 %collective-permute-done.6 = f32[768,256]{1,0:T(8,128)} collective-permute-done((f32[768,256]{1,0:T(8,128)}, f32[768,256]{1,0:T(8,128)}, u32[]{:S(2)}, u32[]{:S(2)}) %collective-permute-start.6) | collective-permute-done | bytes 786464 | tf_op jit(solution)/shard_map/ppermute | solution.py:50
  59.3 2.7 %convolution_bitcast_fusion = f32[384,256]{0,1:T(8,128)S(1)} fusion(f32[1536,256]{1,0:T(8,128)S(1)} %bitcast.137, f32[1536,384]{1,0:T(8,128)S(1)} %copy-done), kind=kOutput, calls=%fused_computation.7 | convolution fusion | flops 1811939328 | bytes 4325376 | tf_op jit(solution)/shard_map/dot_general | solution.py:135
  68.5 2.6 %collective-permute-done.8 = f32[96,256]{1,0:T(8,128)} collective-permute-done((f32[96,256]{1,0:T(8,128)}, f32[96,256]{1,0:T(8,128)}, u32[]{:S(2)}, u32[]{:S(2)}) %collective-permute-start.8) | collective-permute-done | bytes 98336 | tf_op jit(solution)/shard_map/ppermute | solution.py:78
  71.1 2.3 %collective-permute-done.9 = f32[96,256]{1,0:T(8,128)} collective-permute-done((f32[96,256]{1,0:T(8,128)}, f32[96,256]{1,0:T(8,128)}, u32[]{:S(2)}, u32[]{:S(2)}) %collective-permute-start.9) | collective-permute-done | bytes 98336 | tf_op jit(solution)/shard_map/ppermute | solution.py:78
  74.4 3.0 %collective-permute-start.10 = (f32[48,256]{1,0:T(8,128)S(1)}, f32[48,256]{1,0:T(8,128)S(1)}, u32[]{:S(2)}, u32[]{:S(2)}) collective-permute-start(f32[48,256]{1,0:T(8,128)S(1)} %dynamic-slice_bitcast_fusion.14), channel_id=1, source_target_pairs={{0,128},{32,160},{64,192},{96,224},{128,0},{160,32},{192,64},{224,... | collective-permute-start | bytes 147464 | tf_op jit(solution)/shard_map/ppermute | solution.py:78
  79.0 5.1 %collective-permute-start.11 = (f32[48,256]{1,0:T(8,128)S(1)}, f32[48,256]{1,0:T(8,128)}, u32[]{:S(2)}, u32[]{:S(2)}) collective-permute-start(f32[48,256]{1,0:T(8,128)S(1)} %bitcast_add_fusion.2), channel_id=1, source_target_pairs={{0,0},{1,8},{2,16},{3,24},{4,32},{5,40},{6,48},{7,56},{8,64},{9,72... | collective-permute-start | bytes 147464 | tf_op jit(solution)/shard_map/ppermute | solution.py:145
  85.5 3.1 %collective-permute-done.11 = f32[48,256]{1,0:T(8,128)} collective-permute-done((f32[48,256]{1,0:T(8,128)S(1)}, f32[48,256]{1,0:T(8,128)}, u32[]{:S(2)}, u32[]{:S(2)}) %collective-permute-start.11) | collective-permute-done | bytes 49184 | tf_op jit(solution)/shard_map/ppermute | solution.py:145
  90.8 3.1 %collective-permute-start.13 = (f32[64,256]{1,0:T(8,128)}, f32[64,256]{1,0:T(8,128)S(1)}, u32[]{:S(2)}, u32[]{:S(2)}) collective-permute-start(f32[64,256]{1,0:T(8,128)} %get-tuple-element.19), channel_id=1, source_target_pairs={{0,64},{1,65},{2,66},{3,67},{4,68},{5,69},{6,70},{7,71},{8,72},{9,... | collective-permute-start | bytes 196616 | tf_op jit(solution)/shard_map/ppermute | solution.py:78
  96.0 2.4 %collective-permute-done.14 = f32[64,256]{1,0:T(8,128)S(1)} collective-permute-done((f32[64,256]{1,0:T(8,128)S(1)}, f32[64,256]{1,0:T(8,128)S(1)}, u32[]{:S(2)}, u32[]{:S(2)}) %collective-permute-start.14) | collective-permute-done | bytes 65568 | tf_op jit(solution)/shard_map/ppermute | solution.py:78
  102.1 4.1 %collective-permute-done.16 = f32[64,256]{1,0:T(8,128)S(1)} collective-permute-done((f32[64,256]{1,0:T(8,128)S(1)}, f32[64,256]{1,0:T(8,128)S(1)}, u32[]{:S(2)}, u32[]{:S(2)}) %collective-permute-start.16) | collective-permute-done | bytes 65568 | tf_op jit(solution)/shard_map/ppermute | solution.py:50
  106.3 7.3 %collective-permute-start.18 = (f32[64,256]{1,0:T(8,128)S(1)}, f32[64,256]{1,0:T(8,128)S(1)}, u32[]{:S(2)}, u32[]{:S(2)}) collective-permute-start(f32[64,256]{1,0:T(8,128)S(1)} %fusion.167), channel_id=1, source_target_pairs={{0,4},{1,5},{2,6},{3,7},{4,0},{5,1},{6,2},{7,3},{8,12},{9,13},{10,... | collective-permute-start | bytes 196616 | tf_op jit(solution)/shard_map/ppermute | solution.py:50
  116.7 5.3 %collective-permute-done.20 = f32[64,256]{1,0:T(8,128)S(1)} collective-permute-done((f32[64,256]{1,0:T(8,128)S(1)}, f32[64,256]{1,0:T(8,128)S(1)}, u32[]{:S(2)}, u32[]{:S(2)}) %collective-permute-start.20) | collective-permute-done | bytes 65568 | tf_op jit(solution)/shard_map/ppermute | solution.py:50
  122.1 3.9 %collective-permute-start.21 = (f32[64,256]{1,0:T(8,128)S(1)}, f32[64,256]{1,0:T(8,128)S(1)}, u32[]{:S(2)}, u32[]{:S(2)}) collective-permute-start(f32[64,256]{1,0:T(8,128)S(1)} %fusion.166), channel_id=1, source_target_pairs={{0,16},{1,17},{2,18},{3,19},{4,20},{5,21},{6,22},{7,23},{8,24},{9,... | collective-permute-start | bytes 196616 | tf_op jit(solution)/shard_map/ppermute | solution.py:50
  128.8 2.1 %collective-permute-done.22 = f32[64,256]{1,0:T(8,128)S(1)} collective-permute-done((f32[64,256]{1,0:T(8,128)S(1)}, f32[64,256]{1,0:T(8,128)S(1)}, u32[]{:S(2)}, u32[]{:S(2)}) %collective-permute-start.22) | collective-permute-done | bytes 65568 | tf_op jit(solution)/shard_map/ppermute | solution.py:50
  130.9 3.3 %collective-permute-done.23 = f32[64,256]{1,0:T(8,128)S(1)} collective-permute-done((f32[64,256]{1,0:T(8,128)S(1)}, f32[64,256]{1,0:T(8,128)S(1)}, u32[]{:S(2)}, u32[]{:S(2)}) %collective-permute-start.23) | collective-permute-done | bytes 65568 | tf_op jit(solution)/shard_map/ppermute | solution.py:50
  134.2 5.2 %collective-permute-start.24 = (f32[64,256]{1,0:T(8,128)S(1)}, f32[64,256]{1,0:T(8,128)S(1)}, u32[]{:S(2)}, u32[]{:S(2)}) collective-permute-start(f32[64,256]{1,0:T(8,128)S(1)} %fusion.165), channel_id=1, source_target_pairs={{0,32},{1,33},{2,34},{3,35},{4,36},{5,37},{6,38},{7,39},{8,40},{9,... | collective-permute-start | bytes 196616 | tf_op jit(solution)/shard_map/ppermute | solution.py:50
  145.4 2.3 %gather_fusion.1 = f32[256]{0:T(256)S(1)} fusion(f32[256,256]{1,0:T(8,128)S(1)} %bitcast.135, s32[256]{0:T(256)S(1)} %bitcast.134), kind=kCustom, calls=%fused_computation.1 | custom fusion | bytes 4096 | tf_op jit(solution)/shard_map/jit(_diag)/jit(diagonal)/cond/branch_0_fun/gather | solution.py:29
  (109 shorter events, 50.1 us)
Async XLA Ops:
  0.7 12.3 %collective-permute-start = (f32[48,256]{1,0:T(8,128)}, f32[48,256]{1,0:T(8,128)S(1)}, u32[]{:S(2)}, u32[]{:S(2)}) collective-permute-start(f32[48,256]{1,0:T(8,128)} %param.6), channel_id=1, source_target_pairs={{0,8},{1,9},{2,10},{3,11},{4,12},{5,13},{6,14},{7,15},{8,0},{9,1},... | collective-permute-start | bytes 147464 | tf_op jit(solution)/shard_map/ppermute | solution.py:50
  2.8 10.2 %collective-permute-start.1 = (f32[48,256]{1,0:T(8,128)}, f32[48,256]{1,0:T(8,128)S(1)}, u32[]{:S(2)}, u32[]{:S(2)}) collective-permute-start(f32[48,256]{1,0:T(8,128)} %param.6), channel_id=1, source_target_pairs={{0,16},{1,17},{2,18},{3,19},{4,20},{5,21},{6,22},{7,23},{8,24},{9,... | collective-permute-start | bytes 147464 | tf_op jit(solution)/shard_map/ppermute | solution.py:50
  5.2 7.8 %collective-permute-start.2 = (f32[48,256]{1,0:T(8,128)}, f32[48,256]{1,0:T(8,128)S(1)}, u32[]{:S(2)}, u32[]{:S(2)}) collective-permute-start(f32[48,256]{1,0:T(8,128)} %param.6), channel_id=1, source_target_pairs={{0,24},{1,25},{2,26},{3,27},{4,28},{5,29},{6,30},{7,31},{8,16},{9,... | collective-permute-start | bytes 147464 | tf_op jit(solution)/shard_map/ppermute | solution.py:50
  13.1 11.5 %collective-permute-start.4 = (f32[192,256]{1,0:T(8,128)S(1)}, f32[192,256]{1,0:T(8,128)S(1)}, u32[]{:S(2)}, u32[]{:S(2)}) collective-permute-start(f32[192,256]{1,0:T(8,128)S(1)} %get-tuple-element.21), channel_id=1, source_target_pairs={{0,2},{1,3},{2,0},{3,1},{4,6},{5,7},{6,4},{7,5},{8,10},{9,11},{10,... | collective-permute-start | bytes 589832 | tf_op jit(solution)/shard_map/ppermute | solution.py:50
  16.4 10.2 %collective-permute-start.5 = (f32[192,256]{1,0:T(8,128)S(1)}, f32[192,256]{1,0:T(8,128)S(1)}, u32[]{:S(2)}, u32[]{:S(2)}) collective-permute-start(f32[192,256]{1,0:T(8,128)S(1)} %get-tuple-element.21), channel_id=1, source_target_pairs={{0,6},{1,7},{2,4},{3,5},{4,2},{5,3},{6,0},{7,1},{8,14},{9,15},{10,... | collective-permute-start | bytes 589832 | tf_op jit(solution)/shard_map/ppermute | solution.py:50
  20.6 11.3 %collective-permute-start.3 = (f32[192,256]{1,0:T(8,128)S(1)}, f32[192,256]{1,0:T(8,128)S(1)}, u32[]{:S(2)}, u32[]{:S(2)}) collective-permute-start(f32[192,256]{1,0:T(8,128)S(1)} %get-tuple-element.21), channel_id=1, source_target_pairs={{0,4},{1,5},{2,6},{3,7},{4,0},{5,1},{6,2},{7,3},{8,12},{9,13},{10,... | collective-permute-start | bytes 589832 | tf_op jit(solution)/shard_map/ppermute | solution.py:50
  33.0 24.6 %collective-permute-start.6 = (f32[768,256]{1,0:T(8,128)}, f32[768,256]{1,0:T(8,128)}, u32[]{:S(2)}, u32[]{:S(2)}) collective-permute-start(f32[768,256]{1,0:T(8,128)} %get-tuple-element.4), channel_id=1, source_target_pairs={{0,1},{1,0},{2,3},{3,2},{4,5},{5,4},{6,7},{7,6},{8,9},{9,8},{10,11... | collective-permute-start | bytes 2359304 | tf_op jit(solution)/shard_map/ppermute | solution.py:50
  64.7 3.8 %collective-permute-start.7 = (f32[96,256]{1,0:T(8,128)}, f32[96,256]{1,0:T(8,128)S(1)}, u32[]{:S(2)}, u32[]{:S(2)}) collective-permute-start(f32[96,256]{1,0:T(8,128)} %get-tuple-element.10), channel_id=1, source_target_pairs={{0,32},{32,0},{64,96},{96,64},{128,160},{160,128},{192,224},{224,1... | collective-permute-start | bytes 294920 | tf_op jit(solution)/shard_map/ppermute | solution.py:78
  66.5 4.7 %collective-permute-start.8 = (f32[96,256]{1,0:T(8,128)}, f32[96,256]{1,0:T(8,128)}, u32[]{:S(2)}, u32[]{:S(2)}) collective-permute-start(f32[96,256]{1,0:T(8,128)} %get-tuple-element.12), channel_id=1, source_target_pairs={{0,64},{32,96},{64,0},{96,32},{128,192},{160,224},{192,128},{224,1... | collective-permute-start | bytes 294920 | tf_op jit(solution)/shard_map/ppermute | solution.py:78
  67.8 5.6 %collective-permute-start.9 = (f32[96,256]{1,0:T(8,128)}, f32[96,256]{1,0:T(8,128)}, u32[]{:S(2)}, u32[]{:S(2)}) collective-permute-start(f32[96,256]{1,0:T(8,128)} %get-tuple-element.11), channel_id=1, source_target_pairs={{0,96},{32,64},{64,32},{96,0},{128,224},{160,192},{192,160},{224,1... | collective-permute-start | bytes 294920 | tf_op jit(solution)/shard_map/ppermute | solution.py:78
  74.4 4.5 %collective-permute-start.10 = (f32[48,256]{1,0:T(8,128)S(1)}, f32[48,256]{1,0:T(8,128)S(1)}, u32[]{:S(2)}, u32[]{:S(2)}) collective-permute-start(f32[48,256]{1,0:T(8,128)S(1)} %dynamic-slice_bitcast_fusion.14), channel_id=1, source_target_pairs={{0,128},{32,160},{64,192},{96,224},{128,0},{160,32},{192,64},{224,... | collective-permute-start | bytes 147464 | tf_op jit(solution)/shard_map/ppermute | solution.py:78
  79.0 9.6 %collective-permute-start.11 = (f32[48,256]{1,0:T(8,128)S(1)}, f32[48,256]{1,0:T(8,128)}, u32[]{:S(2)}, u32[]{:S(2)}) collective-permute-start(f32[48,256]{1,0:T(8,128)S(1)} %bitcast_add_fusion.2), channel_id=1, source_target_pairs={{0,0},{1,8},{2,16},{3,24},{4,32},{5,40},{6,48},{7,56},{8,64},{9,72... | collective-permute-start | bytes 147464 | tf_op jit(solution)/shard_map/ppermute | solution.py:145
  90.8 5.2 %collective-permute-start.13 = (f32[64,256]{1,0:T(8,128)}, f32[64,256]{1,0:T(8,128)S(1)}, u32[]{:S(2)}, u32[]{:S(2)}) collective-permute-start(f32[64,256]{1,0:T(8,128)} %get-tuple-element.19), channel_id=1, source_target_pairs={{0,64},{1,65},{2,66},{3,67},{4,68},{5,69},{6,70},{7,71},{8,72},{9,... | collective-permute-start | bytes 196616 | tf_op jit(solution)/shard_map/ppermute | solution.py:78
  93.9 4.6 %collective-permute-start.14 = (f32[64,256]{1,0:T(8,128)S(1)}, f32[64,256]{1,0:T(8,128)S(1)}, u32[]{:S(2)}, u32[]{:S(2)}) collective-permute-start(f32[64,256]{1,0:T(8,128)S(1)} %get-tuple-element.18), channel_id=1, source_target_pairs={{0,96},{1,97},{2,98},{3,99},{4,100},{5,101},{6,102},{7,103},{8,104... | collective-permute-start | bytes 196616 | tf_op jit(solution)/shard_map/ppermute | solution.py:78
  98.5 3.6 %collective-permute-start.15 = (f32[64,256]{1,0:T(8,128)S(1)}, f32[64,256]{1,0:T(8,128)S(1)}, u32[]{:S(2)}, u32[]{:S(2)}) collective-permute-start(f32[64,256]{1,0:T(8,128)S(1)} %fusion.112), channel_id=1, source_target_pairs={{0,1},{1,0},{2,3},{3,2},{4,5},{5,4},{6,7},{7,6},{8,9},{9,8},{10,11... | collective-permute-start | bytes 196616 | tf_op jit(solution)/shard_map/ppermute | solution.py:50
  99.6 6.6 %collective-permute-start.16 = (f32[64,256]{1,0:T(8,128)S(1)}, f32[64,256]{1,0:T(8,128)S(1)}, u32[]{:S(2)}, u32[]{:S(2)}) collective-permute-start(f32[64,256]{1,0:T(8,128)S(1)} %fusion.112), channel_id=1, source_target_pairs={{0,2},{1,3},{2,0},{3,1},{4,6},{5,7},{6,4},{7,5},{8,10},{9,11},{10,... | collective-permute-start | bytes 196616 | tf_op jit(solution)/shard_map/ppermute | solution.py:50
  100.5 5.7 %collective-permute-start.17 = (f32[64,256]{1,0:T(8,128)S(1)}, f32[64,256]{1,0:T(8,128)S(1)}, u32[]{:S(2)}, u32[]{:S(2)}) collective-permute-start(f32[64,256]{1,0:T(8,128)S(1)} %fusion.112), channel_id=1, source_target_pairs={{0,3},{1,2},{2,1},{3,0},{4,7},{5,6},{6,5},{7,4},{8,11},{9,10},{10,... | collective-permute-start | bytes 196616 | tf_op jit(solution)/shard_map/ppermute | solution.py:50
  106.3 9.0 %collective-permute-start.18 = (f32[64,256]{1,0:T(8,128)S(1)}, f32[64,256]{1,0:T(8,128)S(1)}, u32[]{:S(2)}, u32[]{:S(2)}) collective-permute-start(f32[64,256]{1,0:T(8,128)S(1)} %fusion.167), channel_id=1, source_target_pairs={{0,4},{1,5},{2,6},{3,7},{4,0},{5,1},{6,2},{7,3},{8,12},{9,13},{10,... | collective-permute-start | bytes 196616 | tf_op jit(solution)/shard_map/ppermute | solution.py:50
  113.5 8.4 %collective-permute-start.20 = (f32[64,256]{1,0:T(8,128)S(1)}, f32[64,256]{1,0:T(8,128)S(1)}, u32[]{:S(2)}, u32[]{:S(2)}) collective-permute-start(f32[64,256]{1,0:T(8,128)S(1)} %fusion.167), channel_id=1, source_target_pairs={{0,12},{1,13},{2,14},{3,15},{4,8},{5,9},{6,10},{7,11},{8,4},{9,5},... | collective-permute-start | bytes 196616 | tf_op jit(solution)/shard_map/ppermute | solution.py:50
  122.1 6.7 %collective-permute-start.21 = (f32[64,256]{1,0:T(8,128)S(1)}, f32[64,256]{1,0:T(8,128)S(1)}, u32[]{:S(2)}, u32[]{:S(2)}) collective-permute-start(f32[64,256]{1,0:T(8,128)S(1)} %fusion.166), channel_id=1, source_target_pairs={{0,16},{1,17},{2,18},{3,19},{4,20},{5,21},{6,22},{7,23},{8,24},{9,... | collective-permute-start | bytes 196616 | tf_op jit(solution)/shard_map/ppermute | solution.py:50
  126.0 4.9 %collective-permute-start.22 = (f32[64,256]{1,0:T(8,128)S(1)}, f32[64,256]{1,0:T(8,128)S(1)}, u32[]{:S(2)}, u32[]{:S(2)}) collective-permute-start(f32[64,256]{1,0:T(8,128)S(1)} %fusion.166), channel_id=1, source_target_pairs={{0,128},{1,129},{2,130},{3,131},{4,132},{5,133},{6,134},{7,135},{8... | collective-permute-start | bytes 196616 | tf_op jit(solution)/shard_map/ppermute | solution.py:50
  127.1 7.1 %collective-permute-start.23 = (f32[64,256]{1,0:T(8,128)S(1)}, f32[64,256]{1,0:T(8,128)S(1)}, u32[]{:S(2)}, u32[]{:S(2)}) collective-permute-start(f32[64,256]{1,0:T(8,128)S(1)} %fusion.166), channel_id=1, source_target_pairs={{0,144},{1,145},{2,146},{3,147},{4,148},{5,149},{6,150},{7,151},{8... | collective-permute-start | bytes 196616 | tf_op jit(solution)/shard_map/ppermute | solution.py:50
  134.2 6.9 %collective-permute-start.24 = (f32[64,256]{1,0:T(8,128)S(1)}, f32[64,256]{1,0:T(8,128)S(1)}, u32[]{:S(2)}, u32[]{:S(2)}) collective-permute-start(f32[64,256]{1,0:T(8,128)S(1)} %fusion.165), channel_id=1, source_target_pairs={{0,32},{1,33},{2,34},{3,35},{4,36},{5,37},{6,38},{7,39},{8,40},{9,... | collective-permute-start | bytes 196616 | tf_op jit(solution)/shard_map/ppermute | solution.py:50
  140.0 4.6 %collective-permute-start.26 = (f32[64,256]{1,0:T(8,128)S(1)}, f32[64,256]{1,0:T(8,128)S(1)}, u32[]{:S(2)}, u32[]{:S(2)}) collective-permute-start(f32[64,256]{1,0:T(8,128)S(1)} %fusion.165), channel_id=1, source_target_pairs={{0,96},{1,97},{2,98},{3,99},{4,100},{5,101},{6,102},{7,103},{8,104... | collective-permute-start | bytes 196616 | tf_op jit(solution)/shard_map/ppermute | solution.py:50
  (12 other events, 181.8 us)

commit v9 on v8

--- a/solution.py
+++ b/solution.py
@@ -83,8 +83,8 @@
     bits = [1 << k for k in range(ncol.bit_length() - 1)]
     low = [m for m in bits if m < 8][::-1]
     high = [m for m in bits if m >= 8]
-    groups = [tuple(high[i : i + 2]) for i in range(0, len(high), 2)]
-    return groups + [tuple(low[i : i + 2]) for i in range(0, len(low), 2)]
+    groups = [tuple(low[i : i + 2]) for i in range(0, len(low), 2)]
+    return groups + [tuple(high[i : i + 2]) for i in range(0, len(high), 2)]
 
 
 def kept_chunk(idx, groups, nblocks):
@@ -116,10 +116,13 @@
         (r * ncol + c, c * nrow + kept_chunk(r, row_groups, nrow)) for r in range(nrow) for c in range(ncol)
     ]
 
+    fetch_perm = [(dst, src) for src, dst in owner_perm]
+
     def inner(trailing_adjoint, panel, panel_adjoint, diag_factor, diag_adjoint):
         r = lax.axis_index("row")
         c = lax.axis_index("col")
         inverse = lower_inverse(diag_factor)
+        own_rows = lax.ppermute(jnp.stack([panel, panel_adjoint]), ALL, fetch_perm)
 
         groups = gather_groups(ncol)
         gathered = panel
@@ -142,13 +145,10 @@
 
         for masks in row_groups:
             share = scatter_step(share, "row", nrow, masks)
-        product = lax.ppermute(share, ALL, owner_perm)
-
-        updated = panel_adjoint - 2.0 * product
-        off_adjoint = mm(updated, inverse)
-        local_term = jnp.dot(
-            off_adjoint.T, panel, precision=lax.Precision.HIGHEST, preferred_element_type=jnp.float32
-        )
+        updated = own_rows[1] - 2.0 * share
+        off_rows = mm(updated, inverse)
+        local_term = mm(off_rows.T, own_rows[0])
+        off_adjoint = lax.ppermute(off_rows, ALL, owner_perm)
         rows, cols = diag_adjoint.shape
         placed = lax.dynamic_update_slice(
             jnp.zeros((rows * nrow, cols * ncol), jnp.float32), diag_adjoint, (r * rows, c * cols)

time: 150 us -> 142 us (0.947)
  waiting for transfers between devices: 55.5 us -> 50.6 us
  matrix products: 17.9 us -> 15.3 us
  starting transfers between devices: 61.4 us -> 59.3 us
    ppermute x19, waiting for transfers between devices: 42.3 us -> 33.1 us  [exchange(): got.append(lax.ppermute(value, axis, xor_perm(size, offset(k, masks))))]
    ppermute x1 -> x2, starting transfers between devices: 5.13 us -> 10.5 us  [the longest x1 7.73 us: inner(): own_rows = lax.ppermute(jnp.stack([panel, panel_adjoint]), ALL, fetch_perm)]
    ppermute x19, starting transfers between devices: 46.4 us -> 42.3 us  [exchange(): got.append(lax.ppermute(value, axis, xor_perm(size, offset(k, masks))))]
    ppermute x1 -> x2, waiting for transfers between devices: 3.09 us -> 6.69 us  [the longest x1 6.68 us: inner(): off_adjoint = lax.ppermute(off_rows, ALL, owner_perm)]
    ppermute x7, starting transfers between devices: 9.93 us -> 6.5 us  [scatter_step(): total = total + lax.ppermute(send, axis, xor_perm(size, offset(k, masks)))]
    dot_general x20 -> x21, matrix products: 14.8 us -> 12.6 us  [mm(): jnp.dot(a, b, precision=lax.Precision.HIGHEST, preferred_element_type=jnp...]
    another operation x0 -> x1, other arithmetic: none -> 1.51 us  [inner(): own_rows = lax.ppermute(jnp.stack([panel, panel_adjoint]), ALL, fetch_perm)]
  transfers between devices with their start and end apart: 27 -> 28, of which waited for: 18 -> 16; matrix products, arithmetic and copies ran while one was open for 10% -> 15% of each run, Pallas kernels for 0% -> 0%
where the time goes in v9:
time: 142 us; the launch traced here: 140 us
  starting transfers between devices  59.3 us (42%)
  waiting for transfers between devices  50.6 us (36%)
  matrix products  15.3 us (11%)
  local copies, waits for them, and re-layouts  10.9 us (8%)
  other arithmetic  3.12 us (2%)
    ppermute x19, starting transfers between devices, exchange(): got.append(lax.ppermute(value, axis, xor_perm(size, offset(k, masks))))  42.3 us
    ppermute x19, waiting for transfers between devices, exchange(): got.append(lax.ppermute(value, axis, xor_perm(size, offset(k, masks))))  33.1 us
    dot_general x21, matrix products, mm(): jnp.dot(a, b, precision=lax.Precision.HIGHEST, preferred_element_type=jnp...  12.6 us
    ppermute x7, waiting for transfers between devices, scatter_step(): total = total + lax.ppermute(send, axis, xor_perm(size, offset(k, masks)))  10.8 us
    ppermute x1, starting transfers between devices, inner(): own_rows = lax.ppermute(jnp.stack([panel, panel_adjoint]), ALL, fetch_perm)  7.73 us
    ppermute x1, waiting for transfers between devices, inner(): off_adjoint = lax.ppermute(off_rows, ALL, owner_perm)  6.68 us
    ppermute x7, starting transfers between devices, scatter_step(): total = total + lax.ppermute(send, axis, xor_perm(size, offset(k, masks)))  6.5 us
    squeeze x3, local copies, waits for them, and re-layouts, scatter_step(): send = lax.dynamic_index_in_dim(chunks, p ^ k, keepdims=False)  2.99 us
  transfers between devices with their start and end apart: 28, of which 16 were waited for; matrix products, arithmetic and copies ran while one was open for 15% of the time, Pallas kernels for 0%

profile of v9, /device:TPU:1, one launch (start us, length us, event | category | flops | bytes accessed | tf_op | source)
XLA Modules:
  0.0 140.5 jit_solution(12410444866677429672)
XLA Ops:
  0.7 7.8 %collective-permute-start.1 = (f32[48,256]{1,0:T(8,128)}, f32[48,256]{1,0:T(8,128)S(1)}, u32[]{:S(2)}, u32[]{:S(2)}) collective-permute-start(f32[48,256]{1,0:T(8,128)} %param.6), channel_id=1, source_target_pairs={{0,4},{1,5},{2,6},{3,7},{4,0},{5,1},{6,2},{7,3},{8,12},{9,13},{10,... | collective-permute-start | bytes 147464 | tf_op jit(solution)/shard_map/ppermute | solution.py:50
  11.2 7.7 %collective-permute-start = (f32[2,48,256]{2,1,0:T(8,128)}, f32[2,48,256]{2,1,0:T(8,128)}, u32[]{:S(2)}, u32[]{:S(2)}) collective-permute-start(f32[2,48,256]{2,1,0:T(8,128)} %pad_maximum_fusion.9), channel_id=1, source_target_pairs={{0,0},{8,1},{16,2},{24,3},{32,4},{40,5},{48,6},{56,7},{64,8},{72,9... | collective-permute-start | bytes 294920 | tf_op jit(solution)/shard_map/ppermute | solution.py:125
  19.0 2.6 %gather_fusion = f32[256]{0:T(256)S(1)} fusion(f32[256,256]{1,0:T(8,128)} %param.8, s32[256]{0:T(256)S(1)} %bitcast.146), kind=kCustom, calls=%fused_computation | custom fusion | bytes 4096 | tf_op jit(solution)/shard_map/jit(diagonal)/cond/branch_0_fun/gather | solution.py:16
  27.7 3.0 %collective-permute-start.4 = (f32[192,256]{1,0:T(8,128)S(1)}, f32[192,256]{1,0:T(8,128)S(1)}, u32[]{:S(2)}, u32[]{:S(2)}) collective-permute-start(f32[192,256]{1,0:T(8,128)S(1)} %get-tuple-element.20), channel_id=1, source_target_pairs={{0,1},{1,0},{2,3},{3,2},{4,5},{5,4},{6,7},{7,6},{8,9},{9,8},{10,11... | collective-permute-start | bytes 589832 | tf_op jit(solution)/shard_map/ppermute | solution.py:50
  31.1 2.7 %collective-permute-done.4 = f32[192,256]{1,0:T(8,128)S(1)} collective-permute-done((f32[192,256]{1,0:T(8,128)S(1)}, f32[192,256]{1,0:T(8,128)S(1)}, u32[]{:S(2)}, u32[]{:S(2)}) %collective-permute-start.4) | collective-permute-done | bytes 196640 | tf_op jit(solution)/shard_map/ppermute | solution.py:50
  33.9 2.0 %collective-permute-start.5 = (f32[384,256]{1,0:T(8,128)S(1)}, f32[384,256]{1,0:T(8,128)S(1)}, u32[]{:S(2)}, u32[]{:S(2)}) collective-permute-start(f32[384,256]{1,0:T(8,128)S(1)} %get-tuple-element.10), channel_id=1, source_target_pairs={{0,8},{1,9},{2,10},{3,11},{4,12},{5,13},{6,14},{7,15},{8,0},{9,1},... | collective-permute-start | bytes 1179656 | tf_op jit(solution)/shard_map/ppermute | solution.py:50
  39.3 6.3 %collective-permute-done.5 = f32[384,256]{1,0:T(8,128)S(1)} collective-permute-done((f32[384,256]{1,0:T(8,128)S(1)}, f32[384,256]{1,0:T(8,128)S(1)}, u32[]{:S(2)}, u32[]{:S(2)}) %collective-permute-start.5) | collective-permute-done | bytes 393248 | tf_op jit(solution)/shard_map/ppermute | solution.py:50
  45.6 9.6 %collective-permute-done.6 = f32[384,256]{1,0:T(8,128)S(1)} collective-permute-done((f32[384,256]{1,0:T(8,128)S(1)}, f32[384,256]{1,0:T(8,128)S(1)}, u32[]{:S(2)}, u32[]{:S(2)}) %collective-permute-start.6) | collective-permute-done | bytes 393248 | tf_op jit(solution)/shard_map/ppermute | solution.py:50
  55.2 3.1 %collective-permute-done.7 = f32[384,256]{1,0:T(8,128)S(1)} collective-permute-done((f32[384,256]{1,0:T(8,128)S(1)}, f32[384,256]{1,0:T(8,128)S(1)}, u32[]{:S(2)}, u32[]{:S(2)}) %collective-permute-start.7) | collective-permute-done | bytes 393248 | tf_op jit(solution)/shard_map/ppermute | solution.py:50
  58.8 2.7 %convolution_bitcast_fusion = f32[384,256]{0,1:T(8,128)S(1)} fusion(f32[1536,256]{1,0:T(8,128)S(1)} %bitcast.150, f32[1536,384]{1,0:T(8,128)S(1)} %copy-done), kind=kOutput, calls=%fused_computation.4 | convolution fusion | flops 1811939328 | bytes 4325376 | tf_op jit(solution)/shard_map/dot_general | solution.py:138
  66.5 2.9 %collective-permute-done.10 = f32[96,256]{1,0:T(8,128)S(1)} collective-permute-done((f32[96,256]{1,0:T(8,128)}, f32[96,256]{1,0:T(8,128)S(1)}, u32[]{:S(2)}, u32[]{:S(2)}) %collective-permute-start.10) | collective-permute-done | bytes 98336 | tf_op jit(solution)/shard_map/ppermute | solution.py:78
  69.5 2.2 %collective-permute-done.9 = f32[96,256]{1,0:T(8,128)} collective-permute-done((f32[96,256]{1,0:T(8,128)S(1)}, f32[96,256]{1,0:T(8,128)}, u32[]{:S(2)}, u32[]{:S(2)}) %collective-permute-start.9) | collective-permute-done | bytes 98336 | tf_op jit(solution)/shard_map/ppermute | solution.py:78
  75.9 2.1 %collective-permute-done.11 = f32[48,256]{1,0:T(8,128)} collective-permute-done((f32[48,256]{1,0:T(8,128)}, f32[48,256]{1,0:T(8,128)}, u32[]{:S(2)}, u32[]{:S(2)}) %collective-permute-start.11) | collective-permute-done | bytes 49184 | tf_op jit(solution)/shard_map/ppermute | solution.py:78
  84.3 2.0 %collective-permute-done.14 = f32[64,256]{1,0:T(8,128)S(1)} collective-permute-done((f32[64,256]{1,0:T(8,128)S(1)}, f32[64,256]{1,0:T(8,128)S(1)}, u32[]{:S(2)}, u32[]{:S(2)}) %collective-permute-start.14) | collective-permute-done | bytes 65568 | tf_op jit(solution)/shard_map/ppermute | solution.py:78
  89.5 2.2 %collective-permute-start.18 = (f32[64,256]{1,0:T(8,128)S(1)}, f32[64,256]{1,0:T(8,128)S(1)}, u32[]{:S(2)}, u32[]{:S(2)}) collective-permute-start(f32[64,256]{1,0:T(8,128)S(1)} %fusion.112), channel_id=1, source_target_pairs={{0,3},{1,2},{2,1},{3,0},{4,7},{5,6},{6,5},{7,4},{8,11},{9,10},{10,... | collective-permute-start | bytes 196616 | tf_op jit(solution)/shard_map/ppermute | solution.py:50
  91.7 2.8 %collective-permute-start.12 = (f32[48,256]{1,0:T(8,128)}, f32[48,256]{1,0:T(8,128)S(1)}, u32[]{:S(2)}, u32[]{:S(2)}) collective-permute-start(f32[48,256]{1,0:T(8,128)} %copy-done.3), channel_id=1, source_target_pairs={{0,0},{1,8},{2,16},{3,24},{4,32},{5,40},{6,48},{7,56},{8,64},{9,72... | collective-permute-start | bytes 147464 | tf_op jit(solution)/shard_map/ppermute | solution.py:151
  94.5 6.7 %collective-permute-done.12 = f32[48,256]{1,0:T(8,128)S(1)} collective-permute-done((f32[48,256]{1,0:T(8,128)}, f32[48,256]{1,0:T(8,128)S(1)}, u32[]{:S(2)}, u32[]{:S(2)}) %collective-permute-start.12) | collective-permute-done | bytes 49184 | tf_op jit(solution)/shard_map/ppermute | solution.py:151
  102.9 5.2 %collective-permute-start.21 = (f32[64,256]{1,0:T(8,128)S(1)}, f32[64,256]{1,0:T(8,128)S(1)}, u32[]{:S(2)}, u32[]{:S(2)}) collective-permute-start(f32[64,256]{1,0:T(8,128)S(1)} %fusion.170), channel_id=1, source_target_pairs={{0,12},{1,13},{2,14},{3,15},{4,8},{5,9},{6,10},{7,11},{8,4},{9,5},... | collective-permute-start | bytes 196616 | tf_op jit(solution)/shard_map/ppermute | solution.py:50
  108.9 2.2 %collective-permute-done.21 = f32[64,256]{1,0:T(8,128)S(1)} collective-permute-done((f32[64,256]{1,0:T(8,128)S(1)}, f32[64,256]{1,0:T(8,128)S(1)}, u32[]{:S(2)}, u32[]{:S(2)}) %collective-permute-start.21) | collective-permute-done | bytes 65568 | tf_op jit(solution)/shard_map/ppermute | solution.py:50
  111.2 5.5 %collective-permute-start.22 = (f32[64,256]{1,0:T(8,128)S(1)}, f32[64,256]{1,0:T(8,128)S(1)}, u32[]{:S(2)}, u32[]{:S(2)}) collective-permute-start(f32[64,256]{1,0:T(8,128)S(1)} %fusion.169), channel_id=1, source_target_pairs={{0,16},{1,17},{2,18},{3,19},{4,20},{5,21},{6,22},{7,23},{8,24},{9,... | collective-permute-start | bytes 196616 | tf_op jit(solution)/shard_map/ppermute | solution.py:50
  117.4 2.1 %collective-permute-start.24 = (f32[64,256]{1,0:T(8,128)S(1)}, f32[64,256]{1,0:T(8,128)S(1)}, u32[]{:S(2)}, u32[]{:S(2)}) collective-permute-start(f32[64,256]{1,0:T(8,128)S(1)} %fusion.169), channel_id=1, source_target_pairs={{0,144},{1,145},{2,146},{3,147},{4,148},{5,149},{6,150},{7,151},{8... | collective-permute-start | bytes 196616 | tf_op jit(solution)/shard_map/ppermute | solution.py:50
  121.3 3.1 %collective-permute-done.24 = f32[64,256]{1,0:T(8,128)S(1)} collective-permute-done((f32[64,256]{1,0:T(8,128)S(1)}, f32[64,256]{1,0:T(8,128)S(1)}, u32[]{:S(2)}, u32[]{:S(2)}) %collective-permute-start.24) | collective-permute-done | bytes 65568 | tf_op jit(solution)/shard_map/ppermute | solution.py:50
  124.5 5.2 %collective-permute-start.25 = (f32[64,256]{1,0:T(8,128)S(1)}, f32[64,256]{1,0:T(8,128)S(1)}, u32[]{:S(2)}, u32[]{:S(2)}) collective-permute-start(f32[64,256]{1,0:T(8,128)S(1)} %fusion.168), channel_id=1, source_target_pairs={{0,32},{1,33},{2,34},{3,35},{4,36},{5,37},{6,38},{7,39},{8,40},{9,... | collective-permute-start | bytes 196616 | tf_op jit(solution)/shard_map/ppermute | solution.py:50
  135.7 2.3 %gather_fusion.1 = f32[256]{0:T(256)S(1)} fusion(f32[256,256]{1,0:T(8,128)S(1)} %bitcast.148, s32[256]{0:T(256)S(1)} %bitcast.147), kind=kCustom, calls=%fused_computation.1 | custom fusion | bytes 4096 | tf_op jit(solution)/shard_map/jit(_diag)/jit(diagonal)/cond/branch_0_fun/gather | solution.py:29
  (104 shorter events, 45.1 us)
Async XLA Ops:
  0.7 26.9 %collective-permute-start.1 = (f32[48,256]{1,0:T(8,128)}, f32[48,256]{1,0:T(8,128)S(1)}, u32[]{:S(2)}, u32[]{:S(2)}) collective-permute-start(f32[48,256]{1,0:T(8,128)} %param.6), channel_id=1, source_target_pairs={{0,4},{1,5},{2,6},{3,7},{4,0},{5,1},{6,2},{7,3},{8,12},{9,13},{10,... | collective-permute-start | bytes 147464 | tf_op jit(solution)/shard_map/ppermute | solution.py:50
  8.5 19.1 %collective-permute-start.2 = (f32[48,256]{1,0:T(8,128)}, f32[48,256]{1,0:T(8,128)S(1)}, u32[]{:S(2)}, u32[]{:S(2)}) collective-permute-start(f32[48,256]{1,0:T(8,128)} %param.6), channel_id=1, source_target_pairs={{0,2},{1,3},{2,0},{3,1},{4,6},{5,7},{6,4},{7,5},{8,10},{9,11},{10,... | collective-permute-start | bytes 147464 | tf_op jit(solution)/shard_map/ppermute | solution.py:50
  9.7 17.9 %collective-permute-start.3 = (f32[48,256]{1,0:T(8,128)}, f32[48,256]{1,0:T(8,128)S(1)}, u32[]{:S(2)}, u32[]{:S(2)}) collective-permute-start(f32[48,256]{1,0:T(8,128)} %param.6), channel_id=1, source_target_pairs={{0,6},{1,7},{2,4},{3,5},{4,2},{5,3},{6,0},{7,1},{8,14},{9,15},{10,... | collective-permute-start | bytes 147464 | tf_op jit(solution)/shard_map/ppermute | solution.py:50
  11.2 64.8 %collective-permute-start = (f32[2,48,256]{2,1,0:T(8,128)}, f32[2,48,256]{2,1,0:T(8,128)}, u32[]{:S(2)}, u32[]{:S(2)}) collective-permute-start(f32[2,48,256]{2,1,0:T(8,128)} %pad_maximum_fusion.9), channel_id=1, source_target_pairs={{0,0},{8,1},{16,2},{24,3},{32,4},{40,5},{48,6},{56,7},{64,8},{72,9... | collective-permute-start | bytes 294920 | tf_op jit(solution)/shard_map/ppermute | solution.py:125
  27.7 6.1 %collective-permute-start.4 = (f32[192,256]{1,0:T(8,128)S(1)}, f32[192,256]{1,0:T(8,128)S(1)}, u32[]{:S(2)}, u32[]{:S(2)}) collective-permute-start(f32[192,256]{1,0:T(8,128)S(1)} %get-tuple-element.20), channel_id=1, source_target_pairs={{0,1},{1,0},{2,3},{3,2},{4,5},{5,4},{6,7},{7,6},{8,9},{9,8},{10,11... | collective-permute-start | bytes 589832 | tf_op jit(solution)/shard_map/ppermute | solution.py:50
  33.9 11.7 %collective-permute-start.5 = (f32[384,256]{1,0:T(8,128)S(1)}, f32[384,256]{1,0:T(8,128)S(1)}, u32[]{:S(2)}, u32[]{:S(2)}) collective-permute-start(f32[384,256]{1,0:T(8,128)S(1)} %get-tuple-element.10), channel_id=1, source_target_pairs={{0,8},{1,9},{2,10},{3,11},{4,12},{5,13},{6,14},{7,15},{8,0},{9,1},... | collective-permute-start | bytes 1179656 | tf_op jit(solution)/shard_map/ppermute | solution.py:50
  35.9 19.3 %collective-permute-start.6 = (f32[384,256]{1,0:T(8,128)S(1)}, f32[384,256]{1,0:T(8,128)S(1)}, u32[]{:S(2)}, u32[]{:S(2)}) collective-permute-start(f32[384,256]{1,0:T(8,128)S(1)} %get-tuple-element.10), channel_id=1, source_target_pairs={{0,16},{1,17},{2,18},{3,19},{4,20},{5,21},{6,22},{7,23},{8,24},{9,... | collective-permute-start | bytes 1179656 | tf_op jit(solution)/shard_map/ppermute | solution.py:50
  37.7 20.6 %collective-permute-start.7 = (f32[384,256]{1,0:T(8,128)S(1)}, f32[384,256]{1,0:T(8,128)S(1)}, u32[]{:S(2)}, u32[]{:S(2)}) collective-permute-start(f32[384,256]{1,0:T(8,128)S(1)} %get-tuple-element.10), channel_id=1, source_target_pairs={{0,24},{1,25},{2,26},{3,27},{4,28},{5,29},{6,30},{7,31},{8,16},{9,... | collective-permute-start | bytes 1179656 | tf_op jit(solution)/shard_map/ppermute | solution.py:50
  64.1 5.3 %collective-permute-start.10 = (f32[96,256]{1,0:T(8,128)}, f32[96,256]{1,0:T(8,128)S(1)}, u32[]{:S(2)}, u32[]{:S(2)}) collective-permute-start(f32[96,256]{1,0:T(8,128)} %get-tuple-element.7), channel_id=1, source_target_pairs={{0,96},{32,64},{64,32},{96,0},{128,224},{160,192},{192,160},{224,1... | collective-permute-start | bytes 294920 | tf_op jit(solution)/shard_map/ppermute | solution.py:78
  65.5 6.2 %collective-permute-start.9 = (f32[96,256]{1,0:T(8,128)S(1)}, f32[96,256]{1,0:T(8,128)}, u32[]{:S(2)}, u32[]{:S(2)}) collective-permute-start(f32[96,256]{1,0:T(8,128)S(1)} %get-tuple-element.8), channel_id=1, source_target_pairs={{0,64},{32,96},{64,0},{96,32},{128,192},{160,224},{192,128},{224,1... | collective-permute-start | bytes 294920 | tf_op jit(solution)/shard_map/ppermute | solution.py:78
  73.3 4.8 %collective-permute-start.11 = (f32[48,256]{1,0:T(8,128)}, f32[48,256]{1,0:T(8,128)}, u32[]{:S(2)}, u32[]{:S(2)}) collective-permute-start(f32[48,256]{1,0:T(8,128)} %dynamic-slice_bitcast_fusion.14), channel_id=1, source_target_pairs={{0,128},{32,160},{64,192},{96,224},{128,0},{160,32},{192,64},{224,... | collective-permute-start | bytes 147464 | tf_op jit(solution)/shard_map/ppermute | solution.py:78
  83.3 4.7 %collective-permute-start.15 = (f32[64,256]{1,0:T(8,128)S(1)}, f32[64,256]{1,0:T(8,128)S(1)}, u32[]{:S(2)}, u32[]{:S(2)}) collective-permute-start(f32[64,256]{1,0:T(8,128)S(1)} %get-tuple-element.18), channel_id=1, source_target_pairs={{0,96},{1,97},{2,98},{3,99},{4,100},{5,101},{6,102},{7,103},{8,104... | collective-permute-start | bytes 196616 | tf_op jit(solution)/shard_map/ppermute | solution.py:78
  87.9 13.2 %collective-permute-start.16 = (f32[64,256]{1,0:T(8,128)S(1)}, f32[64,256]{1,0:T(8,128)S(1)}, u32[]{:S(2)}, u32[]{:S(2)}) collective-permute-start(f32[64,256]{1,0:T(8,128)S(1)} %fusion.112), channel_id=1, source_target_pairs={{0,1},{1,0},{2,3},{3,2},{4,5},{5,4},{6,7},{7,6},{8,9},{9,8},{10,11... | collective-permute-start | bytes 196616 | tf_op jit(solution)/shard_map/ppermute | solution.py:50
  89.5 11.7 %collective-permute-start.17 = (f32[64,256]{1,0:T(8,128)S(1)}, f32[64,256]{1,0:T(8,128)S(1)}, u32[]{:S(2)}, u32[]{:S(2)}) collective-permute-start(f32[64,256]{1,0:T(8,128)S(1)} %fusion.112), channel_id=1, source_target_pairs={{0,2},{1,3},{2,0},{3,1},{4,6},{5,7},{6,4},{7,5},{8,10},{9,11},{10,... | collective-permute-start | bytes 196616 | tf_op jit(solution)/shard_map/ppermute | solution.py:50
  89.5 11.7 %collective-permute-start.18 = (f32[64,256]{1,0:T(8,128)S(1)}, f32[64,256]{1,0:T(8,128)S(1)}, u32[]{:S(2)}, u32[]{:S(2)}) collective-permute-start(f32[64,256]{1,0:T(8,128)S(1)} %fusion.112), channel_id=1, source_target_pairs={{0,3},{1,2},{2,1},{3,0},{4,7},{5,6},{6,5},{7,4},{8,11},{9,10},{10,... | collective-permute-start | bytes 196616 | tf_op jit(solution)/shard_map/ppermute | solution.py:50
  91.7 9.5 %collective-permute-start.12 = (f32[48,256]{1,0:T(8,128)}, f32[48,256]{1,0:T(8,128)S(1)}, u32[]{:S(2)}, u32[]{:S(2)}) collective-permute-start(f32[48,256]{1,0:T(8,128)} %copy-done.3), channel_id=1, source_target_pairs={{0,0},{1,8},{2,16},{3,24},{4,32},{5,40},{6,48},{7,56},{8,64},{9,72... | collective-permute-start | bytes 147464 | tf_op jit(solution)/shard_map/ppermute | solution.py:151
  101.3 7.6 %collective-permute-start.19 = (f32[64,256]{1,0:T(8,128)S(1)}, f32[64,256]{1,0:T(8,128)S(1)}, u32[]{:S(2)}, u32[]{:S(2)}) collective-permute-start(f32[64,256]{1,0:T(8,128)S(1)} %fusion.170), channel_id=1, source_target_pairs={{0,4},{1,5},{2,6},{3,7},{4,0},{5,1},{6,2},{7,3},{8,12},{9,13},{10,... | collective-permute-start | bytes 196616 | tf_op jit(solution)/shard_map/ppermute | solution.py:50
  101.6 7.3 %collective-permute-start.20 = (f32[64,256]{1,0:T(8,128)S(1)}, f32[64,256]{1,0:T(8,128)S(1)}, u32[]{:S(2)}, u32[]{:S(2)}) collective-permute-start(f32[64,256]{1,0:T(8,128)S(1)} %fusion.170), channel_id=1, source_target_pairs={{0,8},{1,9},{2,10},{3,11},{4,12},{5,13},{6,14},{7,15},{8,0},{9,1},... | collective-permute-start | bytes 196616 | tf_op jit(solution)/shard_map/ppermute | solution.py:50
  102.9 8.2 %collective-permute-start.21 = (f32[64,256]{1,0:T(8,128)S(1)}, f32[64,256]{1,0:T(8,128)S(1)}, u32[]{:S(2)}, u32[]{:S(2)}) collective-permute-start(f32[64,256]{1,0:T(8,128)S(1)} %fusion.170), channel_id=1, source_target_pairs={{0,12},{1,13},{2,14},{3,15},{4,8},{5,9},{6,10},{7,11},{8,4},{9,5},... | collective-permute-start | bytes 196616 | tf_op jit(solution)/shard_map/ppermute | solution.py:50
  111.2 8.3 %collective-permute-start.22 = (f32[64,256]{1,0:T(8,128)S(1)}, f32[64,256]{1,0:T(8,128)S(1)}, u32[]{:S(2)}, u32[]{:S(2)}) collective-permute-start(f32[64,256]{1,0:T(8,128)S(1)} %fusion.169), channel_id=1, source_target_pairs={{0,16},{1,17},{2,18},{3,19},{4,20},{5,21},{6,22},{7,23},{8,24},{9,... | collective-permute-start | bytes 196616 | tf_op jit(solution)/shard_map/ppermute | solution.py:50
  116.7 4.6 %collective-permute-start.23 = (f32[64,256]{1,0:T(8,128)S(1)}, f32[64,256]{1,0:T(8,128)S(1)}, u32[]{:S(2)}, u32[]{:S(2)}) collective-permute-start(f32[64,256]{1,0:T(8,128)S(1)} %fusion.169), channel_id=1, source_target_pairs={{0,128},{1,129},{2,130},{3,131},{4,132},{5,133},{6,134},{7,135},{8... | collective-permute-start | bytes 196616 | tf_op jit(solution)/shard_map/ppermute | solution.py:50
  117.4 7.1 %collective-permute-start.24 = (f32[64,256]{1,0:T(8,128)S(1)}, f32[64,256]{1,0:T(8,128)S(1)}, u32[]{:S(2)}, u32[]{:S(2)}) collective-permute-start(f32[64,256]{1,0:T(8,128)S(1)} %fusion.169), channel_id=1, source_target_pairs={{0,144},{1,145},{2,146},{3,147},{4,148},{5,149},{6,150},{7,151},{8... | collective-permute-start | bytes 196616 | tf_op jit(solution)/shard_map/ppermute | solution.py:50
  124.5 7.0 %collective-permute-start.25 = (f32[64,256]{1,0:T(8,128)S(1)}, f32[64,256]{1,0:T(8,128)S(1)}, u32[]{:S(2)}, u32[]{:S(2)}) collective-permute-start(f32[64,256]{1,0:T(8,128)S(1)} %fusion.168), channel_id=1, source_target_pairs={{0,32},{1,33},{2,34},{3,35},{4,36},{5,37},{6,38},{7,39},{8,40},{9,... | collective-permute-start | bytes 196616 | tf_op jit(solution)/shard_map/ppermute | solution.py:50
  130.8 4.1 %collective-permute-start.27 = (f32[64,256]{1,0:T(8,128)S(1)}, f32[64,256]{1,0:T(8,128)S(1)}, u32[]{:S(2)}, u32[]{:S(2)}) collective-permute-start(f32[64,256]{1,0:T(8,128)S(1)} %fusion.168), channel_id=1, source_target_pairs={{0,96},{1,97},{2,98},{3,99},{4,100},{5,101},{6,102},{7,103},{8,104... | collective-permute-start | bytes 196616 | tf_op jit(solution)/shard_map/ppermute | solution.py:50
  (9 other events, 117.1 us)

commit v10 on v7

--- a/solution.py
+++ b/solution.py
@@ -110,12 +110,17 @@
 
 def make_body(nrow, ncol):
     assert nrow & (nrow - 1) == 0 and ncol & (ncol - 1) == 0
-    ndev = nrow * ncol
     row_bits = [1 << k for k in range(nrow.bit_length() - 1)]
     row_groups = [tuple(row_bits[i : i + 2]) for i in range(0, len(row_bits), 2)]
-    blocks_perm = [(b, (b % nrow) * ncol + b // nrow) for b in range(ndev)]
     owner_perm = [
         (r * ncol + c, c * nrow + kept_chunk(r, row_groups, nrow)) for r in range(nrow) for c in range(ncol)
+    ]
+
+    q = ncol // nrow
+    col_block_perm = [
+        (big * ncol + small, (small // q) * ncol + q * big + small % q)
+        for big in range(nrow)
+        for small in range(ncol)
     ]
 
     def inner(trailing_adjoint, panel, panel_adjoint, diag_factor, diag_adjoint):
@@ -142,25 +147,22 @@
             preferred_element_type=jnp.float32,
         )
 
-        col_panel = lax.ppermute(panel, ALL, blocks_perm)
-        for masks in row_groups:
-            col_panel = gather_step(col_panel, "row", nrow, masks)
+        span = share.shape[0]
+        pick = lax.dynamic_slice_in_dim(gathered, (c % q) * span, span, 0)
+        col_panel = lax.ppermute(pick, ALL, col_block_perm)
 
-        local_term = mm(panel_adjoint.T, panel) - 2.0 * mm(share.T, col_panel)
+        local_term = mm(inverse.T, mm(panel_adjoint.T, panel) - 2.0 * mm(share.T, col_panel))
         rows, cols = diag_adjoint.shape
         placed = lax.dynamic_update_slice(
             jnp.zeros((rows * nrow, cols * ncol), jnp.float32), diag_adjoint, (r * rows, c * cols)
         )
-        summed = all_reduce(jnp.concatenate([local_term, placed], axis=0), nrow, ncol)
-        total, whole = summed[: local_term.shape[0]], summed[local_term.shape[0] :]
+        accumulated = all_reduce(placed - local_term, nrow, ncol)
 
         for masks in row_groups:
             share = scatter_step(share, "row", nrow, masks)
         product = lax.ppermute(share, ALL, owner_perm)
         updated = panel_adjoint - 2.0 * product
         off_adjoint = mm(updated, inverse)
-
-        accumulated = whole - mm(inverse.T, total)
         return (off_adjoint, diagonal_adjoint(diag_factor, inverse, accumulated))
 
     return inner

time: 139 us -> 138 us (level); the launches traced: 136 us -> 137 us
  starting transfers between devices: 63.9 us -> 58.3 us
  local copies, waits for them, and re-layouts: 9.17 us -> 12.9 us
  waiting for transfers between devices: 42.6 us -> 45.5 us
    ppermute x7, waiting for transfers between devices: 2.43 us -> 7.39 us  [scatter_step(): total = total + lax.ppermute(send, axis, xor_perm(size, offset(k, masks)))]
    ppermute x1, starting transfers between devices: 7.76 us -> 11.7 us  [inner(): col_panel = lax.ppermute(pick, ALL, col_block_perm)]
    ppermute x23 -> x19, starting transfers between devices: 41.6 us -> 37.7 us  [exchange(): got.append(lax.ppermute(value, axis, xor_perm(size, offset(k, masks))))]
    ppermute x23 -> x19, waiting for transfers between devices: 40.2 us -> 36.3 us  [exchange(): got.append(lax.ppermute(value, axis, xor_perm(size, offset(k, masks))))]
    ppermute x7, starting transfers between devices: 8.79 us -> 5 us  [scatter_step(): total = total + lax.ppermute(send, axis, xor_perm(size, offset(k, masks)))]
    ppermute x1, starting transfers between devices: 5.72 us -> 3.88 us  [inner(): product = lax.ppermute(share, ALL, owner_perm)]
    dynamic_update_slice x1, local copies, waits for them, and re-layouts: 0.86 us -> 2.69 us  [inner(): lax.dynamic_update_slice(jnp.zeros((rows * nrow, cols * ncol), jnp.float3...]
    ppermute x1, waiting for transfers between devices: 0.01 us -> 1.8 us  [inner(): product = lax.ppermute(share, ALL, owner_perm)]
  transfers between devices with their start and end apart: 32 -> 28, of which waited for: 13 -> 15; matrix products, arithmetic and copies ran while one was open for 13% -> 19% of each run, Pallas kernels for 0% -> 0%
where the time goes in v10:
time: 138 us; the launch traced here: 137 us
  starting transfers between devices  58.3 us (42%)
  waiting for transfers between devices  45.5 us (33%)
  matrix products  17.3 us (13%)
  local copies, waits for them, and re-layouts  12.9 us (9%)
  other arithmetic  1.69 us (1%)
    ppermute x19, starting transfers between devices, exchange(): got.append(lax.ppermute(value, axis, xor_perm(size, offset(k, masks))))  37.7 us
    ppermute x19, waiting for transfers between devices, exchange(): got.append(lax.ppermute(value, axis, xor_perm(size, offset(k, masks))))  36.3 us
    dot_general x23, matrix products, mm(): jnp.dot(a, b, precision=lax.Precision.HIGHEST, preferred_element_type=jnp...  14.6 us
    ppermute x1, starting transfers between devices, inner(): col_panel = lax.ppermute(pick, ALL, col_block_perm)  11.7 us
    ppermute x7, waiting for transfers between devices, scatter_step(): total = total + lax.ppermute(send, axis, xor_perm(size, offset(k, masks)))  7.39 us
    ppermute x7, starting transfers between devices, scatter_step(): total = total + lax.ppermute(send, axis, xor_perm(size, offset(k, masks)))  5 us
    ppermute x1, starting transfers between devices, inner(): product = lax.ppermute(share, ALL, owner_perm)  3.88 us
  transfers between devices with their start and end apart: 28, of which 15 were waited for; matrix products, arithmetic and copies ran while one was open for 19% of the time, Pallas kernels for 0%

profile of v10, /device:TPU:1, one launch (start us, length us, event | category | flops | bytes accessed | tf_op | source)
XLA Modules:
  0.0 137.1 jit_solution(7903617049351336919)
XLA Ops:
  0.7 7.8 %collective-permute-start = (f32[48,256]{1,0:T(8,128)}, f32[48,256]{1,0:T(8,128)S(1)}, u32[]{:S(2)}, u32[]{:S(2)}) collective-permute-start(f32[48,256]{1,0:T(8,128)} %param.6), channel_id=1, source_target_pairs={{0,4},{1,5},{2,6},{3,7},{4,0},{5,1},{6,2},{7,3},{8,12},{9,13},{10,... | collective-permute-start | bytes 147464 | tf_op jit(solution)/shard_map/ppermute | solution.py:50
  9.7 2.6 %gather_fusion = f32[256]{0:T(256)S(1)} fusion(f32[256,256]{1,0:T(8,128)} %param.8, s32[256]{0:T(256)S(1)} %bitcast.136), kind=kCustom, calls=%fused_computation | custom fusion | bytes 4096 | tf_op jit(solution)/shard_map/jit(diagonal)/cond/branch_0_fun/gather | solution.py:16
  20.6 4.1 %collective-permute-done.3 = f32[192,256]{1,0:T(8,128)S(1)} collective-permute-done((f32[192,256]{1,0:T(8,128)S(1)}, f32[192,256]{1,0:T(8,128)S(1)}, u32[]{:S(2)}, u32[]{:S(2)}) %collective-permute-start.3) | collective-permute-done | bytes 196640 | tf_op jit(solution)/shard_map/ppermute | solution.py:50
  26.1 2.4 %collective-permute-start.5 = (f32[384,256]{1,0:T(8,128)S(1)}, f32[384,256]{1,0:T(8,128)S(1)}, u32[]{:S(2)}, u32[]{:S(2)}) collective-permute-start(f32[384,256]{1,0:T(8,128)S(1)} %get-tuple-element.10), channel_id=1, source_target_pairs={{0,16},{1,17},{2,18},{3,19},{4,20},{5,21},{6,22},{7,23},{8,24},{9,... | collective-permute-start | bytes 1179656 | tf_op jit(solution)/shard_map/ppermute | solution.py:50
  29.6 3.8 %collective-permute-done.4 = f32[384,256]{1,0:T(8,128)S(1)} collective-permute-done((f32[384,256]{1,0:T(8,128)S(1)}, f32[384,256]{1,0:T(8,128)S(1)}, u32[]{:S(2)}, u32[]{:S(2)}) %collective-permute-start.4) | collective-permute-done | bytes 393248 | tf_op jit(solution)/shard_map/ppermute | solution.py:50
  33.5 10.7 %collective-permute-done.5 = f32[384,256]{1,0:T(8,128)S(1)} collective-permute-done((f32[384,256]{1,0:T(8,128)S(1)}, f32[384,256]{1,0:T(8,128)S(1)}, u32[]{:S(2)}, u32[]{:S(2)}) %collective-permute-start.5) | collective-permute-done | bytes 393248 | tf_op jit(solution)/shard_map/ppermute | solution.py:50
  45.4 11.7 %collective-permute-start.12 = (f32[384,256]{1,0:T(8,128)}, f32[384,256]{1,0:T(8,128)}, u32[]{:S(2)}, u32[]{:S(2)}) collective-permute-start(f32[384,256]{1,0:T(8,128)} %constant_dynamic-slice_fusion), channel_id=1, source_target_pairs={{0,0},{1,1},{2,2},{3,3},{4,32},{5,33},{6,34},{7,35},{8,64},{9,65},... | collective-permute-start | bytes 1179656 | tf_op jit(solution)/shard_map/ppermute | solution.py:152
  57.1 2.7 %fusion.135 = f32[256,384]{1,0:T(8,128)S(1)} fusion(f32[1536,256]{1,0:T(8,128)S(1)} %bitcast.139, f32[1536,384]{1,0:T(8,128)S(1)} %copy-done), kind=kOutput, calls=%fused_computation.218 | convolution fusion | flops 1811939328 | bytes 4325376 | tf_op jit(solution)/shard_map/dot_general | solution.py:142
  62.5 2.1 %collective-permute-start.9 = (f32[96,256]{1,0:T(8,128)}, f32[96,256]{1,0:T(8,128)}, u32[]{:S(2)}, u32[]{:S(2)}) collective-permute-start(f32[96,256]{1,0:T(8,128)} %get-tuple-element.7), channel_id=1, source_target_pairs={{0,96},{32,64},{64,32},{96,0},{128,224},{160,192},{192,160},{224,1... | collective-permute-start | bytes 294920 | tf_op jit(solution)/shard_map/ppermute | solution.py:78
  67.3 2.7 %dynamic_update_slice.3 = f32[256,256]{1,0:T(8,128)} dynamic-update-slice(f32[256,256]{1,0:T(8,128)} %broadcast_in_dim.46, f32[32,8]{1,0:T(8,128)} %copy.15, s32[]{:T(128)S(6)} %select_n.358, s32[]{:T(128)S(6)} %select_n.359) | dynamic-update-slice | bytes 2052 | tf_op jit(solution)/shard_map/dynamic_update_slice | solution.py:156
  70.0 5.2 %collective-permute-done.8 = f32[96,256]{1,0:T(8,128)} collective-permute-done((f32[96,256]{1,0:T(8,128)}, f32[96,256]{1,0:T(8,128)}, u32[]{:S(2)}, u32[]{:S(2)}) %collective-permute-start.8) | collective-permute-done | bytes 98336 | tf_op jit(solution)/shard_map/ppermute | solution.py:78
  75.2 2.1 %collective-permute-done.9 = f32[96,256]{1,0:T(8,128)} collective-permute-done((f32[96,256]{1,0:T(8,128)}, f32[96,256]{1,0:T(8,128)}, u32[]{:S(2)}, u32[]{:S(2)}) %collective-permute-start.9) | collective-permute-done | bytes 98336 | tf_op jit(solution)/shard_map/ppermute | solution.py:78
  81.3 2.1 %collective-permute-start.14 = (f32[64,256]{1,0:T(8,128)S(1)}, f32[64,256]{1,0:T(8,128)S(1)}, u32[]{:S(2)}, u32[]{:S(2)}) collective-permute-start(f32[64,256]{1,0:T(8,128)S(1)} %get-tuple-element.19), channel_id=1, source_target_pairs={{0,64},{1,65},{2,66},{3,67},{4,68},{5,69},{6,70},{7,71},{8,72},{9,... | collective-permute-start | bytes 196616 | tf_op jit(solution)/shard_map/ppermute | solution.py:78
  83.6 3.9 %collective-permute-start.11 = (f32[48,256]{1,0:T(8,128)S(1)}, f32[48,256]{1,0:T(8,128)S(1)}, u32[]{:S(2)}, u32[]{:S(2)}) collective-permute-start(f32[48,256]{1,0:T(8,128)S(1)} %bitcast_add_fusion.2), channel_id=1, source_target_pairs={{0,0},{1,8},{2,16},{3,24},{4,32},{5,40},{6,48},{7,56},{8,64},{9,72... | collective-permute-start | bytes 147464 | tf_op jit(solution)/shard_map/ppermute | solution.py:163
  88.4 3.3 %collective-permute-start.17 = (f32[64,256]{1,0:T(8,128)S(1)}, f32[64,256]{1,0:T(8,128)S(1)}, u32[]{:S(2)}, u32[]{:S(2)}) collective-permute-start(f32[64,256]{1,0:T(8,128)S(1)} %fusion.113), channel_id=1, source_target_pairs={{0,2},{1,3},{2,0},{3,1},{4,6},{5,7},{6,4},{7,5},{8,10},{9,11},{10,... | collective-permute-start | bytes 196616 | tf_op jit(solution)/shard_map/ppermute | solution.py:50
  94.4 2.5 %collective-permute-done.18 = f32[64,256]{1,0:T(8,128)S(1)} collective-permute-done((f32[64,256]{1,0:T(8,128)S(1)}, f32[64,256]{1,0:T(8,128)S(1)}, u32[]{:S(2)}, u32[]{:S(2)}) %collective-permute-start.18) | collective-permute-done | bytes 65568 | tf_op jit(solution)/shard_map/ppermute | solution.py:50
  96.9 4.5 %collective-permute-start.19 = (f32[64,256]{1,0:T(8,128)S(1)}, f32[64,256]{1,0:T(8,128)S(1)}, u32[]{:S(2)}, u32[]{:S(2)}) collective-permute-start(f32[64,256]{1,0:T(8,128)S(1)} %fusion.174), channel_id=1, source_target_pairs={{0,4},{1,5},{2,6},{3,7},{4,0},{5,1},{6,2},{7,3},{8,12},{9,13},{10,... | collective-permute-start | bytes 196616 | tf_op jit(solution)/shard_map/ppermute | solution.py:50
  101.5 2.0 %collective-permute-start.21 = (f32[64,256]{1,0:T(8,128)S(1)}, f32[64,256]{1,0:T(8,128)S(1)}, u32[]{:S(2)}, u32[]{:S(2)}) collective-permute-start(f32[64,256]{1,0:T(8,128)S(1)} %fusion.174), channel_id=1, source_target_pairs={{0,12},{1,13},{2,14},{3,15},{4,8},{5,9},{6,10},{7,11},{8,4},{9,5},... | collective-permute-start | bytes 196616 | tf_op jit(solution)/shard_map/ppermute | solution.py:50
  104.5 5.1 %collective-permute-done.21 = f32[64,256]{1,0:T(8,128)S(1)} collective-permute-done((f32[64,256]{1,0:T(8,128)S(1)}, f32[64,256]{1,0:T(8,128)S(1)}, u32[]{:S(2)}, u32[]{:S(2)}) %collective-permute-start.21) | collective-permute-done | bytes 65568 | tf_op jit(solution)/shard_map/ppermute | solution.py:50
  109.7 2.2 %collective-permute-start.22 = (f32[64,256]{1,0:T(8,128)S(1)}, f32[64,256]{1,0:T(8,128)S(1)}, u32[]{:S(2)}, u32[]{:S(2)}) collective-permute-start(f32[64,256]{1,0:T(8,128)S(1)} %fusion.173), channel_id=1, source_target_pairs={{0,16},{1,17},{2,18},{3,19},{4,20},{5,21},{6,22},{7,23},{8,24},{9,... | collective-permute-start | bytes 196616 | tf_op jit(solution)/shard_map/ppermute | solution.py:50
  111.9 2.3 %collective-permute-start.23 = (f32[64,256]{1,0:T(8,128)S(1)}, f32[64,256]{1,0:T(8,128)S(1)}, u32[]{:S(2)}, u32[]{:S(2)}) collective-permute-start(f32[64,256]{1,0:T(8,128)S(1)} %fusion.173), channel_id=1, source_target_pairs={{0,128},{1,129},{2,130},{3,131},{4,132},{5,133},{6,134},{7,135},{8... | collective-permute-start | bytes 196616 | tf_op jit(solution)/shard_map/ppermute | solution.py:50
  116.5 4.7 %collective-permute-done.24 = f32[64,256]{1,0:T(8,128)S(1)} collective-permute-done((f32[64,256]{1,0:T(8,128)S(1)}, f32[64,256]{1,0:T(8,128)S(1)}, u32[]{:S(2)}, u32[]{:S(2)}) %collective-permute-start.24) | collective-permute-done | bytes 65568 | tf_op jit(solution)/shard_map/ppermute | solution.py:50
  121.2 5.7 %collective-permute-start.25 = (f32[64,256]{1,0:T(8,128)S(1)}, f32[64,256]{1,0:T(8,128)S(1)}, u32[]{:S(2)}, u32[]{:S(2)}) collective-permute-start(f32[64,256]{1,0:T(8,128)S(1)} %fusion.172), channel_id=1, source_target_pairs={{0,32},{1,33},{2,34},{3,35},{4,36},{5,37},{6,38},{7,39},{8,40},{9,... | collective-permute-start | bytes 196616 | tf_op jit(solution)/shard_map/ppermute | solution.py:50
  133.0 2.3 %gather_fusion.1 = f32[256]{0:T(256)S(1)} fusion(f32[256,256]{1,0:T(8,128)S(1)} %bitcast.140, s32[256]{0:T(256)S(1)} %bitcast.137), kind=kCustom, calls=%fused_computation.1 | custom fusion | bytes 4096 | tf_op jit(solution)/shard_map/jit(_diag)/jit(diagonal)/cond/branch_0_fun/gather | solution.py:29
  (108 shorter events, 37.1 us)
Async XLA Ops:
  0.7 18.6 %collective-permute-start = (f32[48,256]{1,0:T(8,128)}, f32[48,256]{1,0:T(8,128)S(1)}, u32[]{:S(2)}, u32[]{:S(2)}) collective-permute-start(f32[48,256]{1,0:T(8,128)} %param.6), channel_id=1, source_target_pairs={{0,4},{1,5},{2,6},{3,7},{4,0},{5,1},{6,2},{7,3},{8,12},{9,13},{10,... | collective-permute-start | bytes 147464 | tf_op jit(solution)/shard_map/ppermute | solution.py:50
  8.5 10.8 %collective-permute-start.1 = (f32[48,256]{1,0:T(8,128)}, f32[48,256]{1,0:T(8,128)S(1)}, u32[]{:S(2)}, u32[]{:S(2)}) collective-permute-start(f32[48,256]{1,0:T(8,128)} %param.6), channel_id=1, source_target_pairs={{0,2},{1,3},{2,0},{3,1},{4,6},{5,7},{6,4},{7,5},{8,10},{9,11},{10,... | collective-permute-start | bytes 147464 | tf_op jit(solution)/shard_map/ppermute | solution.py:50
  9.7 9.6 %collective-permute-start.2 = (f32[48,256]{1,0:T(8,128)}, f32[48,256]{1,0:T(8,128)S(1)}, u32[]{:S(2)}, u32[]{:S(2)}) collective-permute-start(f32[48,256]{1,0:T(8,128)} %param.6), channel_id=1, source_target_pairs={{0,6},{1,7},{2,4},{3,5},{4,2},{5,3},{6,0},{7,1},{8,14},{9,15},{10,... | collective-permute-start | bytes 147464 | tf_op jit(solution)/shard_map/ppermute | solution.py:50
  19.3 5.3 %collective-permute-start.3 = (f32[192,256]{1,0:T(8,128)S(1)}, f32[192,256]{1,0:T(8,128)S(1)}, u32[]{:S(2)}, u32[]{:S(2)}) collective-permute-start(f32[192,256]{1,0:T(8,128)S(1)} %get-tuple-element.20), channel_id=1, source_target_pairs={{0,1},{1,0},{2,3},{3,2},{4,5},{5,4},{6,7},{7,6},{8,9},{9,8},{10,11... | collective-permute-start | bytes 589832 | tf_op jit(solution)/shard_map/ppermute | solution.py:50
  24.8 8.7 %collective-permute-start.4 = (f32[384,256]{1,0:T(8,128)S(1)}, f32[384,256]{1,0:T(8,128)S(1)}, u32[]{:S(2)}, u32[]{:S(2)}) collective-permute-start(f32[384,256]{1,0:T(8,128)S(1)} %get-tuple-element.10), channel_id=1, source_target_pairs={{0,8},{1,9},{2,10},{3,11},{4,12},{5,13},{6,14},{7,15},{8,0},{9,1},... | collective-permute-start | bytes 1179656 | tf_op jit(solution)/shard_map/ppermute | solution.py:50
  26.1 18.0 %collective-permute-start.5 = (f32[384,256]{1,0:T(8,128)S(1)}, f32[384,256]{1,0:T(8,128)S(1)}, u32[]{:S(2)}, u32[]{:S(2)}) collective-permute-start(f32[384,256]{1,0:T(8,128)S(1)} %get-tuple-element.10), channel_id=1, source_target_pairs={{0,16},{1,17},{2,18},{3,19},{4,20},{5,21},{6,22},{7,23},{8,24},{9,... | collective-permute-start | bytes 1179656 | tf_op jit(solution)/shard_map/ppermute | solution.py:50
  28.6 15.6 %collective-permute-start.6 = (f32[384,256]{1,0:T(8,128)S(1)}, f32[384,256]{1,0:T(8,128)S(1)}, u32[]{:S(2)}, u32[]{:S(2)}) collective-permute-start(f32[384,256]{1,0:T(8,128)S(1)} %get-tuple-element.10), channel_id=1, source_target_pairs={{0,24},{1,25},{2,26},{3,27},{4,28},{5,29},{6,30},{7,31},{8,16},{9,... | collective-permute-start | bytes 1179656 | tf_op jit(solution)/shard_map/ppermute | solution.py:50
  45.4 33.1 %collective-permute-start.12 = (f32[384,256]{1,0:T(8,128)}, f32[384,256]{1,0:T(8,128)}, u32[]{:S(2)}, u32[]{:S(2)}) collective-permute-start(f32[384,256]{1,0:T(8,128)} %constant_dynamic-slice_fusion), channel_id=1, source_target_pairs={{0,0},{1,1},{2,2},{3,3},{4,32},{5,33},{6,34},{7,35},{8,64},{9,65},... | collective-permute-start | bytes 1179656 | tf_op jit(solution)/shard_map/ppermute | solution.py:152
  62.5 7.6 %collective-permute-start.7 = (f32[96,256]{1,0:T(8,128)}, f32[96,256]{1,0:T(8,128)}, u32[]{:S(2)}, u32[]{:S(2)}) collective-permute-start(f32[96,256]{1,0:T(8,128)} %get-tuple-element.6), channel_id=1, source_target_pairs={{0,32},{32,0},{64,96},{96,64},{128,160},{160,128},{192,224},{224,1... | collective-permute-start | bytes 294920 | tf_op jit(solution)/shard_map/ppermute | solution.py:78
  62.5 12.8 %collective-permute-start.8 = (f32[96,256]{1,0:T(8,128)}, f32[96,256]{1,0:T(8,128)}, u32[]{:S(2)}, u32[]{:S(2)}) collective-permute-start(f32[96,256]{1,0:T(8,128)} %get-tuple-element.8), channel_id=1, source_target_pairs={{0,64},{32,96},{64,0},{96,32},{128,192},{160,224},{192,128},{224,1... | collective-permute-start | bytes 294920 | tf_op jit(solution)/shard_map/ppermute | solution.py:78
  62.5 14.9 %collective-permute-start.9 = (f32[96,256]{1,0:T(8,128)}, f32[96,256]{1,0:T(8,128)}, u32[]{:S(2)}, u32[]{:S(2)}) collective-permute-start(f32[96,256]{1,0:T(8,128)} %get-tuple-element.7), channel_id=1, source_target_pairs={{0,96},{32,64},{64,32},{96,0},{128,224},{160,192},{192,160},{224,1... | collective-permute-start | bytes 294920 | tf_op jit(solution)/shard_map/ppermute | solution.py:78
  78.4 5.1 %collective-permute-start.10 = (f32[48,256]{1,0:T(8,128)S(1)}, f32[48,256]{1,0:T(8,128)S(1)}, u32[]{:S(2)}, u32[]{:S(2)}) collective-permute-start(f32[48,256]{1,0:T(8,128)S(1)} %dynamic-slice_bitcast_fusion.14), channel_id=1, source_target_pairs={{0,128},{32,160},{64,192},{96,224},{128,0},{160,32},{192,64},{224,... | collective-permute-start | bytes 147464 | tf_op jit(solution)/shard_map/ppermute | solution.py:78
  80.8 6.7 %collective-permute-start.13 = (f32[64,256]{1,0:T(8,128)S(1)}, f32[64,256]{1,0:T(8,128)S(1)}, u32[]{:S(2)}, u32[]{:S(2)}) collective-permute-start(f32[64,256]{1,0:T(8,128)S(1)} %get-tuple-element.17), channel_id=1, source_target_pairs={{0,32},{1,33},{2,34},{3,35},{4,36},{5,37},{6,38},{7,39},{8,40},{9,... | collective-permute-start | bytes 196616 | tf_op jit(solution)/shard_map/ppermute | solution.py:78
  81.3 6.1 %collective-permute-start.14 = (f32[64,256]{1,0:T(8,128)S(1)}, f32[64,256]{1,0:T(8,128)S(1)}, u32[]{:S(2)}, u32[]{:S(2)}) collective-permute-start(f32[64,256]{1,0:T(8,128)S(1)} %get-tuple-element.19), channel_id=1, source_target_pairs={{0,64},{1,65},{2,66},{3,67},{4,68},{5,69},{6,70},{7,71},{8,72},{9,... | collective-permute-start | bytes 196616 | tf_op jit(solution)/shard_map/ppermute | solution.py:78
  83.6 9.9 %collective-permute-start.11 = (f32[48,256]{1,0:T(8,128)S(1)}, f32[48,256]{1,0:T(8,128)S(1)}, u32[]{:S(2)}, u32[]{:S(2)}) collective-permute-start(f32[48,256]{1,0:T(8,128)S(1)} %bitcast_add_fusion.2), channel_id=1, source_target_pairs={{0,0},{1,8},{2,16},{3,24},{4,32},{5,40},{6,48},{7,56},{8,64},{9,72... | collective-permute-start | bytes 147464 | tf_op jit(solution)/shard_map/ppermute | solution.py:163
  87.6 6.8 %collective-permute-start.16 = (f32[64,256]{1,0:T(8,128)S(1)}, f32[64,256]{1,0:T(8,128)S(1)}, u32[]{:S(2)}, u32[]{:S(2)}) collective-permute-start(f32[64,256]{1,0:T(8,128)S(1)} %fusion.113), channel_id=1, source_target_pairs={{0,1},{1,0},{2,3},{3,2},{4,5},{5,4},{6,7},{7,6},{8,9},{9,8},{10,11... | collective-permute-start | bytes 196616 | tf_op jit(solution)/shard_map/ppermute | solution.py:50
  88.4 6.0 %collective-permute-start.17 = (f32[64,256]{1,0:T(8,128)S(1)}, f32[64,256]{1,0:T(8,128)S(1)}, u32[]{:S(2)}, u32[]{:S(2)}) collective-permute-start(f32[64,256]{1,0:T(8,128)S(1)} %fusion.113), channel_id=1, source_target_pairs={{0,2},{1,3},{2,0},{3,1},{4,6},{5,7},{6,4},{7,5},{8,10},{9,11},{10,... | collective-permute-start | bytes 196616 | tf_op jit(solution)/shard_map/ppermute | solution.py:50
  91.7 5.2 %collective-permute-start.18 = (f32[64,256]{1,0:T(8,128)S(1)}, f32[64,256]{1,0:T(8,128)S(1)}, u32[]{:S(2)}, u32[]{:S(2)}) collective-permute-start(f32[64,256]{1,0:T(8,128)S(1)} %fusion.113), channel_id=1, source_target_pairs={{0,3},{1,2},{2,1},{3,0},{4,7},{5,6},{6,5},{7,4},{8,11},{9,10},{10,... | collective-permute-start | bytes 196616 | tf_op jit(solution)/shard_map/ppermute | solution.py:50
  96.9 7.1 %collective-permute-start.19 = (f32[64,256]{1,0:T(8,128)S(1)}, f32[64,256]{1,0:T(8,128)S(1)}, u32[]{:S(2)}, u32[]{:S(2)}) collective-permute-start(f32[64,256]{1,0:T(8,128)S(1)} %fusion.174), channel_id=1, source_target_pairs={{0,4},{1,5},{2,6},{3,7},{4,0},{5,1},{6,2},{7,3},{8,12},{9,13},{10,... | collective-permute-start | bytes 196616 | tf_op jit(solution)/shard_map/ppermute | solution.py:50
  101.5 8.1 %collective-permute-start.21 = (f32[64,256]{1,0:T(8,128)S(1)}, f32[64,256]{1,0:T(8,128)S(1)}, u32[]{:S(2)}, u32[]{:S(2)}) collective-permute-start(f32[64,256]{1,0:T(8,128)S(1)} %fusion.174), channel_id=1, source_target_pairs={{0,12},{1,13},{2,14},{3,15},{4,8},{5,9},{6,10},{7,11},{8,4},{9,5},... | collective-permute-start | bytes 196616 | tf_op jit(solution)/shard_map/ppermute | solution.py:50
  109.7 5.8 %collective-permute-start.22 = (f32[64,256]{1,0:T(8,128)S(1)}, f32[64,256]{1,0:T(8,128)S(1)}, u32[]{:S(2)}, u32[]{:S(2)}) collective-permute-start(f32[64,256]{1,0:T(8,128)S(1)} %fusion.173), channel_id=1, source_target_pairs={{0,16},{1,17},{2,18},{3,19},{4,20},{5,21},{6,22},{7,23},{8,24},{9,... | collective-permute-start | bytes 196616 | tf_op jit(solution)/shard_map/ppermute | solution.py:50
  114.1 7.0 %collective-permute-start.24 = (f32[64,256]{1,0:T(8,128)S(1)}, f32[64,256]{1,0:T(8,128)S(1)}, u32[]{:S(2)}, u32[]{:S(2)}) collective-permute-start(f32[64,256]{1,0:T(8,128)S(1)} %fusion.173), channel_id=1, source_target_pairs={{0,144},{1,145},{2,146},{3,147},{4,148},{5,149},{6,150},{7,151},{8... | collective-permute-start | bytes 196616 | tf_op jit(solution)/shard_map/ppermute | solution.py:50
  121.2 7.5 %collective-permute-start.25 = (f32[64,256]{1,0:T(8,128)S(1)}, f32[64,256]{1,0:T(8,128)S(1)}, u32[]{:S(2)}, u32[]{:S(2)}) collective-permute-start(f32[64,256]{1,0:T(8,128)S(1)} %fusion.172), channel_id=1, source_target_pairs={{0,32},{1,33},{2,34},{3,35},{4,36},{5,37},{6,38},{7,39},{8,40},{9,... | collective-permute-start | bytes 196616 | tf_op jit(solution)/shard_map/ppermute | solution.py:50
  126.9 5.2 %collective-permute-start.27 = (f32[64,256]{1,0:T(8,128)S(1)}, f32[64,256]{1,0:T(8,128)S(1)}, u32[]{:S(2)}, u32[]{:S(2)}) collective-permute-start(f32[64,256]{1,0:T(8,128)S(1)} %fusion.172), channel_id=1, source_target_pairs={{0,96},{1,97},{2,98},{3,99},{4,100},{5,101},{6,102},{7,103},{8,104... | collective-permute-start | bytes 196616 | tf_op jit(solution)/shard_map/ppermute | solution.py:50
  (10 other events, 118.7 us)

commit v11 on v10

--- a/solution.py
+++ b/solution.py
@@ -117,11 +117,25 @@
     ]
 
     q = ncol // nrow
-    col_block_perm = [
-        (big * ncol + small, (small // q) * ncol + q * big + small % q)
-        for big in range(nrow)
-        for small in range(ncol)
-    ]
+    z_ring = 8 if ncol % 8 == 0 and q == 4 else 0
+
+    def col_block_of(big, small):
+        if not z_ring:
+            return small % q
+        low = (q * big) % z_ring
+        z = small % z_ring
+        target = z if low <= z < low + q else (z_ring - 1 - z) % z_ring
+        return target - low
+
+    col_block_perm = []
+    for big in range(nrow):
+        slots = {}
+        for small in range(ncol):
+            j = col_block_of(big, small)
+            r = slots.setdefault(j, 0)
+            slots[j] = r + 1
+            col_block_perm.append((big * ncol + small, r * ncol + q * big + j))
+    assert sorted(d for _, d in col_block_perm) == list(range(nrow * ncol))
 
     def inner(trailing_adjoint, panel, panel_adjoint, diag_factor, diag_adjoint):
         r = lax.axis_index("row")
@@ -148,7 +162,10 @@
         )
 
         span = share.shape[0]
-        pick = lax.dynamic_slice_in_dim(gathered, (c % q) * span, span, 0)
+        sends = jnp.asarray(
+            [col_block_of(big, small) for big in range(nrow) for small in range(ncol)], jnp.int32
+        )[r * ncol + c]
+        pick = lax.dynamic_slice_in_dim(gathered, sends * span, span, 0)
         col_panel = lax.ppermute(pick, ALL, col_block_perm)
 
         local_term = mm(inverse.T, mm(panel_adjoint.T, panel) - 2.0 * mm(share.T, col_panel))

time: 138 us -> 138 us (level)
  transfers between devices with their start and end apart: 28 -> 28, of which waited for: 15 -> 14; matrix products, arithmetic and copies ran while one was open for 19% -> 19% of each run, Pallas kernels for 0% -> 0%
where the time goes in v11:
time: 138 us; the launch traced here: 137 us
  starting transfers between devices  58 us (42%)
  waiting for transfers between devices  44.8 us (32%)
  matrix products  17.3 us (13%)
  local copies, waits for them, and re-layouts  13.5 us (10%)
  between operations  2.1 us (2%)
  other arithmetic  1.7 us (1%)
    ppermute x19, starting transfers between devices, exchange(): got.append(lax.ppermute(value, axis, xor_perm(size, offset(k, masks))))  38.3 us
    ppermute x19, waiting for transfers between devices, exchange(): got.append(lax.ppermute(value, axis, xor_perm(size, offset(k, masks))))  36.3 us
    dot_general x23, matrix products, mm(): jnp.dot(a, b, precision=lax.Precision.HIGHEST, preferred_element_type=jnp...  14.6 us
    ppermute x1, starting transfers between devices, inner(): col_panel = lax.ppermute(pick, ALL, col_block_perm)  10.4 us
    ppermute x7, waiting for transfers between devices, scatter_step(): total = total + lax.ppermute(send, axis, xor_perm(size, offset(k, masks)))  8.03 us
    ppermute x7, starting transfers between devices, scatter_step(): total = total + lax.ppermute(send, axis, xor_perm(size, offset(k, masks)))  5 us
    ppermute x1, starting transfers between devices, inner(): product = lax.ppermute(share, ALL, owner_perm)  4.31 us
  transfers between devices with their start and end apart: 28, of which 14 were waited for; matrix products, arithmetic and copies ran while one was open for 19% of the time, Pallas kernels for 0%

profile of v11, /device:TPU:1, one launch (start us, length us, event | category | flops | bytes accessed | tf_op | source)
XLA Modules:
  0.0 137.4 jit_solution(17613751162709589056)
XLA Ops:
  0.7 7.8 %collective-permute-start = (f32[48,256]{1,0:T(8,128)}, f32[48,256]{1,0:T(8,128)S(1)}, u32[]{:S(2)}, u32[]{:S(2)}) collective-permute-start(f32[48,256]{1,0:T(8,128)} %param.7), channel_id=1, source_target_pairs={{0,4},{1,5},{2,6},{3,7},{4,0},{5,1},{6,2},{7,3},{8,12},{9,13},{10,... | collective-permute-start | bytes 147464 | tf_op jit(solution)/shard_map/ppermute | solution.py:50
  9.7 2.6 %gather_fusion = f32[256]{0:T(256)S(1)} fusion(f32[256,256]{1,0:T(8,128)} %param.9, s32[256]{0:T(256)S(1)} %bitcast.137), kind=kCustom, calls=%fused_computation | custom fusion | bytes 4096 | tf_op jit(solution)/shard_map/jit(diagonal)/cond/branch_0_fun/gather | solution.py:16
  21.9 4.1 %collective-permute-done.3 = f32[192,256]{1,0:T(8,128)S(1)} collective-permute-done((f32[192,256]{1,0:T(8,128)S(1)}, f32[192,256]{1,0:T(8,128)S(1)}, u32[]{:S(2)}, u32[]{:S(2)}) %collective-permute-start.3) | collective-permute-done | bytes 196640 | tf_op jit(solution)/shard_map/ppermute | solution.py:50
  27.4 2.4 %collective-permute-start.5 = (f32[384,256]{1,0:T(8,128)S(1)}, f32[384,256]{1,0:T(8,128)S(1)}, u32[]{:S(2)}, u32[]{:S(2)}) collective-permute-start(f32[384,256]{1,0:T(8,128)S(1)} %get-tuple-element.10), channel_id=1, source_target_pairs={{0,16},{1,17},{2,18},{3,19},{4,20},{5,21},{6,22},{7,23},{8,24},{9,... | collective-permute-start | bytes 1179656 | tf_op jit(solution)/shard_map/ppermute | solution.py:50
  30.9 3.8 %collective-permute-done.4 = f32[384,256]{1,0:T(8,128)S(1)} collective-permute-done((f32[384,256]{1,0:T(8,128)S(1)}, f32[384,256]{1,0:T(8,128)S(1)}, u32[]{:S(2)}, u32[]{:S(2)}) %collective-permute-start.4) | collective-permute-done | bytes 393248 | tf_op jit(solution)/shard_map/ppermute | solution.py:50
  34.8 10.7 %collective-permute-done.5 = f32[384,256]{1,0:T(8,128)S(1)} collective-permute-done((f32[384,256]{1,0:T(8,128)S(1)}, f32[384,256]{1,0:T(8,128)S(1)}, u32[]{:S(2)}, u32[]{:S(2)}) %collective-permute-start.5) | collective-permute-done | bytes 393248 | tf_op jit(solution)/shard_map/ppermute | solution.py:50
  46.7 10.4 %collective-permute-start.12 = (f32[384,256]{1,0:T(8,128)}, f32[384,256]{1,0:T(8,128)}, u32[]{:S(2)}, u32[]{:S(2)}) collective-permute-start(f32[384,256]{1,0:T(8,128)} %constant_dynamic-slice_fusion), channel_id=1, source_target_pairs={{0,0},{1,1},{2,2},{3,3},{4,35},{5,34},{6,33},{7,32},{8,64},{9,65},... | collective-permute-start | bytes 1179656 | tf_op jit(solution)/shard_map/ppermute | solution.py:169
  57.1 2.7 %fusion.135 = f32[256,384]{1,0:T(8,128)S(1)} fusion(f32[1536,256]{1,0:T(8,128)S(1)} %bitcast.140, f32[1536,384]{1,0:T(8,128)S(1)} %copy-done), kind=kOutput, calls=%fused_computation.218 | convolution fusion | flops 1811939328 | bytes 4325376 | tf_op jit(solution)/shard_map/dot_general | solution.py:156
  62.5 2.1 %collective-permute-start.9 = (f32[96,256]{1,0:T(8,128)}, f32[96,256]{1,0:T(8,128)}, u32[]{:S(2)}, u32[]{:S(2)}) collective-permute-start(f32[96,256]{1,0:T(8,128)} %get-tuple-element.7), channel_id=1, source_target_pairs={{0,96},{32,64},{64,32},{96,0},{128,224},{160,192},{192,160},{224,1... | collective-permute-start | bytes 294920 | tf_op jit(solution)/shard_map/ppermute | solution.py:78
  67.3 2.7 %dynamic_update_slice.3 = f32[256,256]{1,0:T(8,128)} dynamic-update-slice(f32[256,256]{1,0:T(8,128)} %broadcast_in_dim.46, f32[32,8]{1,0:T(8,128)} %copy.16, s32[]{:T(128)S(6)} %select_n.354, s32[]{:T(128)S(6)} %select_n.355) | dynamic-update-slice | bytes 2052 | tf_op jit(solution)/shard_map/dynamic_update_slice | solution.py:173
  70.0 5.9 %collective-permute-done.8 = f32[96,256]{1,0:T(8,128)} collective-permute-done((f32[96,256]{1,0:T(8,128)}, f32[96,256]{1,0:T(8,128)}, u32[]{:S(2)}, u32[]{:S(2)}) %collective-permute-start.8) | collective-permute-done | bytes 98336 | tf_op jit(solution)/shard_map/ppermute | solution.py:78
  75.9 2.1 %collective-permute-done.9 = f32[96,256]{1,0:T(8,128)} collective-permute-done((f32[96,256]{1,0:T(8,128)}, f32[96,256]{1,0:T(8,128)}, u32[]{:S(2)}, u32[]{:S(2)}) %collective-permute-start.9) | collective-permute-done | bytes 98336 | tf_op jit(solution)/shard_map/ppermute | solution.py:78
  82.1 2.1 %collective-permute-start.14 = (f32[64,256]{1,0:T(8,128)S(1)}, f32[64,256]{1,0:T(8,128)S(1)}, u32[]{:S(2)}, u32[]{:S(2)}) collective-permute-start(f32[64,256]{1,0:T(8,128)S(1)} %get-tuple-element.19), channel_id=1, source_target_pairs={{0,64},{1,65},{2,66},{3,67},{4,68},{5,69},{6,70},{7,71},{8,72},{9,... | collective-permute-start | bytes 196616 | tf_op jit(solution)/shard_map/ppermute | solution.py:78
  84.3 4.3 %collective-permute-start.11 = (f32[48,256]{1,0:T(8,128)S(1)}, f32[48,256]{1,0:T(8,128)S(1)}, u32[]{:S(2)}, u32[]{:S(2)}) collective-permute-start(f32[48,256]{1,0:T(8,128)S(1)} %bitcast_add_fusion.2), channel_id=1, source_target_pairs={{0,0},{1,8},{2,16},{3,24},{4,32},{5,40},{6,48},{7,56},{8,64},{9,72... | collective-permute-start | bytes 147464 | tf_op jit(solution)/shard_map/ppermute | solution.py:180
  89.9 3.3 %collective-permute-start.17 = (f32[64,256]{1,0:T(8,128)S(1)}, f32[64,256]{1,0:T(8,128)S(1)}, u32[]{:S(2)}, u32[]{:S(2)}) collective-permute-start(f32[64,256]{1,0:T(8,128)S(1)} %fusion.113), channel_id=1, source_target_pairs={{0,2},{1,3},{2,0},{3,1},{4,6},{5,7},{6,4},{7,5},{8,10},{9,11},{10,... | collective-permute-start | bytes 196616 | tf_op jit(solution)/shard_map/ppermute | solution.py:50
  95.1 3.3 %collective-permute-done.18 = f32[64,256]{1,0:T(8,128)S(1)} collective-permute-done((f32[64,256]{1,0:T(8,128)S(1)}, f32[64,256]{1,0:T(8,128)S(1)}, u32[]{:S(2)}, u32[]{:S(2)}) %collective-permute-start.18) | collective-permute-done | bytes 65568 | tf_op jit(solution)/shard_map/ppermute | solution.py:50
  98.4 4.5 %collective-permute-start.19 = (f32[64,256]{1,0:T(8,128)S(1)}, f32[64,256]{1,0:T(8,128)S(1)}, u32[]{:S(2)}, u32[]{:S(2)}) collective-permute-start(f32[64,256]{1,0:T(8,128)S(1)} %fusion.174), channel_id=1, source_target_pairs={{0,4},{1,5},{2,6},{3,7},{4,0},{5,1},{6,2},{7,3},{8,12},{9,13},{10,... | collective-permute-start | bytes 196616 | tf_op jit(solution)/shard_map/ppermute | solution.py:50
  103.0 2.0 %collective-permute-start.21 = (f32[64,256]{1,0:T(8,128)S(1)}, f32[64,256]{1,0:T(8,128)S(1)}, u32[]{:S(2)}, u32[]{:S(2)}) collective-permute-start(f32[64,256]{1,0:T(8,128)S(1)} %fusion.174), channel_id=1, source_target_pairs={{0,12},{1,13},{2,14},{3,15},{4,8},{5,9},{6,10},{7,11},{8,4},{9,5},... | collective-permute-start | bytes 196616 | tf_op jit(solution)/shard_map/ppermute | solution.py:50
  106.0 5.0 %collective-permute-done.21 = f32[64,256]{1,0:T(8,128)S(1)} collective-permute-done((f32[64,256]{1,0:T(8,128)S(1)}, f32[64,256]{1,0:T(8,128)S(1)}, u32[]{:S(2)}, u32[]{:S(2)}) %collective-permute-start.21) | collective-permute-done | bytes 65568 | tf_op jit(solution)/shard_map/ppermute | solution.py:50
  113.0 3.8 %collective-permute-start.23 = (f32[64,256]{1,0:T(8,128)S(1)}, f32[64,256]{1,0:T(8,128)S(1)}, u32[]{:S(2)}, u32[]{:S(2)}) collective-permute-start(f32[64,256]{1,0:T(8,128)S(1)} %fusion.173), channel_id=1, source_target_pairs={{0,128},{1,129},{2,130},{3,131},{4,132},{5,133},{6,134},{7,135},{8... | collective-permute-start | bytes 196616 | tf_op jit(solution)/shard_map/ppermute | solution.py:50
  116.9 2.6 %collective-permute-start.24 = (f32[64,256]{1,0:T(8,128)S(1)}, f32[64,256]{1,0:T(8,128)S(1)}, u32[]{:S(2)}, u32[]{:S(2)}) collective-permute-start(f32[64,256]{1,0:T(8,128)S(1)} %fusion.173), channel_id=1, source_target_pairs={{0,144},{1,145},{2,146},{3,147},{4,148},{5,149},{6,150},{7,151},{8... | collective-permute-start | bytes 196616 | tf_op jit(solution)/shard_map/ppermute | solution.py:50
  119.5 4.5 %collective-permute-done.24 = f32[64,256]{1,0:T(8,128)S(1)} collective-permute-done((f32[64,256]{1,0:T(8,128)S(1)}, f32[64,256]{1,0:T(8,128)S(1)}, u32[]{:S(2)}, u32[]{:S(2)}) %collective-permute-start.24) | collective-permute-done | bytes 65568 | tf_op jit(solution)/shard_map/ppermute | solution.py:50
  124.0 3.2 %collective-permute-start.25 = (f32[64,256]{1,0:T(8,128)S(1)}, f32[64,256]{1,0:T(8,128)S(1)}, u32[]{:S(2)}, u32[]{:S(2)}) collective-permute-start(f32[64,256]{1,0:T(8,128)S(1)} %fusion.172), channel_id=1, source_target_pairs={{0,32},{1,33},{2,34},{3,35},{4,36},{5,37},{6,38},{7,39},{8,40},{9,... | collective-permute-start | bytes 196616 | tf_op jit(solution)/shard_map/ppermute | solution.py:50
  133.3 2.3 %gather_fusion.1 = f32[256]{0:T(256)S(1)} fusion(f32[256,256]{1,0:T(8,128)S(1)} %bitcast.141, s32[256]{0:T(256)S(1)} %bitcast.138), kind=kCustom, calls=%fused_computation.1 | custom fusion | bytes 4096 | tf_op jit(solution)/shard_map/jit(_diag)/jit(diagonal)/cond/branch_0_fun/gather | solution.py:29
  (111 shorter events, 36.9 us)
Async XLA Ops:
  0.7 19.9 %collective-permute-start = (f32[48,256]{1,0:T(8,128)}, f32[48,256]{1,0:T(8,128)S(1)}, u32[]{:S(2)}, u32[]{:S(2)}) collective-permute-start(f32[48,256]{1,0:T(8,128)} %param.7), channel_id=1, source_target_pairs={{0,4},{1,5},{2,6},{3,7},{4,0},{5,1},{6,2},{7,3},{8,12},{9,13},{10,... | collective-permute-start | bytes 147464 | tf_op jit(solution)/shard_map/ppermute | solution.py:50
  8.5 12.1 %collective-permute-start.1 = (f32[48,256]{1,0:T(8,128)}, f32[48,256]{1,0:T(8,128)S(1)}, u32[]{:S(2)}, u32[]{:S(2)}) collective-permute-start(f32[48,256]{1,0:T(8,128)} %param.7), channel_id=1, source_target_pairs={{0,2},{1,3},{2,0},{3,1},{4,6},{5,7},{6,4},{7,5},{8,10},{9,11},{10,... | collective-permute-start | bytes 147464 | tf_op jit(solution)/shard_map/ppermute | solution.py:50
  9.7 10.9 %collective-permute-start.2 = (f32[48,256]{1,0:T(8,128)}, f32[48,256]{1,0:T(8,128)S(1)}, u32[]{:S(2)}, u32[]{:S(2)}) collective-permute-start(f32[48,256]{1,0:T(8,128)} %param.7), channel_id=1, source_target_pairs={{0,6},{1,7},{2,4},{3,5},{4,2},{5,3},{6,0},{7,1},{8,14},{9,15},{10,... | collective-permute-start | bytes 147464 | tf_op jit(solution)/shard_map/ppermute | solution.py:50
  20.6 5.3 %collective-permute-start.3 = (f32[192,256]{1,0:T(8,128)S(1)}, f32[192,256]{1,0:T(8,128)S(1)}, u32[]{:S(2)}, u32[]{:S(2)}) collective-permute-start(f32[192,256]{1,0:T(8,128)S(1)} %get-tuple-element.20), channel_id=1, source_target_pairs={{0,1},{1,0},{2,3},{3,2},{4,5},{5,4},{6,7},{7,6},{8,9},{9,8},{10,11... | collective-permute-start | bytes 589832 | tf_op jit(solution)/shard_map/ppermute | solution.py:50
  26.1 8.7 %collective-permute-start.4 = (f32[384,256]{1,0:T(8,128)S(1)}, f32[384,256]{1,0:T(8,128)S(1)}, u32[]{:S(2)}, u32[]{:S(2)}) collective-permute-start(f32[384,256]{1,0:T(8,128)S(1)} %get-tuple-element.10), channel_id=1, source_target_pairs={{0,8},{1,9},{2,10},{3,11},{4,12},{5,13},{6,14},{7,15},{8,0},{9,1},... | collective-permute-start | bytes 1179656 | tf_op jit(solution)/shard_map/ppermute | solution.py:50
  27.4 18.0 %collective-permute-start.5 = (f32[384,256]{1,0:T(8,128)S(1)}, f32[384,256]{1,0:T(8,128)S(1)}, u32[]{:S(2)}, u32[]{:S(2)}) collective-permute-start(f32[384,256]{1,0:T(8,128)S(1)} %get-tuple-element.10), channel_id=1, source_target_pairs={{0,16},{1,17},{2,18},{3,19},{4,20},{5,21},{6,22},{7,23},{8,24},{9,... | collective-permute-start | bytes 1179656 | tf_op jit(solution)/shard_map/ppermute | solution.py:50
  29.9 15.6 %collective-permute-start.6 = (f32[384,256]{1,0:T(8,128)S(1)}, f32[384,256]{1,0:T(8,128)S(1)}, u32[]{:S(2)}, u32[]{:S(2)}) collective-permute-start(f32[384,256]{1,0:T(8,128)S(1)} %get-tuple-element.10), channel_id=1, source_target_pairs={{0,24},{1,25},{2,26},{3,27},{4,28},{5,29},{6,30},{7,31},{8,16},{9,... | collective-permute-start | bytes 1179656 | tf_op jit(solution)/shard_map/ppermute | solution.py:50
  46.7 32.5 %collective-permute-start.12 = (f32[384,256]{1,0:T(8,128)}, f32[384,256]{1,0:T(8,128)}, u32[]{:S(2)}, u32[]{:S(2)}) collective-permute-start(f32[384,256]{1,0:T(8,128)} %constant_dynamic-slice_fusion), channel_id=1, source_target_pairs={{0,0},{1,1},{2,2},{3,3},{4,35},{5,34},{6,33},{7,32},{8,64},{9,65},... | collective-permute-start | bytes 1179656 | tf_op jit(solution)/shard_map/ppermute | solution.py:169
  62.5 7.6 %collective-permute-start.7 = (f32[96,256]{1,0:T(8,128)}, f32[96,256]{1,0:T(8,128)}, u32[]{:S(2)}, u32[]{:S(2)}) collective-permute-start(f32[96,256]{1,0:T(8,128)} %get-tuple-element.6), channel_id=1, source_target_pairs={{0,32},{32,0},{64,96},{96,64},{128,160},{160,128},{192,224},{224,1... | collective-permute-start | bytes 294920 | tf_op jit(solution)/shard_map/ppermute | solution.py:78
  62.5 13.5 %collective-permute-start.8 = (f32[96,256]{1,0:T(8,128)}, f32[96,256]{1,0:T(8,128)}, u32[]{:S(2)}, u32[]{:S(2)}) collective-permute-start(f32[96,256]{1,0:T(8,128)} %get-tuple-element.8), channel_id=1, source_target_pairs={{0,64},{32,96},{64,0},{96,32},{128,192},{160,224},{192,128},{224,1... | collective-permute-start | bytes 294920 | tf_op jit(solution)/shard_map/ppermute | solution.py:78
  62.5 15.6 %collective-permute-start.9 = (f32[96,256]{1,0:T(8,128)}, f32[96,256]{1,0:T(8,128)}, u32[]{:S(2)}, u32[]{:S(2)}) collective-permute-start(f32[96,256]{1,0:T(8,128)} %get-tuple-element.7), channel_id=1, source_target_pairs={{0,96},{32,64},{64,32},{96,0},{128,224},{160,192},{192,160},{224,1... | collective-permute-start | bytes 294920 | tf_op jit(solution)/shard_map/ppermute | solution.py:78
  79.1 5.1 %collective-permute-start.10 = (f32[48,256]{1,0:T(8,128)S(1)}, f32[48,256]{1,0:T(8,128)S(1)}, u32[]{:S(2)}, u32[]{:S(2)}) collective-permute-start(f32[48,256]{1,0:T(8,128)S(1)} %dynamic-slice_bitcast_fusion.14), channel_id=1, source_target_pairs={{0,128},{32,160},{64,192},{96,224},{128,0},{160,32},{192,64},{224,... | collective-permute-start | bytes 147464 | tf_op jit(solution)/shard_map/ppermute | solution.py:78
  81.5 7.1 %collective-permute-start.13 = (f32[64,256]{1,0:T(8,128)S(1)}, f32[64,256]{1,0:T(8,128)S(1)}, u32[]{:S(2)}, u32[]{:S(2)}) collective-permute-start(f32[64,256]{1,0:T(8,128)S(1)} %get-tuple-element.17), channel_id=1, source_target_pairs={{0,32},{1,33},{2,34},{3,35},{4,36},{5,37},{6,38},{7,39},{8,40},{9,... | collective-permute-start | bytes 196616 | tf_op jit(solution)/shard_map/ppermute | solution.py:78
  82.1 6.6 %collective-permute-start.14 = (f32[64,256]{1,0:T(8,128)S(1)}, f32[64,256]{1,0:T(8,128)S(1)}, u32[]{:S(2)}, u32[]{:S(2)}) collective-permute-start(f32[64,256]{1,0:T(8,128)S(1)} %get-tuple-element.19), channel_id=1, source_target_pairs={{0,64},{1,65},{2,66},{3,67},{4,68},{5,69},{6,70},{7,71},{8,72},{9,... | collective-permute-start | bytes 196616 | tf_op jit(solution)/shard_map/ppermute | solution.py:78
  84.3 9.4 %collective-permute-start.11 = (f32[48,256]{1,0:T(8,128)S(1)}, f32[48,256]{1,0:T(8,128)S(1)}, u32[]{:S(2)}, u32[]{:S(2)}) collective-permute-start(f32[48,256]{1,0:T(8,128)S(1)} %bitcast_add_fusion.2), channel_id=1, source_target_pairs={{0,0},{1,8},{2,16},{3,24},{4,32},{5,40},{6,48},{7,56},{8,64},{9,72... | collective-permute-start | bytes 147464 | tf_op jit(solution)/shard_map/ppermute | solution.py:180
  88.7 5.9 %collective-permute-start.16 = (f32[64,256]{1,0:T(8,128)S(1)}, f32[64,256]{1,0:T(8,128)S(1)}, u32[]{:S(2)}, u32[]{:S(2)}) collective-permute-start(f32[64,256]{1,0:T(8,128)S(1)} %fusion.113), channel_id=1, source_target_pairs={{0,1},{1,0},{2,3},{3,2},{4,5},{5,4},{6,7},{7,6},{8,9},{9,8},{10,11... | collective-permute-start | bytes 196616 | tf_op jit(solution)/shard_map/ppermute | solution.py:50
  89.9 5.2 %collective-permute-start.17 = (f32[64,256]{1,0:T(8,128)S(1)}, f32[64,256]{1,0:T(8,128)S(1)}, u32[]{:S(2)}, u32[]{:S(2)}) collective-permute-start(f32[64,256]{1,0:T(8,128)S(1)} %fusion.113), channel_id=1, source_target_pairs={{0,2},{1,3},{2,0},{3,1},{4,6},{5,7},{6,4},{7,5},{8,10},{9,11},{10,... | collective-permute-start | bytes 196616 | tf_op jit(solution)/shard_map/ppermute | solution.py:50
  93.2 5.2 %collective-permute-start.18 = (f32[64,256]{1,0:T(8,128)S(1)}, f32[64,256]{1,0:T(8,128)S(1)}, u32[]{:S(2)}, u32[]{:S(2)}) collective-permute-start(f32[64,256]{1,0:T(8,128)S(1)} %fusion.113), channel_id=1, source_target_pairs={{0,3},{1,2},{2,1},{3,0},{4,7},{5,6},{6,5},{7,4},{8,11},{9,10},{10,... | collective-permute-start | bytes 196616 | tf_op jit(solution)/shard_map/ppermute | solution.py:50
  98.4 7.1 %collective-permute-start.19 = (f32[64,256]{1,0:T(8,128)S(1)}, f32[64,256]{1,0:T(8,128)S(1)}, u32[]{:S(2)}, u32[]{:S(2)}) collective-permute-start(f32[64,256]{1,0:T(8,128)S(1)} %fusion.174), channel_id=1, source_target_pairs={{0,4},{1,5},{2,6},{3,7},{4,0},{5,1},{6,2},{7,3},{8,12},{9,13},{10,... | collective-permute-start | bytes 196616 | tf_op jit(solution)/shard_map/ppermute | solution.py:50
  103.0 8.0 %collective-permute-start.21 = (f32[64,256]{1,0:T(8,128)S(1)}, f32[64,256]{1,0:T(8,128)S(1)}, u32[]{:S(2)}, u32[]{:S(2)}) collective-permute-start(f32[64,256]{1,0:T(8,128)S(1)} %fusion.174), channel_id=1, source_target_pairs={{0,12},{1,13},{2,14},{3,15},{4,8},{5,9},{6,10},{7,11},{8,4},{9,5},... | collective-permute-start | bytes 196616 | tf_op jit(solution)/shard_map/ppermute | solution.py:50
  111.1 8.4 %collective-permute-start.22 = (f32[64,256]{1,0:T(8,128)S(1)}, f32[64,256]{1,0:T(8,128)S(1)}, u32[]{:S(2)}, u32[]{:S(2)}) collective-permute-start(f32[64,256]{1,0:T(8,128)S(1)} %fusion.173), channel_id=1, source_target_pairs={{0,16},{1,17},{2,18},{3,19},{4,20},{5,21},{6,22},{7,23},{8,24},{9,... | collective-permute-start | bytes 196616 | tf_op jit(solution)/shard_map/ppermute | solution.py:50
  113.0 6.5 %collective-permute-start.23 = (f32[64,256]{1,0:T(8,128)S(1)}, f32[64,256]{1,0:T(8,128)S(1)}, u32[]{:S(2)}, u32[]{:S(2)}) collective-permute-start(f32[64,256]{1,0:T(8,128)S(1)} %fusion.173), channel_id=1, source_target_pairs={{0,128},{1,129},{2,130},{3,131},{4,132},{5,133},{6,134},{7,135},{8... | collective-permute-start | bytes 196616 | tf_op jit(solution)/shard_map/ppermute | solution.py:50
  116.9 7.1 %collective-permute-start.24 = (f32[64,256]{1,0:T(8,128)S(1)}, f32[64,256]{1,0:T(8,128)S(1)}, u32[]{:S(2)}, u32[]{:S(2)}) collective-permute-start(f32[64,256]{1,0:T(8,128)S(1)} %fusion.173), channel_id=1, source_target_pairs={{0,144},{1,145},{2,146},{3,147},{4,148},{5,149},{6,150},{7,151},{8... | collective-permute-start | bytes 196616 | tf_op jit(solution)/shard_map/ppermute | solution.py:50
  127.3 5.2 %collective-permute-start.27 = (f32[64,256]{1,0:T(8,128)S(1)}, f32[64,256]{1,0:T(8,128)S(1)}, u32[]{:S(2)}, u32[]{:S(2)}) collective-permute-start(f32[64,256]{1,0:T(8,128)S(1)} %fusion.172), channel_id=1, source_target_pairs={{0,96},{1,97},{2,98},{3,99},{4,100},{5,101},{6,102},{7,103},{8,104... | collective-permute-start | bytes 196616 | tf_op jit(solution)/shard_map/ppermute | solution.py:50
  (11 other events, 122.7 us)

commit v12 on v11

--- a/solution.py
+++ b/solution.py
@@ -144,7 +144,14 @@
 
         groups = gather_groups(ncol)
         gathered = panel
-        for masks in groups:
+        rows, cols = diag_adjoint.shape
+        placed = lax.dynamic_update_slice(
+            jnp.zeros((rows * nrow, cols * ncol), jnp.float32), diag_adjoint, (r * rows, c * cols)
+        )
+        own_term = mm(panel_adjoint.T, panel)
+        for step, masks in enumerate(groups):
+            if step == 1:
+                gathered, placed, own_term = lax.optimization_barrier((gathered, placed, own_term))
             gathered = gather_step(gathered, "col", ncol, masks)
         order = [m for masks in groups for m in masks]
         blocks = gathered.reshape((2,) * len(order) + panel.shape)
@@ -168,12 +175,9 @@
         pick = lax.dynamic_slice_in_dim(gathered, sends * span, span, 0)
         col_panel = lax.ppermute(pick, ALL, col_block_perm)
 
-        local_term = mm(inverse.T, mm(panel_adjoint.T, panel) - 2.0 * mm(share.T, col_panel))
-        rows, cols = diag_adjoint.shape
-        placed = lax.dynamic_update_slice(
-            jnp.zeros((rows * nrow, cols * ncol), jnp.float32), diag_adjoint, (r * rows, c * cols)
-        )
-        accumulated = all_reduce(placed - local_term, nrow, ncol)
+        local_term = mm(inverse.T, own_term - 2.0 * mm(share.T, col_panel))
+        share, reduced = lax.optimization_barrier((share, placed - local_term))
+        accumulated = all_reduce(reduced, nrow, ncol)
 
         for masks in row_groups:
             share = scatter_step(share, "row", nrow, masks)

time: 138 us -> 136 us (0.986)
  waiting for transfers between devices: 44.8 us -> 31 us
  starting transfers between devices: 58 us -> 68.5 us
  local copies, waits for them, and re-layouts: 13.5 us -> 11.5 us
  other arithmetic: 1.7 us -> 3.35 us
  matrix products: 17.3 us -> 18.8 us
    ppermute x19, waiting for transfers between devices: 36.3 us -> 25.3 us  [exchange(): got.append(lax.ppermute(value, axis, xor_perm(size, offset(k, masks))))]
    ppermute x7, starting transfers between devices: 5 us -> 15.4 us  [scatter_step(): total = total + lax.ppermute(send, axis, xor_perm(size, offset(k, masks)))]
    ppermute x7, waiting for transfers between devices: 8.03 us -> 0.47 us  [scatter_step(): total = total + lax.ppermute(send, axis, xor_perm(size, offset(k, masks)))]
    ppermute x1, waiting for transfers between devices: 0.01 us -> 5.28 us  [inner(): col_panel = lax.ppermute(pick, ALL, col_block_perm)]
    dynamic_update_slice x1, local copies, waits for them, and re-layouts: 2.69 us -> 0.86 us  [inner(): lax.dynamic_update_slice(jnp.zeros((rows * nrow, cols * ncol), jnp.float3...]
    dot_general x1, matrix products: 2.69 us -> 4.15 us  [inner(): lax.dot_general(trailing_adjoint, gathered, (((0,), (0,)), ((), ())), pre...]
  transfers between devices with their start and end apart: 28 -> 28, of which waited for: 14 -> 10; matrix products, arithmetic and copies ran while one was open for 19% -> 16% of each run, Pallas kernels for 0% -> 0%
where the time goes in v12:
time: 136 us; the launch traced here: 135 us
  starting transfers between devices  68.5 us (50%)
  waiting for transfers between devices  31 us (23%)
  matrix products  18.8 us (14%)
  local copies, waits for them, and re-layouts  11.5 us (8%)
  other arithmetic  3.35 us (2%)
  between operations  2.12 us (2%)
    ppermute x19, starting transfers between devices, exchange(): got.append(lax.ppermute(value, axis, xor_perm(size, offset(k, masks))))  37.5 us
    ppermute x19, waiting for transfers between devices, exchange(): got.append(lax.ppermute(value, axis, xor_perm(size, offset(k, masks))))  25.3 us
    ppermute x7, starting transfers between devices, scatter_step(): total = total + lax.ppermute(send, axis, xor_perm(size, offset(k, masks)))  15.4 us
    dot_general x23, matrix products, mm(): jnp.dot(a, b, precision=lax.Precision.HIGHEST, preferred_element_type=jnp...  14.6 us
    ppermute x1, starting transfers between devices, inner(): col_panel = lax.ppermute(pick, ALL, col_block_perm)  10.2 us
    ppermute x1, starting transfers between devices, inner(): product = lax.ppermute(share, ALL, owner_perm)  5.47 us
    ppermute x1, waiting for transfers between devices, inner(): col_panel = lax.ppermute(pick, ALL, col_block_perm)  5.28 us
    dot_general x1, matrix products, inner(): lax.dot_general(trailing_adjoint, gathered, (((0,), (0,)), ((), ())), pre...  4.15 us
  transfers between devices with their start and end apart: 28, of which 10 were waited for; matrix products, arithmetic and copies ran while one was open for 16% of the time, Pallas kernels for 0%

profile of v12, /device:TPU:1, one launch (start us, length us, event | category | flops | bytes accessed | tf_op | source)
XLA Modules:
  0.0 135.3 jit_solution(16833835855594484847)
XLA Ops:
  0.7 7.8 %collective-permute-start = (f32[48,256]{1,0:T(8,128)}, f32[48,256]{1,0:T(8,128)S(1)}, u32[]{:S(2)}, u32[]{:S(2)}) collective-permute-start(f32[48,256]{1,0:T(8,128)} %param.7), channel_id=1, source_target_pairs={{0,4},{1,5},{2,6},{3,7},{4,0},{5,1},{6,2},{7,3},{8,12},{9,13},{10,... | collective-permute-start | bytes 147464 | tf_op jit(solution)/shard_map/ppermute | solution.py:50
  10.9 2.6 %gather_fusion = f32[256]{0:T(256)S(1)} fusion(f32[256,256]{1,0:T(8,128)} %param.9, s32[256]{0:T(256)S(1)} %bitcast.136), kind=kCustom, calls=%fused_computation | custom fusion | bytes 4096 | tf_op jit(solution)/shard_map/jit(diagonal)/cond/branch_0_fun/gather | solution.py:16
  24.8 3.7 %collective-permute-done.3 = f32[192,256]{1,0:T(8,128)S(1)} collective-permute-done((f32[192,256]{1,0:T(8,128)S(1)}, f32[192,256]{1,0:T(8,128)S(1)}, u32[]{:S(2)}, u32[]{:S(2)}) %collective-permute-start.3) | collective-permute-done | bytes 196640 | tf_op jit(solution)/shard_map/ppermute | solution.py:50
  30.3 2.2 %collective-permute-start.5 = (f32[384,256]{1,0:T(8,128)S(1)}, f32[384,256]{1,0:T(8,128)S(1)}, u32[]{:S(2)}, u32[]{:S(2)}) collective-permute-start(f32[384,256]{1,0:T(8,128)S(1)} %get-tuple-element.20), channel_id=1, source_target_pairs={{0,16},{1,17},{2,18},{3,19},{4,20},{5,21},{6,22},{7,23},{8,24},{9,... | collective-permute-start | bytes 1179656 | tf_op jit(solution)/shard_map/ppermute | solution.py:50
  33.6 3.8 %collective-permute-done.4 = f32[384,256]{1,0:T(8,128)S(1)} collective-permute-done((f32[384,256]{1,0:T(8,128)S(1)}, f32[384,256]{1,0:T(8,128)S(1)}, u32[]{:S(2)}, u32[]{:S(2)}) %collective-permute-start.4) | collective-permute-done | bytes 393248 | tf_op jit(solution)/shard_map/ppermute | solution.py:50
  37.4 10.7 %collective-permute-done.5 = f32[384,256]{1,0:T(8,128)S(1)} collective-permute-done((f32[384,256]{1,0:T(8,128)S(1)}, f32[384,256]{1,0:T(8,128)S(1)}, u32[]{:S(2)}, u32[]{:S(2)}) %collective-permute-start.5) | collective-permute-done | bytes 393248 | tf_op jit(solution)/shard_map/ppermute | solution.py:50
  50.6 10.2 %collective-permute-start.7 = (f32[384,256]{1,0:T(8,128)}, f32[384,256]{1,0:T(8,128)}, u32[]{:S(2)}, u32[]{:S(2)}) collective-permute-start(f32[384,256]{1,0:T(8,128)} %constant_dynamic-slice_fusion), channel_id=1, source_target_pairs={{0,0},{1,1},{2,2},{3,3},{4,35},{5,34},{6,33},{7,32},{8,64},{9,65},... | collective-permute-start | bytes 1179656 | tf_op jit(solution)/shard_map/ppermute | solution.py:176
  61.3 4.1 %fusion.135 = f32[256,384]{1,0:T(8,128)S(1)} fusion(f32[1536,256]{1,0:T(8,128)} %bitcast.139, f32[1536,384]{1,0:T(8,128)S(1)} %copy-done), kind=kOutput, calls=%fused_computation.218 | convolution fusion | flops 1811939328 | bytes 4325376 | tf_op jit(solution)/shard_map/dot_general | solution.py:163
  65.5 5.3 %collective-permute-done.7 = f32[384,256]{1,0:T(8,128)} collective-permute-done((f32[384,256]{1,0:T(8,128)}, f32[384,256]{1,0:T(8,128)}, u32[]{:S(2)}, u32[]{:S(2)}) %collective-permute-start.7) | collective-permute-done | bytes 393248 | tf_op jit(solution)/shard_map/ppermute | solution.py:176
  70.8 1.6 %fusion = f32[256,256]{1,0:T(8,128)S(1)} fusion(f32[256,256]{1,0:T(8,128)S(1)} %fusion.134, f32[256,384]{1,0:T(8,128)S(1)} %fusion.135, f32[384,256]{1,0:T(8,128)} %collective-permute-done.7), kind=kOutput, calls=%fused_computation.15 | convolution fusion | flops 302120960 | bytes 1310720 | tf_op jit(solution)/shard_map/dot_general | solution.py:10
  73.7 9.4 %collective-permute-start.14 = (f32[64,256]{1,0:T(8,128)}, f32[64,256]{1,0:T(8,128)}, u32[]{:S(2)}, u32[]{:S(2)}) collective-permute-start(f32[64,256]{1,0:T(8,128)} %get-tuple-element.29), channel_id=1, source_target_pairs={{0,64},{1,65},{2,66},{3,67},{4,68},{5,69},{6,70},{7,71},{8,72},{9,... | collective-permute-start | bytes 196616 | tf_op jit(solution)/shard_map/ppermute | solution.py:78
  85.0 1.8 %collective-permute-start.10 = (f32[96,256]{1,0:T(8,128)S(1)}, f32[96,256]{1,0:T(8,128)S(1)}, u32[]{:S(2)}, u32[]{:S(2)}) collective-permute-start(f32[96,256]{1,0:T(8,128)S(1)} %get-tuple-element.17), channel_id=1, source_target_pairs={{0,96},{32,64},{64,32},{96,0},{128,224},{160,192},{192,160},{224,1... | collective-permute-start | bytes 294920 | tf_op jit(solution)/shard_map/ppermute | solution.py:78
  90.2 1.7 %collective-permute-start.18 = (f32[64,256]{1,0:T(8,128)S(1)}, f32[64,256]{1,0:T(8,128)S(1)}, u32[]{:S(2)}, u32[]{:S(2)}) collective-permute-start(f32[64,256]{1,0:T(8,128)S(1)} %fusion.113), channel_id=1, source_target_pairs={{0,3},{1,2},{2,1},{3,0},{4,7},{5,6},{6,5},{7,4},{8,11},{9,10},{10,... | collective-permute-start | bytes 196616 | tf_op jit(solution)/shard_map/ppermute | solution.py:50
  92.9 3.8 %collective-permute-start.11 = (f32[48,256]{1,0:T(8,128)S(1)}, f32[48,256]{1,0:T(8,128)S(1)}, u32[]{:S(2)}, u32[]{:S(2)}) collective-permute-start(f32[48,256]{1,0:T(8,128)S(1)} %dynamic-slice_bitcast_fusion.14), channel_id=1, source_target_pairs={{0,128},{32,160},{64,192},{96,224},{128,0},{160,32},{192,64},{224,... | collective-permute-start | bytes 147464 | tf_op jit(solution)/shard_map/ppermute | solution.py:78
  96.9 2.9 %collective-permute-start.19 = (f32[64,256]{1,0:T(8,128)S(1)}, f32[64,256]{1,0:T(8,128)S(1)}, u32[]{:S(2)}, u32[]{:S(2)}) collective-permute-start(f32[64,256]{1,0:T(8,128)S(1)} %fusion.173), channel_id=1, source_target_pairs={{0,4},{1,5},{2,6},{3,7},{4,0},{5,1},{6,2},{7,3},{8,12},{9,13},{10,... | collective-permute-start | bytes 196616 | tf_op jit(solution)/shard_map/ppermute | solution.py:50
  99.7 4.0 %collective-permute-start.21 = (f32[64,256]{1,0:T(8,128)S(1)}, f32[64,256]{1,0:T(8,128)S(1)}, u32[]{:S(2)}, u32[]{:S(2)}) collective-permute-start(f32[64,256]{1,0:T(8,128)S(1)} %fusion.173), channel_id=1, source_target_pairs={{0,12},{1,13},{2,14},{3,15},{4,8},{5,9},{6,10},{7,11},{8,4},{9,5},... | collective-permute-start | bytes 196616 | tf_op jit(solution)/shard_map/ppermute | solution.py:50
  103.7 5.5 %collective-permute-start.12 = (f32[48,256]{1,0:T(8,128)S(1)}, f32[48,256]{1,0:T(8,128)S(1)}, u32[]{:S(2)}, u32[]{:S(2)}) collective-permute-start(f32[48,256]{1,0:T(8,128)S(1)} %bitcast_add_fusion.2), channel_id=1, source_target_pairs={{0,0},{1,8},{2,16},{3,24},{4,32},{5,40},{6,48},{7,56},{8,64},{9,72... | collective-permute-start | bytes 147464 | tf_op jit(solution)/shard_map/ppermute | solution.py:184
  109.3 6.7 %collective-permute-start.22 = (f32[64,256]{1,0:T(8,128)S(1)}, f32[64,256]{1,0:T(8,128)S(1)}, u32[]{:S(2)}, u32[]{:S(2)}) collective-permute-start(f32[64,256]{1,0:T(8,128)S(1)} %fusion.172), channel_id=1, source_target_pairs={{0,16},{1,17},{2,18},{3,19},{4,20},{5,21},{6,22},{7,23},{8,24},{9,... | collective-permute-start | bytes 196616 | tf_op jit(solution)/shard_map/ppermute | solution.py:50
  116.3 2.5 %collective-permute-start.24 = (f32[64,256]{1,0:T(8,128)S(1)}, f32[64,256]{1,0:T(8,128)S(1)}, u32[]{:S(2)}, u32[]{:S(2)}) collective-permute-start(f32[64,256]{1,0:T(8,128)S(1)} %fusion.172), channel_id=1, source_target_pairs={{0,144},{1,145},{2,146},{3,147},{4,148},{5,149},{6,150},{7,151},{8... | collective-permute-start | bytes 196616 | tf_op jit(solution)/shard_map/ppermute | solution.py:50
  121.2 2.1 %collective-permute-done.24 = f32[64,256]{1,0:T(8,128)S(1)} collective-permute-done((f32[64,256]{1,0:T(8,128)S(1)}, f32[64,256]{1,0:T(8,128)S(1)}, u32[]{:S(2)}, u32[]{:S(2)}) %collective-permute-start.24) | collective-permute-done | bytes 65568 | tf_op jit(solution)/shard_map/ppermute | solution.py:50
  123.4 1.7 %collective-permute-start.25 = (f32[64,256]{1,0:T(8,128)S(1)}, f32[64,256]{1,0:T(8,128)S(1)}, u32[]{:S(2)}, u32[]{:S(2)}) collective-permute-start(f32[64,256]{1,0:T(8,128)S(1)} %fusion.171), channel_id=1, source_target_pairs={{0,32},{1,33},{2,34},{3,35},{4,36},{5,37},{6,38},{7,39},{8,40},{9,... | collective-permute-start | bytes 196616 | tf_op jit(solution)/shard_map/ppermute | solution.py:50
  126.9 1.8 %collective-permute-done.26 = f32[64,256]{1,0:T(8,128)S(1)} collective-permute-done((f32[64,256]{1,0:T(8,128)S(1)}, f32[64,256]{1,0:T(8,128)S(1)}, u32[]{:S(2)}, u32[]{:S(2)}) %collective-permute-start.26) | collective-permute-done | bytes 65568 | tf_op jit(solution)/shard_map/ppermute | solution.py:50
  128.7 1.7 %collective-permute-done.27 = f32[64,256]{1,0:T(8,128)S(1)} collective-permute-done((f32[64,256]{1,0:T(8,128)S(1)}, f32[64,256]{1,0:T(8,128)S(1)}, u32[]{:S(2)}, u32[]{:S(2)}) %collective-permute-start.27) | collective-permute-done | bytes 65568 | tf_op jit(solution)/shard_map/ppermute | solution.py:50
  131.2 2.3 %gather_fusion.1 = f32[256]{0:T(256)S(1)} fusion(f32[256,256]{1,0:T(8,128)S(1)} %bitcast.140, s32[256]{0:T(256)S(1)} %bitcast.137), kind=kCustom, calls=%fused_computation.1 | custom fusion | bytes 4096 | tf_op jit(solution)/shard_map/jit(_diag)/jit(diagonal)/cond/branch_0_fun/gather | solution.py:29
  (115 shorter events, 33.1 us)
Async XLA Ops:
  0.7 21.6 %collective-permute-start = (f32[48,256]{1,0:T(8,128)}, f32[48,256]{1,0:T(8,128)S(1)}, u32[]{:S(2)}, u32[]{:S(2)}) collective-permute-start(f32[48,256]{1,0:T(8,128)} %param.7), channel_id=1, source_target_pairs={{0,4},{1,5},{2,6},{3,7},{4,0},{5,1},{6,2},{7,3},{8,12},{9,13},{10,... | collective-permute-start | bytes 147464 | tf_op jit(solution)/shard_map/ppermute | solution.py:50
  8.5 13.8 %collective-permute-start.1 = (f32[48,256]{1,0:T(8,128)}, f32[48,256]{1,0:T(8,128)}, u32[]{:S(2)}, u32[]{:S(2)}) collective-permute-start(f32[48,256]{1,0:T(8,128)} %param.7), channel_id=1, source_target_pairs={{0,2},{1,3},{2,0},{3,1},{4,6},{5,7},{6,4},{7,5},{8,10},{9,11},{10,... | collective-permute-start | bytes 147464 | tf_op jit(solution)/shard_map/ppermute | solution.py:50
  9.7 12.6 %collective-permute-start.2 = (f32[48,256]{1,0:T(8,128)}, f32[48,256]{1,0:T(8,128)}, u32[]{:S(2)}, u32[]{:S(2)}) collective-permute-start(f32[48,256]{1,0:T(8,128)} %param.7), channel_id=1, source_target_pairs={{0,6},{1,7},{2,4},{3,5},{4,2},{5,3},{6,0},{7,1},{8,14},{9,15},{10,... | collective-permute-start | bytes 147464 | tf_op jit(solution)/shard_map/ppermute | solution.py:50
  23.2 5.3 %collective-permute-start.3 = (f32[192,256]{1,0:T(8,128)S(1)}, f32[192,256]{1,0:T(8,128)S(1)}, u32[]{:S(2)}, u32[]{:S(2)}) collective-permute-start(f32[192,256]{1,0:T(8,128)S(1)} %pad_maximum_fusion.8), channel_id=1, source_target_pairs={{0,1},{1,0},{2,3},{3,2},{4,5},{5,4},{6,7},{7,6},{8,9},{9,8},{10,11... | collective-permute-start | bytes 589832 | tf_op jit(solution)/shard_map/ppermute | solution.py:50
  28.7 8.7 %collective-permute-start.4 = (f32[384,256]{1,0:T(8,128)S(1)}, f32[384,256]{1,0:T(8,128)S(1)}, u32[]{:S(2)}, u32[]{:S(2)}) collective-permute-start(f32[384,256]{1,0:T(8,128)S(1)} %get-tuple-element.20), channel_id=1, source_target_pairs={{0,8},{1,9},{2,10},{3,11},{4,12},{5,13},{6,14},{7,15},{8,0},{9,1},... | collective-permute-start | bytes 1179656 | tf_op jit(solution)/shard_map/ppermute | solution.py:50
  30.3 17.8 %collective-permute-start.5 = (f32[384,256]{1,0:T(8,128)S(1)}, f32[384,256]{1,0:T(8,128)S(1)}, u32[]{:S(2)}, u32[]{:S(2)}) collective-permute-start(f32[384,256]{1,0:T(8,128)S(1)} %get-tuple-element.20), channel_id=1, source_target_pairs={{0,16},{1,17},{2,18},{3,19},{4,20},{5,21},{6,22},{7,23},{8,24},{9,... | collective-permute-start | bytes 1179656 | tf_op jit(solution)/shard_map/ppermute | solution.py:50
  32.5 15.6 %collective-permute-start.6 = (f32[384,256]{1,0:T(8,128)S(1)}, f32[384,256]{1,0:T(8,128)S(1)}, u32[]{:S(2)}, u32[]{:S(2)}) collective-permute-start(f32[384,256]{1,0:T(8,128)S(1)} %get-tuple-element.20), channel_id=1, source_target_pairs={{0,24},{1,25},{2,26},{3,27},{4,28},{5,29},{6,30},{7,31},{8,16},{9,... | collective-permute-start | bytes 1179656 | tf_op jit(solution)/shard_map/ppermute | solution.py:50
  50.6 20.2 %collective-permute-start.7 = (f32[384,256]{1,0:T(8,128)}, f32[384,256]{1,0:T(8,128)}, u32[]{:S(2)}, u32[]{:S(2)}) collective-permute-start(f32[384,256]{1,0:T(8,128)} %constant_dynamic-slice_fusion), channel_id=1, source_target_pairs={{0,0},{1,1},{2,2},{3,3},{4,35},{5,34},{6,33},{7,32},{8,64},{9,65},... | collective-permute-start | bytes 1179656 | tf_op jit(solution)/shard_map/ppermute | solution.py:176
  73.7 13.5 %collective-permute-start.13 = (f32[64,256]{1,0:T(8,128)}, f32[64,256]{1,0:T(8,128)}, u32[]{:S(2)}, u32[]{:S(2)}) collective-permute-start(f32[64,256]{1,0:T(8,128)} %get-tuple-element.27), channel_id=1, source_target_pairs={{0,32},{1,33},{2,34},{3,35},{4,36},{5,37},{6,38},{7,39},{8,40},{9,... | collective-permute-start | bytes 196616 | tf_op jit(solution)/shard_map/ppermute | solution.py:78
  73.7 13.5 %collective-permute-start.14 = (f32[64,256]{1,0:T(8,128)}, f32[64,256]{1,0:T(8,128)}, u32[]{:S(2)}, u32[]{:S(2)}) collective-permute-start(f32[64,256]{1,0:T(8,128)} %get-tuple-element.29), channel_id=1, source_target_pairs={{0,64},{1,65},{2,66},{3,67},{4,68},{5,69},{6,70},{7,71},{8,72},{9,... | collective-permute-start | bytes 196616 | tf_op jit(solution)/shard_map/ppermute | solution.py:78
  85.0 5.2 %collective-permute-start.10 = (f32[96,256]{1,0:T(8,128)S(1)}, f32[96,256]{1,0:T(8,128)S(1)}, u32[]{:S(2)}, u32[]{:S(2)}) collective-permute-start(f32[96,256]{1,0:T(8,128)S(1)} %get-tuple-element.17), channel_id=1, source_target_pairs={{0,96},{32,64},{64,32},{96,0},{128,224},{160,192},{192,160},{224,1... | collective-permute-start | bytes 294920 | tf_op jit(solution)/shard_map/ppermute | solution.py:78
  86.9 5.1 %collective-permute-start.8 = (f32[96,256]{1,0:T(8,128)S(1)}, f32[96,256]{1,0:T(8,128)S(1)}, u32[]{:S(2)}, u32[]{:S(2)}) collective-permute-start(f32[96,256]{1,0:T(8,128)S(1)} %get-tuple-element.16), channel_id=1, source_target_pairs={{0,32},{32,0},{64,96},{96,64},{128,160},{160,128},{192,224},{224,1... | collective-permute-start | bytes 294920 | tf_op jit(solution)/shard_map/ppermute | solution.py:78
  87.2 4.8 %collective-permute-start.9 = (f32[96,256]{1,0:T(8,128)S(1)}, f32[96,256]{1,0:T(8,128)S(1)}, u32[]{:S(2)}, u32[]{:S(2)}) collective-permute-start(f32[96,256]{1,0:T(8,128)S(1)} %get-tuple-element.18), channel_id=1, source_target_pairs={{0,64},{32,96},{64,0},{96,32},{128,192},{160,224},{192,128},{224,1... | collective-permute-start | bytes 294920 | tf_op jit(solution)/shard_map/ppermute | solution.py:78
  88.3 8.4 %collective-permute-start.16 = (f32[64,256]{1,0:T(8,128)S(1)}, f32[64,256]{1,0:T(8,128)S(1)}, u32[]{:S(2)}, u32[]{:S(2)}) collective-permute-start(f32[64,256]{1,0:T(8,128)S(1)} %fusion.113), channel_id=1, source_target_pairs={{0,1},{1,0},{2,3},{3,2},{4,5},{5,4},{6,7},{7,6},{8,9},{9,8},{10,11... | collective-permute-start | bytes 196616 | tf_op jit(solution)/shard_map/ppermute | solution.py:50
  88.5 8.3 %collective-permute-start.17 = (f32[64,256]{1,0:T(8,128)S(1)}, f32[64,256]{1,0:T(8,128)S(1)}, u32[]{:S(2)}, u32[]{:S(2)}) collective-permute-start(f32[64,256]{1,0:T(8,128)S(1)} %fusion.113), channel_id=1, source_target_pairs={{0,2},{1,3},{2,0},{3,1},{4,6},{5,7},{6,4},{7,5},{8,10},{9,11},{10,... | collective-permute-start | bytes 196616 | tf_op jit(solution)/shard_map/ppermute | solution.py:50
  90.2 6.5 %collective-permute-start.18 = (f32[64,256]{1,0:T(8,128)S(1)}, f32[64,256]{1,0:T(8,128)S(1)}, u32[]{:S(2)}, u32[]{:S(2)}) collective-permute-start(f32[64,256]{1,0:T(8,128)S(1)} %fusion.113), channel_id=1, source_target_pairs={{0,3},{1,2},{2,1},{3,0},{4,7},{5,6},{6,5},{7,4},{8,11},{9,10},{10,... | collective-permute-start | bytes 196616 | tf_op jit(solution)/shard_map/ppermute | solution.py:50
  92.9 10.8 %collective-permute-start.11 = (f32[48,256]{1,0:T(8,128)S(1)}, f32[48,256]{1,0:T(8,128)S(1)}, u32[]{:S(2)}, u32[]{:S(2)}) collective-permute-start(f32[48,256]{1,0:T(8,128)S(1)} %dynamic-slice_bitcast_fusion.14), channel_id=1, source_target_pairs={{0,128},{32,160},{64,192},{96,224},{128,0},{160,32},{192,64},{224,... | collective-permute-start | bytes 147464 | tf_op jit(solution)/shard_map/ppermute | solution.py:78
  96.9 12.4 %collective-permute-start.19 = (f32[64,256]{1,0:T(8,128)S(1)}, f32[64,256]{1,0:T(8,128)S(1)}, u32[]{:S(2)}, u32[]{:S(2)}) collective-permute-start(f32[64,256]{1,0:T(8,128)S(1)} %fusion.173), channel_id=1, source_target_pairs={{0,4},{1,5},{2,6},{3,7},{4,0},{5,1},{6,2},{7,3},{8,12},{9,13},{10,... | collective-permute-start | bytes 196616 | tf_op jit(solution)/shard_map/ppermute | solution.py:50
  99.7 9.5 %collective-permute-start.20 = (f32[64,256]{1,0:T(8,128)S(1)}, f32[64,256]{1,0:T(8,128)S(1)}, u32[]{:S(2)}, u32[]{:S(2)}) collective-permute-start(f32[64,256]{1,0:T(8,128)S(1)} %fusion.173), channel_id=1, source_target_pairs={{0,8},{1,9},{2,10},{3,11},{4,12},{5,13},{6,14},{7,15},{8,0},{9,1},... | collective-permute-start | bytes 196616 | tf_op jit(solution)/shard_map/ppermute | solution.py:50
  99.7 9.5 %collective-permute-start.21 = (f32[64,256]{1,0:T(8,128)S(1)}, f32[64,256]{1,0:T(8,128)S(1)}, u32[]{:S(2)}, u32[]{:S(2)}) collective-permute-start(f32[64,256]{1,0:T(8,128)S(1)} %fusion.173), channel_id=1, source_target_pairs={{0,12},{1,13},{2,14},{3,15},{4,8},{5,9},{6,10},{7,11},{8,4},{9,5},... | collective-permute-start | bytes 196616 | tf_op jit(solution)/shard_map/ppermute | solution.py:50
  103.7 15.1 %collective-permute-start.12 = (f32[48,256]{1,0:T(8,128)S(1)}, f32[48,256]{1,0:T(8,128)S(1)}, u32[]{:S(2)}, u32[]{:S(2)}) collective-permute-start(f32[48,256]{1,0:T(8,128)S(1)} %bitcast_add_fusion.2), channel_id=1, source_target_pairs={{0,0},{1,8},{2,16},{3,24},{4,32},{5,40},{6,48},{7,56},{8,64},{9,72... | collective-permute-start | bytes 147464 | tf_op jit(solution)/shard_map/ppermute | solution.py:184
  109.3 10.4 %collective-permute-start.22 = (f32[64,256]{1,0:T(8,128)S(1)}, f32[64,256]{1,0:T(8,128)S(1)}, u32[]{:S(2)}, u32[]{:S(2)}) collective-permute-start(f32[64,256]{1,0:T(8,128)S(1)} %fusion.172), channel_id=1, source_target_pairs={{0,16},{1,17},{2,18},{3,19},{4,20},{5,21},{6,22},{7,23},{8,24},{9,... | collective-permute-start | bytes 196616 | tf_op jit(solution)/shard_map/ppermute | solution.py:50
  116.1 5.2 %collective-permute-start.23 = (f32[64,256]{1,0:T(8,128)S(1)}, f32[64,256]{1,0:T(8,128)S(1)}, u32[]{:S(2)}, u32[]{:S(2)}) collective-permute-start(f32[64,256]{1,0:T(8,128)S(1)} %fusion.172), channel_id=1, source_target_pairs={{0,128},{1,129},{2,130},{3,131},{4,132},{5,133},{6,134},{7,135},{8... | collective-permute-start | bytes 196616 | tf_op jit(solution)/shard_map/ppermute | solution.py:50
  116.3 7.0 %collective-permute-start.24 = (f32[64,256]{1,0:T(8,128)S(1)}, f32[64,256]{1,0:T(8,128)S(1)}, u32[]{:S(2)}, u32[]{:S(2)}) collective-permute-start(f32[64,256]{1,0:T(8,128)S(1)} %fusion.172), channel_id=1, source_target_pairs={{0,144},{1,145},{2,146},{3,147},{4,148},{5,149},{6,150},{7,151},{8... | collective-permute-start | bytes 196616 | tf_op jit(solution)/shard_map/ppermute | solution.py:50
  (13 other events, 151.5 us)

commit v13 on v10

--- a/solution.py
+++ b/solution.py
@@ -108,6 +108,15 @@
     return gather_step(value, ALL, ndev, outer)
 
 
+def natural(gathered, order, shape):
+    nbits = len(order)
+    blocks = gathered.reshape((2,) * nbits + shape)
+    axis_of_bit = {m.bit_length() - 1: nbits - 1 - t for t, m in enumerate(order)}
+    low = min(axis_of_bit)
+    perm = [axis_of_bit[low + nbits - 1 - a] for a in range(nbits)] + [nbits, nbits + 1]
+    return blocks.transpose(perm).reshape(((1 << nbits) * shape[0], shape[1]))
+
+
 def make_body(nrow, ncol):
     assert nrow & (nrow - 1) == 0 and ncol & (ncol - 1) == 0
     row_bits = [1 << k for k in range(nrow.bit_length() - 1)]
@@ -117,11 +126,20 @@
     ]
 
     q = ncol // nrow
-    col_block_perm = [
-        (big * ncol + small, (small // q) * ncol + q * big + small % q)
-        for big in range(nrow)
-        for small in range(ncol)
-    ]
+    early = ncol % 8 == 0 and q == ncol // 8 and nrow == 8
+    if early:
+        col_block_perm = [
+            (big * ncol + small, (small % 8) * ncol + q * big + small // 8)
+            for big in range(nrow)
+            for small in range(ncol)
+        ]
+    else:
+        col_block_perm = [
+            (big * ncol + small, (small // q) * ncol + q * big + small % q)
+            for big in range(nrow)
+            for small in range(ncol)
+        ]
+    assert sorted(d for _, d in col_block_perm) == list(range(nrow * ncol))
 
     def inner(trailing_adjoint, panel, panel_adjoint, diag_factor, diag_adjoint):
         r = lax.axis_index("row")
@@ -130,14 +148,14 @@
 
         groups = gather_groups(ncol)
         gathered = panel
-        for masks in groups:
+        zsteps = [g for g in groups if all(m < 8 for m in g)]
+        for step, masks in enumerate(groups):
             gathered = gather_step(gathered, "col", ncol, masks)
-        order = [m for masks in groups for m in masks]
-        blocks = gathered.reshape((2,) * len(order) + panel.shape)
-        nbits = len(order)
-        axis_of_bit = {m.bit_length() - 1: nbits - 1 - t for t, m in enumerate(order)}
-        perm = [axis_of_bit[nbits - 1 - a] for a in range(nbits)] + [nbits, nbits + 1]
-        gathered = blocks.transpose(perm).reshape((ncol * panel.shape[0], panel.shape[1]))
+            if early and step == len(zsteps) - 1:
+                zorder = [m for g in zsteps for m in g]
+                pick = natural(gathered, zorder, panel.shape)
+                col_panel = lax.ppermute(pick, ALL, col_block_perm)
+        gathered = natural(gathered, [m for masks in groups for m in masks], panel.shape)
 
         share = lax.dot_general(
             trailing_adjoint,
@@ -148,15 +166,17 @@
         )
 
         span = share.shape[0]
-        pick = lax.dynamic_slice_in_dim(gathered, (c % q) * span, span, 0)
-        col_panel = lax.ppermute(pick, ALL, col_block_perm)
+        if not early:
+            pick = lax.dynamic_slice_in_dim(gathered, (c % q) * span, span, 0)
+            col_panel = lax.ppermute(pick, ALL, col_block_perm)
 
         local_term = mm(inverse.T, mm(panel_adjoint.T, panel) - 2.0 * mm(share.T, col_panel))
         rows, cols = diag_adjoint.shape
         placed = lax.dynamic_update_slice(
             jnp.zeros((rows * nrow, cols * ncol), jnp.float32), diag_adjoint, (r * rows, c * cols)
         )
-        accumulated = all_reduce(placed - local_term, nrow, ncol)
+        share, reduced = lax.optimization_barrier((share, placed - local_term))
+        accumulated = all_reduce(reduced, nrow, ncol)
 
         for masks in row_groups:
             share = scatter_step(share, "row", nrow, masks)

time: 138 us -> 145 us (1.051)
  starting transfers between devices: 58.3 us -> 93.8 us
  waiting for transfers between devices: 45.5 us -> 21.2 us
  local copies, waits for them, and re-layouts: 12.9 us -> 9.72 us
  matrix products: 17.3 us -> 15.6 us
    ppermute x7, starting transfers between devices: 5 us -> 33.8 us  [scatter_step(): total = total + lax.ppermute(send, axis, xor_perm(size, offset(k, masks)))]
    ppermute x19, waiting for transfers between devices: 36.3 us -> 21 us  [exchange(): got.append(lax.ppermute(value, axis, xor_perm(size, offset(k, masks))))]
    ppermute x7, waiting for transfers between devices: 7.39 us -> 0.26 us  [scatter_step(): total = total + lax.ppermute(send, axis, xor_perm(size, offset(k, masks)))]
    ppermute x19, starting transfers between devices: 37.7 us -> 44.4 us  [exchange(): got.append(lax.ppermute(value, axis, xor_perm(size, offset(k, masks))))]
    ppermute x1, starting transfers between devices: 3.88 us -> 6.3 us  [inner(): product = lax.ppermute(share, ALL, owner_perm)]
    ppermute x1, starting transfers between devices: 11.7 us -> 9.33 us  [inner(): col_panel = lax.ppermute(pick, ALL, col_block_perm)]
    dynamic_update_slice x1, local copies, waits for them, and re-layouts: 2.69 us -> 0.86 us  [inner(): lax.dynamic_update_slice(jnp.zeros((rows * nrow, cols * ncol), jnp.float3...]
    dot_general x23, matrix products: 14.6 us -> 12.8 us  [mm(): jnp.dot(a, b, precision=lax.Precision.HIGHEST, preferred_element_type=jnp...]
  transfers between devices with their start and end apart: 28 -> 28, of which waited for: 15 -> 7; matrix products, arithmetic and copies ran while one was open for 19% -> 14% of each run, Pallas kernels for 0% -> 0%
where the time goes in v13:
time: 145 us; the launch traced here: 144 us
  starting transfers between devices  93.8 us (65%)
  waiting for transfers between devices  21.2 us (15%)
  matrix products  15.6 us (11%)
  local copies, waits for them, and re-layouts  9.72 us (7%)
  other arithmetic  2.48 us (2%)
  between operations  1.52 us (1%)
    ppermute x19, starting transfers between devices, exchange(): got.append(lax.ppermute(value, axis, xor_perm(size, offset(k, masks))))  44.4 us
    ppermute x7, starting transfers between devices, scatter_step(): total = total + lax.ppermute(send, axis, xor_perm(size, offset(k, masks)))  33.8 us
    ppermute x19, waiting for transfers between devices, exchange(): got.append(lax.ppermute(value, axis, xor_perm(size, offset(k, masks))))  21 us
    dot_general x23, matrix products, mm(): jnp.dot(a, b, precision=lax.Precision.HIGHEST, preferred_element_type=jnp...  12.8 us
    ppermute x1, starting transfers between devices, inner(): col_panel = lax.ppermute(pick, ALL, col_block_perm)  9.33 us
    ppermute x1, starting transfers between devices, inner(): product = lax.ppermute(share, ALL, owner_perm)  6.3 us
  transfers between devices with their start and end apart: 28, of which 7 were waited for; matrix products, arithmetic and copies ran while one was open for 14% of the time, Pallas kernels for 0%

profile of v13, /device:TPU:1, one launch (start us, length us, event | category | flops | bytes accessed | tf_op | source)
XLA Modules:
  0.0 144.4 jit_solution(2154812292941411201)
XLA Ops:
  0.7 7.8 %collective-permute-start = (f32[48,256]{1,0:T(8,128)}, f32[48,256]{1,0:T(8,128)S(1)}, u32[]{:S(2)}, u32[]{:S(2)}) collective-permute-start(f32[48,256]{1,0:T(8,128)} %param.6), channel_id=1, source_target_pairs={{0,4},{1,5},{2,6},{3,7},{4,0},{5,1},{6,2},{7,3},{8,12},{9,13},{10,... | collective-permute-start | bytes 147464 | tf_op jit(solution)/shard_map/ppermute | solution.py:50
  9.7 2.6 %gather_fusion = f32[256]{0:T(256)S(1)} fusion(f32[256,256]{1,0:T(8,128)} %param.8, s32[256]{0:T(256)S(1)} %bitcast.140), kind=kCustom, calls=%fused_computation | custom fusion | bytes 4096 | tf_op jit(solution)/shard_map/jit(diagonal)/cond/branch_0_fun/gather | solution.py:16
  22.5 3.7 %collective-permute-done.3 = f32[192,256]{1,0:T(8,128)S(1)} collective-permute-done((f32[192,256]{1,0:T(8,128)S(1)}, f32[192,256]{1,0:T(8,128)S(1)}, u32[]{:S(2)}, u32[]{:S(2)}) %collective-permute-start.3) | collective-permute-done | bytes 196640 | tf_op jit(solution)/shard_map/ppermute | solution.py:50
  26.4 1.6 %collective-permute-start.4 = (f32[384,256]{1,0:T(8,128)S(1)}, f32[384,256]{1,0:T(8,128)S(1)}, u32[]{:S(2)}, u32[]{:S(2)}) collective-permute-start(f32[384,256]{1,0:T(8,128)S(1)} %get-tuple-element.14), channel_id=1, source_target_pairs={{0,8},{1,9},{2,10},{3,11},{4,12},{5,13},{6,14},{7,15},{8,0},{9,1},... | collective-permute-start | bytes 1179656 | tf_op jit(solution)/shard_map/ppermute | solution.py:50
  27.9 2.2 %collective-permute-start.5 = (f32[384,256]{1,0:T(8,128)S(1)}, f32[384,256]{1,0:T(8,128)S(1)}, u32[]{:S(2)}, u32[]{:S(2)}) collective-permute-start(f32[384,256]{1,0:T(8,128)S(1)} %get-tuple-element.14), channel_id=1, source_target_pairs={{0,16},{1,17},{2,18},{3,19},{4,20},{5,21},{6,22},{7,23},{8,24},{9,... | collective-permute-start | bytes 1179656 | tf_op jit(solution)/shard_map/ppermute | solution.py:50
  31.3 9.3 %collective-permute-start.7 = (f32[384,256]{1,0:T(8,128)S(1)}, f32[384,256]{1,0:T(8,128)S(1)}, u32[]{:S(2)}, u32[]{:S(2)}) collective-permute-start(f32[384,256]{1,0:T(8,128)S(1)} %bitcast.154), channel_id=1, source_target_pairs={{0,0},{1,32},{2,64},{3,96},{4,128},{5,160},{6,192},{7,224},{8,1},{... | collective-permute-start | bytes 1179656 | tf_op jit(solution)/shard_map/ppermute | solution.py:157
  40.6 5.1 %collective-permute-done.5 = f32[384,256]{1,0:T(8,128)S(1)} collective-permute-done((f32[384,256]{1,0:T(8,128)S(1)}, f32[384,256]{1,0:T(8,128)S(1)}, u32[]{:S(2)}, u32[]{:S(2)}) %collective-permute-start.5) | collective-permute-done | bytes 393248 | tf_op jit(solution)/shard_map/ppermute | solution.py:50
  46.3 2.8 %fusion.135 = f32[256,384]{1,0:T(8,128)S(1)} fusion(f32[1536,256]{1,0:T(8,128)S(1)} %bitcast.144, f32[1536,384]{1,0:T(8,128)S(1)} %copy-done), kind=kOutput, calls=%fused_computation.217 | convolution fusion | flops 1811939328 | bytes 4325376 | tf_op jit(solution)/shard_map/dot_general | solution.py:160
  51.8 5.6 %collective-permute-start.13 = (f32[64,256]{1,0:T(8,128)}, f32[64,256]{1,0:T(8,128)S(1)}, u32[]{:S(2)}, u32[]{:S(2)}) collective-permute-start(f32[64,256]{1,0:T(8,128)} %get-tuple-element.21), channel_id=1, source_target_pairs={{0,32},{1,33},{2,34},{3,35},{4,36},{5,37},{6,38},{7,39},{8,40},{9,... | collective-permute-start | bytes 196616 | tf_op jit(solution)/shard_map/ppermute | solution.py:78
  57.3 26.0 %collective-permute-start.14 = (f32[64,256]{1,0:T(8,128)}, f32[64,256]{1,0:T(8,128)}, u32[]{:S(2)}, u32[]{:S(2)}) collective-permute-start(f32[64,256]{1,0:T(8,128)} %get-tuple-element.23), channel_id=1, source_target_pairs={{0,64},{1,65},{2,66},{3,67},{4,68},{5,69},{6,70},{7,71},{8,72},{9,... | collective-permute-start | bytes 196616 | tf_op jit(solution)/shard_map/ppermute | solution.py:78
  85.2 1.8 %collective-permute-start.10 = (f32[96,256]{1,0:T(8,128)S(1)}, f32[96,256]{1,0:T(8,128)S(1)}, u32[]{:S(2)}, u32[]{:S(2)}) collective-permute-start(f32[96,256]{1,0:T(8,128)S(1)} %get-tuple-element.11), channel_id=1, source_target_pairs={{0,96},{32,64},{64,32},{96,0},{128,224},{160,192},{192,160},{224,1... | collective-permute-start | bytes 294920 | tf_op jit(solution)/shard_map/ppermute | solution.py:78
  88.5 1.5 %collective-permute-start.16 = (f32[64,256]{1,0:T(8,128)S(1)}, f32[64,256]{1,0:T(8,128)S(1)}, u32[]{:S(2)}, u32[]{:S(2)}) collective-permute-start(f32[64,256]{1,0:T(8,128)S(1)} %fusion.113), channel_id=1, source_target_pairs={{0,1},{1,0},{2,3},{3,2},{4,5},{5,4},{6,7},{7,6},{8,9},{9,8},{10,11... | collective-permute-start | bytes 196616 | tf_op jit(solution)/shard_map/ppermute | solution.py:50
  90.1 8.8 %collective-permute-start.17 = (f32[64,256]{1,0:T(8,128)S(1)}, f32[64,256]{1,0:T(8,128)S(1)}, u32[]{:S(2)}, u32[]{:S(2)}) collective-permute-start(f32[64,256]{1,0:T(8,128)S(1)} %fusion.113), channel_id=1, source_target_pairs={{0,2},{1,3},{2,0},{3,1},{4,6},{5,7},{6,4},{7,5},{8,10},{9,11},{10,... | collective-permute-start | bytes 196616 | tf_op jit(solution)/shard_map/ppermute | solution.py:50
  101.0 3.8 %collective-permute-done.18 = f32[64,256]{1,0:T(8,128)S(1)} collective-permute-done((f32[64,256]{1,0:T(8,128)S(1)}, f32[64,256]{1,0:T(8,128)S(1)}, u32[]{:S(2)}, u32[]{:S(2)}) %collective-permute-start.18) | collective-permute-done | bytes 65568 | tf_op jit(solution)/shard_map/ppermute | solution.py:50
  104.9 4.3 %collective-permute-start.19 = (f32[64,256]{1,0:T(8,128)S(1)}, f32[64,256]{1,0:T(8,128)S(1)}, u32[]{:S(2)}, u32[]{:S(2)}) collective-permute-start(f32[64,256]{1,0:T(8,128)S(1)} %fusion.174), channel_id=1, source_target_pairs={{0,4},{1,5},{2,6},{3,7},{4,0},{5,1},{6,2},{7,3},{8,12},{9,13},{10,... | collective-permute-start | bytes 196616 | tf_op jit(solution)/shard_map/ppermute | solution.py:50
  109.2 2.4 %collective-permute-start.21 = (f32[64,256]{1,0:T(8,128)S(1)}, f32[64,256]{1,0:T(8,128)S(1)}, u32[]{:S(2)}, u32[]{:S(2)}) collective-permute-start(f32[64,256]{1,0:T(8,128)S(1)} %fusion.174), channel_id=1, source_target_pairs={{0,12},{1,13},{2,14},{3,15},{4,8},{5,9},{6,10},{7,11},{8,4},{9,5},... | collective-permute-start | bytes 196616 | tf_op jit(solution)/shard_map/ppermute | solution.py:50
  111.6 6.3 %collective-permute-start.12 = (f32[48,256]{1,0:T(8,128)S(1)}, f32[48,256]{1,0:T(8,128)S(1)}, u32[]{:S(2)}, u32[]{:S(2)}) collective-permute-start(f32[48,256]{1,0:T(8,128)S(1)} %bitcast_add_fusion.2), channel_id=1, source_target_pairs={{0,0},{1,8},{2,16},{3,24},{4,32},{5,40},{6,48},{7,56},{8,64},{9,72... | collective-permute-start | bytes 147464 | tf_op jit(solution)/shard_map/ppermute | solution.py:183
  118.0 1.6 %collective-permute-start.22 = (f32[64,256]{1,0:T(8,128)S(1)}, f32[64,256]{1,0:T(8,128)S(1)}, u32[]{:S(2)}, u32[]{:S(2)}) collective-permute-start(f32[64,256]{1,0:T(8,128)S(1)} %fusion.173), channel_id=1, source_target_pairs={{0,16},{1,17},{2,18},{3,19},{4,20},{5,21},{6,22},{7,23},{8,24},{9,... | collective-permute-start | bytes 196616 | tf_op jit(solution)/shard_map/ppermute | solution.py:50
  119.6 2.7 %collective-permute-start.23 = (f32[64,256]{1,0:T(8,128)S(1)}, f32[64,256]{1,0:T(8,128)S(1)}, u32[]{:S(2)}, u32[]{:S(2)}) collective-permute-start(f32[64,256]{1,0:T(8,128)S(1)} %fusion.173), channel_id=1, source_target_pairs={{0,128},{1,129},{2,130},{3,131},{4,132},{5,133},{6,134},{7,135},{8... | collective-permute-start | bytes 196616 | tf_op jit(solution)/shard_map/ppermute | solution.py:50
  124.6 4.7 %collective-permute-done.24 = f32[64,256]{1,0:T(8,128)S(1)} collective-permute-done((f32[64,256]{1,0:T(8,128)S(1)}, f32[64,256]{1,0:T(8,128)S(1)}, u32[]{:S(2)}, u32[]{:S(2)}) %collective-permute-start.24) | collective-permute-done | bytes 65568 | tf_op jit(solution)/shard_map/ppermute | solution.py:50
  129.4 4.7 %collective-permute-start.25 = (f32[64,256]{1,0:T(8,128)S(1)}, f32[64,256]{1,0:T(8,128)S(1)}, u32[]{:S(2)}, u32[]{:S(2)}) collective-permute-start(f32[64,256]{1,0:T(8,128)S(1)} %fusion.172), channel_id=1, source_target_pairs={{0,32},{1,33},{2,34},{3,35},{4,36},{5,37},{6,38},{7,39},{8,40},{9,... | collective-permute-start | bytes 196616 | tf_op jit(solution)/shard_map/ppermute | solution.py:50
  135.8 1.8 %collective-permute-done.26 = f32[64,256]{1,0:T(8,128)S(1)} collective-permute-done((f32[64,256]{1,0:T(8,128)S(1)}, f32[64,256]{1,0:T(8,128)S(1)}, u32[]{:S(2)}, u32[]{:S(2)}) %collective-permute-start.26) | collective-permute-done | bytes 65568 | tf_op jit(solution)/shard_map/ppermute | solution.py:50
  137.6 1.8 %collective-permute-done.27 = f32[64,256]{1,0:T(8,128)S(1)} collective-permute-done((f32[64,256]{1,0:T(8,128)S(1)}, f32[64,256]{1,0:T(8,128)S(1)}, u32[]{:S(2)}, u32[]{:S(2)}) %collective-permute-start.27) | collective-permute-done | bytes 65568 | tf_op jit(solution)/shard_map/ppermute | solution.py:50
  140.2 2.3 %gather_fusion.1 = f32[256]{0:T(256)S(1)} fusion(f32[256,256]{1,0:T(8,128)S(1)} %bitcast.142, s32[256]{0:T(256)S(1)} %bitcast.141), kind=kCustom, calls=%fused_computation.1 | custom fusion | bytes 4096 | tf_op jit(solution)/shard_map/jit(_diag)/jit(diagonal)/cond/branch_0_fun/gather | solution.py:29
  (114 shorter events, 27.6 us)
Async XLA Ops:
  0.7 20.1 %collective-permute-start = (f32[48,256]{1,0:T(8,128)}, f32[48,256]{1,0:T(8,128)S(1)}, u32[]{:S(2)}, u32[]{:S(2)}) collective-permute-start(f32[48,256]{1,0:T(8,128)} %param.6), channel_id=1, source_target_pairs={{0,4},{1,5},{2,6},{3,7},{4,0},{5,1},{6,2},{7,3},{8,12},{9,13},{10,... | collective-permute-start | bytes 147464 | tf_op jit(solution)/shard_map/ppermute | solution.py:50
  8.5 12.3 %collective-permute-start.1 = (f32[48,256]{1,0:T(8,128)}, f32[48,256]{1,0:T(8,128)S(1)}, u32[]{:S(2)}, u32[]{:S(2)}) collective-permute-start(f32[48,256]{1,0:T(8,128)} %param.6), channel_id=1, source_target_pairs={{0,2},{1,3},{2,0},{3,1},{4,6},{5,7},{6,4},{7,5},{8,10},{9,11},{10,... | collective-permute-start | bytes 147464 | tf_op jit(solution)/shard_map/ppermute | solution.py:50
  9.7 11.1 %collective-permute-start.2 = (f32[48,256]{1,0:T(8,128)}, f32[48,256]{1,0:T(8,128)S(1)}, u32[]{:S(2)}, u32[]{:S(2)}) collective-permute-start(f32[48,256]{1,0:T(8,128)} %param.6), channel_id=1, source_target_pairs={{0,6},{1,7},{2,4},{3,5},{4,2},{5,3},{6,0},{7,1},{8,14},{9,15},{10,... | collective-permute-start | bytes 147464 | tf_op jit(solution)/shard_map/ppermute | solution.py:50
  20.9 5.3 %collective-permute-start.3 = (f32[192,256]{1,0:T(8,128)S(1)}, f32[192,256]{1,0:T(8,128)S(1)}, u32[]{:S(2)}, u32[]{:S(2)}) collective-permute-start(f32[192,256]{1,0:T(8,128)S(1)} %get-tuple-element.24), channel_id=1, source_target_pairs={{0,1},{1,0},{2,3},{3,2},{4,5},{5,4},{6,7},{7,6},{8,9},{9,8},{10,11... | collective-permute-start | bytes 589832 | tf_op jit(solution)/shard_map/ppermute | solution.py:50
  26.4 14.3 %collective-permute-start.4 = (f32[384,256]{1,0:T(8,128)S(1)}, f32[384,256]{1,0:T(8,128)S(1)}, u32[]{:S(2)}, u32[]{:S(2)}) collective-permute-start(f32[384,256]{1,0:T(8,128)S(1)} %get-tuple-element.14), channel_id=1, source_target_pairs={{0,8},{1,9},{2,10},{3,11},{4,12},{5,13},{6,14},{7,15},{8,0},{9,1},... | collective-permute-start | bytes 1179656 | tf_op jit(solution)/shard_map/ppermute | solution.py:50
  27.9 17.8 %collective-permute-start.5 = (f32[384,256]{1,0:T(8,128)S(1)}, f32[384,256]{1,0:T(8,128)S(1)}, u32[]{:S(2)}, u32[]{:S(2)}) collective-permute-start(f32[384,256]{1,0:T(8,128)S(1)} %get-tuple-element.14), channel_id=1, source_target_pairs={{0,16},{1,17},{2,18},{3,19},{4,20},{5,21},{6,22},{7,23},{8,24},{9,... | collective-permute-start | bytes 1179656 | tf_op jit(solution)/shard_map/ppermute | solution.py:50
  30.2 15.6 %collective-permute-start.6 = (f32[384,256]{1,0:T(8,128)S(1)}, f32[384,256]{1,0:T(8,128)S(1)}, u32[]{:S(2)}, u32[]{:S(2)}) collective-permute-start(f32[384,256]{1,0:T(8,128)S(1)} %get-tuple-element.14), channel_id=1, source_target_pairs={{0,24},{1,25},{2,26},{3,27},{4,28},{5,29},{6,30},{7,31},{8,16},{9,... | collective-permute-start | bytes 1179656 | tf_op jit(solution)/shard_map/ppermute | solution.py:50
  31.3 17.9 %collective-permute-start.7 = (f32[384,256]{1,0:T(8,128)S(1)}, f32[384,256]{1,0:T(8,128)S(1)}, u32[]{:S(2)}, u32[]{:S(2)}) collective-permute-start(f32[384,256]{1,0:T(8,128)S(1)} %bitcast.154), channel_id=1, source_target_pairs={{0,0},{1,32},{2,64},{3,96},{4,128},{5,160},{6,192},{7,224},{8,1},{... | collective-permute-start | bytes 1179656 | tf_op jit(solution)/shard_map/ppermute | solution.py:157
  51.8 35.6 %collective-permute-start.13 = (f32[64,256]{1,0:T(8,128)}, f32[64,256]{1,0:T(8,128)S(1)}, u32[]{:S(2)}, u32[]{:S(2)}) collective-permute-start(f32[64,256]{1,0:T(8,128)} %get-tuple-element.21), channel_id=1, source_target_pairs={{0,32},{1,33},{2,34},{3,35},{4,36},{5,37},{6,38},{7,39},{8,40},{9,... | collective-permute-start | bytes 196616 | tf_op jit(solution)/shard_map/ppermute | solution.py:78
  57.3 30.0 %collective-permute-start.14 = (f32[64,256]{1,0:T(8,128)}, f32[64,256]{1,0:T(8,128)}, u32[]{:S(2)}, u32[]{:S(2)}) collective-permute-start(f32[64,256]{1,0:T(8,128)} %get-tuple-element.23), channel_id=1, source_target_pairs={{0,64},{1,65},{2,66},{3,67},{4,68},{5,69},{6,70},{7,71},{8,72},{9,... | collective-permute-start | bytes 196616 | tf_op jit(solution)/shard_map/ppermute | solution.py:78
  85.2 13.6 %collective-permute-start.10 = (f32[96,256]{1,0:T(8,128)S(1)}, f32[96,256]{1,0:T(8,128)S(1)}, u32[]{:S(2)}, u32[]{:S(2)}) collective-permute-start(f32[96,256]{1,0:T(8,128)S(1)} %get-tuple-element.11), channel_id=1, source_target_pairs={{0,96},{32,64},{64,32},{96,0},{128,224},{160,192},{192,160},{224,1... | collective-permute-start | bytes 294920 | tf_op jit(solution)/shard_map/ppermute | solution.py:78
  87.1 12.9 %collective-permute-start.8 = (f32[96,256]{1,0:T(8,128)S(1)}, f32[96,256]{1,0:T(8,128)S(1)}, u32[]{:S(2)}, u32[]{:S(2)}) collective-permute-start(f32[96,256]{1,0:T(8,128)S(1)} %get-tuple-element.10), channel_id=1, source_target_pairs={{0,32},{32,0},{64,96},{96,64},{128,160},{160,128},{192,224},{224,1... | collective-permute-start | bytes 294920 | tf_op jit(solution)/shard_map/ppermute | solution.py:78
  87.4 12.6 %collective-permute-start.9 = (f32[96,256]{1,0:T(8,128)S(1)}, f32[96,256]{1,0:T(8,128)S(1)}, u32[]{:S(2)}, u32[]{:S(2)}) collective-permute-start(f32[96,256]{1,0:T(8,128)S(1)} %get-tuple-element.12), channel_id=1, source_target_pairs={{0,64},{32,96},{64,0},{96,32},{128,192},{160,224},{192,128},{224,1... | collective-permute-start | bytes 294920 | tf_op jit(solution)/shard_map/ppermute | solution.py:78
  88.5 12.5 %collective-permute-start.16 = (f32[64,256]{1,0:T(8,128)S(1)}, f32[64,256]{1,0:T(8,128)S(1)}, u32[]{:S(2)}, u32[]{:S(2)}) collective-permute-start(f32[64,256]{1,0:T(8,128)S(1)} %fusion.113), channel_id=1, source_target_pairs={{0,1},{1,0},{2,3},{3,2},{4,5},{5,4},{6,7},{7,6},{8,9},{9,8},{10,11... | collective-permute-start | bytes 196616 | tf_op jit(solution)/shard_map/ppermute | solution.py:50
  90.1 10.9 %collective-permute-start.17 = (f32[64,256]{1,0:T(8,128)S(1)}, f32[64,256]{1,0:T(8,128)S(1)}, u32[]{:S(2)}, u32[]{:S(2)}) collective-permute-start(f32[64,256]{1,0:T(8,128)S(1)} %fusion.113), channel_id=1, source_target_pairs={{0,2},{1,3},{2,0},{3,1},{4,6},{5,7},{6,4},{7,5},{8,10},{9,11},{10,... | collective-permute-start | bytes 196616 | tf_op jit(solution)/shard_map/ppermute | solution.py:50
  98.9 6.0 %collective-permute-start.18 = (f32[64,256]{1,0:T(8,128)S(1)}, f32[64,256]{1,0:T(8,128)S(1)}, u32[]{:S(2)}, u32[]{:S(2)}) collective-permute-start(f32[64,256]{1,0:T(8,128)S(1)} %fusion.113), channel_id=1, source_target_pairs={{0,3},{1,2},{2,1},{3,0},{4,7},{5,6},{6,5},{7,4},{8,11},{9,10},{10,... | collective-permute-start | bytes 196616 | tf_op jit(solution)/shard_map/ppermute | solution.py:50
  100.9 10.7 %collective-permute-start.11 = (f32[48,256]{1,0:T(8,128)S(1)}, f32[48,256]{1,0:T(8,128)S(1)}, u32[]{:S(2)}, u32[]{:S(2)}) collective-permute-start(f32[48,256]{1,0:T(8,128)S(1)} %dynamic-slice_bitcast_fusion.14), channel_id=1, source_target_pairs={{0,128},{32,160},{64,192},{96,224},{128,0},{160,32},{192,64},{224,... | collective-permute-start | bytes 147464 | tf_op jit(solution)/shard_map/ppermute | solution.py:78
  104.9 13.0 %collective-permute-start.19 = (f32[64,256]{1,0:T(8,128)S(1)}, f32[64,256]{1,0:T(8,128)S(1)}, u32[]{:S(2)}, u32[]{:S(2)}) collective-permute-start(f32[64,256]{1,0:T(8,128)S(1)} %fusion.174), channel_id=1, source_target_pairs={{0,4},{1,5},{2,6},{3,7},{4,0},{5,1},{6,2},{7,3},{8,12},{9,13},{10,... | collective-permute-start | bytes 196616 | tf_op jit(solution)/shard_map/ppermute | solution.py:50
  109.2 8.7 %collective-permute-start.20 = (f32[64,256]{1,0:T(8,128)S(1)}, f32[64,256]{1,0:T(8,128)S(1)}, u32[]{:S(2)}, u32[]{:S(2)}) collective-permute-start(f32[64,256]{1,0:T(8,128)S(1)} %fusion.174), channel_id=1, source_target_pairs={{0,8},{1,9},{2,10},{3,11},{4,12},{5,13},{6,14},{7,15},{8,0},{9,1},... | collective-permute-start | bytes 196616 | tf_op jit(solution)/shard_map/ppermute | solution.py:50
  109.2 8.7 %collective-permute-start.21 = (f32[64,256]{1,0:T(8,128)S(1)}, f32[64,256]{1,0:T(8,128)S(1)}, u32[]{:S(2)}, u32[]{:S(2)}) collective-permute-start(f32[64,256]{1,0:T(8,128)S(1)} %fusion.174), channel_id=1, source_target_pairs={{0,12},{1,13},{2,14},{3,15},{4,8},{5,9},{6,10},{7,11},{8,4},{9,5},... | collective-permute-start | bytes 196616 | tf_op jit(solution)/shard_map/ppermute | solution.py:50
  111.6 12.1 %collective-permute-start.12 = (f32[48,256]{1,0:T(8,128)S(1)}, f32[48,256]{1,0:T(8,128)S(1)}, u32[]{:S(2)}, u32[]{:S(2)}) collective-permute-start(f32[48,256]{1,0:T(8,128)S(1)} %bitcast_add_fusion.2), channel_id=1, source_target_pairs={{0,0},{1,8},{2,16},{3,24},{4,32},{5,40},{6,48},{7,56},{8,64},{9,72... | collective-permute-start | bytes 147464 | tf_op jit(solution)/shard_map/ppermute | solution.py:183
  118.0 6.6 %collective-permute-start.22 = (f32[64,256]{1,0:T(8,128)S(1)}, f32[64,256]{1,0:T(8,128)S(1)}, u32[]{:S(2)}, u32[]{:S(2)}) collective-permute-start(f32[64,256]{1,0:T(8,128)S(1)} %fusion.173), channel_id=1, source_target_pairs={{0,16},{1,17},{2,18},{3,19},{4,20},{5,21},{6,22},{7,23},{8,24},{9,... | collective-permute-start | bytes 196616 | tf_op jit(solution)/shard_map/ppermute | solution.py:50
  122.3 7.0 %collective-permute-start.24 = (f32[64,256]{1,0:T(8,128)S(1)}, f32[64,256]{1,0:T(8,128)S(1)}, u32[]{:S(2)}, u32[]{:S(2)}) collective-permute-start(f32[64,256]{1,0:T(8,128)S(1)} %fusion.173), channel_id=1, source_target_pairs={{0,144},{1,145},{2,146},{3,147},{4,148},{5,149},{6,150},{7,151},{8... | collective-permute-start | bytes 196616 | tf_op jit(solution)/shard_map/ppermute | solution.py:50
  129.4 6.4 %collective-permute-start.25 = (f32[64,256]{1,0:T(8,128)S(1)}, f32[64,256]{1,0:T(8,128)S(1)}, u32[]{:S(2)}, u32[]{:S(2)}) collective-permute-start(f32[64,256]{1,0:T(8,128)S(1)} %fusion.172), channel_id=1, source_target_pairs={{0,32},{1,33},{2,34},{3,35},{4,36},{5,37},{6,38},{7,39},{8,40},{9,... | collective-permute-start | bytes 196616 | tf_op jit(solution)/shard_map/ppermute | solution.py:50
  (13 other events, 138.5 us)

commit v14 on v11

--- a/solution.py
+++ b/solution.py
@@ -111,7 +111,7 @@
 def make_body(nrow, ncol):
     assert nrow & (nrow - 1) == 0 and ncol & (ncol - 1) == 0
     row_bits = [1 << k for k in range(nrow.bit_length() - 1)]
-    row_groups = [tuple(row_bits[i : i + 2]) for i in range(0, len(row_bits), 2)]
+    row_groups = [(m,) for m in row_bits]
     owner_perm = [
         (r * ncol + c, c * nrow + kept_chunk(r, row_groups, nrow)) for r in range(nrow) for c in range(ncol)
     ]
@@ -173,7 +173,8 @@
         placed = lax.dynamic_update_slice(
             jnp.zeros((rows * nrow, cols * ncol), jnp.float32), diag_adjoint, (r * rows, c * cols)
         )
-        accumulated = all_reduce(placed - local_term, nrow, ncol)
+        share, reduced = lax.optimization_barrier((share, placed - local_term))
+        accumulated = all_reduce(reduced, nrow, ncol)
 
         for masks in row_groups:
             share = scatter_step(share, "row", nrow, masks)

time: 138 us -> 144 us (1.043)
  the two profiles are of different devices: /device:TPU:1 before, /device:TPU:39 now
where the time goes in v14:
time: 144 us; the launch traced here: 143 us
  starting transfers between devices  62.8 us (44%)
  waiting for transfers between devices  44.5 us (31%)
  matrix products  18.8 us (13%)
  local copies, waits for them, and re-layouts  13.6 us (9%)
  between operations  2.03 us (1%)
  other arithmetic  1.6 us (1%)
    ppermute x19, waiting for transfers between devices, exchange(): got.append(lax.ppermute(value, axis, xor_perm(size, offset(k, masks))))  33.7 us
    ppermute x19, starting transfers between devices, exchange(): got.append(lax.ppermute(value, axis, xor_perm(size, offset(k, masks))))  32.2 us
    ppermute x1, starting transfers between devices, inner(): col_panel = lax.ppermute(pick, ALL, col_block_perm)  15.7 us
    dot_general x23, matrix products, mm(): jnp.dot(a, b, precision=lax.Precision.HIGHEST, preferred_element_type=jnp...  14.7 us
    ppermute x6, starting transfers between devices, scatter_step(): total = total + lax.ppermute(send, axis, xor_perm(size, offset(k, masks)))  9.63 us
    ppermute x1, waiting for transfers between devices, inner(): product = lax.ppermute(share, ALL, owner_perm)  6.08 us
    ppermute x1, starting transfers between devices, inner(): product = lax.ppermute(share, ALL, owner_perm)  5.26 us
    dot_general x1, matrix products, inner(): lax.dot_general(trailing_adjoint, gathered, (((0,), (0,)), ((), ())), pre...  4.11 us
  transfers between devices with their start and end apart: 27, of which 15 were waited for; matrix products, arithmetic and copies ran while one was open for 18% of the time, Pallas kernels for 0%

profile of v14, /device:TPU:39, one launch (start us, length us, event | category | flops | bytes accessed | tf_op | source)
XLA Modules:
  0.0 143.4 jit_solution(929632354386841409)
XLA Ops:
  0.7 6.1 %collective-permute-start = (f32[48,256]{1,0:T(8,128)}, f32[48,256]{1,0:T(8,128)S(1)}, u32[]{:S(2)}, u32[]{:S(2)}) collective-permute-start(f32[48,256]{1,0:T(8,128)} %param.7), channel_id=1, source_target_pairs={{0,4},{1,5},{2,6},{3,7},{4,0},{5,1},{6,2},{7,3},{8,12},{9,13},{10,... | collective-permute-start | bytes 147464 | tf_op jit(solution)/shard_map/ppermute | solution.py:50
  8.0 2.6 %gather_fusion = f32[256]{0:T(256)S(1)} fusion(f32[256,256]{1,0:T(8,128)} %param.9, s32[256]{0:T(256)S(1)} %bitcast.134), kind=kCustom, calls=%fused_computation | custom fusion | bytes 4096 | tf_op jit(solution)/shard_map/jit(diagonal)/cond/branch_0_fun/gather | solution.py:16
  20.1 4.1 %collective-permute-done.3 = f32[192,256]{1,0:T(8,128)S(1)} collective-permute-done((f32[192,256]{1,0:T(8,128)S(1)}, f32[192,256]{1,0:T(8,128)S(1)}, u32[]{:S(2)}, u32[]{:S(2)}) %collective-permute-start.3) | collective-permute-done | bytes 196640 | tf_op jit(solution)/shard_map/ppermute | solution.py:50
  25.8 2.5 %collective-permute-start.6 = (f32[384,256]{1,0:T(8,128)S(1)}, f32[384,256]{1,0:T(8,128)S(1)}, u32[]{:S(2)}, u32[]{:S(2)}) collective-permute-start(f32[384,256]{1,0:T(8,128)S(1)} %get-tuple-element.11), channel_id=1, source_target_pairs={{0,24},{1,25},{2,26},{3,27},{4,28},{5,29},{6,30},{7,31},{8,16},{9,... | collective-permute-start | bytes 1179656 | tf_op jit(solution)/shard_map/ppermute | solution.py:50
  29.2 3.8 %collective-permute-done.4 = f32[384,256]{1,0:T(8,128)S(1)} collective-permute-done((f32[384,256]{1,0:T(8,128)S(1)}, f32[384,256]{1,0:T(8,128)S(1)}, u32[]{:S(2)}, u32[]{:S(2)}) %collective-permute-start.4) | collective-permute-done | bytes 393248 | tf_op jit(solution)/shard_map/ppermute | solution.py:50
  33.0 8.4 %collective-permute-done.5 = f32[384,256]{1,0:T(8,128)S(1)} collective-permute-done((f32[384,256]{1,0:T(8,128)S(1)}, f32[384,256]{1,0:T(8,128)S(1)}, u32[]{:S(2)}, u32[]{:S(2)}) %collective-permute-start.5) | collective-permute-done | bytes 393248 | tf_op jit(solution)/shard_map/ppermute | solution.py:50
  43.9 15.7 %collective-permute-start.7 = (f32[384,256]{1,0:T(8,128)}, f32[384,256]{1,0:T(8,128)}, u32[]{:S(2)}, u32[]{:S(2)}) collective-permute-start(f32[384,256]{1,0:T(8,128)} %constant_dynamic-slice_fusion), channel_id=1, source_target_pairs={{0,0},{1,1},{2,2},{3,3},{4,35},{5,34},{6,33},{7,32},{8,64},{9,65},... | collective-permute-start | bytes 1179656 | tf_op jit(solution)/shard_map/ppermute | solution.py:169
  60.9 2.2 %dynamic_update_slice.3 = f32[256,256]{1,0:T(8,128)} dynamic-update-slice(f32[256,256]{1,0:T(8,128)} %broadcast_in_dim.45, f32[32,8]{1,0:T(8,128)S(1)} %copy.16, s32[]{:T(128)S(6)} %select_n.331, s32[]{:T(128)S(6)} %select_n.332) | dynamic-update-slice | bytes 2052 | tf_op jit(solution)/shard_map/dynamic_update_slice | solution.py:173
  63.2 4.1 %fusion.133 = f32[256,384]{1,0:T(8,128)S(1)} fusion(f32[1536,256]{1,0:T(8,128)} %bitcast.137, f32[1536,384]{1,0:T(8,128)S(1)} %copy-done), kind=kOutput, calls=%fused_computation.216 | convolution fusion | flops 1811939328 | bytes 4325376 | tf_op jit(solution)/shard_map/dot_general | solution.py:156
  67.3 1.8 %collective-permute-done.7 = f32[384,256]{1,0:T(8,128)} collective-permute-done((f32[384,256]{1,0:T(8,128)}, f32[384,256]{1,0:T(8,128)}, u32[]{:S(2)}, u32[]{:S(2)}) %collective-permute-start.7) | collective-permute-done | bytes 393248 | tf_op jit(solution)/shard_map/ppermute | solution.py:169
  69.0 1.6 %fusion = f32[256,256]{1,0:T(8,128)S(1)} fusion(f32[256,256]{1,0:T(8,128)S(1)} %fusion.134, f32[256,384]{1,0:T(8,128)S(1)} %fusion.133, f32[384,256]{1,0:T(8,128)} %collective-permute-done.7), kind=kOutput, calls=%fused_computation.15 | convolution fusion | flops 302120960 | bytes 1310720 | tf_op jit(solution)/shard_map/dot_general | solution.py:10
  72.9 6.5 %collective-permute-start.12 = (f32[64,256]{1,0:T(8,128)}, f32[64,256]{1,0:T(8,128)}, u32[]{:S(2)}, u32[]{:S(2)}) collective-permute-start(f32[64,256]{1,0:T(8,128)} %get-tuple-element.18), channel_id=1, source_target_pairs={{0,32},{1,33},{2,34},{3,35},{4,36},{5,37},{6,38},{7,39},{8,40},{9,... | collective-permute-start | bytes 196616 | tf_op jit(solution)/shard_map/ppermute | solution.py:78
  79.4 1.6 %collective-permute-start.14 = (f32[64,256]{1,0:T(8,128)}, f32[64,256]{1,0:T(8,128)}, u32[]{:S(2)}, u32[]{:S(2)}) collective-permute-start(f32[64,256]{1,0:T(8,128)} %get-tuple-element.19), channel_id=1, source_target_pairs={{0,96},{1,97},{2,98},{3,99},{4,100},{5,101},{6,102},{7,103},{8,104... | collective-permute-start | bytes 196616 | tf_op jit(solution)/shard_map/ppermute | solution.py:78
  91.0 3.4 %collective-permute-done.17 = f32[64,256]{1,0:T(8,128)S(1)} collective-permute-done((f32[64,256]{1,0:T(8,128)S(1)}, f32[64,256]{1,0:T(8,128)S(1)}, u32[]{:S(2)}, u32[]{:S(2)}) %collective-permute-start.17) | collective-permute-done | bytes 65568 | tf_op jit(solution)/shard_map/ppermute | solution.py:50
  94.6 6.4 %collective-permute-start.20 = (f32[64,256]{1,0:T(8,128)S(1)}, f32[64,256]{1,0:T(8,128)S(1)}, u32[]{:S(2)}, u32[]{:S(2)}) collective-permute-start(f32[64,256]{1,0:T(8,128)S(1)} %fusion.172), channel_id=1, source_target_pairs={{0,12},{1,13},{2,14},{3,15},{4,8},{5,9},{6,10},{7,11},{8,4},{9,5},... | collective-permute-start | bytes 196616 | tf_op jit(solution)/shard_map/ppermute | solution.py:50
  102.4 2.7 %collective-permute-done.20 = f32[64,256]{1,0:T(8,128)S(1)} collective-permute-done((f32[64,256]{1,0:T(8,128)S(1)}, f32[64,256]{1,0:T(8,128)S(1)}, u32[]{:S(2)}, u32[]{:S(2)}) %collective-permute-start.20) | collective-permute-done | bytes 65568 | tf_op jit(solution)/shard_map/ppermute | solution.py:50
  105.2 5.1 %collective-permute-start.22 = (f32[64,256]{1,0:T(8,128)S(1)}, f32[64,256]{1,0:T(8,128)S(1)}, u32[]{:S(2)}, u32[]{:S(2)}) collective-permute-start(f32[64,256]{1,0:T(8,128)S(1)} %fusion.171), channel_id=1, source_target_pairs={{0,128},{1,129},{2,130},{3,131},{4,132},{5,133},{6,134},{7,135},{8... | collective-permute-start | bytes 196616 | tf_op jit(solution)/shard_map/ppermute | solution.py:50
  112.2 5.1 %collective-permute-done.23 = f32[64,256]{1,0:T(8,128)S(1)} collective-permute-done((f32[64,256]{1,0:T(8,128)S(1)}, f32[64,256]{1,0:T(8,128)S(1)}, u32[]{:S(2)}, u32[]{:S(2)}) %collective-permute-start.23) | collective-permute-done | bytes 65568 | tf_op jit(solution)/shard_map/ppermute | solution.py:50
  117.4 3.3 %collective-permute-start.24 = (f32[64,256]{1,0:T(8,128)S(1)}, f32[64,256]{1,0:T(8,128)S(1)}, u32[]{:S(2)}, u32[]{:S(2)}) collective-permute-start(f32[64,256]{1,0:T(8,128)S(1)} %fusion.170), channel_id=1, source_target_pairs={{0,32},{1,33},{2,34},{3,35},{4,36},{5,37},{6,38},{7,39},{8,40},{9,... | collective-permute-start | bytes 196616 | tf_op jit(solution)/shard_map/ppermute | solution.py:50
  122.6 1.6 %collective-permute-done.25 = f32[64,256]{1,0:T(8,128)S(1)} collective-permute-done((f32[64,256]{1,0:T(8,128)S(1)}, f32[64,256]{1,0:T(8,128)S(1)}, u32[]{:S(2)}, u32[]{:S(2)}) %collective-permute-start.25) | collective-permute-done | bytes 65568 | tf_op jit(solution)/shard_map/ppermute | solution.py:50
  124.3 2.0 %collective-permute-done.26 = f32[64,256]{1,0:T(8,128)S(1)} collective-permute-done((f32[64,256]{1,0:T(8,128)S(1)}, f32[64,256]{1,0:T(8,128)S(1)}, u32[]{:S(2)}, u32[]{:S(2)}) %collective-permute-start.26) | collective-permute-done | bytes 65568 | tf_op jit(solution)/shard_map/ppermute | solution.py:50
  127.1 2.3 %gather_fusion.1 = f32[256]{0:T(256)S(1)} fusion(f32[256,256]{1,0:T(8,128)S(1)} %bitcast.138, s32[256]{0:T(256)S(1)} %bitcast.135), kind=kCustom, calls=%fused_computation.1 | custom fusion | bytes 4096 | tf_op jit(solution)/shard_map/jit(_diag)/jit(diagonal)/cond/branch_0_fun/gather | solution.py:29
  130.1 5.3 %collective-permute-start.11 = (f32[48,256]{1,0:T(8,128)S(1)}, f32[48,256]{1,0:T(8,128)S(1)}, u32[]{:S(2)}, u32[]{:S(2)}) collective-permute-start(f32[48,256]{1,0:T(8,128)S(1)} %bitcast_add_fusion.3), channel_id=1, source_target_pairs={{0,0},{1,8},{2,16},{3,24},{4,32},{5,40},{6,48},{7,56},{8,64},{9,72... | collective-permute-start | bytes 147464 | tf_op jit(solution)/shard_map/ppermute | solution.py:181
  136.5 6.1 %collective-permute-done.11 = f32[48,256]{1,0:T(8,128)S(1)} collective-permute-done((f32[48,256]{1,0:T(8,128)S(1)}, f32[48,256]{1,0:T(8,128)S(1)}, u32[]{:S(2)}, u32[]{:S(2)}) %collective-permute-start.11) | collective-permute-done | bytes 49184 | tf_op jit(solution)/shard_map/ppermute | solution.py:181
  (115 shorter events, 37.0 us)
Async XLA Ops:
  0.7 18.1 %collective-permute-start = (f32[48,256]{1,0:T(8,128)}, f32[48,256]{1,0:T(8,128)S(1)}, u32[]{:S(2)}, u32[]{:S(2)}) collective-permute-start(f32[48,256]{1,0:T(8,128)} %param.7), channel_id=1, source_target_pairs={{0,4},{1,5},{2,6},{3,7},{4,0},{5,1},{6,2},{7,3},{8,12},{9,13},{10,... | collective-permute-start | bytes 147464 | tf_op jit(solution)/shard_map/ppermute | solution.py:50
  6.8 12.0 %collective-permute-start.1 = (f32[48,256]{1,0:T(8,128)}, f32[48,256]{1,0:T(8,128)S(1)}, u32[]{:S(2)}, u32[]{:S(2)}) collective-permute-start(f32[48,256]{1,0:T(8,128)} %param.7), channel_id=1, source_target_pairs={{0,2},{1,3},{2,0},{3,1},{4,6},{5,7},{6,4},{7,5},{8,10},{9,11},{10,... | collective-permute-start | bytes 147464 | tf_op jit(solution)/shard_map/ppermute | solution.py:50
  7.9 10.8 %collective-permute-start.2 = (f32[48,256]{1,0:T(8,128)}, f32[48,256]{1,0:T(8,128)S(1)}, u32[]{:S(2)}, u32[]{:S(2)}) collective-permute-start(f32[48,256]{1,0:T(8,128)} %param.7), channel_id=1, source_target_pairs={{0,6},{1,7},{2,4},{3,5},{4,2},{5,3},{6,0},{7,1},{8,14},{9,15},{10,... | collective-permute-start | bytes 147464 | tf_op jit(solution)/shard_map/ppermute | solution.py:50
  18.9 5.3 %collective-permute-start.3 = (f32[192,256]{1,0:T(8,128)S(1)}, f32[192,256]{1,0:T(8,128)S(1)}, u32[]{:S(2)}, u32[]{:S(2)}) collective-permute-start(f32[192,256]{1,0:T(8,128)S(1)} %get-tuple-element.21), channel_id=1, source_target_pairs={{0,1},{1,0},{2,3},{3,2},{4,5},{5,4},{6,7},{7,6},{8,9},{9,8},{10,11... | collective-permute-start | bytes 589832 | tf_op jit(solution)/shard_map/ppermute | solution.py:50
  24.4 8.7 %collective-permute-start.4 = (f32[384,256]{1,0:T(8,128)S(1)}, f32[384,256]{1,0:T(8,128)S(1)}, u32[]{:S(2)}, u32[]{:S(2)}) collective-permute-start(f32[384,256]{1,0:T(8,128)S(1)} %get-tuple-element.11), channel_id=1, source_target_pairs={{0,8},{1,9},{2,10},{3,11},{4,12},{5,13},{6,14},{7,15},{8,0},{9,1},... | collective-permute-start | bytes 1179656 | tf_op jit(solution)/shard_map/ppermute | solution.py:50
  25.0 16.4 %collective-permute-start.5 = (f32[384,256]{1,0:T(8,128)S(1)}, f32[384,256]{1,0:T(8,128)S(1)}, u32[]{:S(2)}, u32[]{:S(2)}) collective-permute-start(f32[384,256]{1,0:T(8,128)S(1)} %get-tuple-element.11), channel_id=1, source_target_pairs={{0,16},{1,17},{2,18},{3,19},{4,20},{5,21},{6,22},{7,23},{8,24},{9,... | collective-permute-start | bytes 1179656 | tf_op jit(solution)/shard_map/ppermute | solution.py:50
  25.8 15.6 %collective-permute-start.6 = (f32[384,256]{1,0:T(8,128)S(1)}, f32[384,256]{1,0:T(8,128)S(1)}, u32[]{:S(2)}, u32[]{:S(2)}) collective-permute-start(f32[384,256]{1,0:T(8,128)S(1)} %get-tuple-element.11), channel_id=1, source_target_pairs={{0,24},{1,25},{2,26},{3,27},{4,28},{5,29},{6,30},{7,31},{8,16},{9,... | collective-permute-start | bytes 1179656 | tf_op jit(solution)/shard_map/ppermute | solution.py:50
  43.9 25.1 %collective-permute-start.7 = (f32[384,256]{1,0:T(8,128)}, f32[384,256]{1,0:T(8,128)}, u32[]{:S(2)}, u32[]{:S(2)}) collective-permute-start(f32[384,256]{1,0:T(8,128)} %constant_dynamic-slice_fusion), channel_id=1, source_target_pairs={{0,0},{1,1},{2,2},{3,3},{4,35},{5,34},{6,33},{7,32},{8,64},{9,65},... | collective-permute-start | bytes 1179656 | tf_op jit(solution)/shard_map/ppermute | solution.py:169
  72.9 9.0 %collective-permute-start.12 = (f32[64,256]{1,0:T(8,128)}, f32[64,256]{1,0:T(8,128)}, u32[]{:S(2)}, u32[]{:S(2)}) collective-permute-start(f32[64,256]{1,0:T(8,128)} %get-tuple-element.18), channel_id=1, source_target_pairs={{0,32},{1,33},{2,34},{3,35},{4,36},{5,37},{6,38},{7,39},{8,40},{9,... | collective-permute-start | bytes 196616 | tf_op jit(solution)/shard_map/ppermute | solution.py:78
  79.4 5.5 %collective-permute-start.14 = (f32[64,256]{1,0:T(8,128)}, f32[64,256]{1,0:T(8,128)}, u32[]{:S(2)}, u32[]{:S(2)}) collective-permute-start(f32[64,256]{1,0:T(8,128)} %get-tuple-element.19), channel_id=1, source_target_pairs={{0,96},{1,97},{2,98},{3,99},{4,100},{5,101},{6,102},{7,103},{8,104... | collective-permute-start | bytes 196616 | tf_op jit(solution)/shard_map/ppermute | solution.py:78
  85.8 4.8 %collective-permute-start.15 = (f32[64,256]{1,0:T(8,128)S(1)}, f32[64,256]{1,0:T(8,128)S(1)}, u32[]{:S(2)}, u32[]{:S(2)}) collective-permute-start(f32[64,256]{1,0:T(8,128)S(1)} %fusion.111), channel_id=1, source_target_pairs={{0,1},{1,0},{2,3},{3,2},{4,5},{5,4},{6,7},{7,6},{8,9},{9,8},{10,11... | collective-permute-start | bytes 196616 | tf_op jit(solution)/shard_map/ppermute | solution.py:50
  87.8 6.6 %collective-permute-start.17 = (f32[64,256]{1,0:T(8,128)S(1)}, f32[64,256]{1,0:T(8,128)S(1)}, u32[]{:S(2)}, u32[]{:S(2)}) collective-permute-start(f32[64,256]{1,0:T(8,128)S(1)} %fusion.111), channel_id=1, source_target_pairs={{0,3},{1,2},{2,1},{3,0},{4,7},{5,6},{6,5},{7,4},{8,11},{9,10},{10,... | collective-permute-start | bytes 196616 | tf_op jit(solution)/shard_map/ppermute | solution.py:50
  89.5 11.6 %collective-permute-start.8 = (f32[192,256]{1,0:T(8,128)S(1)}, f32[192,256]{1,0:T(8,128)S(1)}, u32[]{:S(2)}, u32[]{:S(2)}) collective-permute-start(f32[192,256]{1,0:T(8,128)S(1)} %dynamic-slice_bitcast_fusion.4), channel_id=1, source_target_pairs={{0,32},{32,0},{64,96},{96,64},{128,160},{160,128},{192,224},{224,1... | collective-permute-start | bytes 589832 | tf_op jit(solution)/shard_map/ppermute | solution.py:78
  94.4 8.0 %collective-permute-start.18 = (f32[64,256]{1,0:T(8,128)S(1)}, f32[64,256]{1,0:T(8,128)S(1)}, u32[]{:S(2)}, u32[]{:S(2)}) collective-permute-start(f32[64,256]{1,0:T(8,128)S(1)} %fusion.172), channel_id=1, source_target_pairs={{0,4},{1,5},{2,6},{3,7},{4,0},{5,1},{6,2},{7,3},{8,12},{9,13},{10,... | collective-permute-start | bytes 196616 | tf_op jit(solution)/shard_map/ppermute | solution.py:50
  94.5 7.9 %collective-permute-start.19 = (f32[64,256]{1,0:T(8,128)S(1)}, f32[64,256]{1,0:T(8,128)S(1)}, u32[]{:S(2)}, u32[]{:S(2)}) collective-permute-start(f32[64,256]{1,0:T(8,128)S(1)} %fusion.172), channel_id=1, source_target_pairs={{0,8},{1,9},{2,10},{3,11},{4,12},{5,13},{6,14},{7,15},{8,0},{9,1},... | collective-permute-start | bytes 196616 | tf_op jit(solution)/shard_map/ppermute | solution.py:50
  94.6 10.4 %collective-permute-start.20 = (f32[64,256]{1,0:T(8,128)S(1)}, f32[64,256]{1,0:T(8,128)S(1)}, u32[]{:S(2)}, u32[]{:S(2)}) collective-permute-start(f32[64,256]{1,0:T(8,128)S(1)} %fusion.172), channel_id=1, source_target_pairs={{0,12},{1,13},{2,14},{3,15},{4,8},{5,9},{6,10},{7,11},{8,4},{9,5},... | collective-permute-start | bytes 196616 | tf_op jit(solution)/shard_map/ppermute | solution.py:50
  101.2 21.3 %collective-permute-start.9 = (f32[96,256]{1,0:T(8,128)S(1)}, f32[96,256]{1,0:T(8,128)S(1)}, u32[]{:S(2)}, u32[]{:S(2)}) collective-permute-start(f32[96,256]{1,0:T(8,128)S(1)} %dynamic-slice_bitcast_fusion.5), channel_id=1, source_target_pairs={{0,64},{32,96},{64,0},{96,32},{128,192},{160,224},{192,128},{224,1... | collective-permute-start | bytes 294920 | tf_op jit(solution)/shard_map/ppermute | solution.py:78
  105.1 5.8 %collective-permute-start.21 = (f32[64,256]{1,0:T(8,128)S(1)}, f32[64,256]{1,0:T(8,128)S(1)}, u32[]{:S(2)}, u32[]{:S(2)}) collective-permute-start(f32[64,256]{1,0:T(8,128)S(1)} %fusion.171), channel_id=1, source_target_pairs={{0,16},{1,17},{2,18},{3,19},{4,20},{5,21},{6,22},{7,23},{8,24},{9,... | collective-permute-start | bytes 196616 | tf_op jit(solution)/shard_map/ppermute | solution.py:50
  105.2 7.0 %collective-permute-start.22 = (f32[64,256]{1,0:T(8,128)S(1)}, f32[64,256]{1,0:T(8,128)S(1)}, u32[]{:S(2)}, u32[]{:S(2)}) collective-permute-start(f32[64,256]{1,0:T(8,128)S(1)} %fusion.171), channel_id=1, source_target_pairs={{0,128},{1,129},{2,130},{3,131},{4,132},{5,133},{6,134},{7,135},{8... | collective-permute-start | bytes 196616 | tf_op jit(solution)/shard_map/ppermute | solution.py:50
  110.3 7.0 %collective-permute-start.23 = (f32[64,256]{1,0:T(8,128)S(1)}, f32[64,256]{1,0:T(8,128)S(1)}, u32[]{:S(2)}, u32[]{:S(2)}) collective-permute-start(f32[64,256]{1,0:T(8,128)S(1)} %fusion.171), channel_id=1, source_target_pairs={{0,144},{1,145},{2,146},{3,147},{4,148},{5,149},{6,150},{7,151},{8... | collective-permute-start | bytes 196616 | tf_op jit(solution)/shard_map/ppermute | solution.py:50
  117.4 5.2 %collective-permute-start.24 = (f32[64,256]{1,0:T(8,128)S(1)}, f32[64,256]{1,0:T(8,128)S(1)}, u32[]{:S(2)}, u32[]{:S(2)}) collective-permute-start(f32[64,256]{1,0:T(8,128)S(1)} %fusion.170), channel_id=1, source_target_pairs={{0,32},{1,33},{2,34},{3,35},{4,36},{5,37},{6,38},{7,39},{8,40},{9,... | collective-permute-start | bytes 196616 | tf_op jit(solution)/shard_map/ppermute | solution.py:50
  121.9 4.4 %collective-permute-start.26 = (f32[64,256]{1,0:T(8,128)S(1)}, f32[64,256]{1,0:T(8,128)S(1)}, u32[]{:S(2)}, u32[]{:S(2)}) collective-permute-start(f32[64,256]{1,0:T(8,128)S(1)} %fusion.170), channel_id=1, source_target_pairs={{0,96},{1,97},{2,98},{3,99},{4,100},{5,101},{6,102},{7,103},{8,104... | collective-permute-start | bytes 196616 | tf_op jit(solution)/shard_map/ppermute | solution.py:50
  122.5 7.6 %collective-permute-start.10 = (f32[48,256]{1,0:T(8,128)S(1)}, f32[48,256]{1,0:T(8,128)S(1)}, u32[]{:S(2)}, u32[]{:S(2)}) collective-permute-start(f32[48,256]{1,0:T(8,128)S(1)} %dynamic-slice_bitcast_fusion.13), channel_id=1, source_target_pairs={{0,128},{32,160},{64,192},{96,224},{128,0},{160,32},{192,64},{224,... | collective-permute-start | bytes 147464 | tf_op jit(solution)/shard_map/ppermute | solution.py:78
  130.1 12.4 %collective-permute-start.11 = (f32[48,256]{1,0:T(8,128)S(1)}, f32[48,256]{1,0:T(8,128)S(1)}, u32[]{:S(2)}, u32[]{:S(2)}) collective-permute-start(f32[48,256]{1,0:T(8,128)S(1)} %bitcast_add_fusion.3), channel_id=1, source_target_pairs={{0,0},{1,8},{2,16},{3,24},{4,32},{5,40},{6,48},{7,56},{8,64},{9,72... | collective-permute-start | bytes 147464 | tf_op jit(solution)/shard_map/ppermute | solution.py:181
  (12 other events, 163.4 us)
